TPU v7x, 32 devices: a whole 2x2x4 slice. The times are simulated.
32 devices in a mesh: dp: 8 (over y, x, core), tensor: 4 (over z).
Axes of the slice: x: 2, y: 2, z: 4, core: 2. Of those that a mesh axis runs over, the one named last changes fastest.
Arguments:
- tokens: bfloat16 [16384, 768], P(('dp', 'tensor')), may hold values from -6 to 6
- out_grad: bfloat16 [16384, 768], P(('dp', 'tensor')), may hold values from -6 to 6
- lengths: int32 [32], P('dp'), may hold values from 20 to 512, as said below
- qkv_weight: bfloat16 [3, 768, 768], P(None, None, 'tensor'), may hold values from -0.21875 to 0.21875
- qkv_bias: bfloat16 [2, 768], P(None, 'tensor'), may hold values from -3 to 3
- out_weight: bfloat16 [768, 768], P('tensor'), may hold values from -1.75 to 1.75
- out_bias: float32 [768], replicated, may hold values from -3 to 3
- norm1_gain: float32 [768], replicated, may hold values from 0.5 to 1.5
- norm1_shift: float32 [768], replicated, may hold values from -3 to 3
- up_weight: bfloat16 [768, 3072], P(None, 'tensor'), may hold values from -0.21875 to 0.21875
- up_bias: bfloat16 [3072], P('tensor'), may hold values from -3 to 3
- down_weight: bfloat16 [3072, 768], P('tensor'), may hold values from -0.109375 to 0.109375
- down_bias: float32 [768], replicated, may hold values from -3 to 3
- norm2_gain: float32 [768], replicated, may hold values from 0.5 to 1.5
- norm2_shift: float32 [768], replicated, may hold values from -3 to 3
Outputs:
- layer_out: bfloat16 [16384, 768], P(('dp', 'tensor'))
- input_grad: bfloat16 [16384, 768], P(('dp', 'tensor'))
- grad_qkv_weight: float32 [3, 768, 768], P(None, None, 'tensor')
- grad_qkv_bias: float32 [2, 768], P(None, 'tensor')
- grad_out_weight: float32 [768, 768], P('tensor')
- grad_out_bias: float32 [768], replicated
- grad_norm1_gain: float32 [768], replicated
- grad_norm1_shift: float32 [768], replicated
- grad_up_weight: float32 [768, 3072], P(None, 'tensor')
- grad_up_bias: float32 [3072], P('tensor')
- grad_down_weight: float32 [3072, 768], P('tensor')
- grad_down_bias: float32 [768], replicated
- grad_norm2_gain: float32 [768], replicated
- grad_norm2_shift: float32 [768], replicated
Inputs may be any that keep to these rules, and one draw needn't show every extreme that they name: Keys at positions lengths[p] and beyond of passage p are padding; some passage has exactly 512 and some exactly 20.
All inputs are finite; a program needn't handle non-finite values.
Results may differ from a plain program's by a relative error of at most 0.02.
Values may be sent and summed in bfloat16 or wider, within the bound.
No kernel may reach another device: no remote copies, remote signals or barrier semaphores. Data moves between devices by JAX's collectives and lax.ppermute only.
A program may use at most 128 MiB of HBM per device.

v0:
```python
import jax
import jax.numpy as jnp
from jax import lax
from jax.sharding import PartitionSpec as P

HD = 64
LEN = 512


EPS = 1e-12
NEG = -1e30


def layer_norm(values, gain_vec, shift_vec):
    center = values - jnp.mean(values, axis=-1, keepdims=True)
    spread = jnp.mean(center * center, axis=-1, keepdims=True)
    return center * lax.rsqrt(spread + EPS) * gain_vec + shift_vec


def gelu_exact(values):
    return jax.nn.gelu(values, approximate=False)


def contract(left, right, left_dim, right_dim):
    return lax.dot_general(
        left, right, (((left_dim,), (right_dim,)), ((), ())), preferred_element_type=jnp.float32
    )


def passage_scores(query_one, key_one, usable_one, factor):
    scores = (
        jnp.einsum("qhe,khe->hqk", query_one, key_one, preferred_element_type=jnp.float32) * factor
    )
    return jnp.where(usable_one[None, None, :], scores, NEG)


def attend_forward(queries, key_rows, value_rows, usable):
    factor = queries.shape[-1] ** (-0.5)

    def single(inputs):
        query_one, key_one, value_one, usable_one = inputs
        scores = passage_scores(query_one, key_one, usable_one, factor)
        log_total = jax.nn.logsumexp(scores, axis=-1, keepdims=True)
        attn_probs = jnp.exp(scores - log_total).astype(jnp.bfloat16)
        context = jnp.einsum(
            "hqk,khe->qhe", attn_probs, value_one, preferred_element_type=jnp.float32
        )
        return (context, log_total)

    return lax.map(single, (queries, key_rows, value_rows, usable))


def attend_backward(queries, key_rows, value_rows, usable, log_totals, context_grad):
    factor = queries.shape[-1] ** (-0.5)

    def single(inputs):
        query_one, key_one, value_one, usable_one, log_one, grad_one = inputs
        scores = passage_scores(query_one, key_one, usable_one, factor)
        attn_probs = jnp.exp(scores - log_one)
        prob_grad = jnp.einsum(
            "qhe,khe->hqk", grad_one, value_one, preferred_element_type=jnp.float32
        )
        row_dot = jnp.sum(prob_grad * attn_probs, axis=-1, keepdims=True)
        score_grad = (attn_probs * (prob_grad - row_dot)).astype(jnp.bfloat16)
        query_grad = (
            jnp.einsum("hqk,khe->qhe", score_grad, key_one, preferred_element_type=jnp.float32)
            * factor
        )
        key_grad = (
            jnp.einsum("hqk,qhe->khe", score_grad, query_one, preferred_element_type=jnp.float32)
            * factor
        )
        value_grad = jnp.einsum(
            "hqk,qhe->khe",
            attn_probs.astype(jnp.bfloat16),
            grad_one,
            preferred_element_type=jnp.float32,
        )
        return (query_grad, key_grad, value_grad)

    return lax.map(single, (queries, key_rows, value_rows, usable, log_totals, context_grad))


def per_device(
    tokens,
    out_grad,
    lengths,
    qkv_weight,
    qkv_bias,
    out_weight,
    out_bias,
    norm1_gain,
    norm1_shift,
    up_weight,
    up_bias,
    down_weight,
    down_bias,
    norm2_gain,
    norm2_shift,
):
    own_tokens = tokens.astype(jnp.float32)
    attn_rows = lax.all_gather(tokens, "tensor", axis=0, tiled=True)
    attn_weight, attn_bias, proj_out = (qkv_weight, qkv_bias, out_weight)
    row_total = attn_rows.shape[0]
    width = attn_weight.shape[2]
    four_dims = (row_total // LEN, LEN, width // HD, HD)
    usable = jnp.arange(LEN, dtype=jnp.int32)[None, :] < lengths[:, None]
    projected = jnp.einsum(
        "rd,tde->tre", attn_rows, attn_weight, preferred_element_type=jnp.float32
    )
    queries = (projected[0] + attn_bias[0]).astype(jnp.bfloat16).reshape(four_dims)
    key_rows = projected[1].astype(jnp.bfloat16).reshape(four_dims)
    value_rows = (projected[2] + attn_bias[1]).astype(jnp.bfloat16).reshape(four_dims)
    context, log_totals = attend_forward(queries, key_rows, value_rows, usable)
    context_low = context.reshape(row_total, width).astype(jnp.bfloat16)
    attn_out = lax.psum_scatter(
        jnp.dot(context_low, proj_out, preferred_element_type=jnp.float32).astype(jnp.bfloat16),
        "tensor",
        scatter_dimension=0,
        tiled=True,
    ).astype(jnp.float32)
    middle, norm1_back = jax.vjp(
        layer_norm, own_tokens + attn_out + out_bias, norm1_gain, norm1_shift
    )
    middle_low = middle.astype(jnp.bfloat16)
    ffn_rows = lax.all_gather(middle_low, "tensor", axis=0, tiled=True)
    ffn_up, ffn_up_bias, ffn_down = (up_weight, up_bias, down_weight)
    pre_act = jnp.dot(ffn_rows, ffn_up, preferred_element_type=jnp.float32) + ffn_up_bias
    activated, gelu_back = jax.vjp(gelu_exact, pre_act)
    hidden = activated.astype(jnp.bfloat16)
    ffn_out = lax.psum_scatter(
        jnp.dot(hidden, ffn_down, preferred_element_type=jnp.float32).astype(jnp.bfloat16),
        "tensor",
        scatter_dimension=0,
        tiled=True,
    ).astype(jnp.float32)
    layer_out, norm2_back = jax.vjp(
        layer_norm, middle + ffn_out + down_bias, norm2_gain, norm2_shift
    )
    second_grad, grad_norm2_gain, grad_norm2_shift = norm2_back(out_grad.astype(jnp.float32))
    branch_grad = second_grad.astype(jnp.bfloat16)
    grad_down_bias = jnp.sum(branch_grad, axis=0, dtype=jnp.float32)
    branch_rows = lax.all_gather(branch_grad, "tensor", axis=0, tiled=True)
    hidden_grad = contract(branch_rows, ffn_down, 1, 1)
    grad_down_weight = contract(hidden, branch_rows, 0, 0)
    pre_grad = gelu_back(hidden_grad)[0].astype(jnp.bfloat16)
    grad_up_bias = jnp.sum(pre_grad, axis=0, dtype=jnp.float32)
    grad_up_weight = contract(ffn_rows, pre_grad, 0, 0)
    middle_part = lax.psum_scatter(
        contract(pre_grad, ffn_up, 1, 1).astype(jnp.bfloat16),
        "tensor",
        scatter_dimension=0,
        tiled=True,
    ).astype(jnp.float32)
    first_grad, grad_norm1_gain, grad_norm1_shift = norm1_back(second_grad + middle_part)
    attn_grad = first_grad.astype(jnp.bfloat16)
    grad_out_bias = jnp.sum(attn_grad, axis=0, dtype=jnp.float32)
    attn_grad_rows = lax.all_gather(attn_grad, "tensor", axis=0, tiled=True)
    context_grad = contract(attn_grad_rows, proj_out, 1, 1).astype(jnp.bfloat16).reshape(four_dims)
    grad_out_weight = contract(context_low, attn_grad_rows, 0, 0)
    query_grad, key_grad, value_grad = attend_backward(
        queries, key_rows, value_rows, usable, log_totals, context_grad
    )
    proj_grad = (
        jnp.stack([query_grad, key_grad, value_grad])
        .reshape(3, row_total, width)
        .astype(jnp.bfloat16)
    )
    grad_qkv_bias = jnp.sum(proj_grad[0::2], axis=1, dtype=jnp.float32)
    grad_qkv_weight = jnp.einsum(
        "rd,tre->tde", attn_rows, proj_grad, preferred_element_type=jnp.float32
    )
    input_part = lax.psum_scatter(
        jnp.einsum(
            "tre,tde->rd", proj_grad, attn_weight, preferred_element_type=jnp.float32
        ).astype(jnp.bfloat16),
        "tensor",
        scatter_dimension=0,
        tiled=True,
    ).astype(jnp.float32)
    input_grad = (first_grad + input_part).astype(jnp.bfloat16)
    (
        grad_qkv_weight,
        grad_qkv_bias,
        grad_out_weight,
        grad_up_weight,
        grad_up_bias,
        grad_down_weight,
    ) = lax.psum(
        (
            grad_qkv_weight,
            grad_qkv_bias,
            grad_out_weight,
            grad_up_weight,
            grad_up_bias,
            grad_down_weight,
        ),
        "dp",
    )
    (
        grad_out_bias,
        grad_norm1_gain,
        grad_norm1_shift,
        grad_down_bias,
        grad_norm2_gain,
        grad_norm2_shift,
    ) = lax.psum(
        (
            grad_out_bias,
            grad_norm1_gain,
            grad_norm1_shift,
            grad_down_bias,
            grad_norm2_gain,
            grad_norm2_shift,
        ),
        ("dp", "tensor"),
    )
    return (
        layer_out.astype(jnp.bfloat16),
        input_grad,
        grad_qkv_weight,
        grad_qkv_bias,
        grad_out_weight,
        grad_out_bias,
        grad_norm1_gain,
        grad_norm1_shift,
        grad_up_weight,
        grad_up_bias,
        grad_down_weight,
        grad_down_bias,
        grad_norm2_gain,
        grad_norm2_shift,
    )


def solution(mesh):
    placed = (
        P(("dp", "tensor"), None),
        P(("dp", "tensor"), None),
        P("dp"),
        P(None, None, "tensor"),
        P(None, "tensor"),
        P("tensor", None),
        P(),
        P(),
        P(),
        P(None, "tensor"),
        P("tensor"),
        P("tensor", None),
        P(),
        P(),
        P(),
    )
    return jax.shard_map(
        per_device,
        mesh=mesh,
        in_specs=placed,
        out_specs=(
            P(("dp", "tensor"), None),
            P(("dp", "tensor"), None),
            P(None, None, "tensor"),
            P(None, "tensor"),
            P("tensor", None),
            P(),
            P(),
            P(),
            P(None, "tensor"),
            P("tensor"),
            P("tensor", None),
            P(),
            P(),
            P(),
        ),
        check_vma=False,
    )
```

profile of v0, /device:TPU:0, one launch (start us, length us, event | category | flops | bytes accessed | tf_op | source)
XLA Modules:
  0.0 806.8 jit_solution(15675778311328545606)
XLA Ops:
  9.7 66.1 %all-gather.5.cloned.1.call-done = bf16[2048,768]{1,0:T(8,128)(2,1)} async-done(((bf16[512,768]{1,0:T(8,128)(2,1)}), bf16[2048,768]{1,0:T(8,128)(2,1)}) %all-gather.5.cloned.1.call-update) | async-done | bytes 3145744 | tf_op jit(solution)/shard_map/all_gather | solution.py:102
  75.8 4.2 convolution_bitcast_fusion
  80.0 2.0 fusion.79
  82.1 2.4 squeeze.36
  84.5 3.1 squeeze.37
  89.1 2.2 copy.47
  91.2 3.6 fusion.64
  94.9 19.9 %while.26 = (s32[]{:T(128)}, bf16[4,512,3,64]{1,3,2,0:T(8,128)(2,1)S(1)}, f32[4,3,512,1]{2,1,3,0:T(4,128)}, bf16[4,512,3,64]{1,3,2,0:T(8,128)(2,1)}, pred[4,512]...) while((s32[]{:T(128)}, ...), condition=%wide.region_3.4_spmd, body=%wide.region_0.3_spmd.sunk | while | flops 209989632 | bytes 10503257 | solution.py:50
  94.9 1.8 fusion.124
  98.0 1.8 fusion.126
  99.9 1.8 fusion.124
  103.0 1.8 fusion.126
  104.8 1.8 fusion.124
  108.0 1.8 fusion.126
  109.8 1.8 fusion.124
  112.9 1.8 fusion.126
  115.7 2.7 convolution_convert_fusion.2
  118.5 59.2 %reduce-scatter.5.cloned.1.call-done = bf16[512,768]{1,0:T(8,128)(2,1)} async-done(((bf16[2048,768]{1,0:T(8,128)(2,1)}), bf16[512,768]{1,0:T(8,128)(2,1)}) %reduce-scatter.5.cloned.1.call-update) | async-done | bytes 786448 | tf_op jit(solution)/shard_map/reduce_scatter | solution.py:116
  179.2 1.6 multiply_reduce_fusion.4
  182.0 2.0 fusion.71
  185.6 61.9 %all-gather.7.cloned.1.call-done = bf16[2048,768]{1,0:T(8,128)(2,1)} async-done(((bf16[512,768]{1,0:T(8,128)(2,1)}), bf16[2048,768]{1,0:T(8,128)(2,1)}) %all-gather.7.cloned.1.call-update) | async-done | bytes 3145744 | tf_op jit(solution)/shard_map/all_gather | solution.py:126
  247.5 18.4 %multiply_convert_fusion.1 = (bf16[2048,768]{1,0:T(8,128)(2,1)S(1)}, f32[2048,768]{1,0:T(8,128)}, f32[2048,768]{1,0:T(8,128)}) fusion(f32[768]{0:T(1024)} %convert_element_type.111, bf16[2048,768]{1,0:T(8,128)(2,1)} %all-gather.7.cloned.1.call-done, bf16[768,768]{1,0:T(8,128)(2,1)S(1)} %copy-done), kind=kOutput, calls=%fused_computation.66 | convolution fusion | flops 2519728128 | bytes 20057088 | tf_op jit(solution)/shard_map/dot_general | solution.py:128
  265.9 1.7 copy-done.38
  267.6 4.0 convolution_convert_fusion.1
  271.6 59.2 %reduce-scatter.7.cloned.1.call-done = bf16[512,768]{1,0:T(8,128)(2,1)} async-done(((bf16[2048,768]{1,0:T(8,128)(2,1)}), bf16[512,768]{1,0:T(8,128)(2,1)}) %reduce-scatter.7.cloned.1.call-update) | async-done | bytes 786448 | tf_op jit(solution)/shard_map/reduce_scatter | solution.py:131
  330.8 2.0 fusion.77
  333.1 2.0 fusion.63
  335.1 2.3 fusion.76
  338.6 1.7 convert_reduce_fusion.3
  340.8 63.0 %all-gather.9.cloned.1.call-done = bf16[2048,768]{1,0:T(8,128)(2,1)} async-done(((bf16[512,768]{1,0:T(8,128)(2,1)}), bf16[2048,768]{1,0:T(8,128)(2,1)}) %all-gather.9.cloned.1.call-update) | async-done | bytes 3145744 | tf_op jit(solution)/shard_map/all_gather | solution.py:143
  403.8 11.0 %convert_reduce_fusion = (f32[768]{0:T(1024)}, bf16[2048,768]{1,0:T(8,128)(2,1)S(1)}) fusion(f32[2048,768]{1,0:T(8,128)} %get-tuple-element.212, f32[2048,768]{1,0:T(8,128)} %get-tuple-element.220, f32[768]{0:T(1024)} %convert_element_type.111, bf16[2048,768]{1,0:T(8,128)(2,1)} %all-gather.9.cloned.1.call-done, bf16[768,768]{1,0:T(8,128)(2,1)} %param.30), kind=kOutput, calls=%fused_computation.64 | convolution fusion | flops 2442657024 | bytes 20060160 | tf_op jit(solution)/shard_map/dot_general | solution.py:25
  414.8 1.7 copy-done.39
  416.5 4.0 convolution_convert_fusion
  420.6 59.2 %reduce-scatter.9.cloned.1.call-done = bf16[512,768]{1,0:T(8,128)(2,1)} async-done(((bf16[2048,768]{1,0:T(8,128)(2,1)}), bf16[512,768]{1,0:T(8,128)(2,1)}) %reduce-scatter.9.cloned.1.call-update) | async-done | bytes 786448 | tf_op jit(solution)/shard_map/reduce_scatter | solution.py:149
  479.7 3.3 multiply_reduce_fusion.1
  483.1 2.4 fusion.75
  488.1 63.3 %all-gather.11.cloned.1.call-done = bf16[2048,768]{1,0:T(8,128)(2,1)} async-done(((bf16[512,768]{1,0:T(8,128)(2,1)}), bf16[2048,768]{1,0:T(8,128)(2,1)}) %all-gather.11.cloned.1.call-update) | async-done | bytes 3145744 | tf_op jit(solution)/shard_map/all_gather | solution.py:158
  551.4 3.1 convolution_convert_fusion.3
  558.0 42.5 %while.27 = (s32[]{:T(128)}, bf16[4,512,3,64]{1,3,2,0:T(8,128)(2,1)}, bf16[4,512,3,64]{1,3,2,0:T(8,128)(2,1)}, bf16[4,512,3,64]{1,3,2,0:T(8,128)(2,1)}, bf16[4,5...) while((s32[]{:T(128)}, ...), condition=%wide.region_17.18_spmd, body=%wide.region_15.17_spmd.sunk | while | flops 510589440 | bytes 38769380 | solution.py:81
  558.7 1.9 subtract_exponential_fusion.2
  560.7 1.6 multiply_reduce_fusion.6
  564.9 1.5 fusion.136
  569.4 1.9 subtract_exponential_fusion.2
  571.3 1.6 multiply_reduce_fusion.6
  575.6 1.5 fusion.136
  580.0 1.9 subtract_exponential_fusion.2
  582.0 1.6 multiply_reduce_fusion.6
  586.2 1.5 fusion.136
  590.6 1.9 subtract_exponential_fusion.2
  592.6 1.6 multiply_reduce_fusion.6
  596.8 1.5 fusion.136
  600.6 1.8 copy.51
  605.1 1.7 copy.53
  609.4 6.2 bitcast_convert_fusion
  615.9 7.1 fusion.82
  623.0 4.2 fusion.81
  627.2 1.7 fusion.80
  628.9 3.2 fusion.66
  632.8 43.4 %all-reduce = (f32[768]{0:T(1024)}, f32[768]{0:T(1024)}, f32[768]{0:T(1024)}, f32[768]{0:T(1024)}, f32[768]{0:T(1024)}, /*index=5*/f32[768]{0:T(1024)}) all-reduce(f32[768]{0:T(1024)S(1)} %get-tuple-element.201, f32[768]{0:T(1024)S(1)} %copy-done.32, f32[768]{0:T(1024)S(1)} %copy-done.33, ...), channel_id=1, replica_groups=mesh['dp'=8,'tensor'=4] {'dp','tensor'}, use_global_device_ids=true, to_apply=%region_24.25 | all-reduce | flops 4608 | bytes 36864 | tf_op jit(solution)/shard_map/psum | solution.py:207
  676.3 1.7 convert_reduce_fusion.1
  678.0 14.4 %all-reduce.1 = (f32[2,192]{1,0:T(2,128)}, f32[768]{0:T(1024)}) all-reduce(f32[2,192]{1,0:T(2,128)S(1)} %convert_reduce_fusion.1, f32[768]{0:T(1024)S(1)} %copy-done.34), channel_id=1, replica_groups=mesh['dp'=8,'tensor'=4] {'dp'}, use_global_device_ids=true, to_apply=%region_21.22 | all-reduce | flops 1152 | bytes 9216 | tf_op jit(solution)/shard_map/psum | solution.py:189
  692.3 2.3 add_convert_fusion.1
  694.6 98.8 %all-reduce.5.cloned.1.call-done = (f32[3,768,192]{1,2,0:T(8,128)}, f32[192,768]{1,0:T(8,128)}, f32[768,768]{1,0:T(8,128)}, f32[768,768]{1,0:T(8,128)}) async-done(((f32[3,768,192]{1,2,0:T(8,128)}, f32[192,768]{1,0:T(8,128)}, f32[768,768]{1,0:T(8,128)}, f32[768,768]{1,0:T(8,128)}), (f32[3,768,192]{1,2,0:T(8,128)}, f32[192,768]{1,0:T(8,128)}, f32[768,768]{1,0:T(8,128)}, ...) | async-done | bytes 7077904 | tf_op jit(solution)/shard_map/psum | solution.py:189
  793.4 2.9 copy.99
  (200 shorter events, 55.1 us)
Async XLA Ops:
  7.2 240.3 %copy-start = (bf16[768,768]{1,0:T(8,128)(2,1)S(1)}, bf16[768,768]{1,0:T(8,128)(2,1)}, u32[]{:S(2)}) copy-start(bf16[768,768]{1,0:T(8,128)(2,1)} %param.28) | copy-start | bytes 3538948
  7.2 68.6 %all-gather.5.cloned.1.call-start = ((), (), s32[]{:S(2)}) async-start(), calls=%async_computation.4 | async-start | bytes 3932160 | tf_op jit(solution)/shard_map/all_gather | solution.py:102
  7.9 169.7 %reduce-scatter.5.cloned.1.call-start = ((), (), s32[]{:S(2)}) async-start(), calls=%async_computation.5 | async-start | bytes 3932160 | tf_op jit(solution)/shard_map/reduce_scatter | solution.py:116
  114.7 1.0 copy-start.19
  118.4 59.2 %copy-start.2 = (bf16[512,768]{1,0:T(8,128)(2,1)S(1)}, bf16[512,768]{1,0:T(8,128)(2,1)}, u32[]{:S(2)}) copy-start(bf16[512,768]{1,0:T(8,128)(2,1)} %param.19) | copy-start | bytes 2359300
  118.4 59.2 %copy-start.21 = (f32[768]{0:T(1024)S(1)}, f32[768]{0:T(1024)}, u32[]{:S(2)}) copy-start(f32[768]{0:T(1024)} %param.25) | copy-start | bytes 9220
  118.4 63.5 %copy-start.22 = (f32[768]{0:T(1024)S(1)}, f32[768]{0:T(1024)}, u32[]{:S(2)}) copy-start(f32[768]{0:T(1024)} %param.26) | copy-start | bytes 9220
  118.4 129.1 %all-gather.7.cloned.1.call-start = ((), (), s32[]{:S(2)}) async-start(), calls=%async_computation.6 | async-start | bytes 3932160 | tf_op jit(solution)/shard_map/all_gather | solution.py:126
  177.7 4.3 copy-start.3
  180.8 0.6 copy-start.27
  181.4 0.6 copy-start.23
  184.0 146.8 %reduce-scatter.7.cloned.1.call-start = ((), (), s32[]{:S(2)}) async-start(), calls=%async_computation.7 | async-start | bytes 3932160 | tf_op jit(solution)/shard_map/reduce_scatter | solution.py:131
  247.5 20.1 %copy-start.37 = (bf16[768,768]{1,0:T(8,128)(2,1)S(1)}, bf16[768,768]{1,0:T(8,128)(2,1)}, u32[]{:S(2)}) copy-start(bf16[768,768]{1,0:T(8,128)(2,1)} %param.30) | copy-start | bytes 3538948
  265.9 1.7 copy-start.38
  271.6 132.2 %all-gather.9.cloned.1.call-start = ((), (), s32[]{:S(2)}) async-start(), calls=%async_computation.8 | async-start | bytes 3932160 | tf_op jit(solution)/shard_map/all_gather | solution.py:143
  330.8 2.3 copy-start.8
  337.4 1.1 copy-start.4
  337.4 2.8 copy-start.25
  340.3 139.5 %reduce-scatter.9.cloned.1.call-start = ((), (), s32[]{:S(2)}) async-start(), calls=%async_computation.9 | async-start | bytes 3932160 | tf_op jit(solution)/shard_map/reduce_scatter | solution.py:149
  414.8 1.7 copy-start.39
  420.5 59.2 %copy-start.24 = (f32[512]{0:T(512)S(1)}, f32[512]{0:T(512)}, u32[]{:S(2)}) copy-start(f32[512]{0:T(512)} %copy-done.23) | copy-start | bytes 6148
  420.5 59.2 %copy-start.26 = (f32[512]{0:T(512)S(1)}, f32[512]{0:T(512)}, u32[]{:S(2)}) copy-start(f32[512]{0:T(512)} %copy-done.25) | copy-start | bytes 6148
  420.5 62.5 %copy-start.28 = (f32[512]{0:T(512)S(1)}, f32[512]{0:T(512)}, u32[]{:S(2)}) copy-start(f32[512]{0:T(512)} %copy-done.27) | copy-start | bytes 6148
  420.5 130.8 %all-gather.11.cloned.1.call-start = ((), (), s32[]{:S(2)}) async-start(), calls=%async_computation.10 | async-start | bytes 3932160 | tf_op jit(solution)/shard_map/all_gather | solution.py:158
  479.7 3.3 copy-start.14
  483.1 68.3 %copy-start.20 = (bf16[192,768]{1,0:T(8,128)(2,1)S(1)}, bf16[192,768]{1,0:T(8,128)(2,1)}, u32[]{:S(2)}) copy-start(bf16[192,768]{1,0:T(8,128)(2,1)} %param.24) | copy-start | bytes 884740
  485.5 1.2 copy-start.5
  487.9 204.5 %reduce-scatter.11.cloned.1.call-start = ((), (), s32[]{:S(2)}) async-start(), calls=%async_computation.11 | async-start | bytes 3932160 | tf_op jit(solution)/shard_map/reduce_scatter | solution.py:173
  562.3 1.1 copy-start.11
  562.3 2.7 copy-start.9
  564.9 2.5 copy-start.12
  566.5 0.9 copy-start.10
  572.9 1.1 copy-start.11
  572.9 2.7 copy-start.9
  575.5 2.5 copy-start.12
  577.1 0.9 copy-start.10
  583.5 1.1 copy-start.11
  583.5 2.7 copy-start.9
  586.2 2.5 copy-start.12
  587.8 0.9 copy-start.10
  594.2 1.1 copy-start.11
  594.2 2.7 copy-start.9
  596.8 2.5 copy-start.12
  598.4 0.9 copy-start.10
  600.6 3.4 copy-start.13
  615.6 177.8 %all-reduce.5.cloned.1.call-start = ((), (), s32[]{:S(2)}) async-start(), calls=%async_computation.12 | async-start | bytes 14155776 | tf_op jit(solution)/shard_map/psum | solution.py:189
  615.9 7.1 copy-start.36
  615.9 7.1 copy-start.40
  623.0 4.2 copy-start.7
  623.0 5.8 copy-start.35
  627.2 1.7 copy-start.15
  632.1 0.7 copy-start.29
  632.1 0.7 copy-start.30
  632.1 0.7 copy-start.31
  632.1 0.7 copy-start.32
  632.1 0.7 copy-start.33
  632.1 45.9 %copy-start.34 = (f32[768]{0:T(1024)S(1)}, f32[768]{0:T(1024)}, u32[]{:S(2)}) copy-start(f32[768]{0:T(1024)} %get-tuple-element.203) | copy-start | bytes 9220
  632.1 60.2 %copy-start.6 = (f32[512,768]{1,0:T(8,128)S(1)}, f32[512,768]{1,0:T(8,128)}, u32[]{:S(2)}) copy-start(f32[512,768]{1,0:T(8,128)} %copy-done.5) | copy-start | bytes 4718596
  793.4 3.0 copy-start.18
  793.4 3.8 copy-start.17
  796.4 2.2 copy-start.16
  797.2 2.8 copy-start.1
Sparse Core Ops, SparseCore 0:
  9.6 66.1 all-gather.4
  118.6 59.0 reduce-scatter.4
  184.1 63.3 all-gather.6
  271.7 59.0 reduce-scatter.6
  340.4 63.3 all-gather.8
  420.6 59.0 reduce-scatter.8
  488.0 63.3 all-gather.10
  615.8 60.0 reduce-scatter.10
  680.7 112.6 all-reduce.4
where the time goes:
time: 817 us; the launch traced here: 807 us
  waiting for transfers between devices  531 us (65%)
  matrix products  115 us (14%)
  blocking collectives  57.8 us (7%)
  local copies, waits for them, and re-layouts  46.6 us (6%)
  other arithmetic  39.4 us (5%)
  between operations  14.4 us (2%)
    psum x1, waiting for transfers between devices, per_device(): lax.psum((grad_qkv_weight, grad_qkv_bias, grad_out_weight, grad_up_weight...  98.8 us
    all_gather x1, waiting for transfers between devices, per_device(): attn_rows = lax.all_gather(tokens, 'tensor', axis=0, tiled=True)  66.1 us
    all_gather x1, waiting for transfers between devices, per_device(): attn_grad_rows = lax.all_gather(attn_grad, 'tensor', axis=0, tiled=True)  63.3 us
    all_gather x1, waiting for transfers between devices, per_device(): branch_rows = lax.all_gather(branch_grad, 'tensor', axis=0, tiled=True)  63 us
    all_gather x1, waiting for transfers between devices, per_device(): ffn_rows = lax.all_gather(middle_low, 'tensor', axis=0, tiled=True)  61.9 us
    reduce_scatter x1, waiting for transfers between devices, per_device(): lax.psum_scatter(jnp.dot(hidden, ffn_down, preferred_element_type=jnp.flo...  59.2 us
    reduce_scatter x1, waiting for transfers between devices, per_device(): lax.psum_scatter(contract(pre_grad, ffn_up, 1, 1).astype(jnp.bfloat16), '...  59.2 us
    reduce_scatter x1, waiting for transfers between devices, per_device(): lax.psum_scatter(jnp.dot(context_low, proj_out, preferred_element_type=jn...  59.2 us
  transfers between devices with their start and end apart: 9, of which 8 were waited for; matrix products, arithmetic and copies ran while one was open for 3% of the time, Pallas kernels for 0%

commit v1 on v0

v1 whole, which is shorter than its diff:
```python
import jax
import jax.numpy as jnp
from jax import lax
from jax.sharding import PartitionSpec as P

HD = 64
LEN = 512


EPS = 1e-12
NEG = -1e30


def layer_norm(values, gain_vec, shift_vec):
    center = values - jnp.mean(values, axis=-1, keepdims=True)
    spread = jnp.mean(center * center, axis=-1, keepdims=True)
    return center * lax.rsqrt(spread + EPS) * gain_vec + shift_vec


def gelu_exact(values):
    return jax.nn.gelu(values, approximate=False)


def contract(left, right, left_dim, right_dim):
    return lax.dot_general(
        left, right, (((left_dim,), (right_dim,)), ((), ())), preferred_element_type=jnp.float32
    )


def attend_forward(queries, key_rows, value_rows, usable, factor):
    scores = (
        jnp.einsum("pqhe,pkhe->phqk", queries, key_rows, preferred_element_type=jnp.float32)
        * factor
    )
    scores = jnp.where(usable[:, None, None, :], scores, NEG)
    log_total = jax.nn.logsumexp(scores, axis=-1, keepdims=True)
    attn_probs = jnp.exp(scores - log_total)
    context = jnp.einsum(
        "phqk,pkhe->pqhe",
        attn_probs.astype(jnp.bfloat16),
        value_rows,
        preferred_element_type=jnp.float32,
    )
    return context, attn_probs


def attend_backward(queries, key_rows, value_rows, attn_probs, context_grad, factor):
    prob_grad = jnp.einsum(
        "pqhe,pkhe->phqk", context_grad, value_rows, preferred_element_type=jnp.float32
    )
    row_dot = jnp.sum(prob_grad * attn_probs, axis=-1, keepdims=True)
    score_grad = (attn_probs * (prob_grad - row_dot)).astype(jnp.bfloat16)
    query_grad = (
        jnp.einsum("phqk,pkhe->pqhe", score_grad, key_rows, preferred_element_type=jnp.float32)
        * factor
    )
    key_grad = (
        jnp.einsum("phqk,pqhe->pkhe", score_grad, queries, preferred_element_type=jnp.float32)
        * factor
    )
    value_grad = jnp.einsum(
        "phqk,pqhe->pkhe",
        attn_probs.astype(jnp.bfloat16),
        context_grad,
        preferred_element_type=jnp.float32,
    )
    return query_grad, key_grad, value_grad


def dp_pow2(values, dp_size):
    steps = dp_size.bit_length() - 1
    return dp_size == 1 << steps and values.shape[0] % dp_size == 0


def dp_halve(values, dp_size):
    steps = dp_size.bit_length() - 1
    index = lax.axis_index("dp")
    kept = values
    for step in range(steps):
        bit = (index >> step) & 1
        half = kept.shape[0] // 2
        keep = lax.dynamic_slice_in_dim(kept, bit * half, half)
        give = lax.dynamic_slice_in_dim(kept, (1 - bit) * half, half)
        got = lax.ppermute(give, "dp", [(i, i ^ (1 << step)) for i in range(dp_size)])
        kept = keep + got
    return kept


def dp_double(kept, dp_size):
    steps = dp_size.bit_length() - 1
    index = lax.axis_index("dp")
    for step in reversed(range(steps)):
        bit = (index >> step) & 1
        got = lax.ppermute(kept, "dp", [(i, i ^ (1 << step)) for i in range(dp_size)])
        kept = jnp.where(bit == 0, jnp.concatenate([kept, got]), jnp.concatenate([got, kept]))
    return kept


def make_per_device(dp_size):
    def per_device(
        tokens,
        out_grad,
        lengths,
        qkv_weight,
        qkv_bias,
        out_weight,
        out_bias,
        norm1_gain,
        norm1_shift,
        up_weight,
        up_bias,
        down_weight,
        down_bias,
        norm2_gain,
        norm2_shift,
    ):
        rows, width = tokens.shape
        shard = qkv_weight.shape[2]
        groups = width // shard
        passages = rows // LEN
        heads = width // HD
        factor = HD ** (-0.5)

        packed_w = jnp.concatenate(
            [
                qkv_weight.reshape(3 * width, shard),
                out_weight.T,
                qkv_bias,
            ],
            axis=0,
        )
        w_rows = packed_w.shape[0]
        half_rows = -(-w_rows // 16) * 8
        packed_w = jnp.pad(packed_w, ((0, 2 * half_rows - w_rows), (0, 0)))
        dp_index = lax.axis_index("dp")
        parity = dp_index % 2
        mine = lax.dynamic_slice_in_dim(packed_w, parity * half_rows, half_rows)
        mine = lax.all_gather(mine, "tensor", axis=0, tiled=False)
        other = lax.ppermute(mine, "dp", [(i, i ^ 1) for i in range(dp_size)])
        first = jnp.where(parity == 0, mine, other)
        second = jnp.where(parity == 0, other, mine)
        weights_all = jnp.concatenate([first, second], axis=1)[:, :w_rows]
        qkv_blocks = weights_all[:, : 3 * width].reshape(groups, 3, width, shard)
        proj_blocks = weights_all[:, 3 * width : 4 * width]
        bias_full = weights_all[:, 4 * width :].transpose(1, 0, 2).reshape(2, width)

        tensor_index = lax.axis_index("tensor")
        own_lengths = lax.dynamic_slice_in_dim(lengths, tensor_index * passages, passages)
        usable = jnp.arange(LEN, dtype=jnp.int32)[None, :] < own_lengths[:, None]

        own_tokens = tokens.astype(jnp.float32)
        projected = jnp.einsum(
            "rd,gtdj->trgj", tokens, qkv_blocks, preferred_element_type=jnp.float32
        ).reshape(3, rows, width)
        four_dims = (passages, LEN, heads, HD)
        queries = (projected[0] + bias_full[0]).astype(jnp.bfloat16).reshape(four_dims)
        key_rows = projected[1].astype(jnp.bfloat16).reshape(four_dims)
        value_rows = (projected[2] + bias_full[1]).astype(jnp.bfloat16).reshape(four_dims)
        context, attn_probs = attend_forward(queries, key_rows, value_rows, usable, factor)
        context_low = context.reshape(rows, width).astype(jnp.bfloat16)
        attn_out = jnp.einsum(
            "rgj,gcj->rc",
            context_low.reshape(rows, groups, shard),
            proj_blocks,
            preferred_element_type=jnp.float32,
        )
        middle, norm1_back = jax.vjp(
            layer_norm, own_tokens + attn_out + out_bias, norm1_gain, norm1_shift
        )
        middle_low = middle.astype(jnp.bfloat16)
        ffn_rows = lax.all_gather(middle_low, "tensor", axis=0, tiled=True)
        pre_act = jnp.dot(ffn_rows, up_weight, preferred_element_type=jnp.float32) + up_bias
        activated, gelu_back = jax.vjp(gelu_exact, pre_act)
        hidden = activated.astype(jnp.bfloat16)
        ffn_out = lax.psum_scatter(
            jnp.dot(hidden, down_weight, preferred_element_type=jnp.float32).astype(jnp.bfloat16),
            "tensor",
            scatter_dimension=0,
            tiled=True,
        ).astype(jnp.float32)
        layer_out, norm2_back = jax.vjp(
            layer_norm, middle + ffn_out + down_bias, norm2_gain, norm2_shift
        )
        second_grad, grad_norm2_gain, grad_norm2_shift = norm2_back(out_grad.astype(jnp.float32))
        branch_grad = second_grad.astype(jnp.bfloat16)
        grad_down_bias = jnp.sum(branch_grad, axis=0, dtype=jnp.float32)
        branch_rows = lax.all_gather(branch_grad, "tensor", axis=0, tiled=True)
        hidden_grad = contract(branch_rows, down_weight, 1, 1)
        grad_down_weight = contract(hidden, branch_rows, 0, 0)
        pre_grad = gelu_back(hidden_grad)[0].astype(jnp.bfloat16)
        grad_up_bias = jnp.sum(pre_grad, axis=0, dtype=jnp.float32)
        grad_up_weight = contract(ffn_rows, pre_grad, 0, 0)
        ffn_grads = (grad_up_weight, grad_down_weight)
        halved = all(dp_pow2(g, dp_size) for g in ffn_grads)
        if halved:
            ffn_grads = tuple(dp_halve(g, dp_size) for g in ffn_grads)
        else:
            ffn_grads = lax.psum(ffn_grads, "dp")
        middle_part = lax.psum_scatter(
            contract(pre_grad, up_weight, 1, 1).astype(jnp.bfloat16),
            "tensor",
            scatter_dimension=0,
            tiled=True,
        ).astype(jnp.float32)
        norm1_in, ffn_grads = lax.optimization_barrier((second_grad + middle_part, ffn_grads))
        first_grad, grad_norm1_gain, grad_norm1_shift = norm1_back(norm1_in)
        attn_grad = first_grad.astype(jnp.bfloat16)
        grad_out_bias = jnp.sum(attn_grad, axis=0, dtype=jnp.float32)
        context_grad = (
            jnp.einsum("rc,gcj->rgj", attn_grad, proj_blocks, preferred_element_type=jnp.float32)
            .astype(jnp.bfloat16)
            .reshape(four_dims)
        )
        query_grad, key_grad, value_grad = attend_backward(
            queries, key_rows, value_rows, attn_probs, context_grad, factor
        )
        proj_grad = (
            jnp.stack([query_grad, key_grad, value_grad])
            .reshape(3, rows, width)
            .astype(jnp.bfloat16)
        )
        if halved:
            ffn_grads = tuple(dp_double(g, dp_size) for g in ffn_grads)
            proj_grad, ffn_grads = lax.optimization_barrier((proj_grad, ffn_grads))
        grad_up_weight, grad_down_weight = ffn_grads
        grad_bias_full = jnp.sum(proj_grad[0::2], axis=1, dtype=jnp.float32)
        grad_qkv_full = jnp.einsum(
            "rd,tre->tde", tokens, proj_grad, preferred_element_type=jnp.float32
        )
        input_part = jnp.einsum(
            "trgj,gtdj->rd",
            proj_grad.reshape(3, rows, groups, shard),
            qkv_blocks,
            preferred_element_type=jnp.float32,
        )
        input_grad = (first_grad + input_part).astype(jnp.bfloat16)

        small = jnp.stack(
            [
                grad_out_bias,
                grad_norm1_gain,
                grad_norm1_shift,
                grad_down_bias,
                grad_norm2_gain,
                grad_norm2_shift,
            ]
        )
        n_small = small.shape[0]
        small_rep = jnp.tile(small.reshape(n_small, groups, shard), (1, 1, groups)).reshape(
            n_small * groups, width
        )
        up_parts = grad_up_bias.shape[0] // shard
        own_group = (jnp.arange(width) // shard == tensor_index)[None, :]
        up_rep = jnp.where(
            own_group, jnp.tile(grad_up_bias.reshape(up_parts, shard), (1, groups)), 0.0
        )
        tail = jnp.concatenate([grad_bias_full, small_rep, up_rep], axis=0)
        tail_rows = tail.shape[0]
        unit = dp_size * 8
        tail = jnp.pad(tail, ((0, -(-tail_rows // unit) * unit - tail_rows), (0, 0)))
        early = lax.psum_scatter(
            jnp.concatenate([contract(attn_grad, context_low, 0, 0), tail], axis=0),
            "dp",
            scatter_dimension=0,
            tiled=True,
        )
        late = lax.psum_scatter(
            grad_qkv_full.reshape(3 * width, width), "dp", scatter_dimension=0, tiled=True
        )
        joined = jnp.concatenate([late, early], axis=0)
        joined = lax.psum_scatter(
            joined.reshape(joined.shape[0], groups, shard).transpose(1, 0, 2),
            "tensor",
            scatter_dimension=0,
            tiled=True,
        )[0]
        late_rows = late.shape[0]
        joined = lax.all_gather(joined, "dp", axis=0, tiled=False)
        early = joined[:, late_rows:].reshape(-1, shard)
        pieces = [joined[:, :late_rows].reshape(-1, shard), early[:width], early[width:]]
        grad_qkv_weight = pieces[0].reshape(3, width, shard)
        grad_out_weight = pieces[1].T
        tail = pieces[2]
        grad_qkv_bias = tail[:2]
        small_sum = tail[2 : 2 + n_small * groups].reshape(n_small, width)
        grad_up_bias = tail[2 + n_small * groups : 2 + n_small * groups + up_parts].reshape(-1)
        (
            grad_out_bias,
            grad_norm1_gain,
            grad_norm1_shift,
            grad_down_bias,
            grad_norm2_gain,
            grad_norm2_shift,
        ) = [small_sum[i] for i in range(n_small)]
        return (
            layer_out.astype(jnp.bfloat16),
            input_grad,
            grad_qkv_weight,
            grad_qkv_bias,
            grad_out_weight,
            grad_out_bias,
            grad_norm1_gain,
            grad_norm1_shift,
            grad_up_weight,
            grad_up_bias,
            grad_down_weight,
            grad_down_bias,
            grad_norm2_gain,
            grad_norm2_shift,
        )

    return per_device


def solution(mesh):
    placed = (
        P(("dp", "tensor"), None),
        P(("dp", "tensor"), None),
        P("dp"),
        P(None, None, "tensor"),
        P(None, "tensor"),
        P("tensor", None),
        P(),
        P(),
        P(),
        P(None, "tensor"),
        P("tensor"),
        P("tensor", None),
        P(),
        P(),
        P(),
    )
    return jax.shard_map(
        make_per_device(mesh.shape["dp"]),
        mesh=mesh,
        in_specs=placed,
        out_specs=(
            P(("dp", "tensor"), None),
            P(("dp", "tensor"), None),
            P(None, None, "tensor"),
            P(None, "tensor"),
            P("tensor", None),
            P(),
            P(),
            P(),
            P(None, "tensor"),
            P("tensor"),
            P("tensor", None),
            P(),
            P(),
            P(),
        ),
        check_vma=False,
    )
```

time: 817 us -> 708 us (0.87)
  waiting for transfers between devices: 531 us -> 447 us
  blocking collectives: 57.8 us -> 0 us
  other arithmetic: 39.4 us -> 64.4 us
  matrix products: 115 us -> 90.8 us
  starting transfers between devices: 1.47 us -> 22.6 us
  local copies, waits for them, and re-layouts: 46.6 us -> 57.8 us
    psum x1 -> x0, waiting for transfers between devices: 98.8 us -> none  [per_device(): lax.psum((grad_qkv_weight, grad_qkv_bias, grad_out_weight, grad_up_weight...]
    psum x2 -> x0, blocking collectives: 57.8 us -> none  [the longest x1 43.4 us: per_device(): lax.psum((grad_out_bias, grad_norm1_gain, grad_norm1_shift, grad_down_bia...]
    all_gather x2, waiting for transfers between devices: 129 us -> 84.5 us  [the longest x1 56.9 us: per_device(): mine = lax.all_gather(mine, 'tensor', axis=0, tiled=False)]
    ppermute x0 -> x13, waiting for transfers between devices: none -> 43 us  [the longest x6 21.4 us: dp_double(): got = lax.ppermute(kept, 'dp', [(i, i ^ 1 << step) for i in range(dp_size)])]
    reduce_scatter x4 -> x5, waiting for transfers between devices: 177 us -> 206 us  [the longest x1 69.1 us: per_device(): lax.psum_scatter(grad_qkv_full.reshape(3 * width, width), 'dp', scatter_d...]
    dot_general x34 -> x12, matrix products: 84.4 us -> 65.7 us  [the longest x1 18.5 us: per_device(): jnp.dot(ffn_rows, up_weight, preferred_element_type=jnp.float32) + up_bias]
    select_n x4 -> x9, other arithmetic: 0.02 us -> 13.8 us  [the longest x6 10.9 us: dp_double(): jnp.where(bit == 0, jnp.concatenate([kept, got]), jnp.concatenate([got, k...]
    convert_element_type x7 -> x5, other arithmetic: 10.6 us -> 21.6 us  [the longest x1 10.1 us: attend_forward(): attn_probs.astype(jnp.bfloat16)]
  transfers between devices with their start and end apart: 9 -> 22, of which waited for: 8 -> 16; matrix products, arithmetic and copies ran while one was open for 3% -> 9% of each run, Pallas kernels for 0% -> 0%
where the time goes in v1:
time: 708 us; the launch traced here: 698 us
  waiting for transfers between devices  447 us (63%)
  matrix products  90.8 us (13%)
  other arithmetic  64.4 us (9%)
  local copies, waits for them, and re-layouts  57.8 us (8%)
  starting transfers between devices  22.6 us (3%)
  between operations  15.2 us (2%)
    reduce_scatter x1, waiting for transfers between devices, per_device(): lax.psum_scatter(grad_qkv_full.reshape(3 * width, width), 'dp', scatter_d...  69.1 us
    all_gather x1, waiting for transfers between devices, per_device(): ffn_rows = lax.all_gather(middle_low, 'tensor', axis=0, tiled=True)  61 us
    reduce_scatter x1, waiting for transfers between devices, per_device(): lax.psum_scatter(jnp.dot(hidden, down_weight, preferred_element_type=jnp....  59.1 us
    all_gather x1, waiting for transfers between devices, per_device(): mine = lax.all_gather(mine, 'tensor', axis=0, tiled=False)  56.9 us
    all_gather x1, waiting for transfers between devices, per_device(): branch_rows = lax.all_gather(branch_grad, 'tensor', axis=0, tiled=True)  52.2 us
    reduce_scatter x1, waiting for transfers between devices, per_device(): lax.psum_scatter(jnp.concatenate([contract(attn_grad, context_low, 0, 0),...  37.5 us
    reduce_scatter x1, waiting for transfers between devices, per_device(): lax.psum_scatter(joined.reshape(joined.shape[0], groups, shard).transpose...  35.5 us
    all_gather x1, waiting for transfers between devices, per_device(): joined = lax.all_gather(joined, 'dp', axis=0, tiled=False)  27.6 us
  transfers between devices with their start and end apart: 22, of which 16 were waited for; matrix products, arithmetic and copies ran while one was open for 9% of the time, Pallas kernels for 0%

profile of v1, /device:TPU:0, one launch (start us, length us, event | category | flops | bytes accessed | tf_op | source)
XLA Modules:
  0.0 697.7 jit_solution(14581463789579628879)
XLA Ops:
  9.4 1.8 fusion.37
  11.3 56.9 %all-gather.13.cloned.1.call-done = bf16[4,1544,192]{1,2,0:T(8,128)(2,1)} async-done(((bf16[1,1544,192]{1,2,0:T(8,128)(2,1)}), bf16[4,1544,192]{1,2,0:T(8,128)(2,1)}) %all-gather.13.cloned.1.call-update) | async-done | bytes 2371600 | tf_op jit(solution)/shard_map/all_gather | solution.py:138
  69.5 3.9 collective-permute-done
  73.4 3.0 broadcast_select_fusion.1
  78.2 2.0 fusion.15
  80.4 1.5 fusion.51
  83.1 5.0 fusion
  88.1 2.6 exponential_reduce_fusion
  90.7 1.9 copy-done.2
  92.7 10.1 %fusion.1 = bf16[12,512,512]{1,2,0:T(8,128)(2,1)} fusion(f32[12,512,512]{1,2,0:T(8,128)} %copy-done.2, f32[12,512]{1,0:T(8,128)S(1)} %log_add_fusion, pred[512]{0:T(512)(128)(4,1)S(1)} %iota_compare_fusion.1), kind=kLoop, calls=%fused_computation.7 | loop fusion | flops 12582912 | bytes 18899456 | tf_op jit(solution)/shard_map/convert_element_type | solution.py:40
  102.8 4.1 convolution_convert_fusion.3
  107.0 2.7 fusion.53
  113.8 61.0 %all-gather.7.cloned.1.call-done = bf16[2048,768]{1,0:T(8,128)(2,1)} async-done(((bf16[512,768]{1,0:T(8,128)(2,1)}), bf16[2048,768]{1,0:T(8,128)(2,1)}) %all-gather.7.cloned.1.call-update) | async-done | bytes 3145744 | tf_op jit(solution)/shard_map/all_gather | solution.py:171
  174.8 18.5 %multiply_convert_fusion.1 = (bf16[2048,768]{1,0:T(8,128)(2,1)S(1)}, f32[2048,768]{1,0:T(8,128)}, f32[2048,768]{1,0:T(8,128)}) fusion(f32[768]{0:T(1024)} %convert_element_type.142, bf16[2048,768]{1,0:T(8,128)(2,1)} %all-gather.7.cloned.1.call-done, bf16[768,768]{1,0:T(8,128)(2,1)S(1)} %copy-done), kind=kOutput, calls=%fused_computation.11 | convolution fusion | flops 2519728128 | bytes 20057088 | tf_op jit(solution)/shard_map/dot_general | solution.py:172
  193.3 1.7 copy-done.60
  194.9 3.9 convolution_convert_fusion.1
  198.9 59.1 %reduce-scatter.6.cloned.1.call-done = bf16[512,768]{1,0:T(8,128)(2,1)} async-done(((bf16[2048,768]{1,0:T(8,128)(2,1)}), bf16[512,768]{1,0:T(8,128)(2,1)}) %reduce-scatter.6.cloned.1.call-update) | async-done | bytes 786448 | tf_op jit(solution)/shard_map/reduce_scatter | solution.py:175
  258.1 1.8 fusion.49
  261.5 1.6 fusion.48
  264.3 1.7 convert_reduce_fusion.3
  266.0 11.3 %reduce-scatter.8.cloned.1.call-start = ((), (), s32[]{:S(2)}) async-start(), calls=%async_computation.8 | async-start | bytes 3932160 | tf_op jit(solution)/shard_map/reduce_scatter | solution.py:199
  277.3 52.2 %all-gather.9.cloned.1.call-done = bf16[2048,768]{1,0:T(8,128)(2,1)} async-done(((bf16[512,768]{1,0:T(8,128)(2,1)}), bf16[2048,768]{1,0:T(8,128)(2,1)}) %all-gather.9.cloned.1.call-update) | async-done | bytes 3145744 | tf_op jit(solution)/shard_map/all_gather | solution.py:187
  329.5 11.0 %convert_reduce_fusion = (f32[768]{0:T(1024)}, bf16[2048,768]{1,0:T(8,128)(2,1)S(1)}) fusion(f32[2048,768]{1,0:T(8,128)} %get-tuple-element.103, f32[2048,768]{1,0:T(8,128)} %get-tuple-element.120, f32[768]{0:T(1024)} %convert_element_type.142, bf16[2048,768]{1,0:T(8,128)(2,1)} %all-gather.9.cloned.1.call-done, bf16[768,768]{1,0:T(8,128)(2,1)} %param.26), kind=kOutput, calls=%fused_computation.9 | convolution fusion | flops 2442657024 | bytes 20060160 | tf_op jit(solution)/shard_map/dot_general | solution.py:25
  340.5 1.7 copy-done.61
  342.2 4.0 convolution_convert_fusion
  346.3 5.7 fusion.55
  352.1 2.7 fusion.54
  357.2 2.5 collective-permute-done.4
  359.6 1.8 dynamic-slice_add_fusion
  362.3 1.5 collective-permute-start.5
  363.7 1.4 dynamic-slice_add_fusion.1
  368.2 2.9 slice.115
  377.7 1.4 tile.24
  380.4 1.5 collective-permute-start.6
  382.0 8.6 %collective-permute-done.2 = f32[192,768]{1,0:T(8,128)} collective-permute-done((f32[192,768]{1,0:T(8,128)}, f32[192,768]{1,0:T(8,128)}, u32[]{:S(2)}, u32[]{:S(2)}) %collective-permute-start.2) | collective-permute-done | bytes 589856 | tf_op jit(solution)/shard_map/ppermute | solution.py:84
  391.8 1.5 collective-permute-start.3
  393.4 6.6 collective-permute-done.3
  400.8 4.7 reduce-scatter.8.cloned.1.call-done
  405.5 2.0 convert_add_fusion
  410.8 2.9 convolution_convert_fusion.2
  415.5 10.2 %multiply_reduce_fusion = (f32[12,512]{1,0:T(8,128)S(1)}, f32[12,512,512]{1,2,0:T(8,128)}) fusion(f32[12,512,512]{1,2,0:T(8,128)S(1)} %bitcast.108, f32[12,512]{1,0:T(8,128)S(1)} %copy-done.26, pred[512]{0:T(512)(128)(4,1)S(1)} %copy-done.50, bf16[512,12,64]{0,2,1:T(8,128)(2,1)S(1)} %bitcast.120, f32[512,12,64]{0,2,1:T(8,128)S(1)} %bitcast.112, ...), kind=kOutput, calls=%fused_computation.1 | convolution fusion | flops 419162112 | bytes 27577856 | tf_op jit(solution)/shard_map/pqhe,pkhe->phqk/dot_general | solution.py:48
  425.9 1.5 collective-permute-start.7
  428.0 9.9 %multiply_convert_fusion = bf16[12,512,512]{1,2,0:T(8,128)(2,1)S(1)} fusion(f32[12,512,512]{1,2,0:T(8,128)} %get-tuple-element.122, f32[12,512,512]{1,2,0:T(8,128)} %copy-done.2, f32[12,512]{1,0:T(8,128)S(1)} %get-tuple-element.121, f32[12,512]{1,0:T(8,128)S(1)} %copy-done.26, pred[512]{0:T(512)(128)(4,1)S(1)} %copy-done.50), kind=kLoop, calls=%fused_computation | loop fusion | flops 18874368 | bytes 31506944 | tf_op jit(solution)/shard_map/convert_element_type | solution.py:52
  438.0 1.5 collective-permute-start.8
  440.6 1.5 collective-permute-start.11
  443.3 10.9 %collective-permute-done.8 = f32[192,768]{1,0:T(8,128)S(1)} collective-permute-done((f32[192,768]{1,0:T(8,128)S(1)}, f32[192,768]{1,0:T(8,128)S(1)}, u32[]{:S(2)}, u32[]{:S(2)}) %collective-permute-start.8) | collective-permute-done | bytes 589856 | tf_op jit(solution)/shard_map/ppermute | solution.py:94
  455.4 9.4 %collective-permute-done.11 = f32[192,768]{1,0:T(8,128)S(1)} collective-permute-done((f32[192,768]{1,0:T(8,128)S(1)}, f32[192,768]{1,0:T(8,128)S(1)}, u32[]{:S(2)}, u32[]{:S(2)}) %collective-permute-start.11) | collective-permute-done | bytes 589856 | tf_op jit(solution)/shard_map/ppermute | solution.py:94
  466.1 4.9 multiply_convert_fusion.2
  473.2 4.2 maximum_select_fusion
  477.5 4.3 maximum_select_fusion.1
  482.1 1.7 pad_maximum_fusion.1
  484.9 4.9 fusion.33
  490.1 37.5 %reduce-scatter.12.cloned.1.call-done = f32[104,768]{1,0:T(8,128)} async-done(((f32[832,768]{1,0:T(8,128)}), f32[104,768]{1,0:T(8,128)}) %reduce-scatter.12.cloned.1.call-update) | async-done | bytes 319504 | tf_op jit(solution)/shard_map/reduce_scatter | solution.py:261
  527.6 69.1 %reduce-scatter.10.cloned.1.call-done = f32[288,768]{1,0:T(8,128)} async-done(((f32[2304,768]{1,0:T(8,128)}), f32[288,768]{1,0:T(8,128)}) %reduce-scatter.10.cloned.1.call-update) | async-done | bytes 884752 | tf_op jit(solution)/shard_map/reduce_scatter | solution.py:267
  596.6 2.4 pad_maximum_fusion.3
  599.0 3.2 reshape.335
  602.2 2.6 copy.95
  604.9 35.5 %reduce-scatter.14.cloned.1.call-done = f32[1,392,192]{1,2,0:T(8,128)} async-done(((f32[4,392,192]{1,2,0:T(8,128)}), f32[1,392,192]{1,2,0:T(8,128)}) %reduce-scatter.14.cloned.1.call-update) | async-done | bytes 301072 | tf_op jit(solution)/shard_map/reduce_scatter | solution.py:271
  640.5 5.4 fusion.22
  645.9 27.6 %all-gather.11.cloned.1.call-done = f32[8,392,192]{1,2,0:T(8,128)} async-done(((f32[1,392,192]{1,2,0:T(8,128)}), f32[8,392,192]{1,2,0:T(8,128)}) %all-gather.11.cloned.1.call-update) | async-done | bytes 2408464 | tf_op jit(solution)/shard_map/all_gather | solution.py:278
  673.4 1.7 slice.117
  677.9 1.7 slice-done.5
  679.5 2.1 copy.96
  681.7 3.1 copy.105
  (254 shorter events, 52.8 us)
Async XLA Ops:
  7.2 167.6 %copy-start = (bf16[768,768]{1,0:T(8,128)(2,1)S(1)}, bf16[768,768]{1,0:T(8,128)(2,1)}, u32[]{:S(2)}) copy-start(bf16[768,768]{1,0:T(8,128)(2,1)} %param.24) | copy-start | bytes 3538948
  7.2 61.1 %copy-start.59 = (s32[4]{0:T(128)S(1)}, s32[4]{0:T(128)}, u32[]{:S(2)}) copy-start(s32[4]{0:T(128)} %param.17) | copy-start | bytes 52
  7.2 61.1 %all-gather.13.cloned.1.call-start = ((), (), s32[]{:S(2)}) async-start(), calls=%async_computation.13 | async-start | bytes 3194880 | tf_op jit(solution)/shard_map/all_gather | solution.py:138
  11.3 163.5 %all-gather.7.cloned.1.call-start = ((), (), s32[]{:S(2)}) async-start(), calls=%async_computation.5 | async-start | bytes 3932160 | tf_op jit(solution)/shard_map/all_gather | solution.py:171
  68.3 5.2 collective-permute-start
  69.5 23.2 %copy-start.49 = (pred[512]{0:T(512)(128)(4,1)}, pred[512]{0:T(512)(128)(4,1)S(1)}, u32[]{:S(2)}) copy-start(pred[512]{0:T(512)(128)(4,1)S(1)} %iota_compare_fusion.1) | copy-start | bytes 1540
  81.9 20.9 %copy-start.5 = (f32[1,512,4,192]{1,3,0,2:T(8,128)}, f32[1,512,4,192]{1,3,0,2:T(8,128)S(1)}, u32[]{:S(2)}) copy-start(f32[1,512,4,192]{1,3,0,2:T(8,128)S(1)} %get-tuple-element.106) | copy-start | bytes 4718596
  88.1 4.6 copy-start.2
  92.7 10.1 %copy-start.25 = (f32[12,512]{1,0:T(8,128)}, f32[12,512]{1,0:T(8,128)S(1)}, u32[]{:S(2)}) copy-start(f32[12,512]{1,0:T(8,128)S(1)} %log_add_fusion) | copy-start | bytes 73732
  92.7 10.1 %copy-start.34 = (f32[12,64]{1,0:T(8,128)S(1)}, f32[12,64]{1,0:T(8,128)}, u32[]{:S(2)}) copy-start(f32[12,64]{1,0:T(8,128)} %reshape.338) | copy-start | bytes 9220
  102.8 4.1 copy-start.56
  102.8 4.1 copy-start.58
  107.0 4.3 copy-start.36
  107.0 4.3 copy-start.44
  112.4 145.6 %reduce-scatter.6.cloned.1.call-start = ((), (), s32[]{:S(2)}) async-start(), calls=%async_computation.6 | async-start | bytes 3932160 | tf_op jit(solution)/shard_map/reduce_scatter | solution.py:175
  174.8 20.1 %copy-start.54 = (bf16[768,768]{1,0:T(8,128)(2,1)S(1)}, bf16[768,768]{1,0:T(8,128)(2,1)}, u32[]{:S(2)}) copy-start(bf16[768,768]{1,0:T(8,128)(2,1)} %param.26) | copy-start | bytes 3538948
  198.9 130.6 %all-gather.9.cloned.1.call-start = ((), (), s32[]{:S(2)}) async-start(), calls=%async_computation.7 | async-start | bytes 3932160 | tf_op jit(solution)/shard_map/all_gather | solution.py:187
  266.0 139.5 %reduce-scatter.8.cloned.1.call-start = ((), (), s32[]{:S(2)}) async-start(), calls=%async_computation.8 | async-start | bytes 3932160 | tf_op jit(solution)/shard_map/reduce_scatter | solution.py:199
  346.3 181.3 %reduce-scatter.12.cloned.1.call-start = ((), (), s32[]{:S(2)}) async-start(), calls=%async_computation.10 | async-start | bytes 2875392 | tf_op jit(solution)/shard_map/reduce_scatter | solution.py:261
  346.3 5.7 copy-start.53
  346.3 5.7 copy-start.62
  356.6 3.0 collective-permute-start.4
  356.7 7.1 %collective-permute-start.1 = (f32[384,768]{1,0:T(8,128)}, f32[384,768]{1,0:T(8,128)}, u32[]{:S(2)}, u32[]{:S(2)}) collective-permute-start(f32[384,768]{1,0:T(8,128)} %get-tuple-element.124), channel_id=1, source_target_pairs={{0,4},{4,0},{8,12},{12,8},{16,20},{20,16},{24,28},{28,24},{1,5},{5... | collective-permute-start | bytes 3538952 | tf_op jit(solution)/shard_map/ppermute | solution.py:84
  357.2 6.6 copy-start.21
  362.3 16.9 %collective-permute-start.5 = (f32[192,768]{1,0:T(8,128)}, f32[192,768]{1,0:T(8,128)}, u32[]{:S(2)}, u32[]{:S(2)}) collective-permute-start(f32[192,768]{1,0:T(8,128)} %constant_dynamic-slice_fusion.1), channel_id=1, source_target_pairs={{0,8},{4,12},{8,0},{12,4},{16,24},{20,28},{24,16},{28,20},{1,9},{5... | collective-permute-start | bytes 1769480 | tf_op jit(solution)/shard_map/ppermute | solution.py:84
  367.0 23.5 %collective-permute-start.2 = (f32[192,768]{1,0:T(8,128)}, f32[192,768]{1,0:T(8,128)}, u32[]{:S(2)}, u32[]{:S(2)}) collective-permute-start(f32[192,768]{1,0:T(8,128)} %constant_dynamic-slice_fusion.4), channel_id=1, source_target_pairs={{0,8},{4,12},{8,0},{12,4},{16,24},{20,28},{24,16},{28,20},{1,9},{5... | collective-permute-start | bytes 1769480 | tf_op jit(solution)/shard_map/ppermute | solution.py:84
  379.1 11.4 %copy-start.12 = (f32[384,768]{1,0:T(8,128)S(1)}, f32[384,768]{1,0:T(8,128)}, u32[]{:S(2)}) copy-start(f32[384,768]{1,0:T(8,128)} %copy-done.11) | copy-start | bytes 3538948
  379.1 14.2 %copy-start.39 = (f32[4,768]{1,0:T(4,128)S(1)}, f32[4,768]{1,0:T(4,128)}, u32[]{:S(2)}) copy-start(f32[4,768]{1,0:T(4,128)} %tile.24) | copy-start | bytes 36868
  379.1 14.2 %copy-start.52 = (pred[768]{0:T(1024)(128)(4,1)S(1)}, pred[768]{0:T(1024)(128)(4,1)}, u32[]{:S(2)}) copy-start(pred[768]{0:T(1024)(128)(4,1)} %fusion.40) | copy-start | bytes 2308
  380.4 25.1 %copy-start.41 = (f32[512]{0:T(512)S(1)}, f32[512]{0:T(512)}, u32[]{:S(2)}) copy-start(f32[512]{0:T(512)} %copy-done.40) | copy-start | bytes 6148
  380.4 12.9 %collective-permute-start.6 = (f32[96,768]{1,0:T(8,128)S(1)}, f32[96,768]{1,0:T(8,128)S(1)}, u32[]{:S(2)}, u32[]{:S(2)}) collective-permute-start(f32[96,768]{1,0:T(8,128)S(1)} %constant_dynamic-slice_fusion), channel_id=1, source_target_pairs={{0,16},{4,20},{8,24},{12,28},{16,0},{20,4},{24,8},{28,12},{1,17},{... | collective-permute-start | bytes 884744 | tf_op jit(solution)/shard_map/ppermute | solution.py:84
  391.8 8.3 %collective-permute-start.3 = (f32[96,768]{1,0:T(8,128)S(1)}, f32[96,768]{1,0:T(8,128)S(1)}, u32[]{:S(2)}, u32[]{:S(2)}) collective-permute-start(f32[96,768]{1,0:T(8,128)S(1)} %constant_dynamic-slice_fusion.3), channel_id=1, source_target_pairs={{0,16},{4,20},{8,24},{12,28},{16,0},{20,4},{24,8},{28,12},{1,17},{... | collective-permute-start | bytes 884744 | tf_op jit(solution)/shard_map/ppermute | solution.py:84
  393.4 14.1 %copy-start.38 = (f32[512]{0:T(512)S(1)}, f32[512]{0:T(512)}, u32[]{:S(2)}) copy-start(f32[512]{0:T(512)} %copy-done.37) | copy-start | bytes 6148
  405.5 4.9 slice-start.3
  408.2 5.5 slice-start
  409.5 4.3 slice-start.1
  410.8 4.2 slice-start.2
  410.8 4.6 copy-start.6
  410.8 4.6 copy-start.26
  410.8 4.6 copy-start.35
  410.8 4.6 copy-start.50
  415.5 10.4 %copy-start.24 = (f32[96,768]{1,0:T(8,128)S(1)}, f32[96,768]{1,0:T(8,128)}, u32[]{:S(2)}) copy-start(f32[96,768]{1,0:T(8,128)} %dynamic-slice_add_fusion.5) | copy-start | bytes 884740
  425.9 12.0 %collective-permute-start.7 = (f32[96,768]{1,0:T(8,128)S(1)}, f32[96,768]{1,0:T(8,128)S(1)}, u32[]{:S(2)}, u32[]{:S(2)}) collective-permute-start(f32[96,768]{1,0:T(8,128)S(1)} %copy-done.24), channel_id=1, source_target_pairs={{0,16},{4,20},{8,24},{12,28},{16,0},{20,4},{24,8},{28,12},{1,17},{... | collective-permute-start | bytes 884744 | tf_op jit(solution)/shard_map/ppermute | solution.py:94
  427.4 13.2 %collective-permute-start.10 = (f32[96,768]{1,0:T(8,128)S(1)}, f32[96,768]{1,0:T(8,128)S(1)}, u32[]{:S(2)}, u32[]{:S(2)}) collective-permute-start(f32[96,768]{1,0:T(8,128)S(1)} %dynamic-slice_add_fusion.4), channel_id=1, source_target_pairs={{0,16},{4,20},{8,24},{12,28},{16,0},{20,4},{24,8},{28,12},{1,17},{... | collective-permute-start | bytes 884744 | tf_op jit(solution)/shard_map/ppermute | solution.py:94
  428.0 9.9 %copy-start.48 = (f32[1,1,1,4,1,192]{5,3,1,4,2,0:T(4,128)S(1)}, f32[1,1,1,4,1,192]{5,3,1,4,2,0:T(4,128)}, u32[]{:S(2)}) copy-start(f32[1,1,1,4,1,192]{5,3,1,4,2,0:T(4,128)} %stack.40) | copy-start | bytes 9220
  428.0 11.5 %copy-start.47 = (f32[1,1,1,4,1,192]{5,3,1,4,2,0:T(4,128)S(1)}, f32[1,1,1,4,1,192]{5,3,1,4,2,0:T(4,128)}, u32[]{:S(2)}) copy-start(f32[1,1,1,4,1,192]{5,3,1,4,2,0:T(4,128)} %stack.41) | copy-start | bytes 9220
  437.9 5.4 copy-start.3
  438.0 16.3 %collective-permute-start.8 = (f32[192,768]{1,0:T(8,128)S(1)}, f32[192,768]{1,0:T(8,128)S(1)}, u32[]{:S(2)}, u32[]{:S(2)}) collective-permute-start(f32[192,768]{1,0:T(8,128)S(1)} %maximum_select_fusion.4), channel_id=1, source_target_pairs={{0,8},{4,12},{8,0},{12,4},{16,24},{20,28},{24,16},{28,20},{1,9},{5... | collective-permute-start | bytes 1769480 | tf_op jit(solution)/shard_map/ppermute | solution.py:94
  440.6 24.2 %collective-permute-start.11 = (f32[192,768]{1,0:T(8,128)S(1)}, f32[192,768]{1,0:T(8,128)S(1)}, u32[]{:S(2)}, u32[]{:S(2)}) collective-permute-start(f32[192,768]{1,0:T(8,128)S(1)} %maximum_select_fusion.5), channel_id=1, source_target_pairs={{0,8},{4,12},{8,0},{12,4},{16,24},{20,28},{24,16},{28,20},{1,9},{5... | collective-permute-start | bytes 1769480 | tf_op jit(solution)/shard_map/ppermute | solution.py:94
  443.3 22.7 %copy-start.46 = (f32[1,1,1,4,1,192]{5,3,1,4,2,0:T(4,128)S(1)}, f32[1,1,1,4,1,192]{5,3,1,4,2,0:T(4,128)}, u32[]{:S(2)}) copy-start(f32[1,1,1,4,1,192]{5,3,1,4,2,0:T(4,128)} %stack.42) | copy-start | bytes 9220
  443.3 22.8 %copy-start.8 = (f32[1,512,4,192]{1,3,0,2:T(8,128)S(1)}, f32[1,512,4,192]{1,3,0,2:T(8,128)}, u32[]{:S(2)}) copy-start(f32[1,512,4,192]{1,3,0,2:T(8,128)} %get-tuple-element.107) | copy-start | bytes 4718596
  455.4 17.9 %collective-permute-start.9 = (f32[384,768]{1,0:T(8,128)}, f32[384,768]{1,0:T(8,128)}, u32[]{:S(2)}, u32[]{:S(2)}) collective-permute-start(f32[384,768]{1,0:T(8,128)} %maximum_select_fusion.2), channel_id=1, source_target_pairs={{0,4},{4,0},{8,12},{12,8},{16,20},{20,16},{24,28},{28,24},{1,5},{5... | collective-permute-start | bytes 3538952 | tf_op jit(solution)/shard_map/ppermute | solution.py:94
  466.0 11.5 %collective-permute-start.12 = (f32[384,768]{1,0:T(8,128)}, f32[384,768]{1,0:T(8,128)}, u32[]{:S(2)}, u32[]{:S(2)}) collective-permute-start(f32[384,768]{1,0:T(8,128)} %maximum_select_fusion.3), channel_id=1, source_target_pairs={{0,4},{4,0},{8,12},{12,8},{16,20},{20,16},{24,28},{28,24},{1,5},{5... | collective-permute-start | bytes 3538952 | tf_op jit(solution)/shard_map/ppermute | solution.py:94
  466.1 4.9 copy-start.19
  483.8 112.8 %reduce-scatter.10.cloned.1.call-start = ((), (), s32[]{:S(2)}) async-start(), calls=%async_computation.9 | async-start | bytes 7962624 | tf_op jit(solution)/shard_map/reduce_scatter | solution.py:267
  489.8 150.7 %reduce-scatter.14.cloned.1.call-start = ((), (), s32[]{:S(2)}) async-start(), calls=%async_computation.11 | async-start | bytes 1966080 | tf_op jit(solution)/shard_map/reduce_scatter | solution.py:271
  604.9 68.6 %all-gather.11.cloned.1.call-start = ((), (), s32[]{:S(2)}) async-start(), calls=%async_computation.12 | async-start | bytes 3538944 | tf_op jit(solution)/shard_map/all_gather | solution.py:278
  681.6 4.5 copy-start.32
  681.6 5.3 copy-start.31
  681.6 6.1 copy-start.30
  681.6 6.8 copy-start.29
  681.7 9.1 %copy-start.1 = (bf16[768,768]{1,0:T(8,128)(2,1)S(1)}, bf16[768,768]{1,0:T(8,128)(2,1)}, u32[]{:S(2)}) copy-start(bf16[768,768]{1,0:T(8,128)(2,1)} %param.24) | copy-start | bytes 3538948
  681.7 7.5 %copy-start.28 = (f32[4,192]{0,1:T(8,128)S(1)}, f32[4,192]{0,1:T(8,128)}, u32[]{:S(2)}) copy-start(f32[4,192]{0,1:T(8,128)} %get-tuple-element.114) | copy-start | bytes 9220
  681.7 8.3 %copy-start.27 = (f32[4,192]{0,1:T(8,128)S(1)}, f32[4,192]{0,1:T(8,128)}, u32[]{:S(2)}) copy-start(f32[4,192]{0,1:T(8,128)} %get-tuple-element.115) | copy-start | bytes 9220
  (28 other events, 49.9 us)
Sparse Core Ops, SparseCore 0:
  11.4 56.8 all-gather.12
  112.6 62.2 all-gather.6
  199.0 59.0 reduce-scatter.5
  266.1 63.3 all-gather.8
  346.4 59.0 reduce-scatter.7
  483.9 43.6 reduce-scatter.11
  531.1 65.4 reduce-scatter.9
  605.0 35.4 reduce-scatter.13
  642.3 31.0 all-gather.10

commit v2 on v1

--- a/solution.py
+++ b/solution.py
@@ -211,6 +211,10 @@
             .astype(jnp.bfloat16)
             .reshape(four_dims)
         )
+        context_grad, early = lax.optimization_barrier(
+            (context_grad, contract(attn_grad, context_low, 0, 0))
+        )
+        early = lax.psum_scatter(early, "dp", scatter_dimension=0, tiled=True)
         query_grad, key_grad, value_grad = attend_backward(
             queries, key_rows, value_rows, attn_probs, context_grad, factor
         )
@@ -219,10 +223,7 @@
             .reshape(3, rows, width)
             .astype(jnp.bfloat16)
         )
-        if halved:
-            ffn_grads = tuple(dp_double(g, dp_size) for g in ffn_grads)
-            proj_grad, ffn_grads = lax.optimization_barrier((proj_grad, ffn_grads))
-        grad_up_weight, grad_down_weight = ffn_grads
+        proj_grad, early = lax.optimization_barrier((proj_grad, early))
         grad_bias_full = jnp.sum(proj_grad[0::2], axis=1, dtype=jnp.float32)
         grad_qkv_full = jnp.einsum(
             "rd,tre->tde", tokens, proj_grad, preferred_element_type=jnp.float32
@@ -256,18 +257,15 @@
         )
         tail = jnp.concatenate([grad_bias_full, small_rep, up_rep], axis=0)
         tail_rows = tail.shape[0]
-        unit = dp_size * 8
-        tail = jnp.pad(tail, ((0, -(-tail_rows // unit) * unit - tail_rows), (0, 0)))
-        early = lax.psum_scatter(
-            jnp.concatenate([contract(attn_grad, context_low, 0, 0), tail], axis=0),
-            "dp",
-            scatter_dimension=0,
-            tiled=True,
-        )
+        tail = jnp.pad(tail, ((0, -(-tail_rows // 8) * 8 - tail_rows), (0, 0)))
         late = lax.psum_scatter(
             grad_qkv_full.reshape(3 * width, width), "dp", scatter_dimension=0, tiled=True
         )
-        joined = jnp.concatenate([late, early], axis=0)
+        joined = jnp.concatenate([late, early, tail], axis=0)
+        if halved:
+            ffn_grads = tuple(dp_double(g, dp_size) for g in ffn_grads)
+            joined, ffn_grads = lax.optimization_barrier((joined, ffn_grads))
+        grad_up_weight, grad_down_weight = ffn_grads
         joined = lax.psum_scatter(
             joined.reshape(joined.shape[0], groups, shard).transpose(1, 0, 2),
             "tensor",
@@ -275,9 +273,13 @@
             tiled=True,
         )[0]
         late_rows = late.shape[0]
+        early_rows = early.shape[0]
         joined = lax.all_gather(joined, "dp", axis=0, tiled=False)
-        early = joined[:, late_rows:].reshape(-1, shard)
-        pieces = [joined[:, :late_rows].reshape(-1, shard), early[:width], early[width:]]
+        pieces = [
+            joined[:, :late_rows].reshape(-1, shard),
+            joined[:, late_rows : late_rows + early_rows].reshape(-1, shard),
+            jnp.sum(joined[:, late_rows + early_rows :], axis=0),
+        ]
         grad_qkv_weight = pieces[0].reshape(3, width, shard)
         grad_out_weight = pieces[1].T
         tail = pieces[2]

time: 708 us -> 652 us (0.921)
  waiting for transfers between devices: 447 us -> 379 us
    reduce_scatter x2 -> x1, waiting for transfers between devices: 107 us -> 12.8 us  [per_device(): early = lax.psum_scatter(early, 'dp', scatter_dimension=0, tiled=True)]
    ppermute x6, waiting for transfers between devices: 21.4 us -> 41.3 us  [dp_double(): got = lax.ppermute(kept, 'dp', [(i, i ^ 1 << step) for i in range(dp_size)])]
    unnamed x144 -> x128, local copies, waits for them, and re-layouts: 19.6 us -> 21.8 us
  transfers between devices with their start and end apart: 22 -> 22, of which waited for: 16 -> 17; matrix products, arithmetic and copies ran while one was open for 9% -> 15% of each run, Pallas kernels for 0% -> 0%
where the time goes in v2:
time: 652 us; the launch traced here: 641 us
  waiting for transfers between devices  379 us (58%)
  matrix products  95.7 us (15%)
  other arithmetic  70 us (11%)
  local copies, waits for them, and re-layouts  59 us (9%)
  starting transfers between devices  22.6 us (3%)
  between operations  15.1 us (2%)
    all_gather x1, waiting for transfers between devices, per_device(): ffn_rows = lax.all_gather(middle_low, 'tensor', axis=0, tiled=True)  61 us
    reduce_scatter x1, waiting for transfers between devices, per_device(): lax.psum_scatter(jnp.dot(hidden, down_weight, preferred_element_type=jnp....  59.1 us
    all_gather x1, waiting for transfers between devices, per_device(): mine = lax.all_gather(mine, 'tensor', axis=0, tiled=False)  56.9 us
    all_gather x1, waiting for transfers between devices, per_device(): branch_rows = lax.all_gather(branch_grad, 'tensor', axis=0, tiled=True)  52.4 us
    ppermute x6, waiting for transfers between devices, dp_double(): got = lax.ppermute(kept, 'dp', [(i, i ^ 1 << step) for i in range(dp_size)])  41.3 us
    reduce_scatter x1, waiting for transfers between devices, per_device(): lax.psum_scatter(joined.reshape(joined.shape[0], groups, shard).transpose...  36.5 us
    all_gather x1, waiting for transfers between devices, per_device(): joined = lax.all_gather(joined, 'dp', axis=0, tiled=False)  27.5 us
    dot_general x5, matrix products, contract(): lax.dot_general(left, right, (((left_dim,), (right_dim,)), ((), ())), pre...  25.7 us
  transfers between devices with their start and end apart: 22, of which 17 were waited for; matrix products, arithmetic and copies ran while one was open for 15% of the time, Pallas kernels for 0%

profile of v2, /device:TPU:0, one launch (start us, length us, event | category | flops | bytes accessed | tf_op | source)
XLA Modules:
  0.0 641.3 jit_solution(10494279296528400749)
XLA Ops:
  9.4 1.8 fusion.40
  11.3 56.9 %all-gather.13.cloned.1.call-done = bf16[4,1544,192]{1,2,0:T(8,128)(2,1)} async-done(((bf16[1,1544,192]{1,2,0:T(8,128)(2,1)}), bf16[4,1544,192]{1,2,0:T(8,128)(2,1)}) %all-gather.13.cloned.1.call-update) | async-done | bytes 2371600 | tf_op jit(solution)/shard_map/all_gather | solution.py:138
  69.5 3.9 collective-permute-done
  73.4 3.0 broadcast_select_fusion.1
  78.2 2.0 fusion.15
  80.4 1.5 fusion.53
  83.1 5.0 fusion
  88.1 2.6 exponential_reduce_fusion
  90.7 1.9 copy-done.2
  92.6 10.1 %fusion.1 = bf16[12,512,512]{1,2,0:T(8,128)(2,1)} fusion(f32[12,512,512]{1,2,0:T(8,128)} %copy-done.2, f32[12,512]{1,0:T(8,128)S(1)} %log_add_fusion, pred[512]{0:T(512)(128)(4,1)S(1)} %iota_compare_fusion.1), kind=kLoop, calls=%fused_computation.7 | loop fusion | flops 12582912 | bytes 18899456 | tf_op jit(solution)/shard_map/convert_element_type | solution.py:40
  102.7 4.1 convolution_convert_fusion.3
  106.9 2.7 fusion.55
  113.7 61.0 %all-gather.7.cloned.1.call-done = bf16[2048,768]{1,0:T(8,128)(2,1)} async-done(((bf16[512,768]{1,0:T(8,128)(2,1)}), bf16[2048,768]{1,0:T(8,128)(2,1)}) %all-gather.7.cloned.1.call-update) | async-done | bytes 3145744 | tf_op jit(solution)/shard_map/all_gather | solution.py:171
  174.7 18.4 %multiply_convert_fusion.1 = (bf16[2048,768]{1,0:T(8,128)(2,1)S(1)}, f32[2048,768]{1,0:T(8,128)}, f32[2048,768]{1,0:T(8,128)}) fusion(f32[768]{0:T(1024)} %convert_element_type.142, bf16[2048,768]{1,0:T(8,128)(2,1)} %all-gather.7.cloned.1.call-done, bf16[768,768]{1,0:T(8,128)(2,1)S(1)} %copy-done), kind=kOutput, calls=%fused_computation.11 | convolution fusion | flops 2519728128 | bytes 20057088 | tf_op jit(solution)/shard_map/dot_general | solution.py:172
  193.2 1.6 copy-done.53
  194.8 3.9 convolution_convert_fusion.1
  198.8 59.1 %reduce-scatter.8.cloned.1.call-done = bf16[512,768]{1,0:T(8,128)(2,1)} async-done(((bf16[2048,768]{1,0:T(8,128)(2,1)}), bf16[512,768]{1,0:T(8,128)(2,1)}) %reduce-scatter.8.cloned.1.call-update) | async-done | bytes 786448 | tf_op jit(solution)/shard_map/reduce_scatter | solution.py:175
  258.0 1.8 fusion.51
  261.3 1.6 fusion.50
  264.1 1.7 convert_reduce_fusion.3
  265.8 11.1 %reduce-scatter.10.cloned.1.call-start = ((), (), s32[]{:S(2)}) async-start(), calls=%async_computation.8 | async-start | bytes 3932160 | tf_op jit(solution)/shard_map/reduce_scatter | solution.py:199
  276.9 52.4 %all-gather.9.cloned.1.call-done = bf16[2048,768]{1,0:T(8,128)(2,1)} async-done(((bf16[512,768]{1,0:T(8,128)(2,1)}), bf16[2048,768]{1,0:T(8,128)(2,1)}) %all-gather.9.cloned.1.call-update) | async-done | bytes 3145744 | tf_op jit(solution)/shard_map/all_gather | solution.py:187
  329.3 11.0 %convert_reduce_fusion = (f32[768]{0:T(1024)}, bf16[2048,768]{1,0:T(8,128)(2,1)S(1)}) fusion(f32[2048,768]{1,0:T(8,128)} %get-tuple-element.111, f32[2048,768]{1,0:T(8,128)} %get-tuple-element.128, f32[768]{0:T(1024)} %convert_element_type.142, bf16[2048,768]{1,0:T(8,128)(2,1)} %all-gather.9.cloned.1.call-done, bf16[768,768]{1,0:T(8,128)(2,1)} %param.26), kind=kOutput, calls=%fused_computation.9 | convolution fusion | flops 2442657024 | bytes 20060160 | tf_op jit(solution)/shard_map/dot_general | solution.py:25
  340.3 1.7 copy-done.54
  342.1 4.0 convolution_convert_fusion
  346.2 5.7 fusion.57
  351.9 2.7 fusion.56
  357.0 2.5 collective-permute-done.4
  359.5 1.8 dynamic-slice_add_fusion
  367.5 11.1 %collective-permute-done.5 = f32[192,768]{1,0:T(8,128)} collective-permute-done((f32[192,768]{1,0:T(8,128)}, f32[192,768]{1,0:T(8,128)}, u32[]{:S(2)}, u32[]{:S(2)}) %collective-permute-start.5) | collective-permute-done | bytes 589856 | tf_op jit(solution)/shard_map/ppermute | solution.py:84
  380.6 1.5 collective-permute-start.6
  382.1 8.4 %collective-permute-done.2 = f32[192,768]{1,0:T(8,128)} collective-permute-done((f32[192,768]{1,0:T(8,128)}, f32[192,768]{1,0:T(8,128)}, u32[]{:S(2)}, u32[]{:S(2)}) %collective-permute-start.2) | collective-permute-done | bytes 589856 | tf_op jit(solution)/shard_map/ppermute | solution.py:84
  393.8 2.9 slice.111
  396.7 1.7 dynamic-slice_add_fusion.4
  398.4 2.4 collective-permute-done.3
  400.8 1.7 dynamic-slice_add_fusion.5
  402.5 2.8 reduce-scatter.10.cloned.1.call-done
  405.3 1.8 convert_add_fusion
  412.8 2.2 fusion.59
  415.4 4.9 convolution_convert_fusion.2
  420.4 13.3 %multiply_reduce_fusion = (f32[12,512]{1,0:T(8,128)S(1)}, f32[12,512,512]{1,2,0:T(8,128)}) fusion(f32[12,512,512]{1,2,0:T(8,128)} %copy-done.2, f32[12,512]{1,0:T(8,128)S(1)} %copy-done.25, pred[512]{0:T(512)(128)(4,1)S(1)} %copy-done.42, f32[512,12,64]{0,2,1:T(8,128)S(1)} %bitcast.118, f32[12,64]{1,0:T(8,128)S(1)} %copy-done.29, ...), kind=kOutput, calls=%fused_computation.1 | convolution fusion | flops 419162112 | bytes 27577856 | tf_op jit(solution)/shard_map/pqhe,pkhe->phqk/dot_general | solution.py:48
  433.7 7.2 %multiply_convert_fusion = bf16[12,512,512]{1,2,0:T(8,128)(2,1)S(1)} fusion(f32[12,512,512]{1,2,0:T(8,128)} %get-tuple-element.130, f32[12,512,512]{1,2,0:T(8,128)S(1)} %bitcast.116, f32[12,512]{1,0:T(8,128)S(1)} %get-tuple-element.129, f32[12,512]{1,0:T(8,128)S(1)} %copy-done.25, pred[512]{0:T(512)(128)(4,1)S(1)} %copy-done.42), kind=kLoop, calls=%fused_computation | loop fusion | flops 18874368 | bytes 31506944 | tf_op jit(solution)/shard_map/convert_element_type | solution.py:52
  442.4 2.1 multiply_convert_fusion.2
  444.7 12.8 %reduce-scatter.12.cloned.1.call-done = f32[96,768]{1,0:T(8,128)} async-done(((f32[768,768]{1,0:T(8,128)}), f32[96,768]{1,0:T(8,128)}) %reduce-scatter.12.cloned.1.call-update) | async-done | bytes 294928 | tf_op jit(solution)/shard_map/reduce_scatter | solution.py:217
  457.5 6.0 fusion.33
  466.6 8.0 %collective-permute-done.7 = f32[96,768]{1,0:T(8,128)} collective-permute-done((f32[96,768]{1,0:T(8,128)S(1)}, f32[96,768]{1,0:T(8,128)}, u32[]{:S(2)}, u32[]{:S(2)}) %collective-permute-start.7) | collective-permute-done | bytes 294944 | tf_op jit(solution)/shard_map/ppermute | solution.py:94
  475.7 1.6 collective-permute-start.8
  477.3 2.2 collective-permute-done.10
  479.5 1.9 maximum_select_fusion.5
  483.0 11.1 %collective-permute-done.8 = f32[192,768]{1,0:T(8,128)} collective-permute-done((f32[192,768]{1,0:T(8,128)S(1)}, f32[192,768]{1,0:T(8,128)}, u32[]{:S(2)}, u32[]{:S(2)}) %collective-permute-start.8) | collective-permute-done | bytes 589856 | tf_op jit(solution)/shard_map/ppermute | solution.py:94
  494.0 1.8 maximum_select_fusion.2
  495.9 20.0 %collective-permute-done.11 = f32[192,768]{1,0:T(8,128)} collective-permute-done((f32[192,768]{1,0:T(8,128)}, f32[192,768]{1,0:T(8,128)}, u32[]{:S(2)}, u32[]{:S(2)}) %collective-permute-start.11) | collective-permute-done | bytes 589856 | tf_op jit(solution)/shard_map/ppermute | solution.py:94
  515.9 2.9 maximum_select_fusion.3
  531.8 1.6 tile.21
  533.4 3.3 maximum_select_fusion
  536.7 4.2 maximum_select_fusion.1
  543.0 1.5 copy.125
  544.6 2.6 select_maximum_fusion
  547.2 36.5 %reduce-scatter.14.cloned.1.call-done = f32[1,416,192]{1,2,0:T(8,128)} async-done(((f32[4,416,192]{1,2,0:T(8,128)}), f32[1,416,192]{1,2,0:T(8,128)}) %reduce-scatter.14.cloned.1.call-update) | async-done | bytes 319504 | tf_op jit(solution)/shard_map/reduce_scatter | solution.py:269
  583.7 5.4 fusion.22
  589.1 27.5 %all-gather.11.cloned.1.call-done = f32[8,416,192]{1,2,0:T(8,128)} async-done(((f32[1,416,192]{1,2,0:T(8,128)}), f32[8,416,192]{1,2,0:T(8,128)}) %all-gather.11.cloned.1.call-update) | async-done | bytes 2555920 | tf_op jit(solution)/shard_map/all_gather | solution.py:277
  624.1 3.3 slice.112
  627.3 2.2 copy.104
  629.5 1.8 copy.113
  (232 shorter events, 66.2 us)
Async XLA Ops:
  7.2 167.5 %copy-start = (bf16[768,768]{1,0:T(8,128)(2,1)S(1)}, bf16[768,768]{1,0:T(8,128)(2,1)}, u32[]{:S(2)}) copy-start(bf16[768,768]{1,0:T(8,128)(2,1)} %param.24) | copy-start | bytes 3538948
  7.2 61.1 %copy-start.52 = (s32[4]{0:T(128)S(1)}, s32[4]{0:T(128)}, u32[]{:S(2)}) copy-start(s32[4]{0:T(128)} %param.17) | copy-start | bytes 52
  7.2 61.1 %all-gather.13.cloned.1.call-start = ((), (), s32[]{:S(2)}) async-start(), calls=%async_computation.12 | async-start | bytes 3194880 | tf_op jit(solution)/shard_map/all_gather | solution.py:138
  11.3 163.4 %all-gather.7.cloned.1.call-start = ((), (), s32[]{:S(2)}) async-start(), calls=%async_computation.5 | async-start | bytes 3932160 | tf_op jit(solution)/shard_map/all_gather | solution.py:171
  68.3 5.2 collective-permute-start
  69.5 23.1 %copy-start.41 = (pred[512]{0:T(512)(128)(4,1)}, pred[512]{0:T(512)(128)(4,1)S(1)}, u32[]{:S(2)}) copy-start(pred[512]{0:T(512)(128)(4,1)S(1)} %iota_compare_fusion.1) | copy-start | bytes 1540
  77.9 2.4 copy-start.11
  81.9 20.8 %copy-start.4 = (f32[1,512,4,192]{1,3,0,2:T(8,128)}, f32[1,512,4,192]{1,3,0,2:T(8,128)S(1)}, u32[]{:S(2)}) copy-start(f32[1,512,4,192]{1,3,0,2:T(8,128)S(1)} %get-tuple-element.114) | copy-start | bytes 4718596
  88.1 4.5 copy-start.2
  92.6 10.1 %copy-start.24 = (f32[12,512]{1,0:T(8,128)}, f32[12,512]{1,0:T(8,128)S(1)}, u32[]{:S(2)}) copy-start(f32[12,512]{1,0:T(8,128)S(1)} %log_add_fusion) | copy-start | bytes 73732
  92.6 10.1 %copy-start.28 = (f32[12,64]{1,0:T(8,128)S(1)}, f32[12,64]{1,0:T(8,128)}, u32[]{:S(2)}) copy-start(f32[12,64]{1,0:T(8,128)} %reshape.339) | copy-start | bytes 9220
  102.7 4.1 copy-start.50
  102.7 4.1 copy-start.51
  106.9 2.8 copy-start.13
  106.9 4.3 copy-start.30
  106.9 4.2 copy-start.36
  112.4 145.6 %reduce-scatter.8.cloned.1.call-start = ((), (), s32[]{:S(2)}) async-start(), calls=%async_computation.6 | async-start | bytes 3932160 | tf_op jit(solution)/shard_map/reduce_scatter | solution.py:175
  174.7 20.1 %copy-start.48 = (bf16[768,768]{1,0:T(8,128)(2,1)S(1)}, bf16[768,768]{1,0:T(8,128)(2,1)}, u32[]{:S(2)}) copy-start(bf16[768,768]{1,0:T(8,128)(2,1)} %param.26) | copy-start | bytes 3538948
  198.8 130.6 %all-gather.9.cloned.1.call-start = ((), (), s32[]{:S(2)}) async-start(), calls=%async_computation.7 | async-start | bytes 3932160 | tf_op jit(solution)/shard_map/all_gather | solution.py:187
  263.0 2.8 copy-start.33
  265.8 139.5 %reduce-scatter.10.cloned.1.call-start = ((), (), s32[]{:S(2)}) async-start(), calls=%async_computation.8 | async-start | bytes 3932160 | tf_op jit(solution)/shard_map/reduce_scatter | solution.py:199
  346.1 111.4 %reduce-scatter.12.cloned.1.call-start = ((), (), s32[]{:S(2)}) async-start(), calls=%async_computation.9 | async-start | bytes 2654208 | tf_op jit(solution)/shard_map/reduce_scatter | solution.py:217
  346.2 5.7 copy-start.47
  346.2 5.7 copy-start.55
  351.9 2.8 copy-start.18
  356.5 3.0 collective-permute-start.4
  356.5 7.1 %collective-permute-start.1 = (f32[384,768]{1,0:T(8,128)}, f32[384,768]{1,0:T(8,128)}, u32[]{:S(2)}, u32[]{:S(2)}) collective-permute-start(f32[384,768]{1,0:T(8,128)} %get-tuple-element.132), channel_id=1, source_target_pairs={{0,4},{4,0},{8,12},{12,8},{16,20},{20,16},{24,28},{28,24},{1,5},{5... | collective-permute-start | bytes 3538952 | tf_op jit(solution)/shard_map/ppermute | solution.py:84
  357.0 6.6 %copy-start.17 = (f32[768,768]{1,0:T(8,128)S(1)}, f32[768,768]{1,0:T(8,128)}, u32[]{:S(2)}) copy-start(f32[768,768]{1,0:T(8,128)} %copy-done.16) | copy-start | bytes 7077892
  362.1 16.5 %collective-permute-start.5 = (f32[192,768]{1,0:T(8,128)}, f32[192,768]{1,0:T(8,128)}, u32[]{:S(2)}, u32[]{:S(2)}) collective-permute-start(f32[192,768]{1,0:T(8,128)} %constant_dynamic-slice_fusion.1), channel_id=1, source_target_pairs={{0,8},{4,12},{8,0},{12,4},{16,24},{20,28},{24,16},{28,20},{1,9},{5... | collective-permute-start | bytes 1769480 | tf_op jit(solution)/shard_map/ppermute | solution.py:84
  366.9 23.5 %collective-permute-start.2 = (f32[192,768]{1,0:T(8,128)}, f32[192,768]{1,0:T(8,128)}, u32[]{:S(2)}, u32[]{:S(2)}) collective-permute-start(f32[192,768]{1,0:T(8,128)} %constant_dynamic-slice_fusion.4), channel_id=1, source_target_pairs={{0,8},{4,12},{8,0},{12,4},{16,24},{20,28},{24,16},{28,20},{1,9},{5... | collective-permute-start | bytes 1769480 | tf_op jit(solution)/shard_map/ppermute | solution.py:84
  367.5 23.0 %copy-start.10 = (f32[384,768]{1,0:T(8,128)S(1)}, f32[384,768]{1,0:T(8,128)}, u32[]{:S(2)}) copy-start(f32[384,768]{1,0:T(8,128)} %copy-done.9) | copy-start | bytes 3538948
  379.8 11.8 %copy-start.19 = (f32[192,768]{1,0:T(8,128)}, f32[192,768]{1,0:T(8,128)S(1)}, u32[]{:S(2)}) copy-start(f32[192,768]{1,0:T(8,128)S(1)} %dynamic-slice_add_fusion.2) | copy-start | bytes 1769476
  380.6 16.1 %collective-permute-start.6 = (f32[96,768]{1,0:T(8,128)}, f32[96,768]{1,0:T(8,128)}, u32[]{:S(2)}, u32[]{:S(2)}) collective-permute-start(f32[96,768]{1,0:T(8,128)} %constant_dynamic-slice_fusion), channel_id=1, source_target_pairs={{0,16},{4,20},{8,24},{12,28},{16,0},{20,4},{24,8},{28,12},{1,17},{... | collective-permute-start | bytes 884744 | tf_op jit(solution)/shard_map/ppermute | solution.py:84
  392.3 4.4 copy-start.20
  392.3 8.5 %collective-permute-start.3 = (f32[96,768]{1,0:T(8,128)}, f32[96,768]{1,0:T(8,128)}, u32[]{:S(2)}, u32[]{:S(2)}) collective-permute-start(f32[96,768]{1,0:T(8,128)} %constant_dynamic-slice_fusion.3), channel_id=1, source_target_pairs={{0,16},{4,20},{8,24},{12,28},{16,0},{20,4},{24,8},{28,12},{1,17},{... | collective-permute-start | bytes 884744 | tf_op jit(solution)/shard_map/ppermute | solution.py:84
  398.4 8.8 %copy-start.32 = (f32[512]{0:T(512)S(1)}, f32[512]{0:T(512)}, u32[]{:S(2)}) copy-start(f32[512]{0:T(512)} %copy-done.31) | copy-start | bytes 6148
  409.0 2.7 copy-start.8
  409.1 2.6 copy-start.43
  415.1 5.3 copy-start.5
  415.1 5.3 copy-start.25
  415.1 5.3 copy-start.29
  415.1 5.3 copy-start.42
  415.1 127.9 %reduce-scatter.16.cloned.1.call-start = ((), (), s32[]{:S(2)}) async-start(), calls=%async_computation.13 | async-start | bytes 7962624
  415.4 18.3 %slice-start = ((s8[12582912]{0:T(1024)(128)(4,1)}), s8[4194304]{0:T(1024)(128)(4,1)S(1)}, s32[]{:S(2)}) async-start(s8[12582912]{0:T(1024)(128)(4,1)} %bitcast.115), calls=%async_computation.14 | async-start | bytes 8388608
  420.4 13.3 %slice-start.1 = ((s8[12582912]{0:T(1024)(128)(4,1)}), s8[4194304]{0:T(1024)(128)(4,1)S(1)}, s32[]{:S(2)}) async-start(s8[12582912]{0:T(1024)(128)(4,1)} %bitcast.115), calls=%async_computation.15 | async-start | bytes 8388608
  420.4 13.3 %slice-start.2 = ((s8[12582912]{0:T(1024)(128)(4,1)}), s8[4194304]{0:T(1024)(128)(4,1)S(1)}, s32[]{:S(2)}) async-start(s8[12582912]{0:T(1024)(128)(4,1)} %bitcast.115), calls=%async_computation.16 | async-start | bytes 8388608
  463.6 2.4 copy-start.22
  463.6 120.1 %reduce-scatter.14.cloned.1.call-start = ((), (), s32[]{:S(2)}) async-start(), calls=%async_computation.10 | async-start | bytes 1966080 | tf_op jit(solution)/shard_map/reduce_scatter | solution.py:269
  464.5 10.0 %collective-permute-start.7 = (f32[96,768]{1,0:T(8,128)S(1)}, f32[96,768]{1,0:T(8,128)}, u32[]{:S(2)}, u32[]{:S(2)}) collective-permute-start(f32[96,768]{1,0:T(8,128)S(1)} %copy-done.23), channel_id=1, source_target_pairs={{0,16},{4,20},{8,24},{12,28},{16,0},{20,4},{24,8},{28,12},{1,17},{... | collective-permute-start | bytes 884744 | tf_op jit(solution)/shard_map/ppermute | solution.py:94
  466.0 13.5 %collective-permute-start.10 = (f32[96,768]{1,0:T(8,128)S(1)}, f32[96,768]{1,0:T(8,128)}, u32[]{:S(2)}, u32[]{:S(2)}) collective-permute-start(f32[96,768]{1,0:T(8,128)S(1)} %copy-done.22), channel_id=1, source_target_pairs={{0,16},{4,20},{8,24},{12,28},{16,0},{20,4},{24,8},{28,12},{1,17},{... | collective-permute-start | bytes 884744 | tf_op jit(solution)/shard_map/ppermute | solution.py:94
  475.7 7.3 %copy-start.15 = (f32[192,768]{1,0:T(8,128)}, f32[192,768]{1,0:T(8,128)S(1)}, u32[]{:S(2)}) copy-start(f32[192,768]{1,0:T(8,128)S(1)} %maximum_select_fusion.4) | copy-start | bytes 1769476
  475.7 18.3 %collective-permute-start.8 = (f32[192,768]{1,0:T(8,128)S(1)}, f32[192,768]{1,0:T(8,128)}, u32[]{:S(2)}, u32[]{:S(2)}) collective-permute-start(f32[192,768]{1,0:T(8,128)S(1)} %maximum_select_fusion.4), channel_id=1, source_target_pairs={{0,8},{4,12},{8,0},{12,4},{16,24},{20,28},{24,16},{28,20},{1,9},{5... | collective-permute-start | bytes 1769480 | tf_op jit(solution)/shard_map/ppermute | solution.py:94
  481.5 34.4 %collective-permute-start.11 = (f32[192,768]{1,0:T(8,128)}, f32[192,768]{1,0:T(8,128)}, u32[]{:S(2)}, u32[]{:S(2)}) collective-permute-start(f32[192,768]{1,0:T(8,128)} %maximum_select_fusion.5), channel_id=1, source_target_pairs={{0,8},{4,12},{8,0},{12,4},{16,24},{20,28},{24,16},{28,20},{1,9},{5... | collective-permute-start | bytes 1769480 | tf_op jit(solution)/shard_map/ppermute | solution.py:94
  482.9 36.4 %copy-start.39 = (f32[768]{0:T(1024)S(1)}, f32[768]{0:T(1024)}, u32[]{:S(2)}) copy-start(f32[768]{0:T(1024)} %get-tuple-element.92) | copy-start | bytes 9220
  482.9 37.1 %copy-start.38 = (f32[768]{0:T(1024)S(1)}, f32[768]{0:T(1024)}, u32[]{:S(2)}) copy-start(f32[768]{0:T(1024)} %get-tuple-element.95) | copy-start | bytes 9220
  483.0 37.8 %copy-start.40 = (f32[768]{0:T(1024)S(1)}, f32[768]{0:T(1024)}, u32[]{:S(2)}) copy-start(f32[768]{0:T(1024)} %get-tuple-element.98) | copy-start | bytes 9220
  483.0 38.4 %copy-start.46 = (f32[768]{0:T(1024)S(1)}, f32[768]{0:T(1024)}, u32[]{:S(2)}) copy-start(f32[768]{0:T(1024)} %get-tuple-element.102) | copy-start | bytes 9220
  495.8 37.6 %collective-permute-start.9 = (f32[384,768]{1,0:T(8,128)S(1)}, f32[384,768]{1,0:T(8,128)}, u32[]{:S(2)}, u32[]{:S(2)}) collective-permute-start(f32[384,768]{1,0:T(8,128)S(1)} %maximum_select_fusion.2), channel_id=1, source_target_pairs={{0,4},{4,0},{8,12},{12,8},{16,20},{20,16},{24,28},{28,24},{1,5},{5... | collective-permute-start | bytes 3538952 | tf_op jit(solution)/shard_map/ppermute | solution.py:94
  518.8 17.9 %collective-permute-start.12 = (f32[384,768]{1,0:T(8,128)}, f32[384,768]{1,0:T(8,128)}, u32[]{:S(2)}, u32[]{:S(2)}) collective-permute-start(f32[384,768]{1,0:T(8,128)} %maximum_select_fusion.3), channel_id=1, source_target_pairs={{0,4},{4,0},{8,12},{12,8},{16,20},{20,16},{24,28},{28,24},{1,5},{5... | collective-permute-start | bytes 3538952 | tf_op jit(solution)/shard_map/ppermute | solution.py:94
  536.7 4.2 copy-start.26
  536.7 5.4 copy-start.27
  544.5 39.2 %copy-start.44 = (f32[512]{0:T(512)S(1)}, f32[512]{0:T(512)}, u32[]{:S(2)}) copy-start(f32[512]{0:T(512)} %copy-done.43) | copy-start | bytes 6148
  547.2 69.5 %all-gather.11.cloned.1.call-start = ((), (), s32[]{:S(2)}) async-start(), calls=%async_computation.11 | async-start | bytes 3538944 | tf_op jit(solution)/shard_map/all_gather | solution.py:277
  629.5 4.8 copy-start.1
  (17 other events, 24.2 us)
Sparse Core Ops, SparseCore 0:
  11.4 56.8 all-gather.12
  112.5 62.2 all-gather.6
  198.9 59.0 reduce-scatter.7
  265.9 63.3 all-gather.8
  346.2 59.0 reduce-scatter.9
  415.2 42.2 reduce-scatter.11
  463.7 76.5 reduce-scatter.15
  547.3 36.3 reduce-scatter.13
  585.6 31.0 all-gather.10

commit v3 on v2

--- a/solution.py
+++ b/solution.py
@@ -214,7 +214,9 @@
         context_grad, early = lax.optimization_barrier(
             (context_grad, contract(attn_grad, context_low, 0, 0))
         )
-        early = lax.psum_scatter(early, "dp", scatter_dimension=0, tiled=True)
+        early = lax.psum_scatter(
+            early.astype(jnp.bfloat16), "dp", scatter_dimension=0, tiled=True
+        ).astype(jnp.float32)
         query_grad, key_grad, value_grad = attend_backward(
             queries, key_rows, value_rows, attn_probs, context_grad, factor
         )
@@ -259,8 +261,11 @@
         tail_rows = tail.shape[0]
         tail = jnp.pad(tail, ((0, -(-tail_rows // 8) * 8 - tail_rows), (0, 0)))
         late = lax.psum_scatter(
-            grad_qkv_full.reshape(3 * width, width), "dp", scatter_dimension=0, tiled=True
-        )
+            grad_qkv_full.reshape(3 * width, width).astype(jnp.bfloat16),
+            "dp",
+            scatter_dimension=0,
+            tiled=True,
+        ).astype(jnp.float32)
         joined = jnp.concatenate([late, early, tail], axis=0)
         if halved:
             ffn_grads = tuple(dp_double(g, dp_size) for g in ffn_grads)

time: 652 us -> 640 us (0.982)
  waiting for transfers between devices: 379 us -> 369 us
  matrix products: 95.7 us -> 87.8 us
    ppermute x6, waiting for transfers between devices: 41.3 us -> 32.5 us  [dp_double(): got = lax.ppermute(kept, 'dp', [(i, i ^ 1 << step) for i in range(dp_size)])]
    unnamed x128 -> x126, local copies, waits for them, and re-layouts: 21.8 us -> 22.5 us
  transfers between devices with their start and end apart: 22 -> 22, of which waited for: 17 -> 17; matrix products, arithmetic and copies ran while one was open for 15% -> 14% of each run, Pallas kernels for 0% -> 0%
where the time goes in v3:
time: 640 us; the launch traced here: 629 us
  waiting for transfers between devices  369 us (58%)
  matrix products  87.8 us (14%)
  other arithmetic  75.5 us (12%)
  local copies, waits for them, and re-layouts  58.8 us (9%)
  starting transfers between devices  22.6 us (4%)
  between operations  15.1 us (2%)
    all_gather x1, waiting for transfers between devices, per_device(): ffn_rows = lax.all_gather(middle_low, 'tensor', axis=0, tiled=True)  61 us
    reduce_scatter x1, waiting for transfers between devices, per_device(): lax.psum_scatter(jnp.dot(hidden, down_weight, preferred_element_type=jnp....  59.2 us
    all_gather x1, waiting for transfers between devices, per_device(): mine = lax.all_gather(mine, 'tensor', axis=0, tiled=False)  56.9 us
    all_gather x1, waiting for transfers between devices, per_device(): branch_rows = lax.all_gather(branch_grad, 'tensor', axis=0, tiled=True)  52.4 us
    reduce_scatter x1, waiting for transfers between devices, per_device(): lax.psum_scatter(joined.reshape(joined.shape[0], groups, shard).transpose...  35.7 us
    ppermute x6, waiting for transfers between devices, dp_double(): got = lax.ppermute(kept, 'dp', [(i, i ^ 1 << step) for i in range(dp_size)])  32.5 us
    all_gather x1, waiting for transfers between devices, per_device(): joined = lax.all_gather(joined, 'dp', axis=0, tiled=False)  27.5 us
    dot_general x5, matrix products, contract(): lax.dot_general(left, right, (((left_dim,), (right_dim,)), ((), ())), pre...  25.4 us
  transfers between devices with their start and end apart: 22, of which 17 were waited for; matrix products, arithmetic and copies ran while one was open for 14% of the time, Pallas kernels for 0%

profile of v3, /device:TPU:0, one launch (start us, length us, event | category | flops | bytes accessed | tf_op | source)
XLA Modules:
  0.0 628.8 jit_solution(9249797378092061232)
XLA Ops:
  9.4 1.8 fusion.39
  11.3 56.9 %all-gather.13.cloned.1.call-done = bf16[4,1544,192]{1,2,0:T(8,128)(2,1)} async-done(((bf16[1,1544,192]{1,2,0:T(8,128)(2,1)}), bf16[4,1544,192]{1,2,0:T(8,128)(2,1)}) %all-gather.13.cloned.1.call-update) | async-done | bytes 2371600 | tf_op jit(solution)/shard_map/all_gather | solution.py:138
  69.5 3.9 collective-permute-done
  73.4 3.0 broadcast_select_fusion.1
  78.2 2.0 fusion.15
  83.1 5.0 fusion
  88.1 2.6 exponential_reduce_fusion
  90.7 1.9 copy-done.2
  92.6 10.1 %fusion.1 = bf16[12,512,512]{1,2,0:T(8,128)(2,1)} fusion(f32[12,512,512]{1,2,0:T(8,128)} %copy-done.2, f32[12,512]{1,0:T(8,128)S(1)} %log_add_fusion, pred[512]{0:T(512)(128)(4,1)S(1)} %iota_compare_fusion.1), kind=kLoop, calls=%fused_computation.7 | loop fusion | flops 12582912 | bytes 18899456 | tf_op jit(solution)/shard_map/convert_element_type | solution.py:40
  102.7 4.1 convolution_convert_fusion.4
  106.9 2.7 fusion.54
  113.7 61.0 %all-gather.7.cloned.1.call-done = bf16[2048,768]{1,0:T(8,128)(2,1)} async-done(((bf16[512,768]{1,0:T(8,128)(2,1)}), bf16[2048,768]{1,0:T(8,128)(2,1)}) %all-gather.7.cloned.1.call-update) | async-done | bytes 3145744 | tf_op jit(solution)/shard_map/all_gather | solution.py:171
  174.7 18.4 %multiply_convert_fusion.1 = (bf16[2048,768]{1,0:T(8,128)(2,1)S(1)}, f32[2048,768]{1,0:T(8,128)}, f32[2048,768]{1,0:T(8,128)}) fusion(f32[768]{0:T(1024)} %convert_element_type.160, bf16[2048,768]{1,0:T(8,128)(2,1)} %all-gather.7.cloned.1.call-done, bf16[768,768]{1,0:T(8,128)(2,1)S(1)} %copy-done), kind=kOutput, calls=%fused_computation.11 | convolution fusion | flops 2519728128 | bytes 20057088 | tf_op jit(solution)/shard_map/dot_general | solution.py:172
  193.2 1.6 copy-done.53
  194.8 3.9 convolution_convert_fusion.1
  198.8 59.2 %reduce-scatter.8.cloned.1.call-done = bf16[512,768]{1,0:T(8,128)(2,1)} async-done(((bf16[2048,768]{1,0:T(8,128)(2,1)}), bf16[512,768]{1,0:T(8,128)(2,1)}) %reduce-scatter.8.cloned.1.call-update) | async-done | bytes 786448 | tf_op jit(solution)/shard_map/reduce_scatter | solution.py:175
  258.0 1.8 fusion.50
  261.4 2.1 fusion.49
  264.1 3.1 convert_reduce_fusion.3
  267.2 11.1 %reduce-scatter.10.cloned.1.call-start = ((), (), s32[]{:S(2)}) async-start(), calls=%async_computation.8 | async-start | bytes 3932160 | tf_op jit(solution)/shard_map/reduce_scatter | solution.py:199
  278.3 52.4 %all-gather.9.cloned.1.call-done = bf16[2048,768]{1,0:T(8,128)(2,1)} async-done(((bf16[512,768]{1,0:T(8,128)(2,1)}), bf16[2048,768]{1,0:T(8,128)(2,1)}) %all-gather.9.cloned.1.call-update) | async-done | bytes 3145744 | tf_op jit(solution)/shard_map/all_gather | solution.py:187
  330.7 11.0 %convert_reduce_fusion = (f32[768]{0:T(1024)}, bf16[2048,768]{1,0:T(8,128)(2,1)S(1)}) fusion(f32[2048,768]{1,0:T(8,128)} %get-tuple-element.111, f32[2048,768]{1,0:T(8,128)} %get-tuple-element.128, f32[768]{0:T(1024)} %convert_element_type.160, bf16[2048,768]{1,0:T(8,128)(2,1)} %all-gather.9.cloned.1.call-done, bf16[768,768]{1,0:T(8,128)(2,1)} %param.26), kind=kOutput, calls=%fused_computation.9 | convolution fusion | flops 2442657024 | bytes 20060160 | tf_op jit(solution)/shard_map/dot_general | solution.py:25
  341.7 1.7 copy-done.54
  343.4 4.0 convolution_convert_fusion
  347.6 5.7 fusion.56
  353.3 2.7 fusion.55
  358.4 2.5 collective-permute-done.4
  360.8 1.8 dynamic-slice_add_fusion
  368.8 11.1 %collective-permute-done.5 = f32[192,768]{1,0:T(8,128)} collective-permute-done((f32[192,768]{1,0:T(8,128)}, f32[192,768]{1,0:T(8,128)}, u32[]{:S(2)}, u32[]{:S(2)}) %collective-permute-start.5) | collective-permute-done | bytes 589856 | tf_op jit(solution)/shard_map/ppermute | solution.py:84
  383.4 8.4 %collective-permute-done.2 = f32[192,768]{1,0:T(8,128)} collective-permute-done((f32[192,768]{1,0:T(8,128)}, f32[192,768]{1,0:T(8,128)}, u32[]{:S(2)}, u32[]{:S(2)}) %collective-permute-start.2) | collective-permute-done | bytes 589856 | tf_op jit(solution)/shard_map/ppermute | solution.py:84
  395.2 2.9 slice.111
  398.1 1.7 dynamic-slice_add_fusion.4
  399.8 2.4 collective-permute-done.3
  402.2 1.7 dynamic-slice_add_fusion.5
  403.9 2.8 reduce-scatter.10.cloned.1.call-done
  406.7 1.8 convert_add_fusion
  412.3 1.8 fusion.58
  416.4 9.9 %multiply_reduce_fusion = (f32[12,512]{1,0:T(8,128)S(1)}, f32[12,512,512]{1,2,0:T(8,128)S(1)}) fusion(f32[12,512,512]{1,2,0:T(8,128)} %copy-done.2, f32[12,512]{1,0:T(8,128)S(1)} %copy-done.24, pred[512]{0:T(512)(128)(4,1)S(1)} %copy-done.41, f32[512,12,64]{0,2,1:T(8,128)S(1)} %bitcast.118, f32[12,64]{1,0:T(8,128)S(1)} %copy-done.26, ...), kind=kOutput, calls=%fused_computation.1 | convolution fusion | flops 419162112 | bytes 27577856 | tf_op jit(solution)/shard_map/pqhe,pkhe->phqk/dot_general | solution.py:48
  426.4 7.4 %multiply_convert_fusion = bf16[12,512,512]{1,2,0:T(8,128)(2,1)S(1)} fusion(f32[12,512,512]{1,2,0:T(8,128)S(1)} %get-tuple-element.130, f32[12,512,512]{1,2,0:T(8,128)} %copy-done.2, f32[12,512]{1,0:T(8,128)S(1)} %get-tuple-element.129, f32[12,512]{1,0:T(8,128)S(1)} %copy-done.24, pred[512]{0:T(512)(128)(4,1)S(1)} %copy-done.41), kind=kLoop, calls=%fused_computation | loop fusion | flops 18874368 | bytes 31506944 | tf_op jit(solution)/shard_map/convert_element_type | solution.py:52
  433.8 2.0 convolution_convert_fusion.3
  437.2 2.0 multiply_convert_fusion.2
  439.5 12.4 %reduce-scatter.12.cloned.1.call-done = bf16[96,768]{1,0:T(8,128)(2,1)} async-done(((bf16[768,768]{1,0:T(8,128)(2,1)}), bf16[96,768]{1,0:T(8,128)(2,1)}) %reduce-scatter.12.cloned.1.call-update) | async-done | bytes 147472 | tf_op jit(solution)/shard_map/reduce_scatter | solution.py:217
  451.9 1.6 convert_element_type.175
  453.6 4.9 convolution_convert_fusion.2
  461.5 8.0 %collective-permute-done.7 = f32[96,768]{1,0:T(8,128)} collective-permute-done((f32[96,768]{1,0:T(8,128)S(1)}, f32[96,768]{1,0:T(8,128)}, u32[]{:S(2)}, u32[]{:S(2)}) %collective-permute-start.7) | collective-permute-done | bytes 294944 | tf_op jit(solution)/shard_map/ppermute | solution.py:94
  472.1 2.2 collective-permute-done.10
  474.3 1.9 maximum_select_fusion.5
  481.1 10.3 %collective-permute-done.8 = f32[192,768]{1,0:T(8,128)} collective-permute-done((f32[192,768]{1,0:T(8,128)S(1)}, f32[192,768]{1,0:T(8,128)}, u32[]{:S(2)}, u32[]{:S(2)}) %collective-permute-start.8) | collective-permute-done | bytes 589856 | tf_op jit(solution)/shard_map/ppermute | solution.py:94
  491.4 1.7 maximum_select_fusion.2
  493.2 12.1 %collective-permute-done.11 = f32[192,768]{1,0:T(8,128)} collective-permute-done((f32[192,768]{1,0:T(8,128)}, f32[192,768]{1,0:T(8,128)}, u32[]{:S(2)}, u32[]{:S(2)}) %collective-permute-start.11) | collective-permute-done | bytes 589856 | tf_op jit(solution)/shard_map/ppermute | solution.py:94
  505.3 2.8 maximum_select_fusion.3
  515.0 1.6 tile.21
  516.6 1.9 copy.102
  520.4 1.8 copy.126
  522.2 3.3 maximum_select_fusion
  525.5 4.2 maximum_select_fusion.1
  529.6 2.1 copy.125
  532.8 2.6 select_maximum_fusion
  535.5 35.7 %reduce-scatter.14.cloned.1.call-done = f32[1,416,192]{1,2,0:T(8,128)} async-done(((f32[4,416,192]{1,2,0:T(8,128)}), f32[1,416,192]{1,2,0:T(8,128)}) %reduce-scatter.14.cloned.1.call-update) | async-done | bytes 319504 | tf_op jit(solution)/shard_map/reduce_scatter | solution.py:274
  571.3 5.4 fusion.22
  576.7 27.5 %all-gather.11.cloned.1.call-done = f32[8,416,192]{1,2,0:T(8,128)} async-done(((f32[1,416,192]{1,2,0:T(8,128)}), f32[8,416,192]{1,2,0:T(8,128)}) %all-gather.11.cloned.1.call-update) | async-done | bytes 2555920 | tf_op jit(solution)/shard_map/all_gather | solution.py:282
  611.6 3.3 slice.112
  614.9 2.2 copy.104
  617.1 1.8 copy.113
  (232 shorter events, 68.2 us)
Async XLA Ops:
  7.2 167.6 %copy-start = (bf16[768,768]{1,0:T(8,128)(2,1)S(1)}, bf16[768,768]{1,0:T(8,128)(2,1)}, u32[]{:S(2)}) copy-start(bf16[768,768]{1,0:T(8,128)(2,1)} %param.24) | copy-start | bytes 3538948
  7.2 61.1 %copy-start.52 = (s32[4]{0:T(128)S(1)}, s32[4]{0:T(128)}, u32[]{:S(2)}) copy-start(s32[4]{0:T(128)} %param.17) | copy-start | bytes 52
  7.2 61.1 %all-gather.13.cloned.1.call-start = ((), (), s32[]{:S(2)}) async-start(), calls=%async_computation.12 | async-start | bytes 3194880 | tf_op jit(solution)/shard_map/all_gather | solution.py:138
  11.3 163.5 %all-gather.7.cloned.1.call-start = ((), (), s32[]{:S(2)}) async-start(), calls=%async_computation.5 | async-start | bytes 3932160 | tf_op jit(solution)/shard_map/all_gather | solution.py:171
  68.3 5.2 collective-permute-start
  69.5 23.1 %copy-start.40 = (pred[512]{0:T(512)(128)(4,1)}, pred[512]{0:T(512)(128)(4,1)S(1)}, u32[]{:S(2)}) copy-start(pred[512]{0:T(512)(128)(4,1)S(1)} %iota_compare_fusion.1) | copy-start | bytes 1540
  76.4 3.9 copy-start.3
  77.3 3.0 copy-start.10
  81.9 20.8 %copy-start.4 = (f32[1,512,4,192]{1,3,0,2:T(8,128)}, f32[1,512,4,192]{1,3,0,2:T(8,128)S(1)}, u32[]{:S(2)}) copy-start(f32[1,512,4,192]{1,3,0,2:T(8,128)S(1)} %get-tuple-element.114) | copy-start | bytes 4718596
  88.1 4.5 copy-start.2
  92.6 10.1 %copy-start.23 = (f32[12,512]{1,0:T(8,128)}, f32[12,512]{1,0:T(8,128)S(1)}, u32[]{:S(2)}) copy-start(f32[12,512]{1,0:T(8,128)S(1)} %log_add_fusion) | copy-start | bytes 73732
  92.6 10.1 %copy-start.25 = (f32[12,64]{1,0:T(8,128)S(1)}, f32[12,64]{1,0:T(8,128)}, u32[]{:S(2)}) copy-start(f32[12,64]{1,0:T(8,128)} %reshape.337) | copy-start | bytes 9220
  102.7 4.1 copy-start.50
  102.7 4.1 copy-start.51
  106.9 2.8 copy-start.21
  106.9 4.3 copy-start.27
  106.9 4.2 copy-start.34
  112.4 145.6 %reduce-scatter.8.cloned.1.call-start = ((), (), s32[]{:S(2)}) async-start(), calls=%async_computation.6 | async-start | bytes 3932160 | tf_op jit(solution)/shard_map/reduce_scatter | solution.py:175
  174.7 20.1 %copy-start.48 = (bf16[768,768]{1,0:T(8,128)(2,1)S(1)}, bf16[768,768]{1,0:T(8,128)(2,1)}, u32[]{:S(2)}) copy-start(bf16[768,768]{1,0:T(8,128)(2,1)} %param.26) | copy-start | bytes 3538948
  198.8 131.9 %all-gather.9.cloned.1.call-start = ((), (), s32[]{:S(2)}) async-start(), calls=%async_computation.7 | async-start | bytes 3932160 | tf_op jit(solution)/shard_map/all_gather | solution.py:187
  258.0 2.2 copy-start.11
  258.0 2.2 copy-start.35
  267.2 139.5 %reduce-scatter.10.cloned.1.call-start = ((), (), s32[]{:S(2)}) async-start(), calls=%async_computation.8 | async-start | bytes 3932160 | tf_op jit(solution)/shard_map/reduce_scatter | solution.py:199
  347.5 104.4 %reduce-scatter.12.cloned.1.call-start = ((), (), s32[]{:S(2)}) async-start(), calls=%async_computation.9 | async-start | bytes 1327104 | tf_op jit(solution)/shard_map/reduce_scatter | solution.py:217
  347.5 5.7 copy-start.47
  347.5 5.7 copy-start.55
  353.3 2.8 copy-start.15
  356.1 1.8 copy-start.13
  357.9 3.0 collective-permute-start.4
  357.9 7.1 %collective-permute-start.1 = (f32[384,768]{1,0:T(8,128)}, f32[384,768]{1,0:T(8,128)}, u32[]{:S(2)}, u32[]{:S(2)}) collective-permute-start(f32[384,768]{1,0:T(8,128)} %get-tuple-element.132), channel_id=1, source_target_pairs={{0,4},{4,0},{8,12},{12,8},{16,20},{20,16},{24,28},{28,24},{1,5},{5... | collective-permute-start | bytes 3538952 | tf_op jit(solution)/shard_map/ppermute | solution.py:84
  358.4 6.6 %copy-start.14 = (f32[768,768]{1,0:T(8,128)S(1)}, f32[768,768]{1,0:T(8,128)}, u32[]{:S(2)}) copy-start(f32[768,768]{1,0:T(8,128)} %copy-done.13) | copy-start | bytes 7077892
  363.5 16.5 %collective-permute-start.5 = (f32[192,768]{1,0:T(8,128)}, f32[192,768]{1,0:T(8,128)}, u32[]{:S(2)}, u32[]{:S(2)}) collective-permute-start(f32[192,768]{1,0:T(8,128)} %constant_dynamic-slice_fusion.1), channel_id=1, source_target_pairs={{0,8},{4,12},{8,0},{12,4},{16,24},{20,28},{24,16},{28,20},{1,9},{5... | collective-permute-start | bytes 1769480 | tf_op jit(solution)/shard_map/ppermute | solution.py:84
  368.3 23.5 %collective-permute-start.2 = (f32[192,768]{1,0:T(8,128)}, f32[192,768]{1,0:T(8,128)}, u32[]{:S(2)}, u32[]{:S(2)}) collective-permute-start(f32[192,768]{1,0:T(8,128)} %constant_dynamic-slice_fusion.4), channel_id=1, source_target_pairs={{0,8},{4,12},{8,0},{12,4},{16,24},{20,28},{24,16},{28,20},{1,9},{5... | collective-permute-start | bytes 1769480 | tf_op jit(solution)/shard_map/ppermute | solution.py:84
  368.8 23.0 %copy-start.9 = (f32[384,768]{1,0:T(8,128)S(1)}, f32[384,768]{1,0:T(8,128)}, u32[]{:S(2)}) copy-start(f32[384,768]{1,0:T(8,128)} %copy-done.8) | copy-start | bytes 3538948
  381.1 11.8 %copy-start.16 = (f32[192,768]{1,0:T(8,128)}, f32[192,768]{1,0:T(8,128)S(1)}, u32[]{:S(2)}) copy-start(f32[192,768]{1,0:T(8,128)S(1)} %dynamic-slice_add_fusion.2) | copy-start | bytes 1769476
  381.9 16.1 %collective-permute-start.6 = (f32[96,768]{1,0:T(8,128)}, f32[96,768]{1,0:T(8,128)}, u32[]{:S(2)}, u32[]{:S(2)}) collective-permute-start(f32[96,768]{1,0:T(8,128)} %constant_dynamic-slice_fusion), channel_id=1, source_target_pairs={{0,16},{4,20},{8,24},{12,28},{16,0},{20,4},{24,8},{28,12},{1,17},{... | collective-permute-start | bytes 884744 | tf_op jit(solution)/shard_map/ppermute | solution.py:84
  393.7 4.4 copy-start.17
  393.7 8.5 %collective-permute-start.3 = (f32[96,768]{1,0:T(8,128)}, f32[96,768]{1,0:T(8,128)}, u32[]{:S(2)}, u32[]{:S(2)}) collective-permute-start(f32[96,768]{1,0:T(8,128)} %constant_dynamic-slice_fusion.3), channel_id=1, source_target_pairs={{0,16},{4,20},{8,24},{12,28},{16,0},{20,4},{24,8},{28,12},{1,17},{... | collective-permute-start | bytes 884744 | tf_op jit(solution)/shard_map/ppermute | solution.py:84
  399.8 8.8 %copy-start.29 = (f32[512]{0:T(512)S(1)}, f32[512]{0:T(512)}, u32[]{:S(2)}) copy-start(f32[512]{0:T(512)} %copy-done.28) | copy-start | bytes 6148
  410.4 1.9 copy-start.22
  410.4 3.8 copy-start.42
  411.5 2.6 copy-start.18
  415.2 114.5 %reduce-scatter.16.cloned.1.call-start = ((), (), s32[]{:S(2)}) async-start(), calls=%async_computation.13 | async-start | bytes 3981312
  416.4 17.3 %slice-start = ((s8[6291456]{0:T(1024)(128)(4,1)}), s8[4194304]{0:T(1024)(128)(4,1)S(1)}, s32[]{:S(2)}) async-start(s8[6291456]{0:T(1024)(128)(4,1)} %bitcast.115), calls=%async_computation.14 | async-start | bytes 8388608
  426.3 7.4 %slice-start.1 = ((s8[6291456]{0:T(1024)(128)(4,1)}), s8[2097152]{0:T(1024)(128)(4,1)S(1)}, s32[]{:S(2)}) async-start(s8[6291456]{0:T(1024)(128)(4,1)} %bitcast.115), calls=%async_computation.15 | async-start | bytes 4194304
  458.5 2.4 copy-start.19
  458.5 19.8 %copy-start.37 = (f32[768]{0:T(1024)S(1)}, f32[768]{0:T(1024)}, u32[]{:S(2)}) copy-start(f32[768]{0:T(1024)} %get-tuple-element.92) | copy-start | bytes 9220
  458.5 20.5 %copy-start.36 = (f32[768]{0:T(1024)S(1)}, f32[768]{0:T(1024)}, u32[]{:S(2)}) copy-start(f32[768]{0:T(1024)} %get-tuple-element.95) | copy-start | bytes 9220
  458.5 21.1 %copy-start.38 = (f32[768]{0:T(1024)S(1)}, f32[768]{0:T(1024)}, u32[]{:S(2)}) copy-start(f32[768]{0:T(1024)} %get-tuple-element.98) | copy-start | bytes 9220
  458.5 21.8 %copy-start.45 = (f32[768]{0:T(1024)S(1)}, f32[768]{0:T(1024)}, u32[]{:S(2)}) copy-start(f32[768]{0:T(1024)} %get-tuple-element.102) | copy-start | bytes 9220
  458.5 112.7 %reduce-scatter.14.cloned.1.call-start = ((), (), s32[]{:S(2)}) async-start(), calls=%async_computation.10 | async-start | bytes 1966080 | tf_op jit(solution)/shard_map/reduce_scatter | solution.py:274
  459.4 10.0 %collective-permute-start.7 = (f32[96,768]{1,0:T(8,128)S(1)}, f32[96,768]{1,0:T(8,128)}, u32[]{:S(2)}, u32[]{:S(2)}) collective-permute-start(f32[96,768]{1,0:T(8,128)S(1)} %copy-done.20), channel_id=1, source_target_pairs={{0,16},{4,20},{8,24},{12,28},{16,0},{20,4},{24,8},{28,12},{1,17},{... | collective-permute-start | bytes 884744 | tf_op jit(solution)/shard_map/ppermute | solution.py:94
  460.9 13.4 %collective-permute-start.10 = (f32[96,768]{1,0:T(8,128)S(1)}, f32[96,768]{1,0:T(8,128)}, u32[]{:S(2)}, u32[]{:S(2)}) collective-permute-start(f32[96,768]{1,0:T(8,128)S(1)} %copy-done.19), channel_id=1, source_target_pairs={{0,16},{4,20},{8,24},{12,28},{16,0},{20,4},{24,8},{28,12},{1,17},{... | collective-permute-start | bytes 884744 | tf_op jit(solution)/shard_map/ppermute | solution.py:94
  470.6 10.5 %copy-start.12 = (f32[192,768]{1,0:T(8,128)}, f32[192,768]{1,0:T(8,128)S(1)}, u32[]{:S(2)}) copy-start(f32[192,768]{1,0:T(8,128)S(1)} %maximum_select_fusion.4) | copy-start | bytes 1769476
  470.6 20.8 %collective-permute-start.8 = (f32[192,768]{1,0:T(8,128)S(1)}, f32[192,768]{1,0:T(8,128)}, u32[]{:S(2)}, u32[]{:S(2)}) collective-permute-start(f32[192,768]{1,0:T(8,128)S(1)} %maximum_select_fusion.4), channel_id=1, source_target_pairs={{0,8},{4,12},{8,0},{12,4},{16,24},{20,28},{24,16},{28,20},{1,9},{5... | collective-permute-start | bytes 1769480 | tf_op jit(solution)/shard_map/ppermute | solution.py:94
  476.2 29.1 %collective-permute-start.11 = (f32[192,768]{1,0:T(8,128)}, f32[192,768]{1,0:T(8,128)}, u32[]{:S(2)}, u32[]{:S(2)}) collective-permute-start(f32[192,768]{1,0:T(8,128)} %maximum_select_fusion.5), channel_id=1, source_target_pairs={{0,8},{4,12},{8,0},{12,4},{16,24},{20,28},{24,16},{28,20},{1,9},{5... | collective-permute-start | bytes 1769480 | tf_op jit(solution)/shard_map/ppermute | solution.py:94
  481.1 27.0 %copy-start.30 = (f32[4,768]{1,0:T(4,128)S(1)}, f32[4,768]{1,0:T(4,128)}, u32[]{:S(2)}) copy-start(f32[4,768]{1,0:T(4,128)} %tile.24) | copy-start | bytes 36868
  481.1 27.0 %copy-start.46 = (pred[768]{0:T(1024)(128)(4,1)S(1)}, pred[768]{0:T(1024)(128)(4,1)}, u32[]{:S(2)}) copy-start(pred[768]{0:T(1024)(128)(4,1)} %fusion.41) | copy-start | bytes 2308
  481.1 28.4 %copy-start.39 = (f32[768]{0:T(1024)S(1)}, f32[768]{0:T(1024)}, u32[]{:S(2)}) copy-start(f32[768]{0:T(1024)} %get-tuple-element.94) | copy-start | bytes 9220
  493.1 29.0 %collective-permute-start.9 = (f32[384,768]{1,0:T(8,128)S(1)}, f32[384,768]{1,0:T(8,128)}, u32[]{:S(2)}, u32[]{:S(2)}) collective-permute-start(f32[384,768]{1,0:T(8,128)S(1)} %maximum_select_fusion.2), channel_id=1, source_target_pairs={{0,4},{4,0},{8,12},{12,8},{16,20},{20,16},{24,28},{28,24},{1,5},{5... | collective-permute-start | bytes 3538952 | tf_op jit(solution)/shard_map/ppermute | solution.py:94
  508.1 17.4 %collective-permute-start.12 = (f32[384,768]{1,0:T(8,128)}, f32[384,768]{1,0:T(8,128)}, u32[]{:S(2)}, u32[]{:S(2)}) collective-permute-start(f32[384,768]{1,0:T(8,128)} %maximum_select_fusion.3), channel_id=1, source_target_pairs={{0,4},{4,0},{8,12},{12,8},{16,20},{20,16},{24,28},{28,24},{1,5},{5... | collective-permute-start | bytes 3538952 | tf_op jit(solution)/shard_map/ppermute | solution.py:94
  532.8 38.4 %copy-start.43 = (f32[512]{0:T(512)S(1)}, f32[512]{0:T(512)}, u32[]{:S(2)}) copy-start(f32[512]{0:T(512)} %copy-done.42) | copy-start | bytes 6148
  535.5 68.7 %all-gather.11.cloned.1.call-start = ((), (), s32[]{:S(2)}) async-start(), calls=%async_computation.11 | async-start | bytes 3538944 | tf_op jit(solution)/shard_map/all_gather | solution.py:282
  617.1 4.8 copy-start.1
  (16 other events, 19.7 us)
Sparse Core Ops, SparseCore 0:
  11.4 56.8 all-gather.12
  112.5 62.2 all-gather.6
  198.9 59.0 reduce-scatter.7
  267.3 63.3 all-gather.8
  347.6 59.0 reduce-scatter.9
  415.3 36.5 reduce-scatter.11
  458.7 57.4 reduce-scatter.15
  535.6 35.6 reduce-scatter.13
  573.1 31.0 all-gather.10

commit v4 on v3

--- a/solution.py
+++ b/solution.py
@@ -92,7 +92,9 @@
     for step in reversed(range(steps)):
         bit = (index >> step) & 1
         got = lax.ppermute(kept, "dp", [(i, i ^ (1 << step)) for i in range(dp_size)])
-        kept = jnp.where(bit == 0, jnp.concatenate([kept, got]), jnp.concatenate([got, kept]))
+        kept = jnp.concatenate(
+            [jnp.where(bit == 0, kept, got), jnp.where(bit == 0, got, kept)]
+        )
     return kept
 
 
@@ -225,7 +227,6 @@
             .reshape(3, rows, width)
             .astype(jnp.bfloat16)
         )
-        proj_grad, early = lax.optimization_barrier((proj_grad, early))
         grad_bias_full = jnp.sum(proj_grad[0::2], axis=1, dtype=jnp.float32)
         grad_qkv_full = jnp.einsum(
             "rd,tre->tde", tokens, proj_grad, preferred_element_type=jnp.float32
@@ -267,16 +268,18 @@
             tiled=True,
         ).astype(jnp.float32)
         joined = jnp.concatenate([late, early, tail], axis=0)
-        if halved:
-            ffn_grads = tuple(dp_double(g, dp_size) for g in ffn_grads)
-            joined, ffn_grads = lax.optimization_barrier((joined, ffn_grads))
-        grad_up_weight, grad_down_weight = ffn_grads
         joined = lax.psum_scatter(
             joined.reshape(joined.shape[0], groups, shard).transpose(1, 0, 2),
             "tensor",
             scatter_dimension=0,
             tiled=True,
         )[0]
+        if halved:
+            ffn_grads = tuple(
+                dp_double(g.astype(jnp.bfloat16), dp_size).astype(jnp.float32) for g in ffn_grads
+            )
+            joined, ffn_grads = lax.optimization_barrier((joined, ffn_grads))
+        grad_up_weight, grad_down_weight = ffn_grads
         late_rows = late.shape[0]
         early_rows = early.shape[0]
         joined = lax.all_gather(joined, "dp", axis=0, tiled=False)

time: 640 us -> 610 us (0.953)
  other arithmetic: 75.5 us -> 62.4 us
  waiting for transfers between devices: 369 us -> 357 us
  local copies, waits for them, and re-layouts: 58.8 us -> 49.5 us
    unnamed x10, waiting for transfers between devices: 0.15 us -> 42.9 us
    reduce_scatter x1, waiting for transfers between devices: 35.7 us -> 14.3 us  [per_device(): lax.psum_scatter(joined.reshape(joined.shape[0], groups, shard).transpose...]
    ppermute x6, waiting for transfers between devices: 32.5 us -> 11.2 us  [dp_double(): got = lax.ppermute(kept, 'dp', [(i, i ^ 1 << step) for i in range(dp_size)])]
    reduce_scatter x1, waiting for transfers between devices: 12.4 us -> 0.02 us  [per_device(): lax.psum_scatter(early.astype(jnp.bfloat16), 'dp', scatter_dimension=0, t...]
    select_n x6, other arithmetic: 15 us -> 2.62 us  [dp_double(): jnp.where(bit == 0, kept, got)]
    unnamed x126 -> x124, local copies, waits for them, and re-layouts: 22.5 us -> 19 us
  transfers between devices with their start and end apart: 22 -> 22, of which waited for: 17 -> 16; matrix products, arithmetic and copies ran while one was open for 14% -> 14% of each run, Pallas kernels for 0% -> 0%
where the time goes in v4:
time: 610 us; the launch traced here: 599 us
  waiting for transfers between devices  357 us (59%)
  matrix products  93.7 us (15%)
  other arithmetic  62.4 us (10%)
  local copies, waits for them, and re-layouts  49.5 us (8%)
  starting transfers between devices  21.6 us (4%)
  between operations  15.2 us (2%)
    all_gather x1, waiting for transfers between devices, per_device(): ffn_rows = lax.all_gather(middle_low, 'tensor', axis=0, tiled=True)  61 us
    reduce_scatter x1, waiting for transfers between devices, per_device(): lax.psum_scatter(jnp.dot(hidden, down_weight, preferred_element_type=jnp....  59.2 us
    all_gather x1, waiting for transfers between devices, per_device(): mine = lax.all_gather(mine, 'tensor', axis=0, tiled=False)  56.9 us
    all_gather x1, waiting for transfers between devices, per_device(): branch_rows = lax.all_gather(branch_grad, 'tensor', axis=0, tiled=True)  52.4 us
    unnamed x10, waiting for transfers between devices  42.9 us
    all_gather x1, waiting for transfers between devices, per_device(): joined = lax.all_gather(joined, 'dp', axis=0, tiled=False)  27.8 us
    dot_general x5, matrix products, contract(): lax.dot_general(left, right, (((left_dim,), (right_dim,)), ((), ())), pre...  25.3 us
    ppermute x6, waiting for transfers between devices, dp_halve(): got = lax.ppermute(give, 'dp', [(i, i ^ 1 << step) for i in range(dp_size)])  24.5 us
  transfers between devices with their start and end apart: 22, of which 16 were waited for; matrix products, arithmetic and copies ran while one was open for 14% of the time, Pallas kernels for 0%

profile of v4, /device:TPU:0, one launch (start us, length us, event | category | flops | bytes accessed | tf_op | source)
XLA Modules:
  0.0 599.4 jit_solution(633435165509276025)
XLA Ops:
  9.4 1.8 fusion.43
  11.3 56.9 %all-gather.13.cloned.1.call-done = bf16[4,1544,192]{1,2,0:T(8,128)(2,1)} async-done(((bf16[1,1544,192]{1,2,0:T(8,128)(2,1)}), bf16[4,1544,192]{1,2,0:T(8,128)(2,1)}) %all-gather.13.cloned.1.call-update) | async-done | bytes 2371600 | tf_op jit(solution)/shard_map/all_gather | solution.py:140
  69.5 3.9 collective-permute-done
  73.4 3.0 broadcast_select_fusion.1
  78.2 2.0 fusion.19
  80.4 1.5 fusion.57
  83.1 5.0 fusion
  88.1 2.6 exponential_reduce_fusion
  90.7 1.9 copy-done.2
  92.6 10.1 %fusion.1 = bf16[12,512,512]{1,2,0:T(8,128)(2,1)} fusion(f32[12,512,512]{1,2,0:T(8,128)} %copy-done.2, f32[12,512]{1,0:T(8,128)S(1)} %log_add_fusion, pred[512]{0:T(512)(128)(4,1)S(1)} %iota_compare_fusion.1), kind=kLoop, calls=%fused_computation.7 | loop fusion | flops 12582912 | bytes 18899456 | tf_op jit(solution)/shard_map/convert_element_type | solution.py:40
  102.7 4.1 convolution_convert_fusion.4
  106.9 2.7 fusion.59
  113.7 61.0 %all-gather.9.cloned.1.call-done = bf16[2048,768]{1,0:T(8,128)(2,1)} async-done(((bf16[512,768]{1,0:T(8,128)(2,1)}), bf16[2048,768]{1,0:T(8,128)(2,1)}) %all-gather.9.cloned.1.call-update) | async-done | bytes 3145744 | tf_op jit(solution)/shard_map/all_gather | solution.py:173
  174.7 18.5 %multiply_convert_fusion.1 = (bf16[2048,768]{1,0:T(8,128)(2,1)S(1)}, f32[2048,768]{1,0:T(8,128)}, f32[2048,768]{1,0:T(8,128)}) fusion(f32[768]{0:T(1024)} %convert_element_type.173, bf16[2048,768]{1,0:T(8,128)(2,1)} %all-gather.9.cloned.1.call-done, bf16[768,768]{1,0:T(8,128)(2,1)S(1)} %copy-done), kind=kOutput, calls=%fused_computation.11 | convolution fusion | flops 2519728128 | bytes 20057088 | tf_op jit(solution)/shard_map/dot_general | solution.py:174
  193.2 1.6 copy-done.52
  194.8 4.0 convolution_convert_fusion.1
  198.9 59.2 %reduce-scatter.8.cloned.1.call-done = bf16[512,768]{1,0:T(8,128)(2,1)} async-done(((bf16[2048,768]{1,0:T(8,128)(2,1)}), bf16[512,768]{1,0:T(8,128)(2,1)}) %reduce-scatter.8.cloned.1.call-update) | async-done | bytes 786448 | tf_op jit(solution)/shard_map/reduce_scatter | solution.py:177
  258.0 1.8 fusion.55
  261.4 1.6 fusion.54
  264.2 1.7 convert_reduce_fusion.3
  265.9 11.1 %reduce-scatter.10.cloned.1.call-start = ((), (), s32[]{:S(2)}) async-start(), calls=%async_computation.8 | async-start | bytes 3932160 | tf_op jit(solution)/shard_map/reduce_scatter | solution.py:201
  277.0 52.4 %all-gather.11.cloned.1.call-done = bf16[2048,768]{1,0:T(8,128)(2,1)} async-done(((bf16[512,768]{1,0:T(8,128)(2,1)}), bf16[2048,768]{1,0:T(8,128)(2,1)}) %all-gather.11.cloned.1.call-update) | async-done | bytes 3145744 | tf_op jit(solution)/shard_map/all_gather | solution.py:189
  329.4 11.0 %convert_reduce_fusion = (f32[768]{0:T(1024)}, bf16[2048,768]{1,0:T(8,128)(2,1)S(1)}) fusion(f32[2048,768]{1,0:T(8,128)} %get-tuple-element.107, f32[2048,768]{1,0:T(8,128)} %get-tuple-element.136, f32[768]{0:T(1024)} %convert_element_type.173, bf16[2048,768]{1,0:T(8,128)(2,1)} %all-gather.11.cloned.1.call-done, bf16[768,768]{1,0:T(8,128)(2,1)} %param.26), kind=kOutput, calls=%fused_computation.9 | convolution fusion | flops 2442657024 | bytes 20060160 | tf_op jit(solution)/shard_map/dot_general | solution.py:25
  340.4 1.7 copy-done.53
  342.2 4.0 convolution_convert_fusion
  346.3 5.7 fusion.61
  352.0 2.7 fusion.60
  357.1 2.5 collective-permute-done.4
  359.6 1.8 dynamic-slice_add_fusion
  362.2 1.5 collective-permute-start.5
  363.7 1.4 dynamic-slice_add_fusion.1
  367.6 11.1 %collective-permute-done.5 = f32[192,768]{1,0:T(8,128)} collective-permute-done((f32[192,768]{1,0:T(8,128)}, f32[192,768]{1,0:T(8,128)}, u32[]{:S(2)}, u32[]{:S(2)}) %collective-permute-start.5) | collective-permute-done | bytes 589856 | tf_op jit(solution)/shard_map/ppermute | solution.py:84
  380.7 1.5 collective-permute-start.6
  382.1 8.4 %collective-permute-done.2 = f32[192,768]{1,0:T(8,128)} collective-permute-done((f32[192,768]{1,0:T(8,128)}, f32[192,768]{1,0:T(8,128)}, u32[]{:S(2)}, u32[]{:S(2)}) %collective-permute-start.2) | collective-permute-done | bytes 589856 | tf_op jit(solution)/shard_map/ppermute | solution.py:84
  392.4 1.5 collective-permute-start.3
  393.9 2.9 slice.111
  396.8 1.6 dynamic-slice_add_fusion.4
  398.4 2.5 collective-permute-done.3
  400.9 1.7 dynamic-slice_add_fusion.5
  402.6 2.8 reduce-scatter.10.cloned.1.call-done
  405.4 1.8 convert_add_fusion
  410.8 1.8 fusion.63
  414.9 9.5 %multiply_reduce_fusion = (f32[12,512]{1,0:T(8,128)S(1)}, f32[12,512,512]{1,2,0:T(8,128)S(1)}) fusion(f32[12,512,512]{1,2,0:T(8,128)} %copy-done.2, f32[12,512]{1,0:T(8,128)S(1)} %copy-done.26, pred[512]{0:T(512)(128)(4,1)S(1)} %copy-done.43, f32[512,12,64]{0,2,1:T(8,128)S(1)} %bitcast.130, f32[12,64]{1,0:T(8,128)S(1)} %copy-done.28, ...), kind=kOutput, calls=%fused_computation.1 | convolution fusion | flops 419162112 | bytes 27577856 | tf_op jit(solution)/shard_map/pqhe,pkhe->phqk/dot_general | solution.py:48
  424.4 10.3 %multiply_convert_fusion = bf16[12,512,512]{1,2,0:T(8,128)(2,1)} fusion(f32[12,512,512]{1,2,0:T(8,128)S(1)} %get-tuple-element.138, f32[12,512,512]{1,2,0:T(8,128)} %copy-done.2, f32[12,512]{1,0:T(8,128)S(1)} %get-tuple-element.137, f32[12,512]{1,0:T(8,128)S(1)} %copy-done.26, pred[512]{0:T(512)(128)(4,1)S(1)} %copy-done.43), kind=kLoop, calls=%fused_computation | loop fusion | flops 18874368 | bytes 31506944 | tf_op jit(solution)/shard_map/convert_element_type | solution.py:52
  434.7 2.9 convolution_convert_fusion.3
  437.6 2.4 copy.117
  440.0 4.8 multiply_convert_fusion.2
  446.0 4.0 multiply_convert_fusion.3
  450.3 4.9 convolution_convert_fusion.2
  456.5 1.5 collective-permute-start.7
  460.6 42.8 %reduce-scatter.16.cloned.1.call-done = bf16[288,768]{1,0:T(8,128)(2,1)} async-done(((bf16[2304,768]{1,0:T(8,128)(2,1)}), bf16[288,768]{1,0:T(8,128)(2,1)}) %reduce-scatter.16.cloned.1.call-update) | async-done | bytes 442384
  504.8 1.5 select_maximum_fusion
  507.6 1.5 collective-permute-start.11
  510.8 6.7 %collective-permute-done.11 = bf16[192,768]{1,0:T(8,128)(2,1)S(1)} collective-permute-done((bf16[192,768]{1,0:T(8,128)(2,1)S(1)}, bf16[192,768]{1,0:T(8,128)(2,1)S(1)}, u32[]{:S(2)}, u32[]{:S(2)}) %collective-permute-start.11) | collective-permute-done | bytes 294944 | tf_op jit(solution)/shard_map/ppermute | solution.py:94
  518.5 4.1 collective-permute-done.8
  523.8 1.6 maximum_convert_fusion.1
  526.0 1.6 maximum_convert_fusion
  527.6 14.3 %reduce-scatter.14.cloned.1.call-done = f32[1,416,192]{1,2,0:T(8,128)} async-done(((f32[4,416,192]{1,2,0:T(8,128)}), f32[1,416,192]{1,2,0:T(8,128)}) %reduce-scatter.14.cloned.1.call-update) | async-done | bytes 319504 | tf_op jit(solution)/shard_map/reduce_scatter | solution.py:271
  541.9 5.2 fusion.26
  547.1 27.8 %all-gather.15.cloned.1.call-done = f32[8,416,192]{1,2,0:T(8,128)} async-done(((f32[1,416,192]{1,2,0:T(8,128)}), f32[8,416,192]{1,2,0:T(8,128)}) %all-gather.15.cloned.1.call-update) | async-done | bytes 2555920 | tf_op jit(solution)/shard_map/all_gather | solution.py:285
  582.2 3.2 slice.112
  585.5 2.2 copy.122
  587.7 1.8 copy.131
  589.5 1.4 slice.115
  (238 shorter events, 49.9 us)
Async XLA Ops:
  7.2 167.5 %copy-start = (bf16[768,768]{1,0:T(8,128)(2,1)S(1)}, bf16[768,768]{1,0:T(8,128)(2,1)}, u32[]{:S(2)}) copy-start(bf16[768,768]{1,0:T(8,128)(2,1)} %param.24) | copy-start | bytes 3538948
  7.2 61.1 %copy-start.51 = (s32[4]{0:T(128)S(1)}, s32[4]{0:T(128)}, u32[]{:S(2)}) copy-start(s32[4]{0:T(128)} %param.17) | copy-start | bytes 52
  7.2 61.1 %all-gather.13.cloned.1.call-start = ((), (), s32[]{:S(2)}) async-start(), calls=%async_computation.11 | async-start | bytes 3194880 | tf_op jit(solution)/shard_map/all_gather | solution.py:140
  11.3 163.4 %all-gather.9.cloned.1.call-start = ((), (), s32[]{:S(2)}) async-start(), calls=%async_computation.5 | async-start | bytes 3932160 | tf_op jit(solution)/shard_map/all_gather | solution.py:173
  68.3 5.2 collective-permute-start
  69.5 23.1 %copy-start.42 = (pred[512]{0:T(512)(128)(4,1)}, pred[512]{0:T(512)(128)(4,1)S(1)}, u32[]{:S(2)}) copy-start(pred[512]{0:T(512)(128)(4,1)S(1)} %iota_compare_fusion.1) | copy-start | bytes 1540
  76.4 1.5 copy-start.3
  76.5 1.7 copy-start.48
  77.9 2.4 copy-start.12
  81.9 20.8 %copy-start.4 = (f32[1,512,4,192]{1,3,0,2:T(8,128)}, f32[1,512,4,192]{1,3,0,2:T(8,128)S(1)}, u32[]{:S(2)}) copy-start(f32[1,512,4,192]{1,3,0,2:T(8,128)S(1)} %get-tuple-element.110) | copy-start | bytes 4718596
  88.1 4.5 copy-start.2
  92.6 10.1 %copy-start.25 = (f32[12,512]{1,0:T(8,128)}, f32[12,512]{1,0:T(8,128)S(1)}, u32[]{:S(2)}) copy-start(f32[12,512]{1,0:T(8,128)S(1)} %log_add_fusion) | copy-start | bytes 73732
  92.6 10.1 %copy-start.27 = (f32[12,64]{1,0:T(8,128)S(1)}, f32[12,64]{1,0:T(8,128)}, u32[]{:S(2)}) copy-start(f32[12,64]{1,0:T(8,128)} %reshape.340) | copy-start | bytes 9220
  102.7 4.1 copy-start.49
  102.7 4.1 copy-start.50
  106.8 2.8 copy-start.23
  106.9 4.3 copy-start.29
  106.9 4.2 copy-start.35
  112.4 145.7 %reduce-scatter.8.cloned.1.call-start = ((), (), s32[]{:S(2)}) async-start(), calls=%async_computation.6 | async-start | bytes 3932160 | tf_op jit(solution)/shard_map/reduce_scatter | solution.py:177
  174.7 20.1 %copy-start.47 = (bf16[768,768]{1,0:T(8,128)(2,1)S(1)}, bf16[768,768]{1,0:T(8,128)(2,1)}, u32[]{:S(2)}) copy-start(bf16[768,768]{1,0:T(8,128)(2,1)} %param.26) | copy-start | bytes 3538948
  193.2 1.6 copy-start.52
  198.8 130.6 %all-gather.11.cloned.1.call-start = ((), (), s32[]{:S(2)}) async-start(), calls=%async_computation.7 | async-start | bytes 3932160 | tf_op jit(solution)/shard_map/all_gather | solution.py:189
  258.0 2.2 copy-start.16
  258.0 2.2 copy-start.36
  259.8 1.6 copy-start.44
  263.0 2.8 copy-start.32
  265.9 139.5 %reduce-scatter.10.cloned.1.call-start = ((), (), s32[]{:S(2)}) async-start(), calls=%async_computation.8 | async-start | bytes 3932160 | tf_op jit(solution)/shard_map/reduce_scatter | solution.py:201
  340.4 1.7 copy-start.53
  346.2 113.3 %reduce-scatter.12.cloned.1.call-start = ((), (), s32[]{:S(2)}) async-start(), calls=%async_computation.9 | async-start | bytes 1327104 | tf_op jit(solution)/shard_map/reduce_scatter | solution.py:219
  346.3 5.7 copy-start.46
  346.3 5.7 copy-start.54
  352.0 2.8 copy-start.19
  354.8 1.8 copy-start.17
  356.6 3.0 collective-permute-start.4
  356.6 7.1 %collective-permute-start.1 = (f32[384,768]{1,0:T(8,128)}, f32[384,768]{1,0:T(8,128)}, u32[]{:S(2)}, u32[]{:S(2)}) collective-permute-start(f32[384,768]{1,0:T(8,128)} %get-tuple-element.140), channel_id=1, source_target_pairs={{0,4},{4,0},{8,12},{12,8},{16,20},{20,16},{24,28},{28,24},{1,5},{5... | collective-permute-start | bytes 3538952 | tf_op jit(solution)/shard_map/ppermute | solution.py:84
  357.1 6.6 %copy-start.18 = (f32[768,768]{1,0:T(8,128)S(1)}, f32[768,768]{1,0:T(8,128)}, u32[]{:S(2)}) copy-start(f32[768,768]{1,0:T(8,128)} %copy-done.17) | copy-start | bytes 7077892
  362.2 16.5 %collective-permute-start.5 = (f32[192,768]{1,0:T(8,128)}, f32[192,768]{1,0:T(8,128)}, u32[]{:S(2)}, u32[]{:S(2)}) collective-permute-start(f32[192,768]{1,0:T(8,128)} %constant_dynamic-slice_fusion.1), channel_id=1, source_target_pairs={{0,8},{4,12},{8,0},{12,4},{16,24},{20,28},{24,16},{28,20},{1,9},{5... | collective-permute-start | bytes 1769480 | tf_op jit(solution)/shard_map/ppermute | solution.py:84
  367.0 23.5 %collective-permute-start.2 = (f32[192,768]{1,0:T(8,128)}, f32[192,768]{1,0:T(8,128)}, u32[]{:S(2)}, u32[]{:S(2)}) collective-permute-start(f32[192,768]{1,0:T(8,128)} %constant_dynamic-slice_fusion.4), channel_id=1, source_target_pairs={{0,8},{4,12},{8,0},{12,4},{16,24},{20,28},{24,16},{28,20},{1,9},{5... | collective-permute-start | bytes 1769480 | tf_op jit(solution)/shard_map/ppermute | solution.py:84
  367.6 23.0 %copy-start.11 = (f32[384,768]{1,0:T(8,128)S(1)}, f32[384,768]{1,0:T(8,128)}, u32[]{:S(2)}) copy-start(f32[384,768]{1,0:T(8,128)} %copy-done.10) | copy-start | bytes 3538948
  379.9 11.8 %copy-start.20 = (f32[192,768]{1,0:T(8,128)}, f32[192,768]{1,0:T(8,128)S(1)}, u32[]{:S(2)}) copy-start(f32[192,768]{1,0:T(8,128)S(1)} %dynamic-slice_add_fusion.2) | copy-start | bytes 1769476
  380.7 16.1 %collective-permute-start.6 = (f32[96,768]{1,0:T(8,128)}, f32[96,768]{1,0:T(8,128)}, u32[]{:S(2)}, u32[]{:S(2)}) collective-permute-start(f32[96,768]{1,0:T(8,128)} %constant_dynamic-slice_fusion), channel_id=1, source_target_pairs={{0,16},{4,20},{8,24},{12,28},{16,0},{20,4},{24,8},{28,12},{1,17},{... | collective-permute-start | bytes 884744 | tf_op jit(solution)/shard_map/ppermute | solution.py:84
  392.4 4.4 copy-start.21
  392.4 8.5 %collective-permute-start.3 = (f32[96,768]{1,0:T(8,128)}, f32[96,768]{1,0:T(8,128)}, u32[]{:S(2)}, u32[]{:S(2)}) collective-permute-start(f32[96,768]{1,0:T(8,128)} %constant_dynamic-slice_fusion.3), channel_id=1, source_target_pairs={{0,16},{4,20},{8,24},{12,28},{16,0},{20,4},{24,8},{28,12},{1,17},{... | collective-permute-start | bytes 884744 | tf_op jit(solution)/shard_map/ppermute | solution.py:84
  398.4 8.8 %copy-start.31 = (f32[512]{0:T(512)S(1)}, f32[512]{0:T(512)}, u32[]{:S(2)}) copy-start(f32[512]{0:T(512)} %copy-done.30) | copy-start | bytes 6148
  409.1 1.7 copy-start.24
  410.3 2.4 copy-start.22
  413.5 1.4 copy-start.5
  413.5 1.4 copy-start.26
  413.7 89.7 %reduce-scatter.16.cloned.1.call-start = ((), (), s32[]{:S(2)}) async-start(), calls=%async_computation.13 | async-start | bytes 3981312
  414.9 19.8 %slice-start = ((s8[6291456]{0:T(1024)(128)(4,1)}), s8[2097152]{0:T(1024)(128)(4,1)S(1)}, s32[]{:S(2)}) async-start(s8[6291456]{0:T(1024)(128)(4,1)} %bitcast.127), calls=%async_computation.14 | async-start | bytes 4194304
  424.4 10.3 %slice-start.1 = ((s8[6291456]{0:T(1024)(128)(4,1)}), s8[4194304]{0:T(1024)(128)(4,1)S(1)}, s32[]{:S(2)}) async-start(s8[6291456]{0:T(1024)(128)(4,1)} %bitcast.127), calls=%async_computation.15 | async-start | bytes 8388608
  437.6 2.4 copy-start.7
  446.0 4.3 copy-start.15
  455.3 86.6 %reduce-scatter.14.cloned.1.call-start = ((), (), s32[]{:S(2)}) async-start(), calls=%async_computation.10 | async-start | bytes 1966080 | tf_op jit(solution)/shard_map/reduce_scatter | solution.py:271
  456.5 52.7 %collective-permute-start.7 = (bf16[96,768]{1,0:T(8,128)(2,1)}, bf16[96,768]{1,0:T(8,128)(2,1)}, u32[]{:S(2)}, u32[]{:S(2)}) collective-permute-start(bf16[96,768]{1,0:T(8,128)(2,1)} %dynamic-slice_add_fusion.5), channel_id=1, source_target_pairs={{0,16},{4,20},{8,24},{12,28},{16,0},{20,4},{24,8},{28,12},{1,17},{... | collective-permute-start | bytes 442376 | tf_op jit(solution)/shard_map/ppermute | solution.py:94
  458.0 48.6 %collective-permute-start.10 = (bf16[96,768]{1,0:T(8,128)(2,1)}, bf16[96,768]{1,0:T(8,128)(2,1)}, u32[]{:S(2)}, u32[]{:S(2)}) collective-permute-start(bf16[96,768]{1,0:T(8,128)(2,1)} %dynamic-slice_add_fusion.4), channel_id=1, source_target_pairs={{0,16},{4,20},{8,24},{12,28},{16,0},{20,4},{24,8},{28,12},{1,17},{... | collective-permute-start | bytes 442376 | tf_op jit(solution)/shard_map/ppermute | solution.py:94
  506.3 68.6 %all-gather.15.cloned.1.call-start = ((), (), s32[]{:S(2)}) async-start(), calls=%async_computation.12 | async-start | bytes 3538944 | tf_op jit(solution)/shard_map/all_gather | solution.py:285
  507.6 9.9 %collective-permute-start.11 = (bf16[192,768]{1,0:T(8,128)(2,1)S(1)}, bf16[192,768]{1,0:T(8,128)(2,1)S(1)}, u32[]{:S(2)}, u32[]{:S(2)}) collective-permute-start(bf16[192,768]{1,0:T(8,128)(2,1)S(1)} %pad_maximum_fusion.5), channel_id=1, source_target_pairs={{0,8},{4,12},{8,0},{12,4},{16,24},{20,28},{24,16},{28,20},{1,9},{5... | collective-permute-start | bytes 884744 | tf_op jit(solution)/shard_map/ppermute | solution.py:94
  510.2 12.4 %collective-permute-start.8 = (bf16[192,768]{1,0:T(8,128)(2,1)S(1)}, bf16[192,768]{1,0:T(8,128)(2,1)S(1)}, u32[]{:S(2)}, u32[]{:S(2)}) collective-permute-start(bf16[192,768]{1,0:T(8,128)(2,1)S(1)} %pad_maximum_fusion.4), channel_id=1, source_target_pairs={{0,8},{4,12},{8,0},{12,4},{16,24},{20,28},{24,16},{28,20},{1,9},{5... | collective-permute-start | bytes 884744 | tf_op jit(solution)/shard_map/ppermute | solution.py:94
  518.5 5.0 collective-permute-start.12
  523.5 2.2 collective-permute-start.9
  526.0 15.9 %copy-start.9 = (f32[512,768]{1,0:T(8,128)S(1)}, f32[512,768]{1,0:T(8,128)}, u32[]{:S(2)}) copy-start(f32[512,768]{1,0:T(8,128)} %copy-done.8) | copy-start | bytes 4718596
  526.0 15.9 %copy-start.14 = (bf16[12,64,512]{2,1,0:T(8,128)(2,1)S(1)}, bf16[12,64,512]{2,1,0:T(8,128)(2,1)}, u32[]{:S(2)}) copy-start(bf16[12,64,512]{2,1,0:T(8,128)(2,1)} %copy-done.13) | copy-start | bytes 2359300
  587.7 4.8 copy-start.1
  (15 other events, 14.9 us)
Sparse Core Ops, SparseCore 0:
  11.4 56.8 all-gather.12
  112.5 62.2 all-gather.8
  198.9 59.0 reduce-scatter.7
  266.0 63.3 all-gather.10
  346.3 59.0 reduce-scatter.9
  413.8 36.6 reduce-scatter.11
  455.4 47.9 reduce-scatter.15
  506.4 35.4 reduce-scatter.13
  543.7 31.0 all-gather.14

commit v5 on v4

--- a/solution.py
+++ b/solution.py
@@ -72,18 +72,24 @@
     return dp_size == 1 << steps and values.shape[0] % dp_size == 0
 
 
-def dp_halve(values, dp_size):
+def dp_halve(values, dp_size, sum_dtype=None):
     steps = dp_size.bit_length() - 1
     index = lax.axis_index("dp")
-    kept = values
+    link = values.dtype
+    kept = values if sum_dtype is None else values.astype(sum_dtype)
     for step in range(steps):
         bit = (index >> step) & 1
         half = kept.shape[0] // 2
         keep = lax.dynamic_slice_in_dim(kept, bit * half, half)
-        give = lax.dynamic_slice_in_dim(kept, (1 - bit) * half, half)
+        give = lax.dynamic_slice_in_dim(kept, (1 - bit) * half, half).astype(link)
         got = lax.ppermute(give, "dp", [(i, i ^ (1 << step)) for i in range(dp_size)])
-        kept = keep + got
+        kept = keep + got.astype(kept.dtype)
     return kept
+
+
+def bit_reversed(count):
+    steps = count.bit_length() - 1
+    return [int(format(i, f"0{steps}b")[::-1], 2) if steps else 0 for i in range(count)]
 
 
 def dp_double(kept, dp_size):
@@ -213,12 +219,12 @@
             .astype(jnp.bfloat16)
             .reshape(four_dims)
         )
-        context_grad, early = lax.optimization_barrier(
-            (context_grad, contract(attn_grad, context_low, 0, 0))
-        )
-        early = lax.psum_scatter(
-            early.astype(jnp.bfloat16), "dp", scatter_dimension=0, tiled=True
-        ).astype(jnp.float32)
+        early = contract(attn_grad, context_low, 0, 0)
+        early_halved = dp_pow2(early, dp_size)
+        if early_halved:
+            early = dp_halve(early.astype(jnp.bfloat16), dp_size, jnp.float32)
+        else:
+            early = lax.psum_scatter(early, "dp", scatter_dimension=0, tiled=True)
         query_grad, key_grad, value_grad = attend_backward(
             queries, key_rows, value_rows, attn_probs, context_grad, factor
         )
@@ -283,9 +289,14 @@
         late_rows = late.shape[0]
         early_rows = early.shape[0]
         joined = lax.all_gather(joined, "dp", axis=0, tiled=False)
+        early = joined[:, late_rows : late_rows + early_rows]
+        if early_halved:
+            order = bit_reversed(dp_size)
+            place = [order.index(b) for b in range(dp_size)]
+            early = jnp.concatenate([early[p] for p in place], axis=0)
         pieces = [
             joined[:, :late_rows].reshape(-1, shard),
-            joined[:, late_rows : late_rows + early_rows].reshape(-1, shard),
+            early.reshape(-1, shard),
             jnp.sum(joined[:, late_rows + early_rows :], axis=0),
         ]
         grad_qkv_weight = pieces[0].reshape(3, width, shard)

time: 610 us -> 597 us (0.979)
    unnamed x10 -> x8, waiting for transfers between devices: 42.9 us -> 0.13 us
    reduce_scatter x1, waiting for transfers between devices: 0.02 us -> 25.5 us  [per_device(): lax.psum_scatter(grad_qkv_full.reshape(3 * width, width).astype(jnp.bfloa...]
    ppermute x6 -> x9, waiting for transfers between devices: 24.5 us -> 37.6 us  [dp_halve(): got = lax.ppermute(give, 'dp', [(i, i ^ 1 << step) for i in range(dp_size)])]
    unnamed x124 -> x122, local copies, waits for them, and re-layouts: 19 us -> 16.4 us
  transfers between devices with their start and end apart: 22 -> 24, of which waited for: 16 -> 19; matrix products, arithmetic and copies ran while one was open for 14% -> 8% of each run, Pallas kernels for 0% -> 0%
where the time goes in v5:
time: 597 us; the launch traced here: 587 us
  waiting for transfers between devices  353 us (59%)
  matrix products  89.3 us (15%)
  other arithmetic  58.8 us (10%)
  local copies, waits for them, and re-layouts  46.3 us (8%)
  starting transfers between devices  24.3 us (4%)
  between operations  15.5 us (3%)
    all_gather x1, waiting for transfers between devices, per_device(): ffn_rows = lax.all_gather(middle_low, 'tensor', axis=0, tiled=True)  61 us
    reduce_scatter x1, waiting for transfers between devices, per_device(): lax.psum_scatter(jnp.dot(hidden, down_weight, preferred_element_type=jnp....  59.1 us
    all_gather x1, waiting for transfers between devices, per_device(): mine = lax.all_gather(mine, 'tensor', axis=0, tiled=False)  56.9 us
    all_gather x1, waiting for transfers between devices, per_device(): branch_rows = lax.all_gather(branch_grad, 'tensor', axis=0, tiled=True)  52.3 us
    ppermute x9, waiting for transfers between devices, dp_halve(): got = lax.ppermute(give, 'dp', [(i, i ^ 1 << step) for i in range(dp_size)])  37.6 us
    all_gather x1, waiting for transfers between devices, per_device(): joined = lax.all_gather(joined, 'dp', axis=0, tiled=False)  27.7 us
    dot_general x5, matrix products, contract(): lax.dot_general(left, right, (((left_dim,), (right_dim,)), ((), ())), pre...  25.7 us
    reduce_scatter x1, waiting for transfers between devices, per_device(): lax.psum_scatter(grad_qkv_full.reshape(3 * width, width).astype(jnp.bfloa...  25.5 us
  transfers between devices with their start and end apart: 24, of which 19 were waited for; matrix products, arithmetic and copies ran while one was open for 8% of the time, Pallas kernels for 0%

profile of v5, /device:TPU:0, one launch (start us, length us, event | category | flops | bytes accessed | tf_op | source)
XLA Modules:
  0.0 587.0 jit_solution(9950485908794336362)
XLA Ops:
  9.4 1.8 fusion.41
  11.3 56.9 %all-gather.13.cloned.1.call-done = bf16[4,1544,192]{1,2,0:T(8,128)(2,1)} async-done(((bf16[1,1544,192]{1,2,0:T(8,128)(2,1)}), bf16[4,1544,192]{1,2,0:T(8,128)(2,1)}) %all-gather.13.cloned.1.call-update) | async-done | bytes 2371600 | tf_op jit(solution)/shard_map/all_gather | solution.py:146
  69.5 3.9 collective-permute-done
  73.4 3.0 broadcast_select_fusion.1
  78.2 2.0 fusion.19
  80.4 1.5 fusion.56
  83.1 5.0 fusion
  88.1 2.6 exponential_reduce_fusion
  90.7 1.9 copy-done.2
  92.7 10.1 %fusion.1 = bf16[12,512,512]{1,2,0:T(8,128)(2,1)} fusion(f32[12,512,512]{1,2,0:T(8,128)} %copy-done.2, f32[12,512]{1,0:T(8,128)S(1)} %log_add_fusion, pred[512]{0:T(512)(128)(4,1)S(1)} %iota_compare_fusion.1), kind=kLoop, calls=%fused_computation.7 | loop fusion | flops 12582912 | bytes 18899456 | tf_op jit(solution)/shard_map/convert_element_type | solution.py:40
  102.8 4.1 convolution_convert_fusion.5
  107.0 2.7 fusion.58
  113.8 61.0 %all-gather.9.cloned.1.call-done = bf16[2048,768]{1,0:T(8,128)(2,1)} async-done(((bf16[512,768]{1,0:T(8,128)(2,1)}), bf16[2048,768]{1,0:T(8,128)(2,1)}) %all-gather.9.cloned.1.call-update) | async-done | bytes 3145744 | tf_op jit(solution)/shard_map/all_gather | solution.py:179
  174.8 18.5 %multiply_convert_fusion.1 = (bf16[2048,768]{1,0:T(8,128)(2,1)S(1)}, f32[2048,768]{1,0:T(8,128)}, f32[2048,768]{1,0:T(8,128)}) fusion(f32[768]{0:T(1024)} %convert_element_type.191, bf16[2048,768]{1,0:T(8,128)(2,1)} %all-gather.9.cloned.1.call-done, bf16[768,768]{1,0:T(8,128)(2,1)S(1)} %copy-done), kind=kOutput, calls=%fused_computation.11 | convolution fusion | flops 2519728128 | bytes 20057088 | tf_op jit(solution)/shard_map/dot_general | solution.py:180
  193.3 1.6 copy-done.49
  194.9 3.9 convolution_convert_fusion.1
  198.9 59.1 %reduce-scatter.5.cloned.1.call-done = bf16[512,768]{1,0:T(8,128)(2,1)} async-done(((bf16[2048,768]{1,0:T(8,128)(2,1)}), bf16[512,768]{1,0:T(8,128)(2,1)}) %reduce-scatter.5.cloned.1.call-update) | async-done | bytes 786448 | tf_op jit(solution)/shard_map/reduce_scatter | solution.py:183
  258.0 1.8 fusion.54
  261.4 1.6 fusion.53
  264.3 1.7 convert_reduce_fusion.3
  265.9 11.2 %reduce-scatter.7.cloned.1.call-start = ((), (), s32[]{:S(2)}) async-start(), calls=%async_computation.7 | async-start | bytes 3932160 | tf_op jit(solution)/shard_map/reduce_scatter | solution.py:207
  277.1 52.3 %all-gather.11.cloned.1.call-done = bf16[2048,768]{1,0:T(8,128)(2,1)} async-done(((bf16[512,768]{1,0:T(8,128)(2,1)}), bf16[2048,768]{1,0:T(8,128)(2,1)}) %all-gather.11.cloned.1.call-update) | async-done | bytes 3145744 | tf_op jit(solution)/shard_map/all_gather | solution.py:195
  329.5 11.0 %convert_reduce_fusion = (f32[768]{0:T(1024)}, bf16[2048,768]{1,0:T(8,128)(2,1)S(1)}) fusion(f32[2048,768]{1,0:T(8,128)} %get-tuple-element.89, f32[2048,768]{1,0:T(8,128)} %get-tuple-element.126, f32[768]{0:T(1024)} %convert_element_type.191, bf16[2048,768]{1,0:T(8,128)(2,1)} %all-gather.11.cloned.1.call-done, bf16[768,768]{1,0:T(8,128)(2,1)} %param.26), kind=kOutput, calls=%fused_computation.9 | convolution fusion | flops 2442657024 | bytes 20060160 | tf_op jit(solution)/shard_map/dot_general | solution.py:25
  340.5 1.7 copy-done.50
  342.2 4.0 convolution_convert_fusion
  346.3 5.7 fusion.60
  352.1 2.7 fusion.59
  357.2 2.5 collective-permute-done.4
  359.6 1.8 dynamic-slice_add_fusion
  362.3 1.5 collective-permute-start.5
  367.6 11.1 %collective-permute-done.5 = f32[192,768]{1,0:T(8,128)} collective-permute-done((f32[192,768]{1,0:T(8,128)}, f32[192,768]{1,0:T(8,128)}, u32[]{:S(2)}, u32[]{:S(2)}) %collective-permute-start.5) | collective-permute-done | bytes 589856 | tf_op jit(solution)/shard_map/ppermute | solution.py:85
  380.7 1.5 collective-permute-start.6
  382.2 8.4 %collective-permute-done.2 = f32[192,768]{1,0:T(8,128)} collective-permute-done((f32[192,768]{1,0:T(8,128)}, f32[192,768]{1,0:T(8,128)}, u32[]{:S(2)}, u32[]{:S(2)}) %collective-permute-start.2) | collective-permute-done | bytes 589856 | tf_op jit(solution)/shard_map/ppermute | solution.py:85
  392.5 1.5 collective-permute-start.3
  393.9 2.9 slice.148
  396.8 1.7 dynamic-slice_add_fusion.4
  398.5 2.5 collective-permute-done.3
  401.0 1.7 dynamic-slice_add_fusion.5
  402.6 2.8 reduce-scatter.7.cloned.1.call-done
  405.4 2.0 convert_add_fusion
  410.8 2.9 convolution_convert_fusion.4
  415.4 10.3 %multiply_reduce_fusion = (f32[12,512]{1,0:T(8,128)S(1)}, f32[12,512,512]{1,2,0:T(8,128)}) fusion(f32[12,512,512]{1,2,0:T(8,128)S(1)} %bitcast.136, f32[12,512]{1,0:T(8,128)S(1)} %copy-done.25, pred[512]{0:T(512)(128)(4,1)S(1)} %copy-done.40, bf16[512,12,64]{0,2,1:T(8,128)(2,1)S(1)} %bitcast.148, f32[512,12,64]{0,2,1:T(8,128)S(1)} %bitcast.140, ...), kind=kOutput, calls=%fused_computation.1 | convolution fusion | flops 419162112 | bytes 27577856 | tf_op jit(solution)/shard_map/pqhe,pkhe->phqk/dot_general | solution.py:48
  425.7 7.2 %multiply_convert_fusion = bf16[12,512,512]{1,2,0:T(8,128)(2,1)S(1)} fusion(f32[12,512,512]{1,2,0:T(8,128)} %get-tuple-element.128, f32[12,512,512]{1,2,0:T(8,128)S(1)} %bitcast.136, f32[12,512]{1,0:T(8,128)S(1)} %get-tuple-element.127, f32[12,512]{1,0:T(8,128)S(1)} %copy-done.25, pred[512]{0:T(512)(128)(4,1)S(1)} %copy-done.40), kind=kLoop, calls=%fused_computation | loop fusion | flops 18874368 | bytes 31506944 | tf_op jit(solution)/shard_map/convert_element_type | solution.py:52
  432.9 2.1 multiply_convert_fusion.2
  438.1 4.9 convolution_convert_fusion.2
  444.3 1.5 collective-permute-start.10
  446.4 2.2 fusion.28
  449.1 2.0 collective-permute-done.7
  452.9 7.4 %collective-permute-done.8 = bf16[192,768]{1,0:T(8,128)(2,1)S(1)} collective-permute-done((bf16[192,768]{1,0:T(8,128)(2,1)S(1)}, bf16[192,768]{1,0:T(8,128)(2,1)S(1)}, u32[]{:S(2)}, u32[]{:S(2)}) %collective-permute-start.8) | collective-permute-done | bytes 294944 | tf_op jit(solution)/shard_map/ppermute | solution.py:85
  462.0 3.6 collective-permute-done.9
  465.7 25.5 %reduce-scatter.9.cloned.1.call-done = bf16[288,768]{1,0:T(8,128)(2,1)} async-done(((bf16[2304,768]{1,0:T(8,128)(2,1)}), bf16[288,768]{1,0:T(8,128)(2,1)}) %reduce-scatter.9.cloned.1.call-update) | async-done | bytes 442384 | tf_op jit(solution)/shard_map/reduce_scatter | solution.py:270
  492.4 1.6 copy.94
  495.1 1.5 collective-permute-start.14
  498.3 6.7 %collective-permute-done.14 = bf16[192,768]{1,0:T(8,128)(2,1)S(1)} collective-permute-done((bf16[192,768]{1,0:T(8,128)(2,1)S(1)}, bf16[192,768]{1,0:T(8,128)(2,1)S(1)}, u32[]{:S(2)}, u32[]{:S(2)}) %collective-permute-start.14) | collective-permute-done | bytes 294944 | tf_op jit(solution)/shard_map/ppermute | solution.py:100
  506.0 4.1 collective-permute-done.11
  511.2 1.6 maximum_convert_fusion.1
  513.5 1.6 maximum_convert_fusion
  515.0 14.5 %reduce-scatter.11.cloned.1.call-done = f32[1,416,192]{1,2,0:T(8,128)} async-done(((f32[4,416,192]{1,2,0:T(8,128)}), f32[1,416,192]{1,2,0:T(8,128)}) %reduce-scatter.11.cloned.1.call-update) | async-done | bytes 319504 | tf_op jit(solution)/shard_map/reduce_scatter | solution.py:277
  529.6 5.2 fusion.26
  534.8 27.7 %all-gather.15.cloned.1.call-done = f32[8,416,192]{1,2,0:T(8,128)} async-done(((f32[1,416,192]{1,2,0:T(8,128)}), f32[8,416,192]{1,2,0:T(8,128)}) %all-gather.15.cloned.1.call-update) | async-done | bytes 2555920 | tf_op jit(solution)/shard_map/all_gather | solution.py:291
  569.9 3.2 slice.149
  573.2 2.2 copy.95
  575.4 1.8 copy.103
  577.2 1.5 slice_bitcast_fusion.1
  (245 shorter events, 53.3 us)
Async XLA Ops:
  7.2 167.6 %copy-start = (bf16[768,768]{1,0:T(8,128)(2,1)S(1)}, bf16[768,768]{1,0:T(8,128)(2,1)}, u32[]{:S(2)}) copy-start(bf16[768,768]{1,0:T(8,128)(2,1)} %param.24) | copy-start | bytes 3538948
  7.2 61.1 %copy-start.48 = (s32[4]{0:T(128)S(1)}, s32[4]{0:T(128)}, u32[]{:S(2)}) copy-start(s32[4]{0:T(128)} %param.17) | copy-start | bytes 52
  7.2 61.1 %all-gather.13.cloned.1.call-start = ((), (), s32[]{:S(2)}) async-start(), calls=%async_computation.10 | async-start | bytes 3194880 | tf_op jit(solution)/shard_map/all_gather | solution.py:146
  11.3 163.5 %all-gather.9.cloned.1.call-start = ((), (), s32[]{:S(2)}) async-start(), calls=%async_computation.4 | async-start | bytes 3932160 | tf_op jit(solution)/shard_map/all_gather | solution.py:179
  68.3 5.2 collective-permute-start
  69.5 23.2 %copy-start.39 = (pred[512]{0:T(512)(128)(4,1)}, pred[512]{0:T(512)(128)(4,1)S(1)}, u32[]{:S(2)}) copy-start(pred[512]{0:T(512)(128)(4,1)S(1)} %iota_compare_fusion.1) | copy-start | bytes 1540
  77.9 2.4 copy-start.12
  81.9 20.9 %copy-start.4 = (f32[1,512,4,192]{1,3,0,2:T(8,128)}, f32[1,512,4,192]{1,3,0,2:T(8,128)S(1)}, u32[]{:S(2)}) copy-start(f32[1,512,4,192]{1,3,0,2:T(8,128)S(1)} %get-tuple-element.92) | copy-start | bytes 4718596
  88.1 4.6 copy-start.2
  92.7 10.1 %copy-start.24 = (f32[12,512]{1,0:T(8,128)}, f32[12,512]{1,0:T(8,128)S(1)}, u32[]{:S(2)}) copy-start(f32[12,512]{1,0:T(8,128)S(1)} %log_add_fusion) | copy-start | bytes 73732
  92.7 10.1 %copy-start.26 = (f32[12,64]{1,0:T(8,128)S(1)}, f32[12,64]{1,0:T(8,128)}, u32[]{:S(2)}) copy-start(f32[12,64]{1,0:T(8,128)} %reshape.335) | copy-start | bytes 9220
  102.8 4.1 copy-start.46
  102.8 4.1 copy-start.47
  106.9 2.8 copy-start.16
  107.0 4.3 copy-start.28
  107.0 4.2 copy-start.34
  112.4 145.6 %reduce-scatter.5.cloned.1.call-start = ((), (), s32[]{:S(2)}) async-start(), calls=%async_computation.5 | async-start | bytes 3932160 | tf_op jit(solution)/shard_map/reduce_scatter | solution.py:183
  174.8 20.1 %copy-start.44 = (bf16[768,768]{1,0:T(8,128)(2,1)S(1)}, bf16[768,768]{1,0:T(8,128)(2,1)}, u32[]{:S(2)}) copy-start(bf16[768,768]{1,0:T(8,128)(2,1)} %param.26) | copy-start | bytes 3538948
  198.9 130.6 %all-gather.11.cloned.1.call-start = ((), (), s32[]{:S(2)}) async-start(), calls=%async_computation.6 | async-start | bytes 3932160 | tf_op jit(solution)/shard_map/all_gather | solution.py:195
  258.0 2.2 copy-start.15
  258.0 2.2 copy-start.35
  263.1 2.9 copy-start.31
  265.9 139.5 %reduce-scatter.7.cloned.1.call-start = ((), (), s32[]{:S(2)}) async-start(), calls=%async_computation.7 | async-start | bytes 3932160 | tf_op jit(solution)/shard_map/reduce_scatter | solution.py:207
  346.3 144.9 %reduce-scatter.9.cloned.1.call-start = ((), (), s32[]{:S(2)}) async-start(), calls=%async_computation.8 | async-start | bytes 3981312 | tf_op jit(solution)/shard_map/reduce_scatter | solution.py:270
  346.3 5.7 copy-start.43
  346.3 5.7 copy-start.51
  352.1 2.8 copy-start.20
  354.8 1.8 copy-start.18
  356.6 3.0 collective-permute-start.4
  356.6 7.1 %collective-permute-start.1 = (f32[384,768]{1,0:T(8,128)}, f32[384,768]{1,0:T(8,128)}, u32[]{:S(2)}, u32[]{:S(2)}) collective-permute-start(f32[384,768]{1,0:T(8,128)} %get-tuple-element.130), channel_id=1, source_target_pairs={{0,4},{4,0},{8,12},{12,8},{16,20},{20,16},{24,28},{28,24},{1,5},{5... | collective-permute-start | bytes 3538952 | tf_op jit(solution)/shard_map/ppermute | solution.py:85
  357.2 6.6 %copy-start.19 = (f32[768,768]{1,0:T(8,128)S(1)}, f32[768,768]{1,0:T(8,128)}, u32[]{:S(2)}) copy-start(f32[768,768]{1,0:T(8,128)} %copy-done.18) | copy-start | bytes 7077892
  362.3 16.5 %collective-permute-start.5 = (f32[192,768]{1,0:T(8,128)}, f32[192,768]{1,0:T(8,128)}, u32[]{:S(2)}, u32[]{:S(2)}) collective-permute-start(f32[192,768]{1,0:T(8,128)} %constant_dynamic-slice_fusion.1), channel_id=1, source_target_pairs={{0,8},{4,12},{8,0},{12,4},{16,24},{20,28},{24,16},{28,20},{1,9},{5... | collective-permute-start | bytes 1769480 | tf_op jit(solution)/shard_map/ppermute | solution.py:85
  367.0 23.5 %collective-permute-start.2 = (f32[192,768]{1,0:T(8,128)}, f32[192,768]{1,0:T(8,128)}, u32[]{:S(2)}, u32[]{:S(2)}) collective-permute-start(f32[192,768]{1,0:T(8,128)} %constant_dynamic-slice_fusion.4), channel_id=1, source_target_pairs={{0,8},{4,12},{8,0},{12,4},{16,24},{20,28},{24,16},{28,20},{1,9},{5... | collective-permute-start | bytes 1769480 | tf_op jit(solution)/shard_map/ppermute | solution.py:85
  367.6 23.0 %copy-start.11 = (f32[384,768]{1,0:T(8,128)S(1)}, f32[384,768]{1,0:T(8,128)}, u32[]{:S(2)}) copy-start(f32[384,768]{1,0:T(8,128)} %copy-done.10) | copy-start | bytes 3538948
  379.9 11.8 %copy-start.21 = (f32[192,768]{1,0:T(8,128)}, f32[192,768]{1,0:T(8,128)S(1)}, u32[]{:S(2)}) copy-start(f32[192,768]{1,0:T(8,128)S(1)} %dynamic-slice_add_fusion.2) | copy-start | bytes 1769476
  380.7 16.1 %collective-permute-start.6 = (f32[96,768]{1,0:T(8,128)}, f32[96,768]{1,0:T(8,128)}, u32[]{:S(2)}, u32[]{:S(2)}) collective-permute-start(f32[96,768]{1,0:T(8,128)} %constant_dynamic-slice_fusion), channel_id=1, source_target_pairs={{0,16},{4,20},{8,24},{12,28},{16,0},{20,4},{24,8},{28,12},{1,17},{... | collective-permute-start | bytes 884744 | tf_op jit(solution)/shard_map/ppermute | solution.py:85
  392.5 4.3 copy-start.22
  392.5 8.5 %collective-permute-start.3 = (f32[96,768]{1,0:T(8,128)}, f32[96,768]{1,0:T(8,128)}, u32[]{:S(2)}, u32[]{:S(2)}) collective-permute-start(f32[96,768]{1,0:T(8,128)} %constant_dynamic-slice_fusion.3), channel_id=1, source_target_pairs={{0,16},{4,20},{8,24},{12,28},{16,0},{20,4},{24,8},{28,12},{1,17},{... | collective-permute-start | bytes 884744 | tf_op jit(solution)/shard_map/ppermute | solution.py:85
  398.5 9.0 %copy-start.30 = (f32[512]{0:T(512)S(1)}, f32[512]{0:T(512)}, u32[]{:S(2)}) copy-start(f32[512]{0:T(512)} %copy-done.29) | copy-start | bytes 6148
  405.4 4.9 slice-start.3
  408.2 2.6 slice-start.4
  408.2 5.6 slice-start
  409.4 4.3 slice-start.1
  410.8 4.2 slice-start.2
  410.8 4.6 copy-start.5
  410.8 4.6 copy-start.25
  410.8 4.6 copy-start.27
  410.8 4.6 copy-start.40
  425.7 7.2 %copy-start.7 = (f32[1,512,4,192]{1,3,0,2:T(8,128)S(1)}, f32[1,512,4,192]{1,3,0,2:T(8,128)}, u32[]{:S(2)}) copy-start(f32[1,512,4,192]{1,3,0,2:T(8,128)} %get-tuple-element.93) | copy-start | bytes 4718596
  435.0 2.6 copy-start.13
  443.1 86.5 %reduce-scatter.11.cloned.1.call-start = ((), (), s32[]{:S(2)}) async-start(), calls=%async_computation.9 | async-start | bytes 1966080 | tf_op jit(solution)/shard_map/reduce_scatter | solution.py:277
  444.3 52.3 %collective-permute-start.10 = (bf16[96,768]{1,0:T(8,128)(2,1)}, bf16[96,768]{1,0:T(8,128)(2,1)}, u32[]{:S(2)}, u32[]{:S(2)}) collective-permute-start(bf16[96,768]{1,0:T(8,128)(2,1)} %dynamic-slice_add_fusion.5), channel_id=1, source_target_pairs={{0,16},{4,20},{8,24},{12,28},{16,0},{20,4},{24,8},{28,12},{1,17},{... | collective-permute-start | bytes 442376 | tf_op jit(solution)/shard_map/ppermute | solution.py:100
  445.8 48.2 %collective-permute-start.13 = (bf16[96,768]{1,0:T(8,128)(2,1)}, bf16[96,768]{1,0:T(8,128)(2,1)}, u32[]{:S(2)}, u32[]{:S(2)}) collective-permute-start(bf16[96,768]{1,0:T(8,128)(2,1)} %dynamic-slice_add_fusion.4), channel_id=1, source_target_pairs={{0,16},{4,20},{8,24},{12,28},{16,0},{20,4},{24,8},{28,12},{1,17},{... | collective-permute-start | bytes 442376 | tf_op jit(solution)/shard_map/ppermute | solution.py:100
  448.7 2.4 collective-permute-start.7
  451.2 9.1 %collective-permute-start.8 = (bf16[192,768]{1,0:T(8,128)(2,1)S(1)}, bf16[192,768]{1,0:T(8,128)(2,1)S(1)}, u32[]{:S(2)}, u32[]{:S(2)}) collective-permute-start(bf16[192,768]{1,0:T(8,128)(2,1)S(1)} %dynamic-slice_convert_fusion.1), channel_id=1, source_target_pairs={{0,8},{4,12},{8,0},{12,4},{16,24},{20,28},{24,16},{28,20},{1,9},{5... | collective-permute-start | bytes 884744 | tf_op jit(solution)/shard_map/ppermute | solution.py:85
  460.4 5.2 collective-permute-start.9
  494.0 68.5 %all-gather.15.cloned.1.call-start = ((), (), s32[]{:S(2)}) async-start(), calls=%async_computation.11 | async-start | bytes 3538944 | tf_op jit(solution)/shard_map/all_gather | solution.py:291
  495.1 9.9 %collective-permute-start.14 = (bf16[192,768]{1,0:T(8,128)(2,1)S(1)}, bf16[192,768]{1,0:T(8,128)(2,1)S(1)}, u32[]{:S(2)}, u32[]{:S(2)}) collective-permute-start(bf16[192,768]{1,0:T(8,128)(2,1)S(1)} %pad_maximum_fusion.6), channel_id=1, source_target_pairs={{0,8},{4,12},{8,0},{12,4},{16,24},{20,28},{24,16},{28,20},{1,9},{5... | collective-permute-start | bytes 884744 | tf_op jit(solution)/shard_map/ppermute | solution.py:100
  497.7 12.4 %collective-permute-start.11 = (bf16[192,768]{1,0:T(8,128)(2,1)S(1)}, bf16[192,768]{1,0:T(8,128)(2,1)S(1)}, u32[]{:S(2)}, u32[]{:S(2)}) collective-permute-start(bf16[192,768]{1,0:T(8,128)(2,1)S(1)} %pad_maximum_fusion.5), channel_id=1, source_target_pairs={{0,8},{4,12},{8,0},{12,4},{16,24},{20,28},{24,16},{28,20},{1,9},{5... | collective-permute-start | bytes 884744 | tf_op jit(solution)/shard_map/ppermute | solution.py:100
  506.0 5.0 collective-permute-start.15
  511.0 2.2 collective-permute-start.12
  513.4 16.2 %copy-start.9 = (f32[512,768]{1,0:T(8,128)S(1)}, f32[512,768]{1,0:T(8,128)}, u32[]{:S(2)}) copy-start(f32[512,768]{1,0:T(8,128)} %copy-done.8) | copy-start | bytes 4718596
  513.5 16.2 %copy-start.14 = (bf16[12,64,512]{2,1,0:T(8,128)(2,1)S(1)}, bf16[12,64,512]{2,1,0:T(8,128)(2,1)}, u32[]{:S(2)}) copy-start(bf16[12,64,512]{2,1,0:T(8,128)(2,1)} %copy-done.13) | copy-start | bytes 2359300
  575.4 4.4 copy-start.1
  (17 other events, 19.3 us)
Sparse Core Ops, SparseCore 0:
  11.4 56.8 all-gather.12
  112.6 62.2 all-gather.8
  199.0 59.0 reduce-scatter.4
  266.1 63.3 all-gather.10
  346.4 59.0 reduce-scatter.6
  443.2 47.9 reduce-scatter.8
  494.1 35.4 reduce-scatter.10
  531.5 31.0 all-gather.14

commit v6 on v5

--- a/solution.py
+++ b/solution.py
@@ -1,6 +1,10 @@
+import functools
+
 import jax
 import jax.numpy as jnp
 from jax import lax
+from jax.experimental import pallas as pl
+from jax.experimental.pallas import tpu as pltpu
 from jax.sharding import PartitionSpec as P
 
 HD = 64
@@ -27,44 +31,95 @@
     )
 
 
-def attend_forward(queries, key_rows, value_rows, usable, factor):
-    scores = (
-        jnp.einsum("pqhe,pkhe->phqk", queries, key_rows, preferred_element_type=jnp.float32)
-        * factor
-    )
-    scores = jnp.where(usable[:, None, None, :], scores, NEG)
-    log_total = jax.nn.logsumexp(scores, axis=-1, keepdims=True)
-    attn_probs = jnp.exp(scores - log_total)
-    context = jnp.einsum(
-        "phqk,pkhe->pqhe",
-        attn_probs.astype(jnp.bfloat16),
-        value_rows,
-        preferred_element_type=jnp.float32,
-    )
-    return context, attn_probs
-
-
-def attend_backward(queries, key_rows, value_rows, attn_probs, context_grad, factor):
-    prob_grad = jnp.einsum(
-        "pqhe,pkhe->phqk", context_grad, value_rows, preferred_element_type=jnp.float32
-    )
-    row_dot = jnp.sum(prob_grad * attn_probs, axis=-1, keepdims=True)
-    score_grad = (attn_probs * (prob_grad - row_dot)).astype(jnp.bfloat16)
-    query_grad = (
-        jnp.einsum("phqk,pkhe->pqhe", score_grad, key_rows, preferred_element_type=jnp.float32)
-        * factor
-    )
-    key_grad = (
-        jnp.einsum("phqk,pqhe->pkhe", score_grad, queries, preferred_element_type=jnp.float32)
-        * factor
-    )
-    value_grad = jnp.einsum(
-        "phqk,pqhe->pkhe",
-        attn_probs.astype(jnp.bfloat16),
-        context_grad,
-        preferred_element_type=jnp.float32,
-    )
-    return query_grad, key_grad, value_grad
+def _probs(q, k, length, factor):
+    scores = lax.dot_general(q, k, (((1,), (1,)), ((), ())), preferred_element_type=jnp.float32) * factor
+    col = lax.broadcasted_iota(jnp.int32, scores.shape, 1)
+    scores = jnp.where(col < length, scores, NEG)
+    top = jnp.max(scores, axis=1, keepdims=True)
+    raised = jnp.exp(scores - top)
+    return raised / jnp.sum(raised, axis=1, keepdims=True)
+
+
+def _fwd_kernel(len_ref, qkv_ref, out_ref, *, heads, factor):
+    length = len_ref[pl.program_id(0)]
+    for h in range(heads):
+        cols = slice(h * HD, (h + 1) * HD)
+        q = qkv_ref[0, :, cols]
+        k = qkv_ref[1, :, cols]
+        v = qkv_ref[2, :, cols]
+        probs = _probs(q, k, length, factor)
+        out_ref[:, cols] = jnp.dot(
+            probs.astype(jnp.bfloat16), v, preferred_element_type=jnp.float32
+        ).astype(out_ref.dtype)
+
+
+def _bwd_kernel(len_ref, qkv_ref, grad_ref, out_ref, *, heads, factor):
+    length = len_ref[pl.program_id(0)]
+    for h in range(heads):
+        cols = slice(h * HD, (h + 1) * HD)
+        q = qkv_ref[0, :, cols]
+        k = qkv_ref[1, :, cols]
+        v = qkv_ref[2, :, cols]
+        g = grad_ref[:, cols]
+        probs = _probs(q, k, length, factor)
+        prob_grad = lax.dot_general(g, v, (((1,), (1,)), ((), ())), preferred_element_type=jnp.float32)
+        row_dot = jnp.sum(prob_grad * probs, axis=1, keepdims=True)
+        score_grad = (probs * (prob_grad - row_dot)).astype(jnp.bfloat16)
+        out_ref[0, :, cols] = (
+            jnp.dot(score_grad, k, preferred_element_type=jnp.float32) * factor
+        ).astype(out_ref.dtype)
+        out_ref[1, :, cols] = (
+            lax.dot_general(score_grad, q, (((0,), (0,)), ((), ())), preferred_element_type=jnp.float32)
+            * factor
+        ).astype(out_ref.dtype)
+        out_ref[2, :, cols] = lax.dot_general(
+            probs.astype(jnp.bfloat16), g, (((0,), (0,)), ((), ())), preferred_element_type=jnp.float32
+        ).astype(out_ref.dtype)
+
+
+def attention_forward(qkv, lengths, factor, pair=2):
+    _, rows, width = qkv.shape
+    passages = rows // LEN
+    block = pair * HD
+    grid = (passages, width // block)
+    return pl.pallas_call(
+        functools.partial(_fwd_kernel, heads=pair, factor=factor),
+        out_shape=jax.ShapeDtypeStruct((rows, width), jnp.bfloat16),
+        grid_spec=pltpu.PrefetchScalarGridSpec(
+            num_scalar_prefetch=1,
+            grid=grid,
+            in_specs=[pl.BlockSpec((3, LEN, block), lambda p, i, n: (0, p, i))],
+            out_specs=pl.BlockSpec((LEN, block), lambda p, i, n: (p, i)),
+        ),
+        cost_estimate=pl.CostEstimate(
+            flops=4 * rows * LEN * width, transcendentals=rows * LEN * width // HD,
+            bytes_accessed=4 * rows * width * 2,
+        ),
+    )(lengths, qkv)
+
+
+def attention_backward(qkv, context_grad, lengths, factor, pair=2):
+    _, rows, width = qkv.shape
+    passages = rows // LEN
+    block = pair * HD
+    grid = (passages, width // block)
+    return pl.pallas_call(
+        functools.partial(_bwd_kernel, heads=pair, factor=factor),
+        out_shape=jax.ShapeDtypeStruct((3, rows, width), jnp.bfloat16),
+        grid_spec=pltpu.PrefetchScalarGridSpec(
+            num_scalar_prefetch=1,
+            grid=grid,
+            in_specs=[
+                pl.BlockSpec((3, LEN, block), lambda p, i, n: (0, p, i)),
+                pl.BlockSpec((LEN, block), lambda p, i, n: (p, i)),
+            ],
+            out_specs=pl.BlockSpec((3, LEN, block), lambda p, i, n: (0, p, i)),
+        ),
+        cost_estimate=pl.CostEstimate(
+            flops=10 * rows * LEN * width, transcendentals=rows * LEN * width // HD,
+            bytes_accessed=8 * rows * width * 2,
+        ),
+    )(lengths, qkv, context_grad)
 
 
 def dp_pow2(values, dp_size):
@@ -126,7 +181,6 @@
         shard = qkv_weight.shape[2]
         groups = width // shard
         passages = rows // LEN
-        heads = width // HD
         factor = HD ** (-0.5)
 
         packed_w = jnp.concatenate(
@@ -154,18 +208,14 @@
 
         tensor_index = lax.axis_index("tensor")
         own_lengths = lax.dynamic_slice_in_dim(lengths, tensor_index * passages, passages)
-        usable = jnp.arange(LEN, dtype=jnp.int32)[None, :] < own_lengths[:, None]
 
         own_tokens = tokens.astype(jnp.float32)
         projected = jnp.einsum(
             "rd,gtdj->trgj", tokens, qkv_blocks, preferred_element_type=jnp.float32
         ).reshape(3, rows, width)
-        four_dims = (passages, LEN, heads, HD)
-        queries = (projected[0] + bias_full[0]).astype(jnp.bfloat16).reshape(four_dims)
-        key_rows = projected[1].astype(jnp.bfloat16).reshape(four_dims)
-        value_rows = (projected[2] + bias_full[1]).astype(jnp.bfloat16).reshape(four_dims)
-        context, attn_probs = attend_forward(queries, key_rows, value_rows, usable, factor)
-        context_low = context.reshape(rows, width).astype(jnp.bfloat16)
+        bias3 = jnp.stack([bias_full[0], jnp.zeros_like(bias_full[0]), bias_full[1]])
+        qkv_low = (projected + bias3[:, None, :]).astype(jnp.bfloat16)
+        context_low = attention_forward(qkv_low, own_lengths, factor)
         attn_out = jnp.einsum(
             "rgj,gcj->rc",
             context_low.reshape(rows, groups, shard),
@@ -217,7 +267,7 @@
         context_grad = (
             jnp.einsum("rc,gcj->rgj", attn_grad, proj_blocks, preferred_element_type=jnp.float32)
             .astype(jnp.bfloat16)
-            .reshape(four_dims)
+            .reshape(rows, width)
         )
         early = contract(attn_grad, context_low, 0, 0)
         early_halved = dp_pow2(early, dp_size)
@@ -225,14 +275,7 @@
             early = dp_halve(early.astype(jnp.bfloat16), dp_size, jnp.float32)
         else:
             early = lax.psum_scatter(early, "dp", scatter_dimension=0, tiled=True)
-        query_grad, key_grad, value_grad = attend_backward(
-            queries, key_rows, value_rows, attn_probs, context_grad, factor
-        )
-        proj_grad = (
-            jnp.stack([query_grad, key_grad, value_grad])
-            .reshape(3, rows, width)
-            .astype(jnp.bfloat16)
-        )
+        proj_grad = attention_backward(qkv_low, context_grad, own_lengths, factor)
         grad_bias_full = jnp.sum(proj_grad[0::2], axis=1, dtype=jnp.float32)
         grad_qkv_full = jnp.einsum(
             "rd,tre->tde", tokens, proj_grad, preferred_element_type=jnp.float32

time: 597 us -> 592 us (level)
  Pallas kernels: 0 us -> 31.3 us
  matrix products: 89.3 us -> 64.4 us
  other arithmetic: 58.8 us -> 41.9 us
  waiting for transfers between devices: 353 us -> 364 us
  starting transfers between devices: 24.3 us -> 13.4 us
  local copies, waits for them, and re-layouts: 46.3 us -> 53.7 us
    pallas_call x0 -> x2, Pallas kernels: none -> 31.3 us  [the longest x1 18.3 us: attention_backward(): pl.pallas_call(functools.partial(_bwd_kernel, heads=pair, factor=factor),...]
    dot_general x6 -> x0, matrix products: 25.5 us -> none  [the longest x1 10.3 us: attend_backward(): jnp.einsum('pqhe,pkhe->phqk', context_grad, value_rows, preferred_element...]
    convert_element_type x3 -> x2, other arithmetic: 17.6 us -> 4.2 us  [per_device(): qkv_low = (projected + bias3[:, None, :]).astype(jnp.bfloat16)]
    reduce_scatter x1, starting transfers between devices: 11.2 us -> 0.04 us  [per_device(): lax.psum_scatter(contract(pre_grad, up_weight, 1, 1).astype(jnp.bfloat16)...]
    all_gather x1, waiting for transfers between devices: 52.3 us -> 63.5 us  [per_device(): branch_rows = lax.all_gather(branch_grad, 'tensor', axis=0, tiled=True)]
    reshape x0 -> x2, local copies, waits for them, and re-layouts: none -> 7.31 us  [the longest x1 6.15 us: per_device(): projected = jnp.einsum('rd,gtdj->trgj', tokens, qkv_blocks, preferred_ele...]
    unnamed x122 -> x78, local copies, waits for them, and re-layouts: 16.4 us -> 13.9 us
  transfers between devices with their start and end apart: 24 -> 24, of which waited for: 19 -> 18; matrix products, arithmetic and copies ran while one was open for 8% -> 8% of each run, Pallas kernels for 0% -> 0%
where the time goes in v6:
time: 592 us; the launch traced here: 584 us
  waiting for transfers between devices  364 us (61%)
  matrix products  64.4 us (11%)
  local copies, waits for them, and re-layouts  53.7 us (9%)
  other arithmetic  41.9 us (7%)
  Pallas kernels  31.3 us (5%)
  between operations  15.4 us (3%)
  starting transfers between devices  13.4 us (2%)
    all_gather x1, waiting for transfers between devices, per_device(): branch_rows = lax.all_gather(branch_grad, 'tensor', axis=0, tiled=True)  63.5 us
    all_gather x1, waiting for transfers between devices, per_device(): ffn_rows = lax.all_gather(middle_low, 'tensor', axis=0, tiled=True)  62.1 us
    reduce_scatter x1, waiting for transfers between devices, per_device(): lax.psum_scatter(jnp.dot(hidden, down_weight, preferred_element_type=jnp....  59.1 us
    all_gather x1, waiting for transfers between devices, per_device(): mine = lax.all_gather(mine, 'tensor', axis=0, tiled=False)  56.9 us
    ppermute x9, waiting for transfers between devices, dp_halve(): got = lax.ppermute(give, 'dp', [(i, i ^ 1 << step) for i in range(dp_size)])  35.8 us
    reduce_scatter x1, waiting for transfers between devices, per_device(): lax.psum_scatter(grad_qkv_full.reshape(3 * width, width).astype(jnp.bfloa...  26 us
    dot_general x5, matrix products, contract(): lax.dot_general(left, right, (((left_dim,), (right_dim,)), ((), ())), pre...  24.9 us
    all_gather x1, waiting for transfers between devices, per_device(): joined = lax.all_gather(joined, 'dp', axis=0, tiled=False)  24 us
  transfers between devices with their start and end apart: 24, of which 18 were waited for; matrix products, arithmetic and copies ran while one was open for 8% of the time, Pallas kernels for 0%

profile of v6, /device:TPU:0, one launch (start us, length us, event | category | flops | bytes accessed | tf_op | source)
XLA Modules:
  0.0 584.0 jit_solution(9237166241333641629)
XLA Ops:
  9.4 1.8 fusion.35
  11.3 56.9 %all-gather.13.cloned.1.call-done = bf16[4,1544,192]{1,2,0:T(8,128)(2,1)} async-done(((bf16[1,1544,192]{1,2,0:T(8,128)(2,1)}), bf16[4,1544,192]{1,2,0:T(8,128)(2,1)}) %all-gather.13.cloned.1.call-update) | async-done | bytes 2371600 | tf_op jit(solution)/shard_map/all_gather | solution.py:200
  68.9 4.5 collective-permute-done
  73.4 4.4 broadcast_select_fusion.1
  77.9 1.5 copy-done.2
  79.9 2.9 pad_maximum_fusion
  82.8 2.1 fusion.13
  84.9 2.6 copy.68
  87.5 6.2 %copy.69 = f32[3,512,768]{2,1,0:T(8,128)} copy(f32[3,512,768]{1,2,0:T(8,128)} %bitcast.94) | data formatting | bytes 9437184 | tf_op jit(solution)/shard_map/reshape | solution.py:215
  93.8 4.1 add_convert_fusion.1.qkv_ref
  97.9 12.9 %shard_map.254 = bf16[512,768]{1,0:T(8,128)(2,1)} custom-call(s32[1]{0:T(128)} %dynamic_slice.60.len_ref, bf16[3,512,768]{2,1,0:T(8,128)(2,1)} %add_convert_fusion.1.qkv_ref), custom_call_target="tpu_custom_call" | custom-call | flops 805306368 | bytes 3145728 | tf_op jit(solution)/shard_map/pallas_call | solution.py:85
  110.8 1.4 copy.70
  112.3 2.6 fusion.48
  116.7 62.1 %all-gather.9.cloned.1.call-done = bf16[2048,768]{1,0:T(8,128)(2,1)} async-done(((bf16[512,768]{1,0:T(8,128)(2,1)}), bf16[2048,768]{1,0:T(8,128)(2,1)}) %all-gather.9.cloned.1.call-update) | async-done | bytes 3145744 | tf_op jit(solution)/shard_map/all_gather | solution.py:229
  178.9 18.4 %multiply_convert_fusion = (bf16[2048,768]{1,0:T(8,128)(2,1)S(1)}, f32[2048,768]{1,0:T(8,128)}, f32[2048,768]{1,0:T(8,128)}) fusion(f32[768]{0:T(1024)S(1)} %convert_element_type.124, bf16[2048,768]{1,0:T(8,128)(2,1)} %all-gather.9.cloned.1.call-done, bf16[768,768]{1,0:T(8,128)(2,1)S(1)} %copy-done), kind=kOutput, calls=%fused_computation.4 | convolution fusion | flops 2519728128 | bytes 20057088 | tf_op jit(solution)/shard_map/dot_general | solution.py:230
  197.3 1.7 copy-done.32
  199.0 4.0 convolution_convert_fusion.1
  203.1 59.1 %reduce-scatter.5.cloned.1.call-done = bf16[512,768]{1,0:T(8,128)(2,1)} async-done(((bf16[2048,768]{1,0:T(8,128)(2,1)}), bf16[512,768]{1,0:T(8,128)(2,1)}) %reduce-scatter.5.cloned.1.call-update) | async-done | bytes 786448 | tf_op jit(solution)/shard_map/reduce_scatter | solution.py:233
  262.3 1.7 fusion.45
  264.3 2.0 fusion.19
  266.3 1.6 fusion.44
  270.2 63.5 %all-gather.11.cloned.1.call-done = bf16[2048,768]{1,0:T(8,128)(2,1)} async-done(((bf16[512,768]{1,0:T(8,128)(2,1)}), bf16[2048,768]{1,0:T(8,128)(2,1)}) %all-gather.11.cloned.1.call-update) | async-done | bytes 3145744 | tf_op jit(solution)/shard_map/all_gather | solution.py:245
  333.7 10.5 %convert_reduce_fusion = (f32[768]{0:T(1024)S(1)}, bf16[2048,768]{1,0:T(8,128)(2,1)S(1)}) fusion(f32[2048,768]{1,0:T(8,128)} %get-tuple-element.89, f32[2048,768]{1,0:T(8,128)} %get-tuple-element.122, f32[768]{0:T(1024)S(1)} %copy-done.24, bf16[2048,768]{1,0:T(8,128)(2,1)} %all-gather.11.cloned.1.call-done, bf16[768,768]{1,0:T(8,128)(2,1)} %param.26), kind=kOutput, calls=%fused_computation.2 | convolution fusion | flops 2442657024 | bytes 20060160 | tf_op jit(solution)/shard_map/dot_general | solution.py:29
  344.2 1.7 copy-done.33
  345.9 4.0 convolution_convert_fusion
  350.2 5.7 fusion.50
  355.9 2.7 fusion.49
  358.7 1.3 constant_dynamic-slice_fusion.2
  361.0 2.5 collective-permute-done.4
  363.5 1.8 dynamic-slice_add_fusion
  365.3 1.5 collective-permute-start.5
  366.8 1.4 dynamic-slice_add_fusion.1
  370.7 10.9 %collective-permute-done.5 = f32[192,768]{1,0:T(8,128)} collective-permute-done((f32[192,768]{1,0:T(8,128)S(1)}, f32[192,768]{1,0:T(8,128)}, u32[]{:S(2)}, u32[]{:S(2)}) %collective-permute-start.5) | collective-permute-done | bytes 589856 | tf_op jit(solution)/shard_map/ppermute | solution.py:140
  383.5 1.5 collective-permute-start.6
  385.0 8.5 %collective-permute-done.2 = f32[192,768]{1,0:T(8,128)} collective-permute-done((f32[192,768]{1,0:T(8,128)}, f32[192,768]{1,0:T(8,128)}, u32[]{:S(2)}, u32[]{:S(2)}) %collective-permute-start.2) | collective-permute-done | bytes 589856 | tf_op jit(solution)/shard_map/ppermute | solution.py:140
  395.4 1.5 collective-permute-start.3
  396.8 2.9 slice.129
  400.4 3.3 collective-permute-done.3
  404.5 4.6 reduce-scatter.7.cloned.1.call-done
  409.1 1.9 convert_add_fusion
  412.6 1.6 copy-done.14
  416.3 18.3 %shard_map.255 = bf16[3,512,768]{2,1,0:T(8,128)(2,1)} custom-call(s32[1]{0:T(128)} %dynamic_slice.60.len_ref, bf16[3,512,768]{2,1,0:T(8,128)(2,1)} %add_convert_fusion.1.qkv_ref, bf16[512,768]{1,0:T(8,128)(2,1)} %copy.71.grad_ref), custom_call_target="tpu_custom_call" | custom-call | flops 2013265920 | bytes 6291456 | tf_op jit(solution)/shard_map/pallas_call | solution.py:106
  434.6 5.5 convolution_convert_fusion.2
  441.7 1.9 fusion.22
  444.0 1.5 collective-permute-start.10
  446.2 1.4 convert_add_fusion.1
  447.6 1.5 collective-permute-start.8
  450.0 6.7 %collective-permute-done.8 = bf16[192,768]{1,0:T(8,128)(2,1)S(1)} collective-permute-done((bf16[192,768]{1,0:T(8,128)(2,1)S(1)}, bf16[192,768]{1,0:T(8,128)(2,1)S(1)}, u32[]{:S(2)}, u32[]{:S(2)}) %collective-permute-start.8) | collective-permute-done | bytes 294944 | tf_op jit(solution)/shard_map/ppermute | solution.py:140
  458.2 3.8 collective-permute-done.9
  462.1 26.0 %reduce-scatter.9.cloned.1.call-done = bf16[288,768]{1,0:T(8,128)(2,1)} async-done(((bf16[2304,768]{1,0:T(8,128)(2,1)}), bf16[288,768]{1,0:T(8,128)(2,1)}) %reduce-scatter.9.cloned.1.call-update) | async-done | bytes 442384 | tf_op jit(solution)/shard_map/reduce_scatter | solution.py:313
  489.2 1.7 copy.76
  492.0 1.5 collective-permute-start.14
  495.2 6.7 %collective-permute-done.14 = bf16[192,768]{1,0:T(8,128)(2,1)S(1)} collective-permute-done((bf16[192,768]{1,0:T(8,128)(2,1)S(1)}, bf16[192,768]{1,0:T(8,128)(2,1)S(1)}, u32[]{:S(2)}, u32[]{:S(2)}) %collective-permute-start.14) | collective-permute-done | bytes 294944 | tf_op jit(solution)/shard_map/ppermute | solution.py:155
  502.2 4.8 collective-permute-done.11
  507.5 1.6 maximum_convert_fusion.1
  509.4 1.6 maximum_convert_fusion
  511.0 15.5 %reduce-scatter.11.cloned.1.call-done = f32[1,416,192]{1,2,0:T(8,128)} async-done(((f32[4,416,192]{1,2,0:T(8,128)}), f32[1,416,192]{1,2,0:T(8,128)}) %reduce-scatter.11.cloned.1.call-update) | async-done | bytes 319504 | tf_op jit(solution)/shard_map/reduce_scatter | solution.py:320
  526.6 2.8 copy.72
  529.4 6.1 %fusion.20 = bf16[512,768]{1,0:T(8,128)(2,1)} fusion(bf16[4,24,3,8,768]{4,3,2,1,0:T(8,128)(2,1)} %bitcast.101, bf16[3,512,4,192]{1,3,2,0:T(8,128)(2,1)} %bitcast.103, f32[512,768]{1,0:T(8,128)} %copy-done.6, f32[512]{0:T(512)S(1)} %copy-done.21), kind=kOutput, calls=%fused_computation.44 | convolution fusion | flops 1813118976 | bytes 8259584 | tf_op jit(solution)/shard_map/trgj,gtdj->rd/dot_general | solution.py:283
  535.4 24.0 %all-gather.15.cloned.1.call-done = f32[8,416,192]{1,2,0:T(8,128)} async-done(((f32[1,416,192]{1,2,0:T(8,128)}), f32[8,416,192]{1,2,0:T(8,128)}) %all-gather.15.cloned.1.call-update) | async-done | bytes 2555920 | tf_op jit(solution)/shard_map/all_gather | solution.py:334
  566.9 3.2 slice.130
  570.1 2.2 copy.77
  572.3 1.8 copy.85
  574.2 1.5 slice_bitcast_fusion.1
  (191 shorter events, 39.1 us)
Async XLA Ops:
  7.2 171.7 %copy-start = (bf16[768,768]{1,0:T(8,128)(2,1)S(1)}, bf16[768,768]{1,0:T(8,128)(2,1)}, u32[]{:S(2)}) copy-start(bf16[768,768]{1,0:T(8,128)(2,1)} %param.24) | copy-start | bytes 3538948
  7.2 61.1 %copy-start.31 = (s32[4]{0:T(128)S(1)}, s32[4]{0:T(128)}, u32[]{:S(2)}) copy-start(s32[4]{0:T(128)} %param.17) | copy-start | bytes 52
  7.2 61.1 %all-gather.13.cloned.1.call-start = ((), (), s32[]{:S(2)}) async-start(), calls=%async_computation.10 | async-start | bytes 3194880 | tf_op jit(solution)/shard_map/all_gather | solution.py:200
  11.3 167.6 %all-gather.9.cloned.1.call-start = ((), (), s32[]{:S(2)}) async-start(), calls=%async_computation.4 | async-start | bytes 3932160 | tf_op jit(solution)/shard_map/all_gather | solution.py:229
  68.3 5.2 collective-permute-start
  77.9 1.5 copy-start.2
  79.9 2.9 copy-start.28
  82.8 2.1 copy-start.9
  97.9 14.4 %copy-start.30 = (f32[768]{0:T(1024)S(1)}, f32[768]{0:T(1024)}, u32[]{:S(2)}) copy-start(f32[768]{0:T(1024)} %param.21) | copy-start | bytes 9220
  112.2 3.0 copy-start.15
  112.3 3.0 copy-start.16
  114.9 1.8 copy-start.25
  116.5 145.8 %reduce-scatter.5.cloned.1.call-start = ((), (), s32[]{:S(2)}) async-start(), calls=%async_computation.5 | async-start | bytes 3932160 | tf_op jit(solution)/shard_map/reduce_scatter | solution.py:233
  116.7 80.5 %copy-start.23 = (f32[768]{0:T(1024)}, f32[768]{0:T(1024)S(1)}, u32[]{:S(2)}) copy-start(f32[768]{0:T(1024)S(1)} %convert_element_type.124) | copy-start | bytes 9220
  178.9 20.1 %copy-start.27 = (bf16[768,768]{1,0:T(8,128)(2,1)S(1)}, bf16[768,768]{1,0:T(8,128)(2,1)}, u32[]{:S(2)}) copy-start(bf16[768,768]{1,0:T(8,128)(2,1)} %param.26) | copy-start | bytes 3538948
  197.3 1.7 copy-start.32
  203.0 61.3 %copy-start.10 = (bf16[512,768]{1,0:T(8,128)(2,1)S(1)}, bf16[512,768]{1,0:T(8,128)(2,1)}, u32[]{:S(2)}) copy-start(bf16[512,768]{1,0:T(8,128)(2,1)} %param.16) | copy-start | bytes 2359300
  203.1 130.6 %all-gather.11.cloned.1.call-start = ((), (), s32[]{:S(2)}) async-start(), calls=%async_computation.6 | async-start | bytes 3932160 | tf_op jit(solution)/shard_map/all_gather | solution.py:245
  264.0 2.3 copy-start.17
  264.0 2.3 copy-start.22
  267.9 1.1 copy-start.3
  267.9 65.8 %copy-start.24 = (f32[768]{0:T(1024)S(1)}, f32[768]{0:T(1024)}, u32[]{:S(2)}) copy-start(f32[768]{0:T(1024)} %copy-done.23) | copy-start | bytes 9220
  270.2 138.9 %reduce-scatter.7.cloned.1.call-start = ((), (), s32[]{:S(2)}) async-start(), calls=%async_computation.7 | async-start | bytes 3932160 | tf_op jit(solution)/shard_map/reduce_scatter | solution.py:257
  344.2 1.7 copy-start.33
  349.9 138.2 %reduce-scatter.9.cloned.1.call-start = ((), (), s32[]{:S(2)}) async-start(), calls=%async_computation.8 | async-start | bytes 3981312 | tf_op jit(solution)/shard_map/reduce_scatter | solution.py:313
  350.2 5.7 copy-start.26
  350.2 5.7 copy-start.34
  355.9 2.8 copy-start.13
  358.7 1.8 copy-start.11
  360.5 3.0 collective-permute-start.4
  360.5 6.3 %collective-permute-start.1 = (f32[384,768]{1,0:T(8,128)}, f32[384,768]{1,0:T(8,128)}, u32[]{:S(2)}, u32[]{:S(2)}) collective-permute-start(f32[384,768]{1,0:T(8,128)} %get-tuple-element.124), channel_id=1, source_target_pairs={{0,4},{4,0},{8,12},{12,8},{16,20},{20,16},{24,28},{28,24},{1,5},{5... | collective-permute-start | bytes 3538952 | tf_op jit(solution)/shard_map/ppermute | solution.py:140
  361.0 5.8 copy-start.12
  365.3 16.4 %collective-permute-start.5 = (f32[192,768]{1,0:T(8,128)S(1)}, f32[192,768]{1,0:T(8,128)}, u32[]{:S(2)}, u32[]{:S(2)}) collective-permute-start(f32[192,768]{1,0:T(8,128)S(1)} %constant_dynamic-slice_fusion.1), channel_id=1, source_target_pairs={{0,8},{4,12},{8,0},{12,4},{16,24},{20,28},{24,16},{28,20},{1,9},{5... | collective-permute-start | bytes 1769480 | tf_op jit(solution)/shard_map/ppermute | solution.py:140
  368.3 1.0 copy-start.7
  370.1 23.3 %collective-permute-start.2 = (f32[192,768]{1,0:T(8,128)}, f32[192,768]{1,0:T(8,128)}, u32[]{:S(2)}, u32[]{:S(2)}) collective-permute-start(f32[192,768]{1,0:T(8,128)} %constant_dynamic-slice_fusion.4), channel_id=1, source_target_pairs={{0,8},{4,12},{8,0},{12,4},{16,24},{20,28},{24,16},{28,20},{1,9},{5... | collective-permute-start | bytes 1769480 | tf_op jit(solution)/shard_map/ppermute | solution.py:140
  370.7 22.8 %copy-start.8 = (f32[384,768]{1,0:T(8,128)S(1)}, f32[384,768]{1,0:T(8,128)}, u32[]{:S(2)}) copy-start(f32[384,768]{1,0:T(8,128)} %copy-done.7) | copy-start | bytes 3538948
  383.5 16.2 %collective-permute-start.6 = (f32[96,768]{1,0:T(8,128)}, f32[96,768]{1,0:T(8,128)S(1)}, u32[]{:S(2)}, u32[]{:S(2)}) collective-permute-start(f32[96,768]{1,0:T(8,128)} %constant_dynamic-slice_fusion), channel_id=1, source_target_pairs={{0,16},{4,20},{8,24},{12,28},{16,0},{20,4},{24,8},{28,12},{1,17},{... | collective-permute-start | bytes 884744 | tf_op jit(solution)/shard_map/ppermute | solution.py:140
  395.4 8.4 %collective-permute-start.3 = (f32[96,768]{1,0:T(8,128)}, f32[96,768]{1,0:T(8,128)S(1)}, u32[]{:S(2)}, u32[]{:S(2)}) collective-permute-start(f32[96,768]{1,0:T(8,128)} %constant_dynamic-slice_fusion.3), channel_id=1, source_target_pairs={{0,16},{4,20},{8,24},{12,28},{16,0},{20,4},{24,8},{28,12},{1,17},{... | collective-permute-start | bytes 884744 | tf_op jit(solution)/shard_map/ppermute | solution.py:140
  412.3 2.7 copy-start.6
  412.3 1.8 copy-start.14
  412.3 2.6 copy-start.20
  416.3 18.4 %copy-start.29 = (bf16[512,768]{1,0:T(8,128)(2,1)S(1)}, bf16[512,768]{1,0:T(8,128)(2,1)}, u32[]{:S(2)}) copy-start(bf16[512,768]{1,0:T(8,128)(2,1)} %param.15) | copy-start | bytes 2359300
  440.1 0.7 copy-start.19
  440.1 1.4 copy-start.18
  440.1 86.4 %reduce-scatter.11.cloned.1.call-start = ((), (), s32[]{:S(2)}) async-start(), calls=%async_computation.9 | async-start | bytes 1966080 | tf_op jit(solution)/shard_map/reduce_scatter | solution.py:320
  443.8 2.4 collective-permute-start.7
  444.0 49.5 %collective-permute-start.10 = (bf16[96,768]{1,0:T(8,128)(2,1)}, bf16[96,768]{1,0:T(8,128)(2,1)}, u32[]{:S(2)}, u32[]{:S(2)}) collective-permute-start(bf16[96,768]{1,0:T(8,128)(2,1)} %dynamic-slice_add_fusion.5), channel_id=1, source_target_pairs={{0,16},{4,20},{8,24},{12,28},{16,0},{20,4},{24,8},{28,12},{1,17},{... | collective-permute-start | bytes 442376 | tf_op jit(solution)/shard_map/ppermute | solution.py:155
  445.5 45.5 %collective-permute-start.13 = (bf16[96,768]{1,0:T(8,128)(2,1)}, bf16[96,768]{1,0:T(8,128)(2,1)}, u32[]{:S(2)}, u32[]{:S(2)}) collective-permute-start(bf16[96,768]{1,0:T(8,128)(2,1)} %dynamic-slice_add_fusion.4), channel_id=1, source_target_pairs={{0,16},{4,20},{8,24},{12,28},{16,0},{20,4},{24,8},{28,12},{1,17},{... | collective-permute-start | bytes 442376 | tf_op jit(solution)/shard_map/ppermute | solution.py:155
  446.1 3.6 copy-start.4
  447.6 9.1 %collective-permute-start.8 = (bf16[192,768]{1,0:T(8,128)(2,1)S(1)}, bf16[192,768]{1,0:T(8,128)(2,1)S(1)}, u32[]{:S(2)}, u32[]{:S(2)}) collective-permute-start(bf16[192,768]{1,0:T(8,128)(2,1)S(1)} %dynamic-slice_convert_fusion.1), channel_id=1, source_target_pairs={{0,8},{4,12},{8,0},{12,4},{16,24},{20,28},{24,16},{28,20},{1,9},{5... | collective-permute-start | bytes 884744 | tf_op jit(solution)/shard_map/ppermute | solution.py:140
  456.8 5.2 collective-permute-start.9
  490.9 68.6 %all-gather.15.cloned.1.call-start = ((), (), s32[]{:S(2)}) async-start(), calls=%async_computation.11 | async-start | bytes 3538944 | tf_op jit(solution)/shard_map/all_gather | solution.py:334
  492.0 9.9 %collective-permute-start.14 = (bf16[192,768]{1,0:T(8,128)(2,1)S(1)}, bf16[192,768]{1,0:T(8,128)(2,1)S(1)}, u32[]{:S(2)}, u32[]{:S(2)}) collective-permute-start(bf16[192,768]{1,0:T(8,128)(2,1)S(1)} %pad_maximum_fusion.5), channel_id=1, source_target_pairs={{0,8},{4,12},{8,0},{12,4},{16,24},{20,28},{24,16},{28,20},{1,9},{5... | collective-permute-start | bytes 884744 | tf_op jit(solution)/shard_map/ppermute | solution.py:155
  494.6 12.4 %collective-permute-start.11 = (bf16[192,768]{1,0:T(8,128)(2,1)S(1)}, bf16[192,768]{1,0:T(8,128)(2,1)S(1)}, u32[]{:S(2)}, u32[]{:S(2)}) collective-permute-start(bf16[192,768]{1,0:T(8,128)(2,1)S(1)} %pad_maximum_fusion.4), channel_id=1, source_target_pairs={{0,8},{4,12},{8,0},{12,4},{16,24},{20,28},{24,16},{28,20},{1,9},{5... | collective-permute-start | bytes 884744 | tf_op jit(solution)/shard_map/ppermute | solution.py:155
  502.1 5.1 collective-permute-start.15
  507.1 2.1 collective-permute-start.12
  509.4 17.1 %copy-start.5 = (bf16[3,512,768]{2,1,0:T(8,128)(2,1)S(1)}, bf16[3,512,768]{2,1,0:T(8,128)(2,1)}, u32[]{:S(2)}) copy-start(bf16[3,512,768]{2,1,0:T(8,128)(2,1)} %shard_map.255) | copy-start | bytes 7077892
  526.6 2.8 copy-start.21
  572.3 4.4 copy-start.1
Sparse Core Ops, SparseCore 0:
  11.4 56.8 all-gather.12
  116.6 62.2 all-gather.8
  203.2 59.0 reduce-scatter.4
  270.3 63.3 all-gather.10
  350.0 59.0 reduce-scatter.6
  440.2 47.8 reduce-scatter.8
  491.0 35.4 reduce-scatter.10
  528.4 31.0 all-gather.14

commit v7 on v6

--- a/solution.py
+++ b/solution.py
@@ -40,26 +40,24 @@
     return raised / jnp.sum(raised, axis=1, keepdims=True)
 
 
-def _fwd_kernel(len_ref, qkv_ref, out_ref, *, heads, factor):
+def _fwd_kernel(len_ref, q_ref, k_ref, v_ref, out_ref, *, heads, factor):
     length = len_ref[pl.program_id(0)]
     for h in range(heads):
         cols = slice(h * HD, (h + 1) * HD)
-        q = qkv_ref[0, :, cols]
-        k = qkv_ref[1, :, cols]
-        v = qkv_ref[2, :, cols]
-        probs = _probs(q, k, length, factor)
+        v = v_ref[:, cols]
+        probs = _probs(q_ref[:, cols], k_ref[:, cols], length, factor)
         out_ref[:, cols] = jnp.dot(
             probs.astype(jnp.bfloat16), v, preferred_element_type=jnp.float32
         ).astype(out_ref.dtype)
 
 
-def _bwd_kernel(len_ref, qkv_ref, grad_ref, out_ref, *, heads, factor):
+def _bwd_kernel(len_ref, q_ref, k_ref, v_ref, grad_ref, out_ref, *, heads, factor):
     length = len_ref[pl.program_id(0)]
     for h in range(heads):
         cols = slice(h * HD, (h + 1) * HD)
-        q = qkv_ref[0, :, cols]
-        k = qkv_ref[1, :, cols]
-        v = qkv_ref[2, :, cols]
+        q = q_ref[:, cols]
+        k = k_ref[:, cols]
+        v = v_ref[:, cols]
         g = grad_ref[:, cols]
         probs = _probs(q, k, length, factor)
         prob_grad = lax.dot_general(g, v, (((1,), (1,)), ((), ())), preferred_element_type=jnp.float32)
@@ -77,49 +75,48 @@
         ).astype(out_ref.dtype)
 
 
-def attention_forward(qkv, lengths, factor, pair=2):
-    _, rows, width = qkv.shape
-    passages = rows // LEN
-    block = pair * HD
-    grid = (passages, width // block)
+def _row_block(pair):
+    return pl.BlockSpec((LEN, pair * HD), lambda p, i, n: (p, i))
+
+
+def attention_forward(queries, keys, values, lengths, factor, pair=2):
+    rows, width = queries.shape
+    grid = (rows // LEN, width // (pair * HD))
     return pl.pallas_call(
         functools.partial(_fwd_kernel, heads=pair, factor=factor),
         out_shape=jax.ShapeDtypeStruct((rows, width), jnp.bfloat16),
         grid_spec=pltpu.PrefetchScalarGridSpec(
             num_scalar_prefetch=1,
             grid=grid,
-            in_specs=[pl.BlockSpec((3, LEN, block), lambda p, i, n: (0, p, i))],
-            out_specs=pl.BlockSpec((LEN, block), lambda p, i, n: (p, i)),
+            in_specs=[_row_block(pair)] * 3,
+            out_specs=_row_block(pair),
         ),
         cost_estimate=pl.CostEstimate(
-            flops=4 * rows * LEN * width, transcendentals=rows * LEN * width // HD,
+            flops=4 * rows * LEN * width,
+            transcendentals=rows * LEN * width // HD,
             bytes_accessed=4 * rows * width * 2,
         ),
-    )(lengths, qkv)
-
-
-def attention_backward(qkv, context_grad, lengths, factor, pair=2):
-    _, rows, width = qkv.shape
-    passages = rows // LEN
-    block = pair * HD
-    grid = (passages, width // block)
+    )(lengths, queries, keys, values)
+
+
+def attention_backward(queries, keys, values, context_grad, lengths, factor, pair=2):
+    rows, width = queries.shape
+    grid = (rows // LEN, width // (pair * HD))
     return pl.pallas_call(
         functools.partial(_bwd_kernel, heads=pair, factor=factor),
         out_shape=jax.ShapeDtypeStruct((3, rows, width), jnp.bfloat16),
         grid_spec=pltpu.PrefetchScalarGridSpec(
             num_scalar_prefetch=1,
             grid=grid,
-            in_specs=[
-                pl.BlockSpec((3, LEN, block), lambda p, i, n: (0, p, i)),
-                pl.BlockSpec((LEN, block), lambda p, i, n: (p, i)),
-            ],
-            out_specs=pl.BlockSpec((3, LEN, block), lambda p, i, n: (0, p, i)),
+            in_specs=[_row_block(pair)] * 4,
+            out_specs=pl.BlockSpec((3, LEN, pair * HD), lambda p, i, n: (0, p, i)),
         ),
         cost_estimate=pl.CostEstimate(
-            flops=10 * rows * LEN * width, transcendentals=rows * LEN * width // HD,
-            bytes_accessed=8 * rows * width * 2,
+            flops=10 * rows * LEN * width,
+            transcendentals=rows * LEN * width // HD,
+            bytes_accessed=7 * rows * width * 2,
         ),
-    )(lengths, qkv, context_grad)
+    )(lengths, queries, keys, values, context_grad)
 
 
 def dp_pow2(values, dp_size):
@@ -183,45 +180,42 @@
         passages = rows // LEN
         factor = HD ** (-0.5)
 
-        packed_w = jnp.concatenate(
-            [
-                qkv_weight.reshape(3 * width, shard),
-                out_weight.T,
-                qkv_bias,
-            ],
-            axis=0,
-        )
-        w_rows = packed_w.shape[0]
-        half_rows = -(-w_rows // 16) * 8
-        packed_w = jnp.pad(packed_w, ((0, 2 * half_rows - w_rows), (0, 0)))
+        half_rows = -(-(2 * width + 2) // 8) * 8
+        first_half = jnp.pad(
+            jnp.concatenate([qkv_weight[0], qkv_weight[1], qkv_bias], axis=0),
+            ((0, half_rows - 2 * width - 2), (0, 0)),
+        )
+        second_half = jnp.pad(
+            jnp.concatenate([qkv_weight[2], out_weight.T], axis=0),
+            ((0, half_rows - 2 * width), (0, 0)),
+        )
         dp_index = lax.axis_index("dp")
         parity = dp_index % 2
-        mine = lax.dynamic_slice_in_dim(packed_w, parity * half_rows, half_rows)
-        mine = lax.all_gather(mine, "tensor", axis=0, tiled=False)
+        mine = jnp.where(parity == 0, first_half, second_half)
+        mine = lax.all_gather(mine, "tensor", axis=1, tiled=False).reshape(half_rows, width)
         other = lax.ppermute(mine, "dp", [(i, i ^ 1) for i in range(dp_size)])
-        first = jnp.where(parity == 0, mine, other)
-        second = jnp.where(parity == 0, other, mine)
-        weights_all = jnp.concatenate([first, second], axis=1)[:, :w_rows]
-        qkv_blocks = weights_all[:, : 3 * width].reshape(groups, 3, width, shard)
-        proj_blocks = weights_all[:, 3 * width : 4 * width]
-        bias_full = weights_all[:, 4 * width :].transpose(1, 0, 2).reshape(2, width)
+        first_half = jnp.where(parity == 0, mine, other)
+        second_half = jnp.where(parity == 0, other, mine)
+        query_weight = first_half[:width]
+        key_weight = first_half[width : 2 * width]
+        query_bias = first_half[2 * width]
+        value_bias = first_half[2 * width + 1]
+        value_weight = second_half[:width]
+        proj_t = second_half[width : 2 * width]
 
         tensor_index = lax.axis_index("tensor")
         own_lengths = lax.dynamic_slice_in_dim(lengths, tensor_index * passages, passages)
 
         own_tokens = tokens.astype(jnp.float32)
-        projected = jnp.einsum(
-            "rd,gtdj->trgj", tokens, qkv_blocks, preferred_element_type=jnp.float32
-        ).reshape(3, rows, width)
-        bias3 = jnp.stack([bias_full[0], jnp.zeros_like(bias_full[0]), bias_full[1]])
-        qkv_low = (projected + bias3[:, None, :]).astype(jnp.bfloat16)
-        context_low = attention_forward(qkv_low, own_lengths, factor)
-        attn_out = jnp.einsum(
-            "rgj,gcj->rc",
-            context_low.reshape(rows, groups, shard),
-            proj_blocks,
-            preferred_element_type=jnp.float32,
-        )
+        def project(weight, bias=None):
+            out = jnp.dot(tokens, weight, preferred_element_type=jnp.float32)
+            return (out if bias is None else out + bias).astype(jnp.bfloat16)
+
+        query_low = project(query_weight, query_bias)
+        key_low = project(key_weight)
+        value_low = project(value_weight, value_bias)
+        context_low = attention_forward(query_low, key_low, value_low, own_lengths, factor)
+        attn_out = contract(context_low, proj_t, 1, 1)
         middle, norm1_back = jax.vjp(
             layer_norm, own_tokens + attn_out + out_bias, norm1_gain, norm1_shift
         )
@@ -264,10 +258,8 @@
         first_grad, grad_norm1_gain, grad_norm1_shift = norm1_back(norm1_in)
         attn_grad = first_grad.astype(jnp.bfloat16)
         grad_out_bias = jnp.sum(attn_grad, axis=0, dtype=jnp.float32)
-        context_grad = (
-            jnp.einsum("rc,gcj->rgj", attn_grad, proj_blocks, preferred_element_type=jnp.float32)
-            .astype(jnp.bfloat16)
-            .reshape(rows, width)
+        context_grad = jnp.dot(attn_grad, proj_t, preferred_element_type=jnp.float32).astype(
+            jnp.bfloat16
         )
         early = contract(attn_grad, context_low, 0, 0)
         early_halved = dp_pow2(early, dp_size)
@@ -275,16 +267,17 @@
             early = dp_halve(early.astype(jnp.bfloat16), dp_size, jnp.float32)
         else:
             early = lax.psum_scatter(early, "dp", scatter_dimension=0, tiled=True)
-        proj_grad = attention_backward(qkv_low, context_grad, own_lengths, factor)
+        proj_grad = attention_backward(
+            query_low, key_low, value_low, context_grad, own_lengths, factor
+        )
         grad_bias_full = jnp.sum(proj_grad[0::2], axis=1, dtype=jnp.float32)
         grad_qkv_full = jnp.einsum(
             "rd,tre->tde", tokens, proj_grad, preferred_element_type=jnp.float32
         )
-        input_part = jnp.einsum(
-            "trgj,gtdj->rd",
-            proj_grad.reshape(3, rows, groups, shard),
-            qkv_blocks,
-            preferred_element_type=jnp.float32,
+        input_part = (
+            contract(proj_grad[0], query_weight, 1, 1)
+            + contract(proj_grad[1], key_weight, 1, 1)
+            + contract(proj_grad[2], value_weight, 1, 1)
         )
         input_grad = (first_grad + input_part).astype(jnp.bfloat16)
 

time: 592 us -> 594 us (level)
  matrix products: 64.4 us -> 71.6 us
    dot_general x5 -> x9, matrix products: 24.9 us -> 35.1 us  [contract(): lax.dot_general(left, right, (((left_dim,), (right_dim,)), ((), ())), pre...]
    reshape x3 -> x0, local copies, waits for them, and re-layouts: 8.54 us -> none  [the longest x1 6.15 us: per_device(): projected = jnp.einsum('rd,gtdj->trgj', tokens, qkv_blocks, preferred_ele...]
    ppermute x9, waiting for transfers between devices: 35.8 us -> 43.2 us  [dp_halve(): got = lax.ppermute(give, 'dp', [(i, i ^ 1 << step) for i in range(dp_size)])]
    reduce_scatter x1, waiting for transfers between devices: 26 us -> 19.5 us  [per_device(): lax.psum_scatter(grad_qkv_full.reshape(3 * width, width).astype(jnp.bfloa...]
    unnamed x78 -> x90, local copies, waits for them, and re-layouts: 13.9 us -> 14.6 us
  transfers between devices with their start and end apart: 24 -> 24, of which waited for: 18 -> 18; matrix products, arithmetic and copies ran while one was open for 8% -> 9% of each run, Pallas kernels for 0% -> 0%
where the time goes in v7:
time: 594 us; the launch traced here: 584 us
  waiting for transfers between devices  364 us (61%)
  matrix products  71.6 us (12%)
  local copies, waits for them, and re-layouts  52 us (9%)
  other arithmetic  37 us (6%)
  Pallas kernels  31.5 us (5%)
  between operations  15.2 us (3%)
  starting transfers between devices  13.4 us (2%)
    all_gather x1, waiting for transfers between devices, per_device(): branch_rows = lax.all_gather(branch_grad, 'tensor', axis=0, tiled=True)  63.5 us
    all_gather x1, waiting for transfers between devices, per_device(): ffn_rows = lax.all_gather(middle_low, 'tensor', axis=0, tiled=True)  62.3 us
    reduce_scatter x1, waiting for transfers between devices, per_device(): lax.psum_scatter(jnp.dot(hidden, down_weight, preferred_element_type=jnp....  59 us
    all_gather x1, waiting for transfers between devices, per_device(): lax.all_gather(mine, 'tensor', axis=1, tiled=False)  56.5 us
    ppermute x9, waiting for transfers between devices, dp_halve(): got = lax.ppermute(give, 'dp', [(i, i ^ 1 << step) for i in range(dp_size)])  43.2 us
    dot_general x9, matrix products, contract(): lax.dot_general(left, right, (((left_dim,), (right_dim,)), ((), ())), pre...  35.1 us
    all_gather x1, waiting for transfers between devices, per_device(): joined = lax.all_gather(joined, 'dp', axis=0, tiled=False)  25.6 us
    reduce_scatter x1, waiting for transfers between devices, per_device(): lax.psum_scatter(grad_qkv_full.reshape(3 * width, width).astype(jnp.bfloa...  19.5 us
  transfers between devices with their start and end apart: 24, of which 18 were waited for; matrix products, arithmetic and copies ran while one was open for 9% of the time, Pallas kernels for 0%

profile of v7, /device:TPU:0, one launch (start us, length us, event | category | flops | bytes accessed | tf_op | source)
XLA Modules:
  0.0 584.4 jit_solution(13597367863616995356)
XLA Ops:
  9.4 2.0 fusion.36
  11.4 56.5 %all-gather.12.cloned.1.call-done = bf16[1544,768]{0,1:T(8,128)(2,1)} async-done(((bf16[1544,192]{0,1:T(8,128)(2,1)}), bf16[1544,768]{0,1:T(8,128)(2,1)}) %all-gather.12.cloned.1.call-update) | async-done | bytes 2371600 | tf_op jit(solution)/shard_map/all_gather | solution.py:195
  67.9 4.5 copy.75
  73.0 4.2 collective-permute-done
  77.1 3.9 copy.76
  81.0 3.0 broadcast_select_fusion
  84.4 2.2 fusion.13.k_ref
  86.6 1.7 fusion.11.q_ref
  88.3 1.7 fusion.12.v_ref
  90.0 13.0 %shard_map.254 = bf16[512,768]{1,0:T(8,128)(2,1)} custom-call(s32[1]{0:T(128)} %dynamic_slice.57.len_ref, bf16[512,768]{1,0:T(8,128)(2,1)} %fusion.11.q_ref, bf16[512,768]{1,0:T(8,128)(2,1)} %fusion.13.k_ref, bf16[512,768]{1,0:T(8,128)(2,1)} %fusion.12.v_ref), custom_call_target="tpu_custom_call" | custom-call | flops 805306368 | bytes 3145728 | tf_op jit(solution)/shard_map/pallas_call | solution.py:85
  103.0 2.6 fusion.49
  107.3 62.3 %all-gather.8.cloned.1.call-done = bf16[2048,768]{1,0:T(8,128)(2,1)} async-done(((bf16[512,768]{1,0:T(8,128)(2,1)}), bf16[2048,768]{1,0:T(8,128)(2,1)}) %all-gather.8.cloned.1.call-update) | async-done | bytes 3145744 | tf_op jit(solution)/shard_map/all_gather | solution.py:223
  169.6 18.4 %multiply_convert_fusion = (bf16[2048,768]{1,0:T(8,128)(2,1)S(1)}, f32[2048,768]{1,0:T(8,128)}, f32[2048,768]{1,0:T(8,128)}) fusion(f32[768]{0:T(1024)S(1)} %convert_element_type.138, bf16[2048,768]{1,0:T(8,128)(2,1)} %all-gather.8.cloned.1.call-done, bf16[768,768]{1,0:T(8,128)(2,1)S(1)} %copy-done), kind=kOutput, calls=%fused_computation.4 | convolution fusion | flops 2519728128 | bytes 20057088 | tf_op jit(solution)/shard_map/dot_general | solution.py:224
  188.0 1.7 copy-done.38
  189.7 4.0 convolution_convert_fusion.1
  193.9 59.0 %reduce-scatter.5.cloned.1.call-done = bf16[512,768]{1,0:T(8,128)(2,1)} async-done(((bf16[2048,768]{1,0:T(8,128)(2,1)}), bf16[512,768]{1,0:T(8,128)(2,1)}) %reduce-scatter.5.cloned.1.call-update) | async-done | bytes 786448 | tf_op jit(solution)/shard_map/reduce_scatter | solution.py:227
  252.9 1.7 fusion.46
  255.0 2.0 fusion.9
  257.0 1.6 fusion.45
  260.9 63.5 %all-gather.10.cloned.1.call-done = bf16[2048,768]{1,0:T(8,128)(2,1)} async-done(((bf16[512,768]{1,0:T(8,128)(2,1)}), bf16[2048,768]{1,0:T(8,128)(2,1)}) %all-gather.10.cloned.1.call-update) | async-done | bytes 3145744 | tf_op jit(solution)/shard_map/all_gather | solution.py:239
  324.3 10.5 %convert_reduce_fusion = (f32[768]{0:T(1024)S(1)}, bf16[2048,768]{1,0:T(8,128)(2,1)S(1)}) fusion(f32[2048,768]{1,0:T(8,128)} %get-tuple-element.103, f32[2048,768]{1,0:T(8,128)} %get-tuple-element.139, f32[768]{0:T(1024)S(1)} %copy-done.29, bf16[2048,768]{1,0:T(8,128)(2,1)} %all-gather.10.cloned.1.call-done, bf16[768,768]{1,0:T(8,128)(2,1)} %param.26), kind=kOutput, calls=%fused_computation.2 | convolution fusion | flops 2442657024 | bytes 20060160 | tf_op jit(solution)/shard_map/dot_general | solution.py:29
  334.9 1.7 copy-done.39
  336.5 4.0 convolution_convert_fusion
  340.9 5.7 fusion.51
  346.6 2.7 fusion.50
  349.4 1.7 constant_dynamic-slice_fusion.2
  352.1 2.7 collective-permute-done.1
  354.7 1.8 dynamic-slice_add_fusion.1
  356.6 1.5 collective-permute-start.2
  358.1 1.4 dynamic-slice_add_fusion
  361.4 11.6 %collective-permute-done.2 = f32[192,768]{1,0:T(8,128)} collective-permute-done((f32[192,768]{1,0:T(8,128)S(1)}, f32[192,768]{1,0:T(8,128)}, u32[]{:S(2)}, u32[]{:S(2)}) %collective-permute-start.2) | collective-permute-done | bytes 589856 | tf_op jit(solution)/shard_map/ppermute | solution.py:137
  375.0 1.5 collective-permute-start.3
  376.5 8.3 %collective-permute-done.5 = f32[192,768]{1,0:T(8,128)} collective-permute-done((f32[192,768]{1,0:T(8,128)}, f32[192,768]{1,0:T(8,128)}, u32[]{:S(2)}, u32[]{:S(2)}) %collective-permute-start.5) | collective-permute-done | bytes 589856 | tf_op jit(solution)/shard_map/ppermute | solution.py:137
  387.5 1.5 collective-permute-start.6
  388.9 1.6 dynamic-slice_add_fusion.5
  390.6 5.4 collective-permute-done.6
  396.0 1.7 dynamic-slice_add_fusion.4
  397.7 2.1 reduce-scatter.7.cloned.1.call-done
  399.8 1.9 convert_add_fusion
  406.3 3.0 convolution_convert_fusion.4.grad_ref
  409.3 18.5 %shard_map.255 = bf16[3,512,768]{2,1,0:T(8,128)(2,1)} custom-call(s32[1]{0:T(128)} %dynamic_slice.57.len_ref, bf16[512,768]{1,0:T(8,128)(2,1)} %fusion.11.q_ref, bf16[512,768]{1,0:T(8,128)(2,1)} %fusion.13.k_ref, bf16[512,768]{1,0:T(8,128)(2,1)} %fusion.12.v_ref, bf16[512,768]{1,0:T(8,128)(2,1)} %convolution_convert_fusion.4.grad_ref), custom_call_target="tpu_custom_call" | custom-call | flops 2013265920 | bytes 5505024 | tf_op jit(solution)/shard_map/pallas_call | solution.py:105
  427.8 5.5 convolution_convert_fusion.2
  436.7 2.2 fusion.10
  439.8 1.4 stack.21
  441.2 1.4 stack.22
  448.2 1.6 collective-permute-start.8
  450.1 8.9 %collective-permute-done.8 = bf16[192,768]{1,0:T(8,128)(2,1)S(1)} collective-permute-done((bf16[192,768]{1,0:T(8,128)(2,1)S(1)}, bf16[192,768]{1,0:T(8,128)(2,1)S(1)}, u32[]{:S(2)}, u32[]{:S(2)}) %collective-permute-start.8) | collective-permute-done | bytes 294944 | tf_op jit(solution)/shard_map/ppermute | solution.py:137
  462.6 6.4 %collective-permute-done.9 = bf16[96,768]{1,0:T(8,128)(2,1)S(1)} collective-permute-done((bf16[96,768]{1,0:T(8,128)(2,1)S(1)}, bf16[96,768]{1,0:T(8,128)(2,1)S(1)}, u32[]{:S(2)}, u32[]{:S(2)}) %collective-permute-start.9) | collective-permute-done | bytes 147488 | tf_op jit(solution)/shard_map/ppermute | solution.py:137
  469.0 19.5 %reduce-scatter.9.cloned.1.call-done = bf16[288,768]{1,0:T(8,128)(2,1)} async-done(((bf16[2304,768]{1,0:T(8,128)(2,1)}), bf16[288,768]{1,0:T(8,128)(2,1)}) %reduce-scatter.9.cloned.1.call-update) | async-done | bytes 442384 | tf_op jit(solution)/shard_map/reduce_scatter | solution.py:306
  489.7 1.7 copy.82
  491.5 1.5 collective-permute-start.11
  493.7 7.7 %collective-permute-done.11 = bf16[192,768]{1,0:T(8,128)(2,1)S(1)} collective-permute-done((bf16[192,768]{1,0:T(8,128)(2,1)S(1)}, bf16[192,768]{1,0:T(8,128)(2,1)S(1)}, u32[]{:S(2)}, u32[]{:S(2)}) %collective-permute-start.11) | collective-permute-done | bytes 294944 | tf_op jit(solution)/shard_map/ppermute | solution.py:152
  502.4 4.1 collective-permute-done.14
  507.6 1.6 maximum_convert_fusion
  509.8 1.6 maximum_convert_fusion.1
  511.4 15.5 %reduce-scatter.11.cloned.1.call-done = f32[1,416,192]{1,2,0:T(8,128)} async-done(((f32[4,416,192]{1,2,0:T(8,128)}), f32[1,416,192]{1,2,0:T(8,128)}) %reduce-scatter.11.cloned.1.call-update) | async-done | bytes 319504 | tf_op jit(solution)/shard_map/reduce_scatter | solution.py:313
  526.9 2.1 fusion.30
  529.0 2.2 fusion.27
  531.2 3.1 add_convert_fusion.1
  534.3 25.6 %all-gather.14.cloned.1.call-done = f32[8,416,192]{1,2,0:T(8,128)} async-done(((f32[1,416,192]{1,2,0:T(8,128)}), f32[8,416,192]{1,2,0:T(8,128)}) %all-gather.14.cloned.1.call-update) | async-done | bytes 2555920 | tf_op jit(solution)/shard_map/all_gather | solution.py:327
  559.9 3.3 slice.155
  563.1 2.2 copy.83
  565.3 1.8 copy.91
  574.6 1.5 slice_bitcast_fusion.9
  (195 shorter events, 47.1 us)
Async XLA Ops:
  7.2 162.4 %copy-start = (bf16[768,768]{1,0:T(8,128)(2,1)S(1)}, bf16[768,768]{1,0:T(8,128)(2,1)}, u32[]{:S(2)}) copy-start(bf16[768,768]{1,0:T(8,128)(2,1)} %param.24) | copy-start | bytes 3538948
  7.2 60.7 %all-gather.12.cloned.1.call-start = ((), (), s32[]{:S(2)}) async-start(), calls=%async_computation.10 | async-start | bytes 3194880 | tf_op jit(solution)/shard_map/all_gather | solution.py:195
  11.3 61.0 %copy-start.37 = (s32[4]{0:T(128)S(1)}, s32[4]{0:T(128)}, u32[]{:S(2)}) copy-start(s32[4]{0:T(128)} %param.17) | copy-start | bytes 52
  11.4 158.2 %all-gather.8.cloned.1.call-start = ((), (), s32[]{:S(2)}) async-start(), calls=%async_computation.4 | async-start | bytes 3932160 | tf_op jit(solution)/shard_map/all_gather | solution.py:223
  72.4 4.8 collective-permute-start
  81.0 3.3 copy-start.34
  84.1 4.2 copy-start.9
  84.1 4.2 copy-start.5
  90.0 13.0 %copy-start.36 = (f32[768]{0:T(1024)S(1)}, f32[768]{0:T(1024)}, u32[]{:S(2)}) copy-start(f32[768]{0:T(1024)} %param.21) | copy-start | bytes 9220
  103.0 3.0 copy-start.19
  103.0 3.0 copy-start.21
  105.7 1.6 copy-start.30
  107.2 145.7 %reduce-scatter.5.cloned.1.call-start = ((), (), s32[]{:S(2)}) async-start(), calls=%async_computation.5 | async-start | bytes 3932160 | tf_op jit(solution)/shard_map/reduce_scatter | solution.py:227
  107.3 80.7 %copy-start.28 = (f32[768]{0:T(1024)}, f32[768]{0:T(1024)S(1)}, u32[]{:S(2)}) copy-start(f32[768]{0:T(1024)S(1)} %convert_element_type.138) | copy-start | bytes 9220
  169.6 20.1 %copy-start.33 = (bf16[768,768]{1,0:T(8,128)(2,1)S(1)}, bf16[768,768]{1,0:T(8,128)(2,1)}, u32[]{:S(2)}) copy-start(bf16[768,768]{1,0:T(8,128)(2,1)} %param.26) | copy-start | bytes 3538948
  188.0 1.7 copy-start.38
  193.7 61.3 %copy-start.10 = (bf16[512,768]{1,0:T(8,128)(2,1)S(1)}, bf16[512,768]{1,0:T(8,128)(2,1)}, u32[]{:S(2)}) copy-start(bf16[512,768]{1,0:T(8,128)(2,1)} %param.16) | copy-start | bytes 2359300
  193.7 130.6 %all-gather.10.cloned.1.call-start = ((), (), s32[]{:S(2)}) async-start(), calls=%async_computation.6 | async-start | bytes 3932160 | tf_op jit(solution)/shard_map/all_gather | solution.py:239
  254.7 2.3 copy-start.22
  254.7 2.3 copy-start.27
  258.6 1.1 copy-start.1
  258.6 65.7 %copy-start.29 = (f32[768]{0:T(1024)S(1)}, f32[768]{0:T(1024)}, u32[]{:S(2)}) copy-start(f32[768]{0:T(1024)} %copy-done.28) | copy-start | bytes 9220
  260.8 138.9 %reduce-scatter.7.cloned.1.call-start = ((), (), s32[]{:S(2)}) async-start(), calls=%async_computation.7 | async-start | bytes 3932160 | tf_op jit(solution)/shard_map/reduce_scatter | solution.py:251
  334.9 1.7 copy-start.39
  340.6 147.9 %reduce-scatter.9.cloned.1.call-start = ((), (), s32[]{:S(2)}) async-start(), calls=%async_computation.8 | async-start | bytes 3981312 | tf_op jit(solution)/shard_map/reduce_scatter | solution.py:306
  340.8 5.7 copy-start.32
  340.8 5.7 copy-start.40
  346.6 2.8 copy-start.11
  349.4 2.2 copy-start.13
  351.6 3.2 collective-permute-start.1
  351.6 6.6 %collective-permute-start.4 = (f32[384,768]{1,0:T(8,128)}, f32[384,768]{1,0:T(8,128)}, u32[]{:S(2)}, u32[]{:S(2)}) collective-permute-start(f32[384,768]{1,0:T(8,128)} %get-tuple-element.140), channel_id=1, source_target_pairs={{0,4},{4,0},{8,12},{12,8},{16,20},{20,16},{24,28},{28,24},{1,5},{5... | collective-permute-start | bytes 3538952 | tf_op jit(solution)/shard_map/ppermute | solution.py:137
  352.1 6.1 %copy-start.12 = (f32[768,768]{1,0:T(8,128)S(1)}, f32[768,768]{1,0:T(8,128)}, u32[]{:S(2)}) copy-start(f32[768,768]{1,0:T(8,128)} %copy-done.11) | copy-start | bytes 7077892
  356.5 3.0 copy-start.6
  356.6 16.4 %collective-permute-start.2 = (f32[192,768]{1,0:T(8,128)S(1)}, f32[192,768]{1,0:T(8,128)}, u32[]{:S(2)}, u32[]{:S(2)}) collective-permute-start(f32[192,768]{1,0:T(8,128)S(1)} %constant_dynamic-slice_fusion.4), channel_id=1, source_target_pairs={{0,8},{4,12},{8,0},{12,4},{16,24},{20,28},{24,16},{28,20},{1,9},{5... | collective-permute-start | bytes 1769480 | tf_op jit(solution)/shard_map/ppermute | solution.py:137
  359.6 1.2 copy-start.7
  360.8 24.0 %collective-permute-start.5 = (f32[192,768]{1,0:T(8,128)}, f32[192,768]{1,0:T(8,128)}, u32[]{:S(2)}, u32[]{:S(2)}) collective-permute-start(f32[192,768]{1,0:T(8,128)} %constant_dynamic-slice_fusion.1), channel_id=1, source_target_pairs={{0,8},{4,12},{8,0},{12,4},{16,24},{20,28},{24,16},{28,20},{1,9},{5... | collective-permute-start | bytes 1769480 | tf_op jit(solution)/shard_map/ppermute | solution.py:137
  361.4 23.4 %copy-start.8 = (f32[384,768]{1,0:T(8,128)S(1)}, f32[384,768]{1,0:T(8,128)}, u32[]{:S(2)}) copy-start(f32[384,768]{1,0:T(8,128)} %copy-done.7) | copy-start | bytes 3538948
  375.0 13.9 %collective-permute-start.3 = (f32[96,768]{1,0:T(8,128)}, f32[96,768]{1,0:T(8,128)}, u32[]{:S(2)}, u32[]{:S(2)}) collective-permute-start(f32[96,768]{1,0:T(8,128)} %constant_dynamic-slice_fusion.3), channel_id=1, source_target_pairs={{0,16},{4,20},{8,24},{12,28},{16,0},{20,4},{24,8},{28,12},{1,17},{... | collective-permute-start | bytes 884744 | tf_op jit(solution)/shard_map/ppermute | solution.py:137
  387.5 8.5 %collective-permute-start.6 = (f32[96,768]{1,0:T(8,128)}, f32[96,768]{1,0:T(8,128)}, u32[]{:S(2)}, u32[]{:S(2)}) collective-permute-start(f32[96,768]{1,0:T(8,128)} %constant_dynamic-slice_fusion), channel_id=1, source_target_pairs={{0,16},{4,20},{8,24},{12,28},{16,0},{20,4},{24,8},{28,12},{1,17},{... | collective-permute-start | bytes 884744 | tf_op jit(solution)/shard_map/ppermute | solution.py:137
  403.5 1.1 copy-start.2
  405.5 0.9 copy-start.4
  409.3 18.5 %copy-start.35 = (bf16[512,768]{1,0:T(8,128)(2,1)S(1)}, bf16[512,768]{1,0:T(8,128)(2,1)}, u32[]{:S(2)}) copy-start(bf16[512,768]{1,0:T(8,128)(2,1)} %param.15) | copy-start | bytes 2359300
  433.3 1.3 copy-start.24
  433.3 2.0 copy-start.23
  433.3 93.6 %reduce-scatter.11.cloned.1.call-start = ((), (), s32[]{:S(2)}) async-start(), calls=%async_computation.9 | async-start | bytes 1966080 | tf_op jit(solution)/shard_map/reduce_scatter | solution.py:313
  436.7 3.1 copy-start.20
  436.7 3.1 copy-start.31
  439.8 7.2 %collective-permute-start.7 = (bf16[384,768]{1,0:T(8,128)(2,1)}, bf16[384,768]{1,0:T(8,128)(2,1)}, u32[]{:S(2)}, u32[]{:S(2)}) collective-permute-start(bf16[384,768]{1,0:T(8,128)(2,1)} %dynamic-slice_convert_fusion), channel_id=1, source_target_pairs={{0,4},{4,0},{8,12},{12,8},{16,20},{20,16},{24,28},{28,24},{1,5},{5... | collective-permute-start | bytes 1769480 | tf_op jit(solution)/shard_map/ppermute | solution.py:137
  443.9 5.9 %copy-start.26 = (f32[1,1,1,4,1,192]{5,3,1,4,2,0:T(4,128)S(1)}, f32[1,1,1,4,1,192]{5,3,1,4,2,0:T(4,128)}, u32[]{:S(2)}) copy-start(f32[1,1,1,4,1,192]{5,3,1,4,2,0:T(4,128)} %stack.25) | copy-start | bytes 9220
  443.9 5.9 %copy-start.14 = (bf16[3,512,768]{2,1,0:T(8,128)(2,1)S(1)}, bf16[3,512,768]{2,1,0:T(8,128)(2,1)}, u32[]{:S(2)}) copy-start(bf16[3,512,768]{2,1,0:T(8,128)(2,1)} %shard_map.255) | copy-start | bytes 7077892
  448.2 12.2 %copy-start.25 = (f32[1,1,1,4,1,192]{5,3,1,4,2,0:T(4,128)S(1)}, f32[1,1,1,4,1,192]{5,3,1,4,2,0:T(4,128)}, u32[]{:S(2)}) copy-start(f32[1,1,1,4,1,192]{5,3,1,4,2,0:T(4,128)} %stack.26) | copy-start | bytes 9220
  448.2 12.3 %copy-start.18 = (bf16[96,768]{1,0:T(8,128)(2,1)S(1)}, bf16[96,768]{1,0:T(8,128)(2,1)}, u32[]{:S(2)}) copy-start(bf16[96,768]{1,0:T(8,128)(2,1)} %dynamic-slice_add_fusion.5) | copy-start | bytes 442372
  448.2 13.2 %copy-start.17 = (bf16[96,768]{1,0:T(8,128)(2,1)S(1)}, bf16[96,768]{1,0:T(8,128)(2,1)}, u32[]{:S(2)}) copy-start(bf16[96,768]{1,0:T(8,128)(2,1)} %dynamic-slice_add_fusion.4) | copy-start | bytes 442372
  448.2 10.7 %collective-permute-start.8 = (bf16[192,768]{1,0:T(8,128)(2,1)S(1)}, bf16[192,768]{1,0:T(8,128)(2,1)S(1)}, u32[]{:S(2)}, u32[]{:S(2)}) collective-permute-start(bf16[192,768]{1,0:T(8,128)(2,1)S(1)} %dynamic-slice_convert_fusion.1), channel_id=1, source_target_pairs={{0,8},{4,12},{8,0},{12,4},{16,24},{20,28},{24,16},{28,20},{1,9},{5... | collective-permute-start | bytes 884744 | tf_op jit(solution)/shard_map/ppermute | solution.py:137
  459.0 9.9 %collective-permute-start.9 = (bf16[96,768]{1,0:T(8,128)(2,1)S(1)}, bf16[96,768]{1,0:T(8,128)(2,1)S(1)}, u32[]{:S(2)}, u32[]{:S(2)}) collective-permute-start(bf16[96,768]{1,0:T(8,128)(2,1)S(1)} %dynamic-slice_convert_fusion.2), channel_id=1, source_target_pairs={{0,16},{4,20},{8,24},{12,28},{16,0},{20,4},{24,8},{28,12},{1,17},{... | collective-permute-start | bytes 442376 | tf_op jit(solution)/shard_map/ppermute | solution.py:137
  460.5 30.9 %collective-permute-start.10 = (bf16[96,768]{1,0:T(8,128)(2,1)S(1)}, bf16[96,768]{1,0:T(8,128)(2,1)S(1)}, u32[]{:S(2)}, u32[]{:S(2)}) collective-permute-start(bf16[96,768]{1,0:T(8,128)(2,1)S(1)} %copy-done.18), channel_id=1, source_target_pairs={{0,16},{4,20},{8,24},{12,28},{16,0},{20,4},{24,8},{28,12},{1,17},{... | collective-permute-start | bytes 442376 | tf_op jit(solution)/shard_map/ppermute | solution.py:152
  461.3 31.6 %collective-permute-start.13 = (bf16[96,768]{1,0:T(8,128)(2,1)S(1)}, bf16[96,768]{1,0:T(8,128)(2,1)S(1)}, u32[]{:S(2)}, u32[]{:S(2)}) collective-permute-start(bf16[96,768]{1,0:T(8,128)(2,1)S(1)} %copy-done.17), channel_id=1, source_target_pairs={{0,16},{4,20},{8,24},{12,28},{16,0},{20,4},{24,8},{28,12},{1,17},{... | collective-permute-start | bytes 442376 | tf_op jit(solution)/shard_map/ppermute | solution.py:152
  491.3 68.6 %all-gather.14.cloned.1.call-start = ((), (), s32[]{:S(2)}) async-start(), calls=%async_computation.11 | async-start | bytes 3538944 | tf_op jit(solution)/shard_map/all_gather | solution.py:327
  491.5 9.9 %collective-permute-start.11 = (bf16[192,768]{1,0:T(8,128)(2,1)S(1)}, bf16[192,768]{1,0:T(8,128)(2,1)S(1)}, u32[]{:S(2)}, u32[]{:S(2)}) collective-permute-start(bf16[192,768]{1,0:T(8,128)(2,1)S(1)} %pad_maximum_fusion.3), channel_id=1, source_target_pairs={{0,8},{4,12},{8,0},{12,4},{16,24},{20,28},{24,16},{28,20},{1,9},{5... | collective-permute-start | bytes 884744 | tf_op jit(solution)/shard_map/ppermute | solution.py:152
  493.1 13.4 %collective-permute-start.14 = (bf16[192,768]{1,0:T(8,128)(2,1)S(1)}, bf16[192,768]{1,0:T(8,128)(2,1)S(1)}, u32[]{:S(2)}, u32[]{:S(2)}) collective-permute-start(bf16[192,768]{1,0:T(8,128)(2,1)S(1)} %pad_maximum_fusion.4), channel_id=1, source_target_pairs={{0,8},{4,12},{8,0},{12,4},{16,24},{20,28},{24,16},{28,20},{1,9},{5... | collective-permute-start | bytes 884744 | tf_op jit(solution)/shard_map/ppermute | solution.py:152
  502.4 5.0 collective-permute-start.12
  507.4 2.2 collective-permute-start.15
  509.8 17.1 %copy-start.15 = (bf16[3,512,768]{2,1,0:T(8,128)(2,1)S(1)}, bf16[3,512,768]{2,1,0:T(8,128)(2,1)}, u32[]{:S(2)}) copy-start(bf16[3,512,768]{2,1,0:T(8,128)(2,1)} %shard_map.255) | copy-start | bytes 7077892
  529.0 2.2 copy-start.3
  (1 other events, 0.8 us)
Sparse Core Ops, SparseCore 0:
  11.5 56.3 all-gather.11
  107.3 62.2 all-gather.7
  193.8 59.0 reduce-scatter.4
  261.0 63.3 all-gather.9
  340.7 59.0 reduce-scatter.6
  433.4 55.0 reduce-scatter.8
  491.4 35.4 reduce-scatter.10
  528.8 31.0 all-gather.13

commit v8 on v7

--- a/solution.py
+++ b/solution.py
@@ -21,8 +21,10 @@
     return center * lax.rsqrt(spread + EPS) * gain_vec + shift_vec
 
 
-def gelu_exact(values):
-    return jax.nn.gelu(values, approximate=False)
+def gelu_and_slope(values):
+    cdf = 0.5 * (1.0 + lax.erf(values * (2.0 ** -0.5)))
+    density = jnp.exp(-0.5 * values * values) * ((2.0 * jnp.pi) ** -0.5)
+    return values * cdf, cdf + values * density
 
 
 def contract(left, right, left_dim, right_dim):
@@ -222,7 +224,7 @@
         middle_low = middle.astype(jnp.bfloat16)
         ffn_rows = lax.all_gather(middle_low, "tensor", axis=0, tiled=True)
         pre_act = jnp.dot(ffn_rows, up_weight, preferred_element_type=jnp.float32) + up_bias
-        activated, gelu_back = jax.vjp(gelu_exact, pre_act)
+        activated, gelu_slope = gelu_and_slope(pre_act)
         hidden = activated.astype(jnp.bfloat16)
         ffn_out = lax.psum_scatter(
             jnp.dot(hidden, down_weight, preferred_element_type=jnp.float32).astype(jnp.bfloat16),
@@ -239,7 +241,7 @@
         branch_rows = lax.all_gather(branch_grad, "tensor", axis=0, tiled=True)
         hidden_grad = contract(branch_rows, down_weight, 1, 1)
         grad_down_weight = contract(hidden, branch_rows, 0, 0)
-        pre_grad = gelu_back(hidden_grad)[0].astype(jnp.bfloat16)
+        pre_grad = (hidden_grad * gelu_slope).astype(jnp.bfloat16)
         grad_up_bias = jnp.sum(pre_grad, axis=0, dtype=jnp.float32)
         grad_up_weight = contract(ffn_rows, pre_grad, 0, 0)
         ffn_grads = (grad_up_weight, grad_down_weight)

time: 594 us -> 563 us (0.948); the launches traced: 584 us -> 562 us
  matrix products: 71.6 us -> 55.9 us
  waiting for transfers between devices: 364 us -> 375 us
  local copies, waits for them, and re-layouts: 52 us -> 42.2 us
  other arithmetic: 37 us -> 29.3 us
    dot_general x1, matrix products: 18.4 us -> 6.73 us  [per_device(): jnp.dot(ffn_rows, up_weight, preferred_element_type=jnp.float32) + up_bias]
    reduce_scatter x1, waiting for transfers between devices: 19.5 us -> 28.3 us  [per_device(): lax.psum_scatter(grad_qkv_full.reshape(3 * width, width).astype(jnp.bfloa...]
    unnamed x90 -> x80, local copies, waits for them, and re-layouts: 14.6 us -> 11 us
  transfers between devices with their start and end apart: 24 -> 24, of which waited for: 18 -> 19; matrix products, arithmetic and copies ran while one was open for 9% -> 7% of each run, Pallas kernels for 0% -> 0%
where the time goes in v8:
time: 563 us; the launch traced here: 562 us
  waiting for transfers between devices  375 us (67%)
  matrix products  55.9 us (10%)
  local copies, waits for them, and re-layouts  42.2 us (7%)
  Pallas kernels  31.4 us (6%)
  other arithmetic  29.3 us (5%)
  between operations  14.9 us (3%)
  starting transfers between devices  13 us (2%)
    all_gather x1, waiting for transfers between devices, per_device(): branch_rows = lax.all_gather(branch_grad, 'tensor', axis=0, tiled=True)  63.3 us
    all_gather x1, waiting for transfers between devices, per_device(): ffn_rows = lax.all_gather(middle_low, 'tensor', axis=0, tiled=True)  62.3 us
    reduce_scatter x1, waiting for transfers between devices, per_device(): lax.psum_scatter(jnp.dot(hidden, down_weight, preferred_element_type=jnp....  59.2 us
    all_gather x1, waiting for transfers between devices, per_device(): lax.all_gather(mine, 'tensor', axis=1, tiled=False)  56.8 us
    ppermute x9, waiting for transfers between devices, dp_halve(): got = lax.ppermute(give, 'dp', [(i, i ^ 1 << step) for i in range(dp_size)])  41 us
    dot_general x9, matrix products, contract(): lax.dot_general(left, right, (((left_dim,), (right_dim,)), ((), ())), pre...  31.3 us
    reduce_scatter x1, waiting for transfers between devices, per_device(): lax.psum_scatter(grad_qkv_full.reshape(3 * width, width).astype(jnp.bfloa...  28.3 us
    all_gather x1, waiting for transfers between devices, per_device(): joined = lax.all_gather(joined, 'dp', axis=0, tiled=False)  25.6 us
  transfers between devices with their start and end apart: 24, of which 19 were waited for; matrix products, arithmetic and copies ran while one was open for 7% of the time, Pallas kernels for 0%

profile of v8, /device:TPU:0, one launch (start us, length us, event | category | flops | bytes accessed | tf_op | source)
XLA Modules:
  0.0 561.6 jit_solution(9994717671567706091)
XLA Ops:
  7.3 1.3 slice_bitcast_fusion.8
  9.8 56.8 %all-gather.12.cloned.1.call-done = bf16[1544,768]{0,1:T(8,128)(2,1)} async-done(((bf16[1544,192]{0,1:T(8,128)(2,1)}), bf16[1544,768]{0,1:T(8,128)(2,1)}) %all-gather.12.cloned.1.call-update) | async-done | bytes 2371600 | tf_op jit(solution)/shard_map/all_gather | solution.py:197
  66.6 4.5 copy.75
  71.6 4.2 collective-permute-done
  75.8 3.9 copy.76
  79.7 3.0 broadcast_select_fusion
  83.1 2.1 fusion.13.k_ref
  85.2 1.7 fusion.11.q_ref
  86.9 1.7 fusion.12.v_ref
  88.6 13.0 %shard_map.254 = bf16[512,768]{1,0:T(8,128)(2,1)} custom-call(s32[1]{0:T(128)} %dynamic_slice.57.len_ref, bf16[512,768]{1,0:T(8,128)(2,1)} %fusion.11.q_ref, bf16[512,768]{1,0:T(8,128)(2,1)} %fusion.13.k_ref, bf16[512,768]{1,0:T(8,128)(2,1)} %fusion.12.v_ref), custom_call_target="tpu_custom_call" | custom-call | flops 805306368 | bytes 3145728 | tf_op jit(solution)/shard_map/pallas_call | solution.py:87
  101.6 2.6 fusion.48
  104.9 1.2 fusion.14
  106.2 62.3 %all-gather.8.cloned.1.call-done = bf16[2048,768]{1,0:T(8,128)(2,1)} async-done(((bf16[512,768]{1,0:T(8,128)(2,1)}), bf16[2048,768]{1,0:T(8,128)(2,1)}) %all-gather.8.cloned.1.call-update) | async-done | bytes 3145744 | tf_op jit(solution)/shard_map/all_gather | solution.py:225
  168.5 6.7 %multiply_convert_fusion = (bf16[2048,768]{1,0:T(8,128)(2,1)S(1)}, f32[2048,768]{1,0:T(8,128)}) fusion(f32[768]{0:T(1024)S(1)} %convert_element_type.138, bf16[2048,768]{1,0:T(8,128)(2,1)} %all-gather.8.cloned.1.call-done, bf16[768,768]{1,0:T(8,128)(2,1)S(1)} %copy-done), kind=kOutput, calls=%fused_computation.8 | convolution fusion | flops 2425356288 | bytes 13765632 | tf_op jit(solution)/shard_map/dot_general | solution.py:226
  175.3 1.7 copy-done.33
  176.9 4.0 convolution_convert_fusion.1
  181.0 59.2 %reduce-scatter.5.cloned.1.call-done = bf16[512,768]{1,0:T(8,128)(2,1)} async-done(((bf16[2048,768]{1,0:T(8,128)(2,1)}), bf16[512,768]{1,0:T(8,128)(2,1)}) %reduce-scatter.5.cloned.1.call-update) | async-done | bytes 786448 | tf_op jit(solution)/shard_map/reduce_scatter | solution.py:229
  240.1 1.7 fusion.46
  243.7 1.6 fusion.45
  247.8 63.3 %all-gather.10.cloned.1.call-done = bf16[2048,768]{1,0:T(8,128)(2,1)} async-done(((bf16[512,768]{1,0:T(8,128)(2,1)}), bf16[2048,768]{1,0:T(8,128)(2,1)}) %all-gather.10.cloned.1.call-update) | async-done | bytes 3145744 | tf_op jit(solution)/shard_map/all_gather | solution.py:241
  311.1 7.0 %convert_reduce_fusion = (f32[768]{0:T(1024)S(1)}, bf16[2048,768]{1,0:T(8,128)(2,1)S(1)}) fusion(f32[2048,768]{1,0:T(8,128)} %get-tuple-element.136, f32[768]{0:T(1024)S(1)} %convert_element_type.138, bf16[2048,768]{1,0:T(8,128)(2,1)} %all-gather.10.cloned.1.call-done, bf16[768,768]{1,0:T(8,128)(2,1)} %param.26), kind=kOutput, calls=%fused_computation.7 | convolution fusion | flops 2436365568 | bytes 13768704 | tf_op jit(solution)/shard_map/dot_general | solution.py:31
  318.1 1.7 copy-done.34
  319.7 4.0 convolution_convert_fusion
  323.8 5.7 %fusion.50 = f32[768,768]{1,0:T(8,128)S(1)} fusion(bf16[2048,768]{1,0:T(8,128)(2,1)} %copy-done.33, bf16[2048,768]{1,0:T(8,128)(2,1)} %all-gather.10.cloned.1.call-done), kind=kOutput, calls=%fused_computation.160 | convolution fusion | flops 2415919104 | bytes 8650752 | tf_op jit(solution)/shard_map/dot_general | solution.py:31
  329.6 2.7 fusion.49
  332.4 1.3 constant_dynamic-slice_fusion.2
  334.7 2.5 collective-permute-done.1
  337.1 1.8 dynamic-slice_add_fusion.1
  339.0 1.5 collective-permute-start.2
  340.5 1.4 dynamic-slice_add_fusion
  344.4 11.0 %collective-permute-done.2 = f32[192,768]{1,0:T(8,128)} collective-permute-done((f32[192,768]{1,0:T(8,128)S(1)}, f32[192,768]{1,0:T(8,128)}, u32[]{:S(2)}, u32[]{:S(2)}) %collective-permute-start.2) | collective-permute-done | bytes 589856 | tf_op jit(solution)/shard_map/ppermute | solution.py:139
  357.2 1.5 collective-permute-start.3
  358.7 8.5 %collective-permute-done.5 = f32[192,768]{1,0:T(8,128)} collective-permute-done((f32[192,768]{1,0:T(8,128)}, f32[192,768]{1,0:T(8,128)}, u32[]{:S(2)}, u32[]{:S(2)}) %collective-permute-start.5) | collective-permute-done | bytes 589856 | tf_op jit(solution)/shard_map/ppermute | solution.py:139
  369.0 1.5 collective-permute-start.6
  371.2 6.2 %collective-permute-done.6 = f32[96,768]{1,0:T(8,128)S(1)} collective-permute-done((f32[96,768]{1,0:T(8,128)}, f32[96,768]{1,0:T(8,128)S(1)}, u32[]{:S(2)}, u32[]{:S(2)}) %collective-permute-start.6) | collective-permute-done | bytes 294944 | tf_op jit(solution)/shard_map/ppermute | solution.py:139
  378.1 4.9 reduce-scatter.7.cloned.1.call-done
  383.0 1.9 convert_add_fusion
  387.5 3.0 convolution_convert_fusion.4.grad_ref
  390.5 18.4 %shard_map.255 = bf16[3,512,768]{2,1,0:T(8,128)(2,1)} custom-call(s32[1]{0:T(128)} %dynamic_slice.57.len_ref, bf16[512,768]{1,0:T(8,128)(2,1)} %fusion.11.q_ref, bf16[512,768]{1,0:T(8,128)(2,1)} %fusion.13.k_ref, bf16[512,768]{1,0:T(8,128)(2,1)} %fusion.12.v_ref, bf16[512,768]{1,0:T(8,128)(2,1)} %convolution_convert_fusion.4.grad_ref), custom_call_target="tpu_custom_call" | custom-call | flops 2013265920 | bytes 5505024 | tf_op jit(solution)/shard_map/pallas_call | solution.py:107
  408.9 5.5 convolution_convert_fusion.2
  416.1 1.9 fusion.10
  418.5 2.1 collective-permute-done.7
  421.8 1.2 collective-permute-start.8
  423.3 7.6 %collective-permute-done.8 = bf16[192,768]{1,0:T(8,128)(2,1)S(1)} collective-permute-done((bf16[192,768]{1,0:T(8,128)(2,1)S(1)}, bf16[192,768]{1,0:T(8,128)(2,1)S(1)}, u32[]{:S(2)}, u32[]{:S(2)}) %collective-permute-start.8) | collective-permute-done | bytes 294944 | tf_op jit(solution)/shard_map/ppermute | solution.py:139
  431.0 1.3 collective-permute-start.9
  433.3 1.2 collective-permute-start.13
  434.5 3.2 collective-permute-done.9
  437.8 28.3 %reduce-scatter.9.cloned.1.call-done = bf16[288,768]{1,0:T(8,128)(2,1)} async-done(((bf16[2304,768]{1,0:T(8,128)(2,1)}), bf16[288,768]{1,0:T(8,128)(2,1)}) %reduce-scatter.9.cloned.1.call-update) | async-done | bytes 442384 | tf_op jit(solution)/shard_map/reduce_scatter | solution.py:308
  467.3 1.7 copy.82
  469.1 1.6 collective-permute-start.11
  471.3 7.7 %collective-permute-done.11 = bf16[192,768]{1,0:T(8,128)(2,1)S(1)} collective-permute-done((bf16[192,768]{1,0:T(8,128)(2,1)S(1)}, bf16[192,768]{1,0:T(8,128)(2,1)S(1)}, u32[]{:S(2)}, u32[]{:S(2)}) %collective-permute-start.11) | collective-permute-done | bytes 294944 | tf_op jit(solution)/shard_map/ppermute | solution.py:154
  479.3 4.8 collective-permute-done.14
  484.6 1.6 maximum_convert_fusion
  486.6 1.6 maximum_convert_fusion.1
  488.1 16.5 %reduce-scatter.11.cloned.1.call-done = f32[1,416,192]{1,2,0:T(8,128)} async-done(((f32[4,416,192]{1,2,0:T(8,128)}), f32[1,416,192]{1,2,0:T(8,128)}) %reduce-scatter.11.cloned.1.call-update) | async-done | bytes 319504 | tf_op jit(solution)/shard_map/reduce_scatter | solution.py:315
  504.7 2.1 fusion.30
  506.7 2.2 fusion.27
  508.9 3.1 add_convert_fusion
  512.0 25.6 %all-gather.14.cloned.1.call-done = f32[8,416,192]{1,2,0:T(8,128)} async-done(((f32[1,416,192]{1,2,0:T(8,128)}), f32[8,416,192]{1,2,0:T(8,128)}) %all-gather.14.cloned.1.call-update) | async-done | bytes 2555920 | tf_op jit(solution)/shard_map/all_gather | solution.py:329
  537.6 3.2 slice.155
  540.8 2.2 copy.83
  543.0 1.8 copy.91
  544.8 1.2 slice_reduce_fusion
  552.2 1.5 slice_bitcast_fusion.9
  (185 shorter events, 33.4 us)
Async XLA Ops:
  7.2 161.3 %copy-start = (bf16[768,768]{1,0:T(8,128)(2,1)S(1)}, bf16[768,768]{1,0:T(8,128)(2,1)}, u32[]{:S(2)}) copy-start(bf16[768,768]{1,0:T(8,128)(2,1)} %param.24) | copy-start | bytes 3538948
  7.2 1.4 copy-start.26
  7.2 1.5 copy-start.17
  7.2 59.4 %all-gather.12.cloned.1.call-start = ((), (), s32[]{:S(2)}) async-start(), calls=%async_computation.10 | async-start | bytes 3194880 | tf_op jit(solution)/shard_map/all_gather | solution.py:197
  9.8 61.3 %copy-start.32 = (s32[4]{0:T(128)S(1)}, s32[4]{0:T(128)}, u32[]{:S(2)}) copy-start(s32[4]{0:T(128)} %param.17) | copy-start | bytes 52
  9.8 158.7 %all-gather.8.cloned.1.call-start = ((), (), s32[]{:S(2)}) async-start(), calls=%async_computation.4 | async-start | bytes 3932160 | tf_op jit(solution)/shard_map/all_gather | solution.py:225
  71.1 4.8 collective-permute-start
  79.7 3.3 copy-start.29
  82.8 2.4 copy-start.8
  82.8 4.1 copy-start.5
  88.6 13.0 %copy-start.31 = (f32[768]{0:T(1024)S(1)}, f32[768]{0:T(1024)}, u32[]{:S(2)}) copy-start(f32[768]{0:T(1024)} %param.21) | copy-start | bytes 9220
  104.2 0.7 copy-start.18
  104.2 0.7 copy-start.19
  104.9 1.3 copy-start.25
  106.2 134.0 %reduce-scatter.5.cloned.1.call-start = ((), (), s32[]{:S(2)}) async-start(), calls=%async_computation.5 | async-start | bytes 3932160 | tf_op jit(solution)/shard_map/reduce_scatter | solution.py:229
  168.5 8.4 %copy-start.28 = (bf16[768,768]{1,0:T(8,128)(2,1)S(1)}, bf16[768,768]{1,0:T(8,128)(2,1)}, u32[]{:S(2)}) copy-start(bf16[768,768]{1,0:T(8,128)(2,1)} %param.26) | copy-start | bytes 3538948
  175.3 1.7 copy-start.33
  180.9 59.2 %copy-start.23 = (f32[768]{0:T(1024)S(1)}, f32[768]{0:T(1024)}, u32[]{:S(2)}) copy-start(f32[768]{0:T(1024)} %param.27) | copy-start | bytes 9220
  180.9 130.2 %all-gather.10.cloned.1.call-start = ((), (), s32[]{:S(2)}) async-start(), calls=%async_computation.6 | async-start | bytes 3932160 | tf_op jit(solution)/shard_map/all_gather | solution.py:241
  241.9 1.1 copy-start.9
  241.9 1.1 copy-start.20
  242.2 1.5 copy-start.24
  245.3 1.1 copy-start.2
  247.6 135.4 %reduce-scatter.7.cloned.1.call-start = ((), (), s32[]{:S(2)}) async-start(), calls=%async_computation.7 | async-start | bytes 3932160 | tf_op jit(solution)/shard_map/reduce_scatter | solution.py:253
  318.1 1.7 copy-start.34
  323.8 142.4 %reduce-scatter.9.cloned.1.call-start = ((), (), s32[]{:S(2)}) async-start(), calls=%async_computation.8 | async-start | bytes 3981312 | tf_op jit(solution)/shard_map/reduce_scatter | solution.py:308
  323.8 5.7 %copy-start.27 = (bf16[2048,768]{1,0:T(8,128)(2,1)S(1)}, bf16[2048,768]{1,0:T(8,128)(2,1)}, u32[]{:S(2)}) copy-start(bf16[2048,768]{1,0:T(8,128)(2,1)} %all-gather.8.cloned.1.call-done) | copy-start | bytes 9437188
  323.8 5.7 %copy-start.35 = (bf16[2048,768]{1,0:T(8,128)(2,1)S(1)}, bf16[2048,768]{1,0:T(8,128)(2,1)}, u32[]{:S(2)}) copy-start(bf16[2048,768]{1,0:T(8,128)(2,1)} %copy-done.34) | copy-start | bytes 9437188
  329.6 2.8 copy-start.10
  332.4 1.8 copy-start.12
  334.1 3.0 collective-permute-start.1
  334.2 6.3 %collective-permute-start.4 = (f32[384,768]{1,0:T(8,128)}, f32[384,768]{1,0:T(8,128)}, u32[]{:S(2)}, u32[]{:S(2)}) collective-permute-start(f32[384,768]{1,0:T(8,128)} %get-tuple-element.139), channel_id=1, source_target_pairs={{0,4},{4,0},{8,12},{12,8},{16,20},{20,16},{24,28},{28,24},{1,5},{5... | collective-permute-start | bytes 3538952 | tf_op jit(solution)/shard_map/ppermute | solution.py:139
  334.7 5.8 %copy-start.11 = (f32[768,768]{1,0:T(8,128)S(1)}, f32[768,768]{1,0:T(8,128)}, u32[]{:S(2)}) copy-start(f32[768,768]{1,0:T(8,128)} %copy-done.10) | copy-start | bytes 7077892
  339.0 16.4 %collective-permute-start.2 = (f32[192,768]{1,0:T(8,128)S(1)}, f32[192,768]{1,0:T(8,128)}, u32[]{:S(2)}, u32[]{:S(2)}) collective-permute-start(f32[192,768]{1,0:T(8,128)S(1)} %constant_dynamic-slice_fusion.4), channel_id=1, source_target_pairs={{0,8},{4,12},{8,0},{12,4},{16,24},{20,28},{24,16},{28,20},{1,9},{5... | collective-permute-start | bytes 1769480 | tf_op jit(solution)/shard_map/ppermute | solution.py:139
  341.9 1.0 copy-start.6
  343.8 23.3 %collective-permute-start.5 = (f32[192,768]{1,0:T(8,128)}, f32[192,768]{1,0:T(8,128)}, u32[]{:S(2)}, u32[]{:S(2)}) collective-permute-start(f32[192,768]{1,0:T(8,128)} %constant_dynamic-slice_fusion.1), channel_id=1, source_target_pairs={{0,8},{4,12},{8,0},{12,4},{16,24},{20,28},{24,16},{28,20},{1,9},{5... | collective-permute-start | bytes 1769480 | tf_op jit(solution)/shard_map/ppermute | solution.py:139
  344.4 22.8 %copy-start.7 = (f32[384,768]{1,0:T(8,128)S(1)}, f32[384,768]{1,0:T(8,128)}, u32[]{:S(2)}) copy-start(f32[384,768]{1,0:T(8,128)} %copy-done.6) | copy-start | bytes 3538948
  357.2 13.3 %collective-permute-start.3 = (f32[96,768]{1,0:T(8,128)}, f32[96,768]{1,0:T(8,128)S(1)}, u32[]{:S(2)}, u32[]{:S(2)}) collective-permute-start(f32[96,768]{1,0:T(8,128)} %constant_dynamic-slice_fusion.3), channel_id=1, source_target_pairs={{0,16},{4,20},{8,24},{12,28},{16,0},{20,4},{24,8},{28,12},{1,17},{... | collective-permute-start | bytes 884744 | tf_op jit(solution)/shard_map/ppermute | solution.py:139
  369.0 8.4 %collective-permute-start.6 = (f32[96,768]{1,0:T(8,128)}, f32[96,768]{1,0:T(8,128)S(1)}, u32[]{:S(2)}, u32[]{:S(2)}) collective-permute-start(f32[96,768]{1,0:T(8,128)} %constant_dynamic-slice_fusion), channel_id=1, source_target_pairs={{0,16},{4,20},{8,24},{12,28},{16,0},{20,4},{24,8},{28,12},{1,17},{... | collective-permute-start | bytes 884744 | tf_op jit(solution)/shard_map/ppermute | solution.py:139
  386.2 1.1 copy-start.3
  390.5 18.4 %copy-start.30 = (bf16[512,768]{1,0:T(8,128)(2,1)S(1)}, bf16[512,768]{1,0:T(8,128)(2,1)}, u32[]{:S(2)}) copy-start(bf16[512,768]{1,0:T(8,128)(2,1)} %param.15) | copy-start | bytes 2359300
  414.4 90.2 %reduce-scatter.11.cloned.1.call-start = ((), (), s32[]{:S(2)}) async-start(), calls=%async_computation.9 | async-start | bytes 1966080 | tf_op jit(solution)/shard_map/reduce_scatter | solution.py:315
  418.1 2.4 collective-permute-start.7
  418.4 4.6 copy-start.22
  418.5 4.6 copy-start.13
  421.8 9.1 %collective-permute-start.8 = (bf16[192,768]{1,0:T(8,128)(2,1)S(1)}, bf16[192,768]{1,0:T(8,128)(2,1)S(1)}, u32[]{:S(2)}, u32[]{:S(2)}) collective-permute-start(bf16[192,768]{1,0:T(8,128)(2,1)S(1)} %dynamic-slice_convert_fusion.1), channel_id=1, source_target_pairs={{0,8},{4,12},{8,0},{12,4},{16,24},{20,28},{24,16},{28,20},{1,9},{5... | collective-permute-start | bytes 884744 | tf_op jit(solution)/shard_map/ppermute | solution.py:139
  423.0 9.3 %copy-start.21 = (f32[1,1,1,4,1,192]{5,3,1,4,2,0:T(4,128)S(1)}, f32[1,1,1,4,1,192]{5,3,1,4,2,0:T(4,128)}, u32[]{:S(2)}) copy-start(f32[1,1,1,4,1,192]{5,3,1,4,2,0:T(4,128)} %stack.26) | copy-start | bytes 9220
  423.0 9.4 %copy-start.16 = (bf16[96,768]{1,0:T(8,128)(2,1)S(1)}, bf16[96,768]{1,0:T(8,128)(2,1)}, u32[]{:S(2)}) copy-start(bf16[96,768]{1,0:T(8,128)(2,1)} %dynamic-slice_add_fusion.5) | copy-start | bytes 442372
  423.1 10.2 %copy-start.15 = (bf16[96,768]{1,0:T(8,128)(2,1)S(1)}, bf16[96,768]{1,0:T(8,128)(2,1)}, u32[]{:S(2)}) copy-start(bf16[96,768]{1,0:T(8,128)(2,1)} %dynamic-slice_add_fusion.4) | copy-start | bytes 442372
  431.0 6.8 %collective-permute-start.9 = (bf16[96,768]{1,0:T(8,128)(2,1)S(1)}, bf16[96,768]{1,0:T(8,128)(2,1)S(1)}, u32[]{:S(2)}, u32[]{:S(2)}) collective-permute-start(bf16[96,768]{1,0:T(8,128)(2,1)S(1)} %dynamic-slice_convert_fusion.2), channel_id=1, source_target_pairs={{0,16},{4,20},{8,24},{12,28},{16,0},{20,4},{24,8},{28,12},{1,17},{... | collective-permute-start | bytes 442376 | tf_op jit(solution)/shard_map/ppermute | solution.py:139
  432.4 36.6 %collective-permute-start.10 = (bf16[96,768]{1,0:T(8,128)(2,1)S(1)}, bf16[96,768]{1,0:T(8,128)(2,1)S(1)}, u32[]{:S(2)}, u32[]{:S(2)}) collective-permute-start(bf16[96,768]{1,0:T(8,128)(2,1)S(1)} %copy-done.16), channel_id=1, source_target_pairs={{0,16},{4,20},{8,24},{12,28},{16,0},{20,4},{24,8},{28,12},{1,17},{... | collective-permute-start | bytes 442376 | tf_op jit(solution)/shard_map/ppermute | solution.py:154
  433.3 37.4 %collective-permute-start.13 = (bf16[96,768]{1,0:T(8,128)(2,1)S(1)}, bf16[96,768]{1,0:T(8,128)(2,1)S(1)}, u32[]{:S(2)}, u32[]{:S(2)}) collective-permute-start(bf16[96,768]{1,0:T(8,128)(2,1)S(1)} %copy-done.15), channel_id=1, source_target_pairs={{0,16},{4,20},{8,24},{12,28},{16,0},{20,4},{24,8},{28,12},{1,17},{... | collective-permute-start | bytes 442376 | tf_op jit(solution)/shard_map/ppermute | solution.py:154
  469.0 68.6 %all-gather.14.cloned.1.call-start = ((), (), s32[]{:S(2)}) async-start(), calls=%async_computation.11 | async-start | bytes 3538944 | tf_op jit(solution)/shard_map/all_gather | solution.py:329
  469.1 9.9 %collective-permute-start.11 = (bf16[192,768]{1,0:T(8,128)(2,1)S(1)}, bf16[192,768]{1,0:T(8,128)(2,1)S(1)}, u32[]{:S(2)}, u32[]{:S(2)}) collective-permute-start(bf16[192,768]{1,0:T(8,128)(2,1)S(1)} %pad_maximum_fusion.3), channel_id=1, source_target_pairs={{0,8},{4,12},{8,0},{12,4},{16,24},{20,28},{24,16},{28,20},{1,9},{5... | collective-permute-start | bytes 884744 | tf_op jit(solution)/shard_map/ppermute | solution.py:154
  470.7 13.4 %collective-permute-start.14 = (bf16[192,768]{1,0:T(8,128)(2,1)S(1)}, bf16[192,768]{1,0:T(8,128)(2,1)S(1)}, u32[]{:S(2)}, u32[]{:S(2)}) collective-permute-start(bf16[192,768]{1,0:T(8,128)(2,1)S(1)} %pad_maximum_fusion.4), channel_id=1, source_target_pairs={{0,8},{4,12},{8,0},{12,4},{16,24},{20,28},{24,16},{28,20},{1,9},{5... | collective-permute-start | bytes 884744 | tf_op jit(solution)/shard_map/ppermute | solution.py:154
  479.2 5.1 collective-permute-start.12
  484.3 2.1 collective-permute-start.15
  486.6 18.1 %copy-start.14 = (bf16[3,512,768]{2,1,0:T(8,128)(2,1)S(1)}, bf16[3,512,768]{2,1,0:T(8,128)(2,1)}, u32[]{:S(2)}) copy-start(bf16[3,512,768]{2,1,0:T(8,128)(2,1)} %shard_map.255) | copy-start | bytes 7077892
  506.7 2.2 copy-start.4
  550.7 4.0 copy-start.1
Sparse Core Ops, SparseCore 0:
  10.2 56.3 all-gather.11
  106.3 62.2 all-gather.7
  181.0 59.0 reduce-scatter.4
  247.7 63.3 all-gather.9
  323.9 59.0 reduce-scatter.6
  414.5 51.5 reduce-scatter.8
  469.1 35.4 reduce-scatter.10
  506.5 31.0 all-gather.13

commit v9 on v8

--- a/solution.py
+++ b/solution.py
@@ -77,46 +77,46 @@
         ).astype(out_ref.dtype)
 
 
-def _row_block(pair):
-    return pl.BlockSpec((LEN, pair * HD), lambda p, i, n: (p, i))
-
-
-def attention_forward(queries, keys, values, lengths, factor, pair=2):
-    rows, width = queries.shape
-    grid = (rows // LEN, width // (pair * HD))
+def _group_block(shard):
+    return pl.BlockSpec((None, LEN, shard), lambda p, g, n: (g, p, 0))
+
+
+def attention_forward(queries, keys, values, lengths, factor):
+    groups, rows, shard = queries.shape
+    grid = (rows // LEN, groups)
     return pl.pallas_call(
-        functools.partial(_fwd_kernel, heads=pair, factor=factor),
-        out_shape=jax.ShapeDtypeStruct((rows, width), jnp.bfloat16),
+        functools.partial(_fwd_kernel, heads=shard // HD, factor=factor),
+        out_shape=jax.ShapeDtypeStruct((groups, rows, shard), jnp.bfloat16),
         grid_spec=pltpu.PrefetchScalarGridSpec(
             num_scalar_prefetch=1,
             grid=grid,
-            in_specs=[_row_block(pair)] * 3,
-            out_specs=_row_block(pair),
+            in_specs=[_group_block(shard)] * 3,
+            out_specs=_group_block(shard),
         ),
         cost_estimate=pl.CostEstimate(
-            flops=4 * rows * LEN * width,
-            transcendentals=rows * LEN * width // HD,
-            bytes_accessed=4 * rows * width * 2,
+            flops=4 * rows * LEN * groups * shard,
+            transcendentals=rows * LEN * groups * shard // HD,
+            bytes_accessed=4 * rows * groups * shard * 2,
         ),
     )(lengths, queries, keys, values)
 
 
-def attention_backward(queries, keys, values, context_grad, lengths, factor, pair=2):
-    rows, width = queries.shape
-    grid = (rows // LEN, width // (pair * HD))
+def attention_backward(queries, keys, values, context_grad, lengths, factor):
+    groups, rows, shard = queries.shape
+    grid = (rows // LEN, groups)
     return pl.pallas_call(
-        functools.partial(_bwd_kernel, heads=pair, factor=factor),
-        out_shape=jax.ShapeDtypeStruct((3, rows, width), jnp.bfloat16),
+        functools.partial(_bwd_kernel, heads=shard // HD, factor=factor),
+        out_shape=jax.ShapeDtypeStruct((3, groups, rows, shard), jnp.bfloat16),
         grid_spec=pltpu.PrefetchScalarGridSpec(
             num_scalar_prefetch=1,
             grid=grid,
-            in_specs=[_row_block(pair)] * 4,
-            out_specs=pl.BlockSpec((3, LEN, pair * HD), lambda p, i, n: (0, p, i)),
+            in_specs=[_group_block(shard)] * 4,
+            out_specs=pl.BlockSpec((3, None, LEN, shard), lambda p, g, n: (0, g, p, 0)),
         ),
         cost_estimate=pl.CostEstimate(
-            flops=10 * rows * LEN * width,
-            transcendentals=rows * LEN * width // HD,
-            bytes_accessed=7 * rows * width * 2,
+            flops=10 * rows * LEN * groups * shard,
+            transcendentals=rows * LEN * groups * shard // HD,
+            bytes_accessed=7 * rows * groups * shard * 2,
         ),
     )(lengths, queries, keys, values, context_grad)
 
@@ -194,30 +194,32 @@
         dp_index = lax.axis_index("dp")
         parity = dp_index % 2
         mine = jnp.where(parity == 0, first_half, second_half)
-        mine = lax.all_gather(mine, "tensor", axis=1, tiled=False).reshape(half_rows, width)
+        mine = lax.all_gather(mine, "tensor", axis=0, tiled=False)
         other = lax.ppermute(mine, "dp", [(i, i ^ 1) for i in range(dp_size)])
         first_half = jnp.where(parity == 0, mine, other)
         second_half = jnp.where(parity == 0, other, mine)
-        query_weight = first_half[:width]
-        key_weight = first_half[width : 2 * width]
-        query_bias = first_half[2 * width]
-        value_bias = first_half[2 * width + 1]
-        value_weight = second_half[:width]
-        proj_t = second_half[width : 2 * width]
+        query_weight = first_half[:, :width]
+        key_weight = first_half[:, width : 2 * width]
+        query_bias = first_half[:, 2 * width]
+        value_bias = first_half[:, 2 * width + 1]
+        value_weight = second_half[:, :width]
+        proj_blocks = second_half[:, width : 2 * width]
 
         tensor_index = lax.axis_index("tensor")
         own_lengths = lax.dynamic_slice_in_dim(lengths, tensor_index * passages, passages)
 
         own_tokens = tokens.astype(jnp.float32)
         def project(weight, bias=None):
-            out = jnp.dot(tokens, weight, preferred_element_type=jnp.float32)
-            return (out if bias is None else out + bias).astype(jnp.bfloat16)
+            out = jnp.einsum("rd,gdj->grj", tokens, weight, preferred_element_type=jnp.float32)
+            return (out if bias is None else out + bias[:, None, :]).astype(jnp.bfloat16)
 
         query_low = project(query_weight, query_bias)
         key_low = project(key_weight)
         value_low = project(value_weight, value_bias)
         context_low = attention_forward(query_low, key_low, value_low, own_lengths, factor)
-        attn_out = contract(context_low, proj_t, 1, 1)
+        attn_out = jnp.einsum(
+            "grj,gcj->rc", context_low, proj_blocks, preferred_element_type=jnp.float32
+        )
         middle, norm1_back = jax.vjp(
             layer_norm, own_tokens + attn_out + out_bias, norm1_gain, norm1_shift
         )
@@ -260,10 +262,12 @@
         first_grad, grad_norm1_gain, grad_norm1_shift = norm1_back(norm1_in)
         attn_grad = first_grad.astype(jnp.bfloat16)
         grad_out_bias = jnp.sum(attn_grad, axis=0, dtype=jnp.float32)
-        context_grad = jnp.dot(attn_grad, proj_t, preferred_element_type=jnp.float32).astype(
-            jnp.bfloat16
-        )
-        early = contract(attn_grad, context_low, 0, 0)
+        context_grad = jnp.einsum(
+            "rc,gcj->grj", attn_grad, proj_blocks, preferred_element_type=jnp.float32
+        ).astype(jnp.bfloat16)
+        early = jnp.einsum(
+            "rc,grj->cgj", attn_grad, context_low, preferred_element_type=jnp.float32
+        ).reshape(width, width)
         early_halved = dp_pow2(early, dp_size)
         if early_halved:
             early = dp_halve(early.astype(jnp.bfloat16), dp_size, jnp.float32)
@@ -272,14 +276,16 @@
         proj_grad = attention_backward(
             query_low, key_low, value_low, context_grad, own_lengths, factor
         )
-        grad_bias_full = jnp.sum(proj_grad[0::2], axis=1, dtype=jnp.float32)
+        grad_bias_full = jnp.sum(proj_grad[0::2], axis=2, dtype=jnp.float32).reshape(2, width)
         grad_qkv_full = jnp.einsum(
-            "rd,tre->tde", tokens, proj_grad, preferred_element_type=jnp.float32
+            "rd,kgrj->kdgj", tokens, proj_grad, preferred_element_type=jnp.float32
         )
         input_part = (
-            contract(proj_grad[0], query_weight, 1, 1)
-            + contract(proj_grad[1], key_weight, 1, 1)
-            + contract(proj_grad[2], value_weight, 1, 1)
+            jnp.einsum("grj,gdj->rd", proj_grad[0], query_weight, preferred_element_type=jnp.float32)
+            + jnp.einsum("grj,gdj->rd", proj_grad[1], key_weight, preferred_element_type=jnp.float32)
+            + jnp.einsum(
+                "grj,gdj->rd", proj_grad[2], value_weight, preferred_element_type=jnp.float32
+            )
         )
         input_grad = (first_grad + input_part).astype(jnp.bfloat16)
 

time: 563 us -> 584 us (1.037); the launches traced: 562 us -> 575 us
  local copies, waits for them, and re-layouts: 42.2 us -> 60.8 us
  waiting for transfers between devices: 375 us -> 367 us
    convert_element_type x0 -> x4, local copies, waits for them, and re-layouts: none -> 19.8 us  [the longest x2 17 us: per_device(): grad_qkv_full.reshape(3 * width, width).astype(jnp.bfloat16)]
    dot_general x5 -> x9, matrix products: 14 us -> 25.8 us  [the longest x3 7.37 us: project(): jnp.einsum('rd,gdj->grj', tokens, weight, preferred_element_type=jnp.floa...]
    dot_general x9 -> x4, matrix products: 31.3 us -> 19.4 us  [contract(): lax.dot_general(left, right, (((left_dim,), (right_dim,)), ((), ())), pre...]
    reduce_scatter x1, waiting for transfers between devices: 28.3 us -> 19.3 us  [per_device(): lax.psum_scatter(grad_qkv_full.reshape(3 * width, width).astype(jnp.bfloa...]
    unnamed x80 -> x86, local copies, waits for them, and re-layouts: 11 us -> 15.8 us
  transfers between devices with their start and end apart: 24 -> 24, of which waited for: 19 -> 19; matrix products, arithmetic and copies ran while one was open for 7% -> 8% of each run, Pallas kernels for 0% -> 0%
where the time goes in v9:
time: 584 us; the launch traced here: 575 us
  waiting for transfers between devices  367 us (63%)
  local copies, waits for them, and re-layouts  60.8 us (10%)
  matrix products  56.8 us (10%)
  other arithmetic  33 us (6%)
  Pallas kernels  28.2 us (5%)
  between operations  15.3 us (3%)
  starting transfers between devices  13.8 us (2%)
    all_gather x1, waiting for transfers between devices, per_device(): branch_rows = lax.all_gather(branch_grad, 'tensor', axis=0, tiled=True)  63.3 us
    all_gather x1, waiting for transfers between devices, per_device(): ffn_rows = lax.all_gather(middle_low, 'tensor', axis=0, tiled=True)  62.3 us
    reduce_scatter x1, waiting for transfers between devices, per_device(): lax.psum_scatter(jnp.dot(hidden, down_weight, preferred_element_type=jnp....  59.2 us
    all_gather x1, waiting for transfers between devices, per_device(): mine = lax.all_gather(mine, 'tensor', axis=0, tiled=False)  56.5 us
    ppermute x9, waiting for transfers between devices, dp_halve(): got = lax.ppermute(give, 'dp', [(i, i ^ 1 << step) for i in range(dp_size)])  44.5 us
    all_gather x1, waiting for transfers between devices, per_device(): joined = lax.all_gather(joined, 'dp', axis=0, tiled=False)  24.9 us
    dot_general x4, matrix products, contract(): lax.dot_general(left, right, (((left_dim,), (right_dim,)), ((), ())), pre...  19.4 us
    reduce_scatter x1, waiting for transfers between devices, per_device(): lax.psum_scatter(grad_qkv_full.reshape(3 * width, width).astype(jnp.bfloa...  19.3 us
  transfers between devices with their start and end apart: 24, of which 19 were waited for; matrix products, arithmetic and copies ran while one was open for 8% of the time, Pallas kernels for 0%

profile of v9, /device:TPU:0, one launch (start us, length us, event | category | flops | bytes accessed | tf_op | source)
XLA Modules:
  0.0 574.5 jit_solution(3925481017786287719)
XLA Ops:
  8.2 1.2 slice_bitcast_fusion.8
  10.5 56.5 %all-gather.13.cloned.1.call-done = bf16[4,1544,192]{1,2,0:T(8,128)(2,1)} async-done(((bf16[1,1544,192]{1,2,0:T(8,128)(2,1)}), bf16[4,1544,192]{1,2,0:T(8,128)(2,1)}) %all-gather.13.cloned.1.call-update) | async-done | bytes 2371600 | tf_op jit(solution)/shard_map/all_gather | solution.py:197
  67.6 4.6 collective-permute-done
  72.2 4.4 broadcast_select_fusion
  78.8 1.3 copy.119
  80.1 3.2 fusion.13.q_ref
  83.4 3.3 fusion.14.v_ref
  86.7 10.8 %shard_map.254 = bf16[4,512,192]{2,1,0:T(8,128)(2,1)} custom-call(s32[1]{0:T(128)} %dynamic_slice.57.len_ref, bf16[4,512,192]{2,1,0:T(8,128)(2,1)} %fusion.13.q_ref, bf16[4,512,192]{2,1,0:T(8,128)(2,1)} %bitcast.112, bf16[4,512,192]{2,1,0:T(8,128)(2,1)} %fusion.14.v_ref), custom_call_target="tpu_custom_call" | custom-call | flops 805306368 | bytes 3145728 | tf_op jit(solution)/shard_map/pallas_call | solution.py:87
  97.5 2.7 fusion.51
  101.0 1.2 fusion.15
  102.3 62.3 %all-gather.9.cloned.1.call-done = bf16[2048,768]{1,0:T(8,128)(2,1)} async-done(((bf16[512,768]{1,0:T(8,128)(2,1)}), bf16[2048,768]{1,0:T(8,128)(2,1)}) %all-gather.9.cloned.1.call-update) | async-done | bytes 3145744 | tf_op jit(solution)/shard_map/all_gather | solution.py:227
  164.6 6.8 %multiply_convert_fusion = (bf16[2048,768]{1,0:T(8,128)(2,1)S(1)}, f32[2048,768]{1,0:T(8,128)}) fusion(f32[768]{0:T(1024)S(1)} %convert_element_type.142, bf16[2048,768]{1,0:T(8,128)(2,1)} %all-gather.9.cloned.1.call-done, bf16[768,768]{1,0:T(8,128)(2,1)S(1)} %copy-done), kind=kOutput, calls=%fused_computation.8 | convolution fusion | flops 2425356288 | bytes 13765632 | tf_op jit(solution)/shard_map/dot_general | solution.py:228
  171.4 1.7 copy-done.35
  173.1 4.0 convolution_convert_fusion.1
  177.1 59.2 %reduce-scatter.5.cloned.1.call-done = bf16[512,768]{1,0:T(8,128)(2,1)} async-done(((bf16[2048,768]{1,0:T(8,128)(2,1)}), bf16[512,768]{1,0:T(8,128)(2,1)}) %reduce-scatter.5.cloned.1.call-update) | async-done | bytes 786448 | tf_op jit(solution)/shard_map/reduce_scatter | solution.py:231
  236.3 1.7 fusion.49
  239.9 1.6 fusion.48
  244.0 63.3 %all-gather.11.cloned.1.call-done = bf16[2048,768]{1,0:T(8,128)(2,1)} async-done(((bf16[512,768]{1,0:T(8,128)(2,1)}), bf16[2048,768]{1,0:T(8,128)(2,1)}) %all-gather.11.cloned.1.call-update) | async-done | bytes 3145744 | tf_op jit(solution)/shard_map/all_gather | solution.py:243
  307.2 7.0 %convert_reduce_fusion = (f32[768]{0:T(1024)S(1)}, bf16[2048,768]{1,0:T(8,128)(2,1)S(1)}) fusion(f32[2048,768]{1,0:T(8,128)} %get-tuple-element.150, f32[768]{0:T(1024)S(1)} %convert_element_type.142, bf16[2048,768]{1,0:T(8,128)(2,1)} %all-gather.11.cloned.1.call-done, bf16[768,768]{1,0:T(8,128)(2,1)} %param.26), kind=kOutput, calls=%fused_computation.7 | convolution fusion | flops 2436365568 | bytes 13768704 | tf_op jit(solution)/shard_map/dot_general | solution.py:31
  314.2 1.7 copy-done.36
  315.9 4.0 convolution_convert_fusion
  320.0 5.7 fusion.53
  325.7 2.7 fusion.52
  328.5 1.3 constant_dynamic-slice_fusion.4
  330.8 2.5 collective-permute-done.4
  333.3 1.8 dynamic-slice_add_fusion
  335.1 1.5 collective-permute-start.5
  336.7 1.5 dynamic-slice_add_fusion.1
  340.5 11.0 %collective-permute-done.5 = f32[192,768]{1,0:T(8,128)} collective-permute-done((f32[192,768]{1,0:T(8,128)S(1)}, f32[192,768]{1,0:T(8,128)}, u32[]{:S(2)}, u32[]{:S(2)}) %collective-permute-start.5) | collective-permute-done | bytes 589856 | tf_op jit(solution)/shard_map/ppermute | solution.py:139
  353.4 1.5 collective-permute-start.6
  354.8 8.5 %collective-permute-done.2 = f32[192,768]{1,0:T(8,128)} collective-permute-done((f32[192,768]{1,0:T(8,128)}, f32[192,768]{1,0:T(8,128)}, u32[]{:S(2)}, u32[]{:S(2)}) %collective-permute-start.2) | collective-permute-done | bytes 589856 | tf_op jit(solution)/shard_map/ppermute | solution.py:139
  365.2 1.5 collective-permute-start.3
  367.3 6.2 %collective-permute-done.3 = f32[96,768]{1,0:T(8,128)S(1)} collective-permute-done((f32[96,768]{1,0:T(8,128)}, f32[96,768]{1,0:T(8,128)S(1)}, u32[]{:S(2)}, u32[]{:S(2)}) %collective-permute-start.3) | collective-permute-done | bytes 294944 | tf_op jit(solution)/shard_map/ppermute | solution.py:139
  374.3 4.9 reduce-scatter.7.cloned.1.call-done
  379.1 1.9 convert_add_fusion
  383.7 2.1 convolution_convert_fusion.2
  385.8 1.5 copy.122
  387.3 17.4 %shard_map.255 = bf16[3,4,512,192]{3,2,1,0:T(8,128)(2,1)} custom-call(s32[1]{0:T(128)} %dynamic_slice.57.len_ref, bf16[4,512,192]{2,1,0:T(8,128)(2,1)} %fusion.13.q_ref, bf16[4,512,192]{2,1,0:T(8,128)(2,1)} %bitcast.113, bf16[4,512,192]{2,1,0:T(8,128)(2,1)} %fusion.14.v_ref, bf16[4,512,192]{2,1,0:T(8,128)(2,1)} %bitcast.114), custom_call_target="tpu_custom_call" | custom-call | flops 2013265920 | bytes 5505024 | tf_op jit(solution)/shard_map/pallas_call | solution.py:107
  404.7 5.7 convert_bitcast_fusion
  410.4 8.1 %copy.127 = bf16[3,768,4,192]{3,2,1,0:T(4,128)(2,1)} copy(bf16[3,768,4,192]{1,3,2,0:T(8,128)(2,1)} %convert_bitcast_fusion) | data formatting | bytes 7077888 | tf_op jit(solution)/shard_map/convert_element_type | solution.py:315
  418.4 8.9 %convert_element_type.158 = bf16[2304,768]{1,0:T(8,128)(2,1)} reshape(bf16[3,768,4,192]{3,2,1,0:T(4,128)(2,1)} %copy.127) | data formatting | bytes 7077888 | tf_op jit(solution)/shard_map/convert_element_type | solution.py:315
  432.1 1.5 collective-permute-start.10
  437.7 1.8 collective-permute-done.7
  440.8 1.6 collective-permute-start.8
  442.7 7.2 %collective-permute-done.8 = bf16[192,768]{1,0:T(8,128)(2,1)S(1)} collective-permute-done((bf16[192,768]{1,0:T(8,128)(2,1)S(1)}, bf16[192,768]{1,0:T(8,128)(2,1)S(1)}, u32[]{:S(2)}, u32[]{:S(2)}) %collective-permute-start.8) | collective-permute-done | bytes 294944 | tf_op jit(solution)/shard_map/ppermute | solution.py:139
  450.0 1.6 collective-permute-start.9
  451.9 7.4 %collective-permute-done.9 = bf16[96,768]{1,0:T(8,128)(2,1)S(1)} collective-permute-done((bf16[96,768]{1,0:T(8,128)(2,1)S(1)}, bf16[96,768]{1,0:T(8,128)(2,1)S(1)}, u32[]{:S(2)}, u32[]{:S(2)}) %collective-permute-start.9) | collective-permute-done | bytes 147488 | tf_op jit(solution)/shard_map/ppermute | solution.py:139
  459.3 19.3 %reduce-scatter.9.cloned.1.call-done = bf16[288,768]{1,0:T(8,128)(2,1)} async-done(((bf16[2304,768]{1,0:T(8,128)(2,1)}), bf16[288,768]{1,0:T(8,128)(2,1)}) %reduce-scatter.9.cloned.1.call-update) | async-done | bytes 442384 | tf_op jit(solution)/shard_map/reduce_scatter | solution.py:314
  479.7 1.7 copy.131
  482.8 1.5 collective-permute-start.14
  486.0 6.8 %collective-permute-done.14 = bf16[192,768]{1,0:T(8,128)(2,1)S(1)} collective-permute-done((bf16[192,768]{1,0:T(8,128)(2,1)S(1)}, bf16[192,768]{1,0:T(8,128)(2,1)S(1)}, u32[]{:S(2)}, u32[]{:S(2)}) %collective-permute-start.14) | collective-permute-done | bytes 294944 | tf_op jit(solution)/shard_map/ppermute | solution.py:154
  493.0 4.8 collective-permute-done.11
  498.3 1.6 maximum_convert_fusion.1
  500.2 1.6 maximum_convert_fusion
  501.8 15.3 %reduce-scatter.11.cloned.1.call-done = f32[1,416,192]{1,2,0:T(8,128)} async-done(((f32[4,416,192]{1,2,0:T(8,128)}), f32[1,416,192]{1,2,0:T(8,128)}) %reduce-scatter.11.cloned.1.call-update) | async-done | bytes 319504 | tf_op jit(solution)/shard_map/reduce_scatter | solution.py:321
  517.1 2.6 fusion.21
  519.7 2.2 fusion.22
  521.9 3.1 fusion.11
  525.1 24.9 %all-gather.15.cloned.1.call-done = f32[8,416,192]{1,2,0:T(8,128)} async-done(((f32[1,416,192]{1,2,0:T(8,128)}), f32[8,416,192]{1,2,0:T(8,128)}) %all-gather.15.cloned.1.call-update) | async-done | bytes 2555920 | tf_op jit(solution)/shard_map/all_gather | solution.py:335
  550.0 1.2 slice_reduce_fusion
  557.4 3.3 slice.155
  560.7 2.2 copy.132
  562.9 1.8 copy.140
  564.7 1.5 slice_bitcast_fusion.9
  (197 shorter events, 44.4 us)
Async XLA Ops:
  7.2 157.4 %copy-start = (bf16[768,768]{1,0:T(8,128)(2,1)S(1)}, bf16[768,768]{1,0:T(8,128)(2,1)}, u32[]{:S(2)}) copy-start(bf16[768,768]{1,0:T(8,128)(2,1)} %param.24) | copy-start | bytes 3538948
  7.2 2.2 copy-start.15
  7.2 59.8 %all-gather.13.cloned.1.call-start = ((), (), s32[]{:S(2)}) async-start(), calls=%async_computation.10 | async-start | bytes 3194880 | tf_op jit(solution)/shard_map/all_gather | solution.py:197
  9.4 57.6 %copy-start.34 = (s32[4]{0:T(128)S(1)}, s32[4]{0:T(128)}, u32[]{:S(2)}) copy-start(s32[4]{0:T(128)} %param.17) | copy-start | bytes 52
  10.4 154.1 %all-gather.9.cloned.1.call-start = ((), (), s32[]{:S(2)}) async-start(), calls=%async_computation.4 | async-start | bytes 3932160 | tf_op jit(solution)/shard_map/all_gather | solution.py:227
  67.0 5.2 collective-permute-start
  67.6 10.4 %copy-start.31 = (bf16[512,768]{1,0:T(8,128)(2,1)S(1)}, bf16[512,768]{1,0:T(8,128)(2,1)}, u32[]{:S(2)}) copy-start(bf16[512,768]{1,0:T(8,128)(2,1)} %param.15) | copy-start | bytes 2359300
  76.6 1.4 copy-start.7
  86.7 10.8 %copy-start.33 = (f32[768]{0:T(1024)S(1)}, f32[768]{0:T(1024)}, u32[]{:S(2)}) copy-start(f32[768]{0:T(1024)} %param.21) | copy-start | bytes 9220
  100.3 0.7 copy-start.16
  100.3 0.7 copy-start.17
  101.0 1.3 copy-start.28
  102.2 134.1 %reduce-scatter.5.cloned.1.call-start = ((), (), s32[]{:S(2)}) async-start(), calls=%async_computation.5 | async-start | bytes 3932160 | tf_op jit(solution)/shard_map/reduce_scatter | solution.py:231
  164.6 8.5 %copy-start.30 = (bf16[768,768]{1,0:T(8,128)(2,1)S(1)}, bf16[768,768]{1,0:T(8,128)(2,1)}, u32[]{:S(2)}) copy-start(bf16[768,768]{1,0:T(8,128)(2,1)} %param.26) | copy-start | bytes 3538948
  171.4 1.7 copy-start.35
  177.0 59.2 %copy-start.26 = (f32[768]{0:T(1024)S(1)}, f32[768]{0:T(1024)}, u32[]{:S(2)}) copy-start(f32[768]{0:T(1024)} %param.27) | copy-start | bytes 9220
  177.1 130.2 %all-gather.11.cloned.1.call-start = ((), (), s32[]{:S(2)}) async-start(), calls=%async_computation.6 | async-start | bytes 3932160 | tf_op jit(solution)/shard_map/all_gather | solution.py:243
  238.0 1.1 copy-start.8
  238.0 1.1 copy-start.18
  238.4 1.5 copy-start.27
  241.5 1.1 copy-start.2
  243.7 135.4 %reduce-scatter.7.cloned.1.call-start = ((), (), s32[]{:S(2)}) async-start(), calls=%async_computation.7 | async-start | bytes 3932160 | tf_op jit(solution)/shard_map/reduce_scatter | solution.py:255
  314.2 1.7 copy-start.36
  319.9 158.6 %reduce-scatter.9.cloned.1.call-start = ((), (), s32[]{:S(2)}) async-start(), calls=%async_computation.8 | async-start | bytes 3981312 | tf_op jit(solution)/shard_map/reduce_scatter | solution.py:314
  320.0 5.7 copy-start.29
  320.0 5.7 copy-start.37
  325.7 2.8 copy-start.11
  328.5 1.8 copy-start.9
  330.3 3.0 collective-permute-start.4
  330.3 6.3 %collective-permute-start.1 = (f32[384,768]{1,0:T(8,128)}, f32[384,768]{1,0:T(8,128)}, u32[]{:S(2)}, u32[]{:S(2)}) collective-permute-start(f32[384,768]{1,0:T(8,128)} %get-tuple-element.154), channel_id=1, source_target_pairs={{0,4},{4,0},{8,12},{12,8},{16,20},{20,16},{24,28},{28,24},{1,5},{5... | collective-permute-start | bytes 3538952 | tf_op jit(solution)/shard_map/ppermute | solution.py:139
  330.8 5.8 %copy-start.10 = (f32[768,768]{1,0:T(8,128)S(1)}, f32[768,768]{1,0:T(8,128)}, u32[]{:S(2)}) copy-start(f32[768,768]{1,0:T(8,128)} %copy-done.9) | copy-start | bytes 7077892
  335.1 16.4 %collective-permute-start.5 = (f32[192,768]{1,0:T(8,128)S(1)}, f32[192,768]{1,0:T(8,128)}, u32[]{:S(2)}, u32[]{:S(2)}) collective-permute-start(f32[192,768]{1,0:T(8,128)S(1)} %constant_dynamic-slice_fusion.3), channel_id=1, source_target_pairs={{0,8},{4,12},{8,0},{12,4},{16,24},{20,28},{24,16},{28,20},{1,9},{5... | collective-permute-start | bytes 1769480 | tf_op jit(solution)/shard_map/ppermute | solution.py:139
  338.1 1.0 copy-start.5
  340.0 23.3 %collective-permute-start.2 = (f32[192,768]{1,0:T(8,128)}, f32[192,768]{1,0:T(8,128)}, u32[]{:S(2)}, u32[]{:S(2)}) collective-permute-start(f32[192,768]{1,0:T(8,128)} %constant_dynamic-slice_fusion.6), channel_id=1, source_target_pairs={{0,8},{4,12},{8,0},{12,4},{16,24},{20,28},{24,16},{28,20},{1,9},{5... | collective-permute-start | bytes 1769480 | tf_op jit(solution)/shard_map/ppermute | solution.py:139
  340.5 22.8 %copy-start.6 = (f32[384,768]{1,0:T(8,128)S(1)}, f32[384,768]{1,0:T(8,128)}, u32[]{:S(2)}) copy-start(f32[384,768]{1,0:T(8,128)} %copy-done.5) | copy-start | bytes 3538948
  353.4 13.3 %collective-permute-start.6 = (f32[96,768]{1,0:T(8,128)}, f32[96,768]{1,0:T(8,128)S(1)}, u32[]{:S(2)}, u32[]{:S(2)}) collective-permute-start(f32[96,768]{1,0:T(8,128)} %constant_dynamic-slice_fusion.2), channel_id=1, source_target_pairs={{0,16},{4,20},{8,24},{12,28},{16,0},{20,4},{24,8},{28,12},{1,17},{... | collective-permute-start | bytes 884744 | tf_op jit(solution)/shard_map/ppermute | solution.py:139
  365.2 8.4 %collective-permute-start.3 = (f32[96,768]{1,0:T(8,128)}, f32[96,768]{1,0:T(8,128)S(1)}, u32[]{:S(2)}, u32[]{:S(2)}) collective-permute-start(f32[96,768]{1,0:T(8,128)} %constant_dynamic-slice_fusion.5), channel_id=1, source_target_pairs={{0,16},{4,20},{8,24},{12,28},{16,0},{20,4},{24,8},{28,12},{1,17},{... | collective-permute-start | bytes 884744 | tf_op jit(solution)/shard_map/ppermute | solution.py:139
  382.3 1.1 copy-start.3
  382.4 1.3 copy-start.24
  387.3 17.4 %copy-start.32 = (bf16[512,768]{1,0:T(8,128)(2,1)S(1)}, bf16[512,768]{1,0:T(8,128)(2,1)}, u32[]{:S(2)}) copy-start(bf16[512,768]{1,0:T(8,128)(2,1)} %param.15) | copy-start | bytes 2359300
  427.4 1.2 copy-start.14
  427.4 89.6 %reduce-scatter.11.cloned.1.call-start = ((), (), s32[]{:S(2)}) async-start(), calls=%async_computation.9 | async-start | bytes 1966080 | tf_op jit(solution)/shard_map/reduce_scatter | solution.py:321
  432.1 52.3 %collective-permute-start.10 = (bf16[96,768]{1,0:T(8,128)(2,1)}, bf16[96,768]{1,0:T(8,128)(2,1)}, u32[]{:S(2)}, u32[]{:S(2)}) collective-permute-start(bf16[96,768]{1,0:T(8,128)(2,1)} %dynamic-slice_add_fusion.5), channel_id=1, source_target_pairs={{0,16},{4,20},{8,24},{12,28},{16,0},{20,4},{24,8},{28,12},{1,17},{... | collective-permute-start | bytes 442376 | tf_op jit(solution)/shard_map/ppermute | solution.py:154
  433.5 48.2 %collective-permute-start.13 = (bf16[96,768]{1,0:T(8,128)(2,1)}, bf16[96,768]{1,0:T(8,128)(2,1)}, u32[]{:S(2)}, u32[]{:S(2)}) collective-permute-start(bf16[96,768]{1,0:T(8,128)(2,1)} %dynamic-slice_add_fusion.4), channel_id=1, source_target_pairs={{0,16},{4,20},{8,24},{12,28},{16,0},{20,4},{24,8},{28,12},{1,17},{... | collective-permute-start | bytes 442376 | tf_op jit(solution)/shard_map/ppermute | solution.py:154
  436.9 2.7 collective-permute-start.7
  436.9 0.7 copy-start.23
  437.0 0.7 copy-start.21
  437.0 0.7 copy-start.22
  437.0 0.7 copy-start.20
  437.7 4.7 copy-start.19
  437.7 4.7 copy-start.12
  440.8 9.1 %collective-permute-start.8 = (bf16[192,768]{1,0:T(8,128)(2,1)S(1)}, bf16[192,768]{1,0:T(8,128)(2,1)S(1)}, u32[]{:S(2)}, u32[]{:S(2)}) collective-permute-start(bf16[192,768]{1,0:T(8,128)(2,1)S(1)} %dynamic-slice_convert_fusion), channel_id=1, source_target_pairs={{0,8},{4,12},{8,0},{12,4},{16,24},{20,28},{24,16},{28,20},{1,9},{5... | collective-permute-start | bytes 884744 | tf_op jit(solution)/shard_map/ppermute | solution.py:139
  450.0 9.3 %collective-permute-start.9 = (bf16[96,768]{1,0:T(8,128)(2,1)S(1)}, bf16[96,768]{1,0:T(8,128)(2,1)S(1)}, u32[]{:S(2)}, u32[]{:S(2)}) collective-permute-start(bf16[96,768]{1,0:T(8,128)(2,1)S(1)} %dynamic-slice_convert_fusion.1), channel_id=1, source_target_pairs={{0,16},{4,20},{8,24},{12,28},{16,0},{20,4},{24,8},{28,12},{1,17},{... | collective-permute-start | bytes 442376 | tf_op jit(solution)/shard_map/ppermute | solution.py:139
  481.5 68.5 %all-gather.15.cloned.1.call-start = ((), (), s32[]{:S(2)}) async-start(), calls=%async_computation.11 | async-start | bytes 3538944 | tf_op jit(solution)/shard_map/all_gather | solution.py:335
  482.8 9.9 %collective-permute-start.14 = (bf16[192,768]{1,0:T(8,128)(2,1)S(1)}, bf16[192,768]{1,0:T(8,128)(2,1)S(1)}, u32[]{:S(2)}, u32[]{:S(2)}) collective-permute-start(bf16[192,768]{1,0:T(8,128)(2,1)S(1)} %pad_maximum_fusion.4), channel_id=1, source_target_pairs={{0,8},{4,12},{8,0},{12,4},{16,24},{20,28},{24,16},{28,20},{1,9},{5... | collective-permute-start | bytes 884744 | tf_op jit(solution)/shard_map/ppermute | solution.py:154
  485.4 12.4 %collective-permute-start.11 = (bf16[192,768]{1,0:T(8,128)(2,1)S(1)}, bf16[192,768]{1,0:T(8,128)(2,1)S(1)}, u32[]{:S(2)}, u32[]{:S(2)}) collective-permute-start(bf16[192,768]{1,0:T(8,128)(2,1)S(1)} %pad_maximum_fusion.3), channel_id=1, source_target_pairs={{0,8},{4,12},{8,0},{12,4},{16,24},{20,28},{24,16},{28,20},{1,9},{5... | collective-permute-start | bytes 884744 | tf_op jit(solution)/shard_map/ppermute | solution.py:154
  492.9 5.1 collective-permute-start.15
  497.9 2.1 collective-permute-start.12
  517.1 2.6 copy-start.13
  519.7 2.3 copy-start.4
  519.7 2.2 copy-start.25
  562.9 4.4 copy-start.1
Sparse Core Ops, SparseCore 0:
  10.6 56.3 all-gather.12
  102.3 62.2 all-gather.8
  177.2 59.0 reduce-scatter.4
  243.9 63.3 all-gather.10
  320.0 59.0 reduce-scatter.6
  427.5 50.9 reduce-scatter.8
  481.6 35.4 reduce-scatter.10
  518.9 31.0 all-gather.14

commit v10 on v9

--- a/solution.py
+++ b/solution.py
@@ -53,28 +53,38 @@
         ).astype(out_ref.dtype)
 
 
-def _bwd_kernel(len_ref, q_ref, k_ref, v_ref, grad_ref, out_ref, *, heads, factor):
+def _bwd_kernel(len_ref, q_ref, k_ref, v_ref, grad_ref, out_ref, *, factor):
     length = len_ref[pl.program_id(0)]
-    for h in range(heads):
-        cols = slice(h * HD, (h + 1) * HD)
-        q = q_ref[:, cols]
-        k = k_ref[:, cols]
-        v = v_ref[:, cols]
-        g = grad_ref[:, cols]
-        probs = _probs(q, k, length, factor)
-        prob_grad = lax.dot_general(g, v, (((1,), (1,)), ((), ())), preferred_element_type=jnp.float32)
-        row_dot = jnp.sum(prob_grad * probs, axis=1, keepdims=True)
-        score_grad = (probs * (prob_grad - row_dot)).astype(jnp.bfloat16)
-        out_ref[0, :, cols] = (
-            jnp.dot(score_grad, k, preferred_element_type=jnp.float32) * factor
-        ).astype(out_ref.dtype)
-        out_ref[1, :, cols] = (
-            lax.dot_general(score_grad, q, (((0,), (0,)), ((), ())), preferred_element_type=jnp.float32)
-            * factor
-        ).astype(out_ref.dtype)
-        out_ref[2, :, cols] = lax.dot_general(
-            probs.astype(jnp.bfloat16), g, (((0,), (0,)), ((), ())), preferred_element_type=jnp.float32
-        ).astype(out_ref.dtype)
+    groups, _, shard = q_ref.shape
+    for group in range(groups):
+        for h in range(shard // HD):
+            cols = slice(h * HD, (h + 1) * HD)
+            wide = slice(group * shard + h * HD, group * shard + (h + 1) * HD)
+            q = q_ref[group, :, cols]
+            k = k_ref[group, :, cols]
+            v = v_ref[group, :, cols]
+            g = grad_ref[group, :, cols]
+            probs = _probs(q, k, length, factor)
+            prob_grad = lax.dot_general(
+                g, v, (((1,), (1,)), ((), ())), preferred_element_type=jnp.float32
+            )
+            row_dot = jnp.sum(prob_grad * probs, axis=1, keepdims=True)
+            score_grad = (probs * (prob_grad - row_dot)).astype(jnp.bfloat16)
+            out_ref[0, :, wide] = (
+                jnp.dot(score_grad, k, preferred_element_type=jnp.float32) * factor
+            ).astype(out_ref.dtype)
+            out_ref[1, :, wide] = (
+                lax.dot_general(
+                    score_grad, q, (((0,), (0,)), ((), ())), preferred_element_type=jnp.float32
+                )
+                * factor
+            ).astype(out_ref.dtype)
+            out_ref[2, :, wide] = lax.dot_general(
+                probs.astype(jnp.bfloat16),
+                g,
+                (((0,), (0,)), ((), ())),
+                preferred_element_type=jnp.float32,
+            ).astype(out_ref.dtype)
 
 
 def _group_block(shard):
@@ -103,20 +113,21 @@
 
 def attention_backward(queries, keys, values, context_grad, lengths, factor):
     groups, rows, shard = queries.shape
-    grid = (rows // LEN, groups)
+    width = groups * shard
+    whole = pl.BlockSpec((groups, LEN, shard), lambda p, n: (0, p, 0))
     return pl.pallas_call(
-        functools.partial(_bwd_kernel, heads=shard // HD, factor=factor),
-        out_shape=jax.ShapeDtypeStruct((3, groups, rows, shard), jnp.bfloat16),
+        functools.partial(_bwd_kernel, factor=factor),
+        out_shape=jax.ShapeDtypeStruct((3, rows, width), jnp.bfloat16),
         grid_spec=pltpu.PrefetchScalarGridSpec(
             num_scalar_prefetch=1,
-            grid=grid,
-            in_specs=[_group_block(shard)] * 4,
-            out_specs=pl.BlockSpec((3, None, LEN, shard), lambda p, g, n: (0, g, p, 0)),
+            grid=(rows // LEN,),
+            in_specs=[whole] * 4,
+            out_specs=pl.BlockSpec((3, LEN, width), lambda p, n: (0, p, 0)),
         ),
         cost_estimate=pl.CostEstimate(
-            flops=10 * rows * LEN * groups * shard,
-            transcendentals=rows * LEN * groups * shard // HD,
-            bytes_accessed=7 * rows * groups * shard * 2,
+            flops=10 * rows * LEN * width,
+            transcendentals=rows * LEN * width // HD,
+            bytes_accessed=7 * rows * width * 2,
         ),
     )(lengths, queries, keys, values, context_grad)
 
@@ -276,16 +287,23 @@
         proj_grad = attention_backward(
             query_low, key_low, value_low, context_grad, own_lengths, factor
         )
-        grad_bias_full = jnp.sum(proj_grad[0::2], axis=2, dtype=jnp.float32).reshape(2, width)
+        grad_bias_full = jnp.sum(proj_grad[0::2], axis=1, dtype=jnp.float32)
         grad_qkv_full = jnp.einsum(
-            "rd,kgrj->kdgj", tokens, proj_grad, preferred_element_type=jnp.float32
-        )
+            "rd,kre->kde", tokens, proj_grad, preferred_element_type=jnp.float32
+        )
+
+        def back_project(grad, weight):
+            return jnp.einsum(
+                "rgj,gdj->rd",
+                grad.reshape(rows, groups, shard),
+                weight,
+                preferred_element_type=jnp.float32,
+            )
+
         input_part = (
-            jnp.einsum("grj,gdj->rd", proj_grad[0], query_weight, preferred_element_type=jnp.float32)
-            + jnp.einsum("grj,gdj->rd", proj_grad[1], key_weight, preferred_element_type=jnp.float32)
-            + jnp.einsum(
-                "grj,gdj->rd", proj_grad[2], value_weight, preferred_element_type=jnp.float32
-            )
+            back_project(proj_grad[0], query_weight)
+            + back_project(proj_grad[1], key_weight)
+            + back_project(proj_grad[2], value_weight)
         )
         input_grad = (first_grad + input_part).astype(jnp.bfloat16)
 

time: 584 us -> 571 us (0.978)
  waiting for transfers between devices: 367 us -> 355 us
  local copies, waits for them, and re-layouts: 60.8 us -> 49.8 us
  other arithmetic: 33 us -> 41.9 us
    convert_element_type x2 -> x0, local copies, waits for them, and re-layouts: 17 us -> none  [per_device(): grad_qkv_full.reshape(3 * width, width).astype(jnp.bfloat16)]
    unnamed x86 -> x88, local copies, waits for them, and re-layouts: 15.8 us -> 17.3 us
  transfers between devices with their start and end apart: 24 -> 24, of which waited for: 19 -> 18; matrix products, arithmetic and copies ran while one was open for 8% -> 10% of each run, Pallas kernels for 0% -> 0%
where the time goes in v10:
time: 571 us; the launch traced here: 561 us
  waiting for transfers between devices  355 us (62%)
  matrix products  56.2 us (10%)
  local copies, waits for them, and re-layouts  49.8 us (9%)
  other arithmetic  41.9 us (7%)
  Pallas kernels  29.2 us (5%)
  between operations  15.3 us (3%)
  starting transfers between devices  14 us (2%)
    all_gather x1, waiting for transfers between devices, per_device(): branch_rows = lax.all_gather(branch_grad, 'tensor', axis=0, tiled=True)  63 us
    all_gather x1, waiting for transfers between devices, per_device(): ffn_rows = lax.all_gather(middle_low, 'tensor', axis=0, tiled=True)  62.3 us
    reduce_scatter x1, waiting for transfers between devices, per_device(): lax.psum_scatter(jnp.dot(hidden, down_weight, preferred_element_type=jnp....  59.2 us
    all_gather x1, waiting for transfers between devices, per_device(): mine = lax.all_gather(mine, 'tensor', axis=0, tiled=False)  56.5 us
    ppermute x9, waiting for transfers between devices, dp_halve(): got = lax.ppermute(give, 'dp', [(i, i ^ 1 << step) for i in range(dp_size)])  42.4 us
    all_gather x1, waiting for transfers between devices, per_device(): joined = lax.all_gather(joined, 'dp', axis=0, tiled=False)  22 us
    dot_general x4, matrix products, contract(): lax.dot_general(left, right, (((left_dim,), (right_dim,)), ((), ())), pre...  19.4 us
    pallas_call x1, Pallas kernels, attention_backward(): pl.pallas_call(functools.partial(_bwd_kernel, factor=factor), out_shape=j...  18.3 us
  transfers between devices with their start and end apart: 24, of which 18 were waited for; matrix products, arithmetic and copies ran while one was open for 10% of the time, Pallas kernels for 0%

profile of v10, /device:TPU:0, one launch (start us, length us, event | category | flops | bytes accessed | tf_op | source)
XLA Modules:
  0.0 561.5 jit_solution(8568329775190347666)
XLA Ops:
  10.5 56.5 %all-gather.13.cloned.1.call-done = bf16[4,1544,192]{1,2,0:T(8,128)(2,1)} async-done(((bf16[1,1544,192]{1,2,0:T(8,128)(2,1)}), bf16[4,1544,192]{1,2,0:T(8,128)(2,1)}) %all-gather.13.cloned.1.call-update) | async-done | bytes 2371600 | tf_op jit(solution)/shard_map/all_gather | solution.py:208
  67.6 4.6 collective-permute-done
  72.2 4.4 broadcast_select_fusion
  78.8 1.3 copy.102
  80.2 3.2 fusion.13.q_ref
  83.4 3.3 fusion.14.v_ref
  86.7 10.9 %shard_map.254 = bf16[4,512,192]{2,1,0:T(8,128)(2,1)} custom-call(s32[1]{0:T(128)} %dynamic_slice.57.len_ref, bf16[4,512,192]{2,1,0:T(8,128)(2,1)} %fusion.13.q_ref, bf16[4,512,192]{2,1,0:T(8,128)(2,1)} %bitcast.109, bf16[4,512,192]{2,1,0:T(8,128)(2,1)} %fusion.14.v_ref), custom_call_target="tpu_custom_call" | custom-call | flops 805306368 | bytes 3145728 | tf_op jit(solution)/shard_map/pallas_call | solution.py:97
  97.6 2.7 fusion.52
  102.3 62.3 %all-gather.9.cloned.1.call-done = bf16[2048,768]{1,0:T(8,128)(2,1)} async-done(((bf16[512,768]{1,0:T(8,128)(2,1)}), bf16[2048,768]{1,0:T(8,128)(2,1)}) %all-gather.9.cloned.1.call-update) | async-done | bytes 3145744 | tf_op jit(solution)/shard_map/all_gather | solution.py:238
  164.6 6.9 %multiply_convert_fusion = (bf16[2048,768]{1,0:T(8,128)(2,1)S(1)}, f32[2048,768]{1,0:T(8,128)}) fusion(f32[768]{0:T(1024)S(1)} %convert_element_type.142, bf16[2048,768]{1,0:T(8,128)(2,1)} %all-gather.9.cloned.1.call-done, bf16[768,768]{1,0:T(8,128)(2,1)S(1)} %copy-done), kind=kOutput, calls=%fused_computation.8 | convolution fusion | flops 2425356288 | bytes 13765632 | tf_op jit(solution)/shard_map/dot_general | solution.py:239
  171.5 1.7 copy-done.36
  173.2 4.0 convolution_convert_fusion.1
  177.2 59.2 %reduce-scatter.5.cloned.1.call-done = bf16[512,768]{1,0:T(8,128)(2,1)} async-done(((bf16[2048,768]{1,0:T(8,128)(2,1)}), bf16[512,768]{1,0:T(8,128)(2,1)}) %reduce-scatter.5.cloned.1.call-update) | async-done | bytes 786448 | tf_op jit(solution)/shard_map/reduce_scatter | solution.py:242
  236.4 1.7 fusion.49
  240.0 1.6 fusion.48
  244.3 63.0 %all-gather.11.cloned.1.call-done = bf16[2048,768]{1,0:T(8,128)(2,1)} async-done(((bf16[512,768]{1,0:T(8,128)(2,1)}), bf16[2048,768]{1,0:T(8,128)(2,1)}) %all-gather.11.cloned.1.call-update) | async-done | bytes 3145744 | tf_op jit(solution)/shard_map/all_gather | solution.py:254
  307.3 7.0 %convert_reduce_fusion = (f32[768]{0:T(1024)S(1)}, bf16[2048,768]{1,0:T(8,128)(2,1)S(1)}) fusion(f32[2048,768]{1,0:T(8,128)} %get-tuple-element.139, f32[768]{0:T(1024)S(1)} %convert_element_type.142, bf16[2048,768]{1,0:T(8,128)(2,1)} %all-gather.11.cloned.1.call-done, bf16[768,768]{1,0:T(8,128)(2,1)} %param.26), kind=kOutput, calls=%fused_computation.7 | convolution fusion | flops 2436365568 | bytes 13768704 | tf_op jit(solution)/shard_map/dot_general | solution.py:31
  314.3 1.7 copy-done.37
  316.0 4.0 convolution_convert_fusion
  320.1 5.7 %fusion.54 = f32[768,768]{1,0:T(8,128)S(1)} fusion(bf16[2048,768]{1,0:T(8,128)(2,1)} %copy-done.36, bf16[2048,768]{1,0:T(8,128)(2,1)} %all-gather.11.cloned.1.call-done), kind=kOutput, calls=%fused_computation.165 | convolution fusion | flops 2415919104 | bytes 8650752 | tf_op jit(solution)/shard_map/dot_general | solution.py:31
  325.8 2.7 fusion.53
  328.6 1.3 constant_dynamic-slice_fusion.4
  330.9 2.5 collective-permute-done.4
  333.4 1.8 dynamic-slice_add_fusion
  335.2 1.5 collective-permute-start.5
  336.7 1.4 dynamic-slice_add_fusion.1
  340.6 11.0 %collective-permute-done.5 = f32[192,768]{1,0:T(8,128)} collective-permute-done((f32[192,768]{1,0:T(8,128)S(1)}, f32[192,768]{1,0:T(8,128)}, u32[]{:S(2)}, u32[]{:S(2)}) %collective-permute-start.5) | collective-permute-done | bytes 589856 | tf_op jit(solution)/shard_map/ppermute | solution.py:150
  353.5 1.5 collective-permute-start.6
  354.9 8.5 %collective-permute-done.2 = f32[192,768]{1,0:T(8,128)} collective-permute-done((f32[192,768]{1,0:T(8,128)}, f32[192,768]{1,0:T(8,128)}, u32[]{:S(2)}, u32[]{:S(2)}) %collective-permute-start.2) | collective-permute-done | bytes 589856 | tf_op jit(solution)/shard_map/ppermute | solution.py:150
  365.3 1.5 collective-permute-start.3
  367.4 6.2 %collective-permute-done.3 = f32[96,768]{1,0:T(8,128)S(1)} collective-permute-done((f32[96,768]{1,0:T(8,128)}, f32[96,768]{1,0:T(8,128)S(1)}, u32[]{:S(2)}, u32[]{:S(2)}) %collective-permute-start.3) | collective-permute-done | bytes 294944 | tf_op jit(solution)/shard_map/ppermute | solution.py:150
  374.4 4.8 reduce-scatter.7.cloned.1.call-done
  379.2 1.9 convert_add_fusion
  383.8 2.1 convolution_convert_fusion.3
  385.9 1.4 copy.105
  387.3 18.3 %shard_map.255 = bf16[3,512,768]{2,1,0:T(8,128)(2,1)} custom-call(s32[1]{0:T(128)} %dynamic_slice.57.len_ref, bf16[4,512,192]{2,1,0:T(8,128)(2,1)} %fusion.13.q_ref, bf16[4,512,192]{2,1,0:T(8,128)(2,1)} %bitcast.110, bf16[4,512,192]{2,1,0:T(8,128)(2,1)} %fusion.14.v_ref, bf16[4,512,192]{2,1,0:T(8,128)(2,1)} %bitcast.111), custom_call_target="tpu_custom_call" | custom-call | flops 2013265920 | bytes 5505024 | tf_op jit(solution)/shard_map/pallas_call | solution.py:118
  405.6 5.5 convolution_convert_fusion.2
  415.8 1.5 collective-permute-start.10
  420.7 1.4 copy.129
  423.2 1.6 convert_add_fusion.1
  424.9 1.6 collective-permute-start.8
  427.3 6.8 %collective-permute-done.8 = bf16[192,768]{1,0:T(8,128)(2,1)S(1)} collective-permute-done((bf16[192,768]{1,0:T(8,128)(2,1)S(1)}, bf16[192,768]{1,0:T(8,128)(2,1)S(1)}, u32[]{:S(2)}, u32[]{:S(2)}) %collective-permute-start.8) | collective-permute-done | bytes 294944 | tf_op jit(solution)/shard_map/ppermute | solution.py:150
  435.1 1.6 collective-permute-start.9
  436.8 1.4 select_maximum_fusion
  438.1 6.4 %collective-permute-done.9 = bf16[96,768]{1,0:T(8,128)(2,1)S(1)} collective-permute-done((bf16[96,768]{1,0:T(8,128)(2,1)S(1)}, bf16[96,768]{1,0:T(8,128)(2,1)S(1)}, u32[]{:S(2)}, u32[]{:S(2)}) %collective-permute-start.9) | collective-permute-done | bytes 147488 | tf_op jit(solution)/shard_map/ppermute | solution.py:150
  445.5 16.8 %reduce-scatter.9.cloned.1.call-done = bf16[288,768]{1,0:T(8,128)(2,1)} async-done(((bf16[2304,768]{1,0:T(8,128)(2,1)}), bf16[288,768]{1,0:T(8,128)(2,1)}) %reduce-scatter.9.cloned.1.call-update) | async-done | bytes 442384 | tf_op jit(solution)/shard_map/reduce_scatter | solution.py:332
  463.4 2.0 pad_maximum_fusion
  465.4 3.0 copy.113
  469.8 1.5 collective-permute-start.14
  473.0 6.7 %collective-permute-done.14 = bf16[192,768]{1,0:T(8,128)(2,1)S(1)} collective-permute-done((bf16[192,768]{1,0:T(8,128)(2,1)S(1)}, bf16[192,768]{1,0:T(8,128)(2,1)S(1)}, u32[]{:S(2)}, u32[]{:S(2)}) %collective-permute-start.14) | collective-permute-done | bytes 294944 | tf_op jit(solution)/shard_map/ppermute | solution.py:165
  480.7 4.1 collective-permute-done.11
  487.0 1.6 maximum_convert_fusion.1
  489.8 1.6 maximum_convert_fusion
  491.4 12.6 %reduce-scatter.11.cloned.1.call-done = f32[1,416,192]{1,2,0:T(8,128)} async-done(((f32[4,416,192]{1,2,0:T(8,128)}), f32[1,416,192]{1,2,0:T(8,128)}) %reduce-scatter.11.cloned.1.call-update) | async-done | bytes 319504 | tf_op jit(solution)/shard_map/reduce_scatter | solution.py:339
  504.0 1.3 fusion.50
  505.3 1.5 copy.108
  507.4 2.1 fusion.25
  509.5 2.2 fusion.28
  511.7 3.3 fusion.11
  515.0 22.0 %all-gather.15.cloned.1.call-done = f32[8,416,192]{1,2,0:T(8,128)} async-done(((f32[1,416,192]{1,2,0:T(8,128)}), f32[8,416,192]{1,2,0:T(8,128)}) %all-gather.15.cloned.1.call-update) | async-done | bytes 2555920 | tf_op jit(solution)/shard_map/all_gather | solution.py:353
  544.4 3.3 slice.155
  547.6 2.2 copy.114
  549.8 1.8 copy.122
  551.6 1.5 slice_bitcast_fusion.3
  (200 shorter events, 53.5 us)
Async XLA Ops:
  7.2 157.4 %copy-start = (bf16[768,768]{1,0:T(8,128)(2,1)S(1)}, bf16[768,768]{1,0:T(8,128)(2,1)}, u32[]{:S(2)}) copy-start(bf16[768,768]{1,0:T(8,128)(2,1)} %param.24) | copy-start | bytes 3538948
  7.2 2.2 copy-start.16
  7.2 59.8 %all-gather.13.cloned.1.call-start = ((), (), s32[]{:S(2)}) async-start(), calls=%async_computation.10 | async-start | bytes 3194880 | tf_op jit(solution)/shard_map/all_gather | solution.py:208
  9.4 57.6 %copy-start.35 = (s32[4]{0:T(128)S(1)}, s32[4]{0:T(128)}, u32[]{:S(2)}) copy-start(s32[4]{0:T(128)} %param.17) | copy-start | bytes 52
  10.4 154.2 %all-gather.9.cloned.1.call-start = ((), (), s32[]{:S(2)}) async-start(), calls=%async_computation.4 | async-start | bytes 3932160 | tf_op jit(solution)/shard_map/all_gather | solution.py:238
  67.0 5.2 collective-permute-start
  67.6 10.4 %copy-start.32 = (bf16[512,768]{1,0:T(8,128)(2,1)S(1)}, bf16[512,768]{1,0:T(8,128)(2,1)}, u32[]{:S(2)}) copy-start(bf16[512,768]{1,0:T(8,128)(2,1)} %param.15) | copy-start | bytes 2359300
  76.6 1.4 copy-start.8
  86.7 10.9 %copy-start.34 = (f32[768]{0:T(1024)S(1)}, f32[768]{0:T(1024)}, u32[]{:S(2)}) copy-start(f32[768]{0:T(1024)} %param.21) | copy-start | bytes 9220
  100.3 0.7 copy-start.17
  100.3 0.7 copy-start.18
  101.0 1.3 copy-start.29
  102.3 134.1 %reduce-scatter.5.cloned.1.call-start = ((), (), s32[]{:S(2)}) async-start(), calls=%async_computation.5 | async-start | bytes 3932160 | tf_op jit(solution)/shard_map/reduce_scatter | solution.py:242
  164.6 8.5 %copy-start.31 = (bf16[768,768]{1,0:T(8,128)(2,1)S(1)}, bf16[768,768]{1,0:T(8,128)(2,1)}, u32[]{:S(2)}) copy-start(bf16[768,768]{1,0:T(8,128)(2,1)} %param.26) | copy-start | bytes 3538948
  171.5 1.7 copy-start.36
  177.1 59.2 %copy-start.27 = (f32[768]{0:T(1024)S(1)}, f32[768]{0:T(1024)}, u32[]{:S(2)}) copy-start(f32[768]{0:T(1024)} %param.27) | copy-start | bytes 9220
  177.2 130.2 %all-gather.11.cloned.1.call-start = ((), (), s32[]{:S(2)}) async-start(), calls=%async_computation.6 | async-start | bytes 3932160 | tf_op jit(solution)/shard_map/all_gather | solution.py:254
  238.1 1.1 copy-start.10
  238.1 1.1 copy-start.19
  238.5 1.5 copy-start.28
  241.6 1.1 copy-start.2
  243.8 135.4 %reduce-scatter.7.cloned.1.call-start = ((), (), s32[]{:S(2)}) async-start(), calls=%async_computation.7 | async-start | bytes 3932160 | tf_op jit(solution)/shard_map/reduce_scatter | solution.py:266
  314.3 1.7 copy-start.37
  320.0 142.3 %reduce-scatter.9.cloned.1.call-start = ((), (), s32[]{:S(2)}) async-start(), calls=%async_computation.8 | async-start | bytes 3981312 | tf_op jit(solution)/shard_map/reduce_scatter | solution.py:332
  320.1 5.7 %copy-start.30 = (bf16[2048,768]{1,0:T(8,128)(2,1)S(1)}, bf16[2048,768]{1,0:T(8,128)(2,1)}, u32[]{:S(2)}) copy-start(bf16[2048,768]{1,0:T(8,128)(2,1)} %all-gather.9.cloned.1.call-done) | copy-start | bytes 9437188
  320.1 5.7 %copy-start.38 = (bf16[2048,768]{1,0:T(8,128)(2,1)S(1)}, bf16[2048,768]{1,0:T(8,128)(2,1)}, u32[]{:S(2)}) copy-start(bf16[2048,768]{1,0:T(8,128)(2,1)} %copy-done.37) | copy-start | bytes 9437188
  325.8 2.8 copy-start.13
  328.6 1.8 copy-start.11
  330.4 3.0 collective-permute-start.4
  330.4 6.3 %collective-permute-start.1 = (f32[384,768]{1,0:T(8,128)}, f32[384,768]{1,0:T(8,128)}, u32[]{:S(2)}, u32[]{:S(2)}) collective-permute-start(f32[384,768]{1,0:T(8,128)} %get-tuple-element.143), channel_id=1, source_target_pairs={{0,4},{4,0},{8,12},{12,8},{16,20},{20,16},{24,28},{28,24},{1,5},{5... | collective-permute-start | bytes 3538952 | tf_op jit(solution)/shard_map/ppermute | solution.py:150
  330.9 5.8 %copy-start.12 = (f32[768,768]{1,0:T(8,128)S(1)}, f32[768,768]{1,0:T(8,128)}, u32[]{:S(2)}) copy-start(f32[768,768]{1,0:T(8,128)} %copy-done.11) | copy-start | bytes 7077892
  335.2 16.4 %collective-permute-start.5 = (f32[192,768]{1,0:T(8,128)S(1)}, f32[192,768]{1,0:T(8,128)}, u32[]{:S(2)}, u32[]{:S(2)}) collective-permute-start(f32[192,768]{1,0:T(8,128)S(1)} %constant_dynamic-slice_fusion.3), channel_id=1, source_target_pairs={{0,8},{4,12},{8,0},{12,4},{16,24},{20,28},{24,16},{28,20},{1,9},{5... | collective-permute-start | bytes 1769480 | tf_op jit(solution)/shard_map/ppermute | solution.py:150
  338.2 1.0 copy-start.6
  340.1 23.3 %collective-permute-start.2 = (f32[192,768]{1,0:T(8,128)}, f32[192,768]{1,0:T(8,128)}, u32[]{:S(2)}, u32[]{:S(2)}) collective-permute-start(f32[192,768]{1,0:T(8,128)} %constant_dynamic-slice_fusion.6), channel_id=1, source_target_pairs={{0,8},{4,12},{8,0},{12,4},{16,24},{20,28},{24,16},{28,20},{1,9},{5... | collective-permute-start | bytes 1769480 | tf_op jit(solution)/shard_map/ppermute | solution.py:150
  340.6 22.8 %copy-start.7 = (f32[384,768]{1,0:T(8,128)S(1)}, f32[384,768]{1,0:T(8,128)}, u32[]{:S(2)}) copy-start(f32[384,768]{1,0:T(8,128)} %copy-done.6) | copy-start | bytes 3538948
  353.5 13.3 %collective-permute-start.6 = (f32[96,768]{1,0:T(8,128)}, f32[96,768]{1,0:T(8,128)S(1)}, u32[]{:S(2)}, u32[]{:S(2)}) collective-permute-start(f32[96,768]{1,0:T(8,128)} %constant_dynamic-slice_fusion.2), channel_id=1, source_target_pairs={{0,16},{4,20},{8,24},{12,28},{16,0},{20,4},{24,8},{28,12},{1,17},{... | collective-permute-start | bytes 884744 | tf_op jit(solution)/shard_map/ppermute | solution.py:150
  365.3 8.4 %collective-permute-start.3 = (f32[96,768]{1,0:T(8,128)}, f32[96,768]{1,0:T(8,128)S(1)}, u32[]{:S(2)}, u32[]{:S(2)}) collective-permute-start(f32[96,768]{1,0:T(8,128)} %constant_dynamic-slice_fusion.5), channel_id=1, source_target_pairs={{0,16},{4,20},{8,24},{12,28},{16,0},{20,4},{24,8},{28,12},{1,17},{... | collective-permute-start | bytes 884744 | tf_op jit(solution)/shard_map/ppermute | solution.py:150
  382.4 1.1 copy-start.4
  382.4 1.3 copy-start.25
  387.3 18.3 %copy-start.33 = (bf16[512,768]{1,0:T(8,128)(2,1)S(1)}, bf16[512,768]{1,0:T(8,128)(2,1)}, u32[]{:S(2)}) copy-start(bf16[512,768]{1,0:T(8,128)(2,1)} %param.15) | copy-start | bytes 2359300
  411.1 1.2 copy-start.15
  411.1 92.9 %reduce-scatter.11.cloned.1.call-start = ((), (), s32[]{:S(2)}) async-start(), calls=%async_computation.9 | async-start | bytes 1966080 | tf_op jit(solution)/shard_map/reduce_scatter | solution.py:339
  415.8 55.5 %collective-permute-start.10 = (bf16[96,768]{1,0:T(8,128)(2,1)}, bf16[96,768]{1,0:T(8,128)(2,1)}, u32[]{:S(2)}, u32[]{:S(2)}) collective-permute-start(bf16[96,768]{1,0:T(8,128)(2,1)} %dynamic-slice_add_fusion.5), channel_id=1, source_target_pairs={{0,16},{4,20},{8,24},{12,28},{16,0},{20,4},{24,8},{28,12},{1,17},{... | collective-permute-start | bytes 442376 | tf_op jit(solution)/shard_map/ppermute | solution.py:165
  417.2 51.5 %collective-permute-start.13 = (bf16[96,768]{1,0:T(8,128)(2,1)}, bf16[96,768]{1,0:T(8,128)(2,1)}, u32[]{:S(2)}, u32[]{:S(2)}) collective-permute-start(bf16[96,768]{1,0:T(8,128)(2,1)} %dynamic-slice_add_fusion.4), channel_id=1, source_target_pairs={{0,16},{4,20},{8,24},{12,28},{16,0},{20,4},{24,8},{28,12},{1,17},{... | collective-permute-start | bytes 442376 | tf_op jit(solution)/shard_map/ppermute | solution.py:165
  420.6 2.7 collective-permute-start.7
  420.6 1.4 copy-start.24
  420.7 1.4 copy-start.22
  420.7 1.4 copy-start.23
  420.7 1.4 copy-start.21
  422.1 4.3 copy-start.20
  422.1 4.3 copy-start.3
  424.9 9.3 %collective-permute-start.8 = (bf16[192,768]{1,0:T(8,128)(2,1)S(1)}, bf16[192,768]{1,0:T(8,128)(2,1)S(1)}, u32[]{:S(2)}, u32[]{:S(2)}) collective-permute-start(bf16[192,768]{1,0:T(8,128)(2,1)S(1)} %dynamic-slice_convert_fusion), channel_id=1, source_target_pairs={{0,8},{4,12},{8,0},{12,4},{16,24},{20,28},{24,16},{28,20},{1,9},{5... | collective-permute-start | bytes 884744 | tf_op jit(solution)/shard_map/ppermute | solution.py:150
  434.2 0.8 copy-start.14
  435.1 9.5 %collective-permute-start.9 = (bf16[96,768]{1,0:T(8,128)(2,1)S(1)}, bf16[96,768]{1,0:T(8,128)(2,1)S(1)}, u32[]{:S(2)}, u32[]{:S(2)}) collective-permute-start(bf16[96,768]{1,0:T(8,128)(2,1)S(1)} %dynamic-slice_convert_fusion.1), channel_id=1, source_target_pairs={{0,16},{4,20},{8,24},{12,28},{16,0},{20,4},{24,8},{28,12},{1,17},{... | collective-permute-start | bytes 442376 | tf_op jit(solution)/shard_map/ppermute | solution.py:150
  468.4 68.6 %all-gather.15.cloned.1.call-start = ((), (), s32[]{:S(2)}) async-start(), calls=%async_computation.11 | async-start | bytes 3538944 | tf_op jit(solution)/shard_map/all_gather | solution.py:353
  469.8 9.9 %collective-permute-start.14 = (bf16[192,768]{1,0:T(8,128)(2,1)S(1)}, bf16[192,768]{1,0:T(8,128)(2,1)S(1)}, u32[]{:S(2)}, u32[]{:S(2)}) collective-permute-start(bf16[192,768]{1,0:T(8,128)(2,1)S(1)} %pad_maximum_fusion.4), channel_id=1, source_target_pairs={{0,8},{4,12},{8,0},{12,4},{16,24},{20,28},{24,16},{28,20},{1,9},{5... | collective-permute-start | bytes 884744 | tf_op jit(solution)/shard_map/ppermute | solution.py:165
  472.3 12.4 %collective-permute-start.11 = (bf16[192,768]{1,0:T(8,128)(2,1)S(1)}, bf16[192,768]{1,0:T(8,128)(2,1)S(1)}, u32[]{:S(2)}, u32[]{:S(2)}) collective-permute-start(bf16[192,768]{1,0:T(8,128)(2,1)S(1)} %pad_maximum_fusion.3), channel_id=1, source_target_pairs={{0,8},{4,12},{8,0},{12,4},{16,24},{20,28},{24,16},{28,20},{1,9},{5... | collective-permute-start | bytes 884744 | tf_op jit(solution)/shard_map/ppermute | solution.py:165
  480.7 5.0 collective-permute-start.15
  485.7 2.9 collective-permute-start.12
  505.3 1.5 copy-start.9
  509.5 2.2 copy-start.5
  509.5 2.2 copy-start.26
  549.8 4.4 copy-start.1
Sparse Core Ops, SparseCore 0:
  10.6 56.3 all-gather.12
  102.4 62.2 all-gather.8
  177.3 59.0 reduce-scatter.4
  243.9 63.3 all-gather.10
  320.1 59.0 reduce-scatter.6
  411.3 51.0 reduce-scatter.8
  468.5 35.4 reduce-scatter.10
  505.9 31.0 all-gather.14

commit v11 on v8

--- a/solution.py
+++ b/solution.py
@@ -46,10 +46,9 @@
     length = len_ref[pl.program_id(0)]
     for h in range(heads):
         cols = slice(h * HD, (h + 1) * HD)
-        v = v_ref[:, cols]
         probs = _probs(q_ref[:, cols], k_ref[:, cols], length, factor)
         out_ref[:, cols] = jnp.dot(
-            probs.astype(jnp.bfloat16), v, preferred_element_type=jnp.float32
+            probs.astype(jnp.bfloat16), v_ref[:, cols], preferred_element_type=jnp.float32
         ).astype(out_ref.dtype)
 
 
@@ -77,21 +76,17 @@
         ).astype(out_ref.dtype)
 
 
-def _row_block(pair):
-    return pl.BlockSpec((LEN, pair * HD), lambda p, i, n: (p, i))
-
-
 def attention_forward(queries, keys, values, lengths, factor, pair=2):
     rows, width = queries.shape
-    grid = (rows // LEN, width // (pair * HD))
+    block = pl.BlockSpec((LEN, pair * HD), lambda p, i, n: (p, i))
     return pl.pallas_call(
         functools.partial(_fwd_kernel, heads=pair, factor=factor),
         out_shape=jax.ShapeDtypeStruct((rows, width), jnp.bfloat16),
         grid_spec=pltpu.PrefetchScalarGridSpec(
             num_scalar_prefetch=1,
-            grid=grid,
-            in_specs=[_row_block(pair)] * 3,
-            out_specs=_row_block(pair),
+            grid=(rows // LEN, width // (pair * HD)),
+            in_specs=[block] * 3,
+            out_specs=block,
         ),
         cost_estimate=pl.CostEstimate(
             flops=4 * rows * LEN * width,
@@ -103,14 +98,14 @@
 
 def attention_backward(queries, keys, values, context_grad, lengths, factor, pair=2):
     rows, width = queries.shape
-    grid = (rows // LEN, width // (pair * HD))
+    block = pl.BlockSpec((LEN, pair * HD), lambda p, i, n: (p, i))
     return pl.pallas_call(
         functools.partial(_bwd_kernel, heads=pair, factor=factor),
         out_shape=jax.ShapeDtypeStruct((3, rows, width), jnp.bfloat16),
         grid_spec=pltpu.PrefetchScalarGridSpec(
             num_scalar_prefetch=1,
-            grid=grid,
-            in_specs=[_row_block(pair)] * 4,
+            grid=(rows // LEN, width // (pair * HD)),
+            in_specs=[block] * 4,
             out_specs=pl.BlockSpec((3, LEN, pair * HD), lambda p, i, n: (0, p, i)),
         ),
         cost_estimate=pl.CostEstimate(
@@ -194,30 +189,36 @@
         dp_index = lax.axis_index("dp")
         parity = dp_index % 2
         mine = jnp.where(parity == 0, first_half, second_half)
-        mine = lax.all_gather(mine, "tensor", axis=1, tiled=False).reshape(half_rows, width)
+        mine = lax.all_gather(mine, "tensor", axis=0, tiled=False)
         other = lax.ppermute(mine, "dp", [(i, i ^ 1) for i in range(dp_size)])
         first_half = jnp.where(parity == 0, mine, other)
         second_half = jnp.where(parity == 0, other, mine)
-        query_weight = first_half[:width]
-        key_weight = first_half[width : 2 * width]
-        query_bias = first_half[2 * width]
-        value_bias = first_half[2 * width + 1]
-        value_weight = second_half[:width]
-        proj_t = second_half[width : 2 * width]
+        query_weight = first_half[:, :width]
+        key_weight = first_half[:, width : 2 * width]
+        query_bias = first_half[:, 2 * width]
+        value_bias = first_half[:, 2 * width + 1]
+        value_weight = second_half[:, :width]
+        proj_blocks = second_half[:, width : 2 * width]
 
         tensor_index = lax.axis_index("tensor")
         own_lengths = lax.dynamic_slice_in_dim(lengths, tensor_index * passages, passages)
 
         own_tokens = tokens.astype(jnp.float32)
         def project(weight, bias=None):
-            out = jnp.dot(tokens, weight, preferred_element_type=jnp.float32)
-            return (out if bias is None else out + bias).astype(jnp.bfloat16)
+            out = jnp.einsum("rd,gdj->rgj", tokens, weight, preferred_element_type=jnp.float32)
+            out = out if bias is None else out + bias
+            return out.astype(jnp.bfloat16).reshape(rows, width)
 
         query_low = project(query_weight, query_bias)
         key_low = project(key_weight)
         value_low = project(value_weight, value_bias)
         context_low = attention_forward(query_low, key_low, value_low, own_lengths, factor)
-        attn_out = contract(context_low, proj_t, 1, 1)
+        attn_out = jnp.einsum(
+            "rgj,gcj->rc",
+            context_low.reshape(rows, groups, shard),
+            proj_blocks,
+            preferred_element_type=jnp.float32,
+        )
         middle, norm1_back = jax.vjp(
             layer_norm, own_tokens + attn_out + out_bias, norm1_gain, norm1_shift
         )
@@ -260,8 +261,10 @@
         first_grad, grad_norm1_gain, grad_norm1_shift = norm1_back(norm1_in)
         attn_grad = first_grad.astype(jnp.bfloat16)
         grad_out_bias = jnp.sum(attn_grad, axis=0, dtype=jnp.float32)
-        context_grad = jnp.dot(attn_grad, proj_t, preferred_element_type=jnp.float32).astype(
-            jnp.bfloat16
+        context_grad = (
+            jnp.einsum("rc,gcj->rgj", attn_grad, proj_blocks, preferred_element_type=jnp.float32)
+            .astype(jnp.bfloat16)
+            .reshape(rows, width)
         )
         early = contract(attn_grad, context_low, 0, 0)
         early_halved = dp_pow2(early, dp_size)
@@ -274,12 +277,21 @@
         )
         grad_bias_full = jnp.sum(proj_grad[0::2], axis=1, dtype=jnp.float32)
         grad_qkv_full = jnp.einsum(
-            "rd,tre->tde", tokens, proj_grad, preferred_element_type=jnp.float32
-        )
+            "rd,kre->kde", tokens, proj_grad, preferred_element_type=jnp.float32
+        )
+
+        def back_project(grad, weight):
+            return jnp.einsum(
+                "rgj,gdj->rd",
+                grad.reshape(rows, groups, shard),
+                weight,
+                preferred_element_type=jnp.float32,
+            )
+
         input_part = (
-            contract(proj_grad[0], query_weight, 1, 1)
-            + contract(proj_grad[1], key_weight, 1, 1)
-            + contract(proj_grad[2], value_weight, 1, 1)
+            back_project(proj_grad[0], query_weight)
+            + back_project(proj_grad[1], key_weight)
+            + back_project(proj_grad[2], value_weight)
         )
         input_grad = (first_grad + input_part).astype(jnp.bfloat16)
 

time: 563 us -> 567 us (level); the launches traced: 562 us -> 558 us
  waiting for transfers between devices: 375 us -> 368 us
    dot_general x9 -> x5, matrix products: 31.3 us -> 21.4 us  [contract(): lax.dot_general(left, right, (((left_dim,), (right_dim,)), ((), ())), pre...]
    slice x0 -> x5, local copies, waits for them, and re-layouts: none -> 5.71 us  [the longest x1 2.36 us: per_device(): proj_blocks = second_half[:, width:2 * width]]
    dot_general x5 -> x8, matrix products: 14 us -> 19.1 us  [the longest x3 7.55 us: back_project(): jnp.einsum('rgj,gdj->rd', grad.reshape(rows, groups, shard), weight, pref...]
    unnamed x80 -> x84, local copies, waits for them, and re-layouts: 11 us -> 11.8 us
  transfers between devices with their start and end apart: 24 -> 24, of which waited for: 19 -> 19; matrix products, arithmetic and copies ran while one was open for 7% -> 8% of each run, Pallas kernels for 0% -> 0%
where the time goes in v11:
time: 567 us; the launch traced here: 558 us
  waiting for transfers between devices  368 us (65%)
  matrix products  52 us (9%)
  local copies, waits for them, and re-layouts  45.9 us (8%)
  Pallas kernels  31.4 us (6%)
  other arithmetic  30.9 us (5%)
  between operations  15.4 us (3%)
  starting transfers between devices  13.9 us (2%)
    all_gather x1, waiting for transfers between devices, per_device(): branch_rows = lax.all_gather(branch_grad, 'tensor', axis=0, tiled=True)  63.3 us
    all_gather x1, waiting for transfers between devices, per_device(): ffn_rows = lax.all_gather(middle_low, 'tensor', axis=0, tiled=True)  62.3 us
    reduce_scatter x1, waiting for transfers between devices, per_device(): lax.psum_scatter(jnp.dot(hidden, down_weight, preferred_element_type=jnp....  59.2 us
    all_gather x1, waiting for transfers between devices, per_device(): mine = lax.all_gather(mine, 'tensor', axis=0, tiled=False)  56.8 us
    ppermute x9, waiting for transfers between devices, dp_halve(): got = lax.ppermute(give, 'dp', [(i, i ^ 1 << step) for i in range(dp_size)])  37.8 us
    reduce_scatter x1, waiting for transfers between devices, per_device(): lax.psum_scatter(grad_qkv_full.reshape(3 * width, width).astype(jnp.bfloa...  28.7 us
    all_gather x1, waiting for transfers between devices, per_device(): joined = lax.all_gather(joined, 'dp', axis=0, tiled=False)  21.9 us
    dot_general x5, matrix products, contract(): lax.dot_general(left, right, (((left_dim,), (right_dim,)), ((), ())), pre...  21.4 us
  transfers between devices with their start and end apart: 24, of which 19 were waited for; matrix products, arithmetic and copies ran while one was open for 8% of the time, Pallas kernels for 0%

profile of v11, /device:TPU:0, one launch (start us, length us, event | category | flops | bytes accessed | tf_op | source)
XLA Modules:
  0.0 557.9 jit_solution(16383434295163765799)
XLA Ops:
  7.3 1.3 slice_bitcast_fusion.2
  9.8 56.8 %all-gather.13.cloned.1.call-done = bf16[4,1544,192]{1,2,0:T(8,128)(2,1)} async-done(((bf16[1,1544,192]{1,2,0:T(8,128)(2,1)}), bf16[4,1544,192]{1,2,0:T(8,128)(2,1)}) %all-gather.13.cloned.1.call-update) | async-done | bytes 2371600 | tf_op jit(solution)/shard_map/all_gather | solution.py:192
  67.2 4.6 collective-permute-done
  71.8 4.4 broadcast_select_fusion
  80.8 2.1 add_convert_fusion.1
  84.0 13.0 %shard_map.254 = bf16[512,768]{1,0:T(8,128)(2,1)} custom-call(s32[1]{0:T(128)} %dynamic_slice.57.len_ref, bf16[512,768]{1,0:T(8,128)(2,1)} %copy.74.q_ref, bf16[512,768]{1,0:T(8,128)(2,1)} %copy.75.k_ref, bf16[512,768]{1,0:T(8,128)(2,1)} %copy.76.v_ref), custom_call_target="tpu_custom_call" | custom-call | flops 805306368 | bytes 3145728 | tf_op jit(solution)/shard_map/pallas_call | solution.py:82
  97.0 1.4 copy.77
  98.5 2.4 fusion.49
  101.6 1.2 fusion.14
  102.9 62.3 %all-gather.9.cloned.1.call-done = bf16[2048,768]{1,0:T(8,128)(2,1)} async-done(((bf16[512,768]{1,0:T(8,128)(2,1)}), bf16[2048,768]{1,0:T(8,128)(2,1)}) %all-gather.9.cloned.1.call-update) | async-done | bytes 3145744 | tf_op jit(solution)/shard_map/all_gather | solution.py:226
  165.2 6.7 %multiply_convert_fusion = (bf16[2048,768]{1,0:T(8,128)(2,1)S(1)}, f32[2048,768]{1,0:T(8,128)}) fusion(f32[768]{0:T(1024)S(1)} %convert_element_type.161, bf16[2048,768]{1,0:T(8,128)(2,1)} %all-gather.9.cloned.1.call-done, bf16[768,768]{1,0:T(8,128)(2,1)S(1)} %copy-done), kind=kOutput, calls=%fused_computation.8 | convolution fusion | flops 2425356288 | bytes 13765632 | tf_op jit(solution)/shard_map/dot_general | solution.py:227
  171.9 1.7 copy-done.35
  173.6 4.0 convolution_convert_fusion.1
  177.7 59.2 %reduce-scatter.5.cloned.1.call-done = bf16[512,768]{1,0:T(8,128)(2,1)} async-done(((bf16[2048,768]{1,0:T(8,128)(2,1)}), bf16[512,768]{1,0:T(8,128)(2,1)}) %reduce-scatter.5.cloned.1.call-update) | async-done | bytes 786448 | tf_op jit(solution)/shard_map/reduce_scatter | solution.py:230
  236.8 1.7 fusion.46
  240.5 1.6 fusion.45
  244.5 63.3 %all-gather.11.cloned.1.call-done = bf16[2048,768]{1,0:T(8,128)(2,1)} async-done(((bf16[512,768]{1,0:T(8,128)(2,1)}), bf16[2048,768]{1,0:T(8,128)(2,1)}) %all-gather.11.cloned.1.call-update) | async-done | bytes 3145744 | tf_op jit(solution)/shard_map/all_gather | solution.py:242
  307.8 7.0 %convert_reduce_fusion = (f32[768]{0:T(1024)S(1)}, bf16[2048,768]{1,0:T(8,128)(2,1)S(1)}) fusion(f32[2048,768]{1,0:T(8,128)} %get-tuple-element.125, f32[768]{0:T(1024)S(1)} %convert_element_type.161, bf16[2048,768]{1,0:T(8,128)(2,1)} %all-gather.11.cloned.1.call-done, bf16[768,768]{1,0:T(8,128)(2,1)} %param.26), kind=kOutput, calls=%fused_computation.7 | convolution fusion | flops 2436365568 | bytes 13768704 | tf_op jit(solution)/shard_map/dot_general | solution.py:31
  314.8 1.7 copy-done.36
  316.5 4.0 convolution_convert_fusion
  320.6 5.7 %fusion.51 = f32[768,768]{1,0:T(8,128)S(1)} fusion(bf16[2048,768]{1,0:T(8,128)(2,1)} %copy-done.35, bf16[2048,768]{1,0:T(8,128)(2,1)} %all-gather.11.cloned.1.call-done), kind=kOutput, calls=%fused_computation.160 | convolution fusion | flops 2415919104 | bytes 8650752 | tf_op jit(solution)/shard_map/dot_general | solution.py:31
  326.3 2.7 fusion.50
  329.1 1.3 constant_dynamic-slice_fusion.2
  331.4 2.5 collective-permute-done.1
  333.9 1.8 dynamic-slice_add_fusion.1
  335.7 1.5 collective-permute-start.2
  337.2 1.5 dynamic-slice_add_fusion
  341.1 11.0 %collective-permute-done.2 = f32[192,768]{1,0:T(8,128)} collective-permute-done((f32[192,768]{1,0:T(8,128)S(1)}, f32[192,768]{1,0:T(8,128)}, u32[]{:S(2)}, u32[]{:S(2)}) %collective-permute-start.2) | collective-permute-done | bytes 589856 | tf_op jit(solution)/shard_map/ppermute | solution.py:134
  353.9 1.5 collective-permute-start.3
  355.4 8.5 %collective-permute-done.5 = f32[192,768]{1,0:T(8,128)} collective-permute-done((f32[192,768]{1,0:T(8,128)}, f32[192,768]{1,0:T(8,128)}, u32[]{:S(2)}, u32[]{:S(2)}) %collective-permute-start.5) | collective-permute-done | bytes 589856 | tf_op jit(solution)/shard_map/ppermute | solution.py:134
  365.7 1.5 collective-permute-start.6
  367.2 2.4 slice.151
  370.3 3.9 collective-permute-done.6
  374.8 4.9 reduce-scatter.7.cloned.1.call-done
  379.7 1.9 convert_add_fusion
  383.2 1.6 copy-done.15
  386.8 18.4 %shard_map.255 = bf16[3,512,768]{2,1,0:T(8,128)(2,1)} custom-call(s32[1]{0:T(128)} %dynamic_slice.57.len_ref, bf16[512,768]{1,0:T(8,128)(2,1)} %copy.74.q_ref, bf16[512,768]{1,0:T(8,128)(2,1)} %copy.75.k_ref, bf16[512,768]{1,0:T(8,128)(2,1)} %copy.76.v_ref, bf16[512,768]{1,0:T(8,128)(2,1)} %copy.81.grad_ref), custom_call_target="tpu_custom_call" | custom-call | flops 2013265920 | bytes 5505024 | tf_op jit(solution)/shard_map/pallas_call | solution.py:102
  405.2 5.5 convolution_convert_fusion.2
  411.8 1.9 fusion.13
  414.2 1.8 collective-permute-done.7
  417.3 1.6 collective-permute-start.8
  419.1 7.3 %collective-permute-done.8 = bf16[192,768]{1,0:T(8,128)(2,1)S(1)} collective-permute-done((bf16[192,768]{1,0:T(8,128)(2,1)S(1)}, bf16[192,768]{1,0:T(8,128)(2,1)S(1)}, u32[]{:S(2)}, u32[]{:S(2)}) %collective-permute-start.8) | collective-permute-done | bytes 294944 | tf_op jit(solution)/shard_map/ppermute | solution.py:134
  426.5 1.5 collective-permute-start.9
  428.8 1.5 collective-permute-start.13
  430.3 3.0 collective-permute-done.9
  433.3 28.7 %reduce-scatter.9.cloned.1.call-done = bf16[288,768]{1,0:T(8,128)(2,1)} async-done(((bf16[2304,768]{1,0:T(8,128)(2,1)}), bf16[288,768]{1,0:T(8,128)(2,1)}) %reduce-scatter.9.cloned.1.call-update) | async-done | bytes 442384 | tf_op jit(solution)/shard_map/reduce_scatter | solution.py:320
  463.1 1.7 copy.86
  465.2 1.5 collective-permute-start.11
  467.4 7.7 %collective-permute-done.11 = bf16[192,768]{1,0:T(8,128)(2,1)S(1)} collective-permute-done((bf16[192,768]{1,0:T(8,128)(2,1)S(1)}, bf16[192,768]{1,0:T(8,128)(2,1)S(1)}, u32[]{:S(2)}, u32[]{:S(2)}) %collective-permute-start.11) | collective-permute-done | bytes 294944 | tf_op jit(solution)/shard_map/ppermute | solution.py:149
  475.4 4.8 collective-permute-done.14
  480.6 1.6 maximum_convert_fusion
  482.6 1.6 maximum_convert_fusion.1
  484.2 16.2 %reduce-scatter.11.cloned.1.call-done = f32[1,416,192]{1,2,0:T(8,128)} async-done(((f32[4,416,192]{1,2,0:T(8,128)}), f32[1,416,192]{1,2,0:T(8,128)}) %reduce-scatter.11.cloned.1.call-update) | async-done | bytes 319504 | tf_op jit(solution)/shard_map/reduce_scatter | solution.py:327
  500.4 1.3 fusion.47
  501.8 1.5 copy.83
  503.8 2.1 fusion.22
  505.9 2.2 fusion.25
  508.2 3.3 fusion.11
  511.4 21.9 %all-gather.15.cloned.1.call-done = f32[8,416,192]{1,2,0:T(8,128)} async-done(((f32[1,416,192]{1,2,0:T(8,128)}), f32[8,416,192]{1,2,0:T(8,128)}) %all-gather.15.cloned.1.call-update) | async-done | bytes 2555920 | tf_op jit(solution)/shard_map/all_gather | solution.py:341
  533.4 3.3 slice.155
  536.6 2.2 copy.87
  538.8 1.8 copy.95
  540.6 1.2 slice_reduce_fusion
  548.1 1.5 slice_bitcast_fusion.3
  (198 shorter events, 39.8 us)
Async XLA Ops:
  7.2 158.0 %copy-start = (bf16[768,768]{1,0:T(8,128)(2,1)S(1)}, bf16[768,768]{1,0:T(8,128)(2,1)}, u32[]{:S(2)}) copy-start(bf16[768,768]{1,0:T(8,128)(2,1)} %param.24) | copy-start | bytes 3538948
  7.2 1.4 copy-start.28
  7.2 1.6 copy-start.18
  7.2 59.4 %all-gather.13.cloned.1.call-start = ((), (), s32[]{:S(2)}) async-start(), calls=%async_computation.10 | async-start | bytes 3194880 | tf_op jit(solution)/shard_map/all_gather | solution.py:192
  8.6 58.0 %copy-start.34 = (s32[4]{0:T(128)S(1)}, s32[4]{0:T(128)}, u32[]{:S(2)}) copy-start(s32[4]{0:T(128)} %param.17) | copy-start | bytes 52
  9.8 155.4 %all-gather.9.cloned.1.call-start = ((), (), s32[]{:S(2)}) async-start(), calls=%async_computation.4 | async-start | bytes 3932160 | tf_op jit(solution)/shard_map/all_gather | solution.py:226
  66.6 5.2 collective-permute-start
  67.2 9.3 %copy-start.31 = (bf16[512,768]{1,0:T(8,128)(2,1)S(1)}, bf16[512,768]{1,0:T(8,128)(2,1)}, u32[]{:S(2)}) copy-start(bf16[512,768]{1,0:T(8,128)(2,1)} %param.15) | copy-start | bytes 2359300
  76.2 1.4 copy-start.9
  97.0 1.4 copy-start.33
  100.9 0.7 copy-start.19
  100.9 0.7 copy-start.20
  101.6 1.3 copy-start.27
  102.8 134.0 %reduce-scatter.5.cloned.1.call-start = ((), (), s32[]{:S(2)}) async-start(), calls=%async_computation.5 | async-start | bytes 3932160 | tf_op jit(solution)/shard_map/reduce_scatter | solution.py:230
  165.2 8.4 %copy-start.30 = (bf16[768,768]{1,0:T(8,128)(2,1)S(1)}, bf16[768,768]{1,0:T(8,128)(2,1)}, u32[]{:S(2)}) copy-start(bf16[768,768]{1,0:T(8,128)(2,1)} %param.26) | copy-start | bytes 3538948
  171.9 1.7 copy-start.35
  177.6 59.2 %copy-start.25 = (f32[768]{0:T(1024)S(1)}, f32[768]{0:T(1024)}, u32[]{:S(2)}) copy-start(f32[768]{0:T(1024)} %param.27) | copy-start | bytes 9220
  177.6 130.2 %all-gather.11.cloned.1.call-start = ((), (), s32[]{:S(2)}) async-start(), calls=%async_computation.6 | async-start | bytes 3932160 | tf_op jit(solution)/shard_map/all_gather | solution.py:242
  238.6 1.1 copy-start.11
  238.6 1.1 copy-start.21
  238.9 1.5 copy-start.26
  242.1 1.1 copy-start.2
  244.3 135.4 %reduce-scatter.7.cloned.1.call-start = ((), (), s32[]{:S(2)}) async-start(), calls=%async_computation.7 | async-start | bytes 3932160 | tf_op jit(solution)/shard_map/reduce_scatter | solution.py:254
  314.8 1.7 copy-start.36
  320.5 141.5 %reduce-scatter.9.cloned.1.call-start = ((), (), s32[]{:S(2)}) async-start(), calls=%async_computation.8 | async-start | bytes 3981312 | tf_op jit(solution)/shard_map/reduce_scatter | solution.py:320
  320.5 5.7 %copy-start.29 = (bf16[2048,768]{1,0:T(8,128)(2,1)S(1)}, bf16[2048,768]{1,0:T(8,128)(2,1)}, u32[]{:S(2)}) copy-start(bf16[2048,768]{1,0:T(8,128)(2,1)} %all-gather.9.cloned.1.call-done) | copy-start | bytes 9437188
  320.6 5.7 %copy-start.37 = (bf16[2048,768]{1,0:T(8,128)(2,1)S(1)}, bf16[2048,768]{1,0:T(8,128)(2,1)}, u32[]{:S(2)}) copy-start(bf16[2048,768]{1,0:T(8,128)(2,1)} %copy-done.36) | copy-start | bytes 9437188
  326.3 2.8 copy-start.12
  329.1 1.8 copy-start.14
  330.9 3.0 collective-permute-start.1
  330.9 6.3 %collective-permute-start.4 = (f32[384,768]{1,0:T(8,128)}, f32[384,768]{1,0:T(8,128)}, u32[]{:S(2)}, u32[]{:S(2)}) collective-permute-start(f32[384,768]{1,0:T(8,128)} %get-tuple-element.128), channel_id=1, source_target_pairs={{0,4},{4,0},{8,12},{12,8},{16,20},{20,16},{24,28},{28,24},{1,5},{5... | collective-permute-start | bytes 3538952 | tf_op jit(solution)/shard_map/ppermute | solution.py:134
  331.4 5.8 %copy-start.13 = (f32[768,768]{1,0:T(8,128)S(1)}, f32[768,768]{1,0:T(8,128)}, u32[]{:S(2)}) copy-start(f32[768,768]{1,0:T(8,128)} %copy-done.12) | copy-start | bytes 7077892
  335.7 16.4 %collective-permute-start.2 = (f32[192,768]{1,0:T(8,128)S(1)}, f32[192,768]{1,0:T(8,128)}, u32[]{:S(2)}, u32[]{:S(2)}) collective-permute-start(f32[192,768]{1,0:T(8,128)S(1)} %constant_dynamic-slice_fusion.4), channel_id=1, source_target_pairs={{0,8},{4,12},{8,0},{12,4},{16,24},{20,28},{24,16},{28,20},{1,9},{5... | collective-permute-start | bytes 1769480 | tf_op jit(solution)/shard_map/ppermute | solution.py:134
  338.7 1.0 copy-start.7
  340.5 23.3 %collective-permute-start.5 = (f32[192,768]{1,0:T(8,128)}, f32[192,768]{1,0:T(8,128)}, u32[]{:S(2)}, u32[]{:S(2)}) collective-permute-start(f32[192,768]{1,0:T(8,128)} %constant_dynamic-slice_fusion.1), channel_id=1, source_target_pairs={{0,8},{4,12},{8,0},{12,4},{16,24},{20,28},{24,16},{28,20},{1,9},{5... | collective-permute-start | bytes 1769480 | tf_op jit(solution)/shard_map/ppermute | solution.py:134
  341.1 22.8 %copy-start.8 = (f32[384,768]{1,0:T(8,128)S(1)}, f32[384,768]{1,0:T(8,128)}, u32[]{:S(2)}) copy-start(f32[384,768]{1,0:T(8,128)} %copy-done.7) | copy-start | bytes 3538948
  353.9 15.6 %collective-permute-start.3 = (f32[96,768]{1,0:T(8,128)}, f32[96,768]{1,0:T(8,128)S(1)}, u32[]{:S(2)}, u32[]{:S(2)}) collective-permute-start(f32[96,768]{1,0:T(8,128)} %constant_dynamic-slice_fusion.3), channel_id=1, source_target_pairs={{0,16},{4,20},{8,24},{12,28},{16,0},{20,4},{24,8},{28,12},{1,17},{... | collective-permute-start | bytes 884744 | tf_op jit(solution)/shard_map/ppermute | solution.py:134
  365.7 8.4 %collective-permute-start.6 = (f32[96,768]{1,0:T(8,128)}, f32[96,768]{1,0:T(8,128)S(1)}, u32[]{:S(2)}, u32[]{:S(2)}) collective-permute-start(f32[96,768]{1,0:T(8,128)} %constant_dynamic-slice_fusion), channel_id=1, source_target_pairs={{0,16},{4,20},{8,24},{12,28},{16,0},{20,4},{24,8},{28,12},{1,17},{... | collective-permute-start | bytes 884744 | tf_op jit(solution)/shard_map/ppermute | solution.py:134
  382.9 2.7 copy-start.5
  382.9 1.8 copy-start.15
  382.9 2.6 copy-start.23
  386.8 18.4 %copy-start.32 = (bf16[512,768]{1,0:T(8,128)(2,1)S(1)}, bf16[512,768]{1,0:T(8,128)(2,1)}, u32[]{:S(2)}) copy-start(bf16[512,768]{1,0:T(8,128)(2,1)} %param.15) | copy-start | bytes 2359300
  410.7 89.7 %reduce-scatter.11.cloned.1.call-start = ((), (), s32[]{:S(2)}) async-start(), calls=%async_computation.9 | async-start | bytes 1966080 | tf_op jit(solution)/shard_map/reduce_scatter | solution.py:327
  413.8 2.2 collective-permute-start.7
  414.2 4.7 copy-start.22
  414.2 4.7 copy-start.3
  417.3 9.1 %collective-permute-start.8 = (bf16[192,768]{1,0:T(8,128)(2,1)S(1)}, bf16[192,768]{1,0:T(8,128)(2,1)S(1)}, u32[]{:S(2)}, u32[]{:S(2)}) collective-permute-start(bf16[192,768]{1,0:T(8,128)(2,1)S(1)} %dynamic-slice_convert_fusion.1), channel_id=1, source_target_pairs={{0,8},{4,12},{8,0},{12,4},{16,24},{20,28},{24,16},{28,20},{1,9},{5... | collective-permute-start | bytes 884744 | tf_op jit(solution)/shard_map/ppermute | solution.py:134
  418.9 9.3 %copy-start.17 = (bf16[96,768]{1,0:T(8,128)(2,1)S(1)}, bf16[96,768]{1,0:T(8,128)(2,1)}, u32[]{:S(2)}) copy-start(bf16[96,768]{1,0:T(8,128)(2,1)} %dynamic-slice_add_fusion.5) | copy-start | bytes 442372
  418.9 9.9 %copy-start.16 = (bf16[96,768]{1,0:T(8,128)(2,1)S(1)}, bf16[96,768]{1,0:T(8,128)(2,1)}, u32[]{:S(2)}) copy-start(bf16[96,768]{1,0:T(8,128)(2,1)} %dynamic-slice_add_fusion.4) | copy-start | bytes 442372
  426.5 6.8 %collective-permute-start.9 = (bf16[96,768]{1,0:T(8,128)(2,1)S(1)}, bf16[96,768]{1,0:T(8,128)(2,1)S(1)}, u32[]{:S(2)}, u32[]{:S(2)}) collective-permute-start(bf16[96,768]{1,0:T(8,128)(2,1)S(1)} %dynamic-slice_convert_fusion.2), channel_id=1, source_target_pairs={{0,16},{4,20},{8,24},{12,28},{16,0},{20,4},{24,8},{28,12},{1,17},{... | collective-permute-start | bytes 442376 | tf_op jit(solution)/shard_map/ppermute | solution.py:134
  428.2 37.0 %collective-permute-start.10 = (bf16[96,768]{1,0:T(8,128)(2,1)S(1)}, bf16[96,768]{1,0:T(8,128)(2,1)S(1)}, u32[]{:S(2)}, u32[]{:S(2)}) collective-permute-start(bf16[96,768]{1,0:T(8,128)(2,1)S(1)} %copy-done.17), channel_id=1, source_target_pairs={{0,16},{4,20},{8,24},{12,28},{16,0},{20,4},{24,8},{28,12},{1,17},{... | collective-permute-start | bytes 442376 | tf_op jit(solution)/shard_map/ppermute | solution.py:149
  428.8 38.0 %collective-permute-start.13 = (bf16[96,768]{1,0:T(8,128)(2,1)S(1)}, bf16[96,768]{1,0:T(8,128)(2,1)S(1)}, u32[]{:S(2)}, u32[]{:S(2)}) collective-permute-start(bf16[96,768]{1,0:T(8,128)(2,1)S(1)} %copy-done.16), channel_id=1, source_target_pairs={{0,16},{4,20},{8,24},{12,28},{16,0},{20,4},{24,8},{28,12},{1,17},{... | collective-permute-start | bytes 442376 | tf_op jit(solution)/shard_map/ppermute | solution.py:149
  464.8 68.6 %all-gather.15.cloned.1.call-start = ((), (), s32[]{:S(2)}) async-start(), calls=%async_computation.11 | async-start | bytes 3538944 | tf_op jit(solution)/shard_map/all_gather | solution.py:341
  465.2 9.9 %collective-permute-start.11 = (bf16[192,768]{1,0:T(8,128)(2,1)S(1)}, bf16[192,768]{1,0:T(8,128)(2,1)S(1)}, u32[]{:S(2)}, u32[]{:S(2)}) collective-permute-start(bf16[192,768]{1,0:T(8,128)(2,1)S(1)} %pad_maximum_fusion.3), channel_id=1, source_target_pairs={{0,8},{4,12},{8,0},{12,4},{16,24},{20,28},{24,16},{28,20},{1,9},{5... | collective-permute-start | bytes 884744 | tf_op jit(solution)/shard_map/ppermute | solution.py:149
  466.8 13.4 %collective-permute-start.14 = (bf16[192,768]{1,0:T(8,128)(2,1)S(1)}, bf16[192,768]{1,0:T(8,128)(2,1)S(1)}, u32[]{:S(2)}, u32[]{:S(2)}) collective-permute-start(bf16[192,768]{1,0:T(8,128)(2,1)S(1)} %pad_maximum_fusion.4), channel_id=1, source_target_pairs={{0,8},{4,12},{8,0},{12,4},{16,24},{20,28},{24,16},{28,20},{1,9},{5... | collective-permute-start | bytes 884744 | tf_op jit(solution)/shard_map/ppermute | solution.py:149
  475.3 5.1 collective-permute-start.12
  480.3 2.1 collective-permute-start.15
  482.6 17.8 %copy-start.4 = (bf16[3,512,768]{2,1,0:T(8,128)(2,1)S(1)}, bf16[3,512,768]{2,1,0:T(8,128)(2,1)}, u32[]{:S(2)}) copy-start(bf16[3,512,768]{2,1,0:T(8,128)(2,1)} %shard_map.255) | copy-start | bytes 7077892
  501.8 1.5 copy-start.10
  505.9 2.2 copy-start.6
  505.9 2.2 copy-start.24
  546.5 4.0 copy-start.1
Sparse Core Ops, SparseCore 0:
  10.2 56.3 all-gather.12
  102.9 62.2 all-gather.8
  177.8 59.0 reduce-scatter.4
  244.4 63.3 all-gather.10
  320.6 59.0 reduce-scatter.6
  410.8 51.0 reduce-scatter.8
  464.9 35.4 reduce-scatter.10
  502.3 31.0 all-gather.14

commit v12 on v11

--- a/solution.py
+++ b/solution.py
@@ -52,7 +52,11 @@
         ).astype(out_ref.dtype)
 
 
-def _bwd_kernel(len_ref, q_ref, k_ref, v_ref, grad_ref, out_ref, *, heads, factor):
+def _bwd_kernel(len_ref, q_ref, k_ref, v_ref, grad_ref, *rest, heads, factor):
+    if len(rest) == 3:
+        tokens_ref, out_ref, wgrad_ref = rest
+    else:
+        (out_ref,), tokens_ref = rest, None
     length = len_ref[pl.program_id(0)]
     for h in range(heads):
         cols = slice(h * HD, (h + 1) * HD)
@@ -74,6 +78,12 @@
         out_ref[2, :, cols] = lax.dot_general(
             probs.astype(jnp.bfloat16), g, (((0,), (0,)), ((), ())), preferred_element_type=jnp.float32
         ).astype(out_ref.dtype)
+    if tokens_ref is not None:
+        tokens = tokens_ref[...]
+        for t in range(3):
+            wgrad_ref[t] = lax.dot_general(
+                tokens, out_ref[t], (((0,), (0,)), ((), ())), preferred_element_type=jnp.float32
+            ).astype(wgrad_ref.dtype)
 
 
 def attention_forward(queries, keys, values, lengths, factor, pair=2):
@@ -96,24 +106,35 @@
     )(lengths, queries, keys, values)
 
 
-def attention_backward(queries, keys, values, context_grad, lengths, factor, pair=2):
+def attention_backward(queries, keys, values, context_grad, lengths, factor, tokens=None, pair=2):
     rows, width = queries.shape
     block = pl.BlockSpec((LEN, pair * HD), lambda p, i, n: (p, i))
+    grad_spec = pl.BlockSpec((3, LEN, pair * HD), lambda p, i, n: (0, p, i))
+    grad_shape = jax.ShapeDtypeStruct((3, rows, width), jnp.bfloat16)
+    operands = [lengths, queries, keys, values, context_grad]
+    in_specs = [block] * 4
+    out_specs, out_shape = grad_spec, grad_shape
+    if tokens is not None:
+        depth = tokens.shape[1]
+        operands.append(tokens)
+        in_specs.append(pl.BlockSpec((LEN, depth), lambda p, i, n: (p, 0)))
+        out_specs = [grad_spec, pl.BlockSpec((3, depth, pair * HD), lambda p, i, n: (0, 0, i))]
+        out_shape = [grad_shape, jax.ShapeDtypeStruct((3, depth, width), jnp.bfloat16)]
     return pl.pallas_call(
         functools.partial(_bwd_kernel, heads=pair, factor=factor),
-        out_shape=jax.ShapeDtypeStruct((3, rows, width), jnp.bfloat16),
+        out_shape=out_shape,
         grid_spec=pltpu.PrefetchScalarGridSpec(
             num_scalar_prefetch=1,
             grid=(rows // LEN, width // (pair * HD)),
-            in_specs=[block] * 4,
-            out_specs=pl.BlockSpec((3, LEN, pair * HD), lambda p, i, n: (0, p, i)),
+            in_specs=in_specs,
+            out_specs=out_specs,
         ),
         cost_estimate=pl.CostEstimate(
-            flops=10 * rows * LEN * width,
+            flops=16 * rows * LEN * width,
             transcendentals=rows * LEN * width // HD,
-            bytes_accessed=7 * rows * width * 2,
+            bytes_accessed=10 * rows * width * 2,
         ),
-    )(lengths, queries, keys, values, context_grad)
+    )(*operands)
 
 
 def dp_pow2(values, dp_size):
@@ -272,13 +293,18 @@
             early = dp_halve(early.astype(jnp.bfloat16), dp_size, jnp.float32)
         else:
             early = lax.psum_scatter(early, "dp", scatter_dimension=0, tiled=True)
-        proj_grad = attention_backward(
-            query_low, key_low, value_low, context_grad, own_lengths, factor
-        )
+        if passages == 1:
+            proj_grad, grad_qkv_low = attention_backward(
+                query_low, key_low, value_low, context_grad, own_lengths, factor, tokens
+            )
+        else:
+            proj_grad = attention_backward(
+                query_low, key_low, value_low, context_grad, own_lengths, factor
+            )
+            grad_qkv_low = jnp.einsum(
+                "rd,kre->kde", tokens, proj_grad, preferred_element_type=jnp.float32
+            ).astype(jnp.bfloat16)
         grad_bias_full = jnp.sum(proj_grad[0::2], axis=1, dtype=jnp.float32)
-        grad_qkv_full = jnp.einsum(
-            "rd,kre->kde", tokens, proj_grad, preferred_element_type=jnp.float32
-        )
 
         def back_project(grad, weight):
             return jnp.einsum(
@@ -318,7 +344,7 @@
         tail_rows = tail.shape[0]
         tail = jnp.pad(tail, ((0, -(-tail_rows // 8) * 8 - tail_rows), (0, 0)))
         late = lax.psum_scatter(
-            grad_qkv_full.reshape(3 * width, width).astype(jnp.bfloat16),
+            grad_qkv_low.reshape(3 * width, width),
             "dp",
             scatter_dimension=0,
             tiled=True,

time: 567 us -> 566 us (level)
    unnamed x84 -> x82, local copies, waits for them, and re-layouts: 11.8 us -> 11.8 us
where the time goes in v12:
time: 566 us; the launch traced here: 557 us
  waiting for transfers between devices  368 us (65%)
  matrix products  46.5 us (8%)
  local copies, waits for them, and re-layouts  45.9 us (8%)
  Pallas kernels  35.9 us (6%)
  other arithmetic  30.9 us (5%)
  between operations  15.1 us (3%)
  starting transfers between devices  14 us (2%)
    all_gather x1, waiting for transfers between devices, per_device(): branch_rows = lax.all_gather(branch_grad, 'tensor', axis=0, tiled=True)  63.1 us
    all_gather x1, waiting for transfers between devices, per_device(): ffn_rows = lax.all_gather(middle_low, 'tensor', axis=0, tiled=True)  62.3 us
    reduce_scatter x1, waiting for transfers between devices, per_device(): lax.psum_scatter(jnp.dot(hidden, down_weight, preferred_element_type=jnp....  59.2 us
    all_gather x1, waiting for transfers between devices, per_device(): mine = lax.all_gather(mine, 'tensor', axis=0, tiled=False)  56.8 us
    ppermute x9, waiting for transfers between devices, dp_halve(): got = lax.ppermute(give, 'dp', [(i, i ^ 1 << step) for i in range(dp_size)])  37.8 us
    reduce_scatter x1, waiting for transfers between devices, per_device(): lax.psum_scatter(grad_qkv_low.reshape(3 * width, width), 'dp', scatter_di...  28.7 us
    pallas_call x1, Pallas kernels, attention_backward(): pl.pallas_call(functools.partial(_bwd_kernel, heads=pair, factor=factor),...  22.9 us
    all_gather x1, waiting for transfers between devices, per_device(): joined = lax.all_gather(joined, 'dp', axis=0, tiled=False)  21.9 us
  transfers between devices with their start and end apart: 24, of which 19 were waited for; matrix products, arithmetic and copies ran while one was open for 8% of the time, Pallas kernels for 0%

profile of v12, /device:TPU:0, one launch (start us, length us, event | category | flops | bytes accessed | tf_op | source)
XLA Modules:
  0.0 556.7 jit_solution(7510926248128379599)
XLA Ops:
  7.3 1.3 slice_bitcast_fusion.2
  9.8 56.8 %all-gather.13.cloned.1.call-done = bf16[4,1544,192]{1,2,0:T(8,128)(2,1)} async-done(((bf16[1,1544,192]{1,2,0:T(8,128)(2,1)}), bf16[4,1544,192]{1,2,0:T(8,128)(2,1)}) %all-gather.13.cloned.1.call-update) | async-done | bytes 2371600 | tf_op jit(solution)/shard_map/all_gather | solution.py:213
  67.2 4.6 collective-permute-done
  71.8 4.4 broadcast_select_fusion
  79.6 1.2 copy.72.k_ref
  80.8 2.1 add_convert_fusion.1
  84.0 13.0 %shard_map.254 = bf16[512,768]{1,0:T(8,128)(2,1)} custom-call(s32[1]{0:T(128)} %dynamic_slice.57.len_ref, bf16[512,768]{1,0:T(8,128)(2,1)} %copy.71.q_ref, bf16[512,768]{1,0:T(8,128)(2,1)} %copy.72.k_ref, bf16[512,768]{1,0:T(8,128)(2,1)} %copy.73.v_ref), custom_call_target="tpu_custom_call" | custom-call | flops 805306368 | bytes 3145728 | tf_op jit(solution)/shard_map/pallas_call | solution.py:92
  97.0 1.4 copy.74
  98.5 2.4 fusion.48
  101.6 1.2 fusion.14
  102.9 62.3 %all-gather.9.cloned.1.call-done = bf16[2048,768]{1,0:T(8,128)(2,1)} async-done(((bf16[512,768]{1,0:T(8,128)(2,1)}), bf16[2048,768]{1,0:T(8,128)(2,1)}) %all-gather.9.cloned.1.call-update) | async-done | bytes 3145744 | tf_op jit(solution)/shard_map/all_gather | solution.py:247
  165.2 6.7 %multiply_convert_fusion = (bf16[2048,768]{1,0:T(8,128)(2,1)S(1)}, f32[2048,768]{1,0:T(8,128)}) fusion(f32[768]{0:T(1024)S(1)} %convert_element_type.152, bf16[2048,768]{1,0:T(8,128)(2,1)} %all-gather.9.cloned.1.call-done, bf16[768,768]{1,0:T(8,128)(2,1)S(1)} %copy-done), kind=kOutput, calls=%fused_computation.8 | convolution fusion | flops 2425356288 | bytes 13765632 | tf_op jit(solution)/shard_map/dot_general | solution.py:248
  171.9 1.7 copy-done.34
  173.6 4.0 convolution_convert_fusion.1
  177.7 59.2 %reduce-scatter.5.cloned.1.call-done = bf16[512,768]{1,0:T(8,128)(2,1)} async-done(((bf16[2048,768]{1,0:T(8,128)(2,1)}), bf16[512,768]{1,0:T(8,128)(2,1)}) %reduce-scatter.5.cloned.1.call-update) | async-done | bytes 786448 | tf_op jit(solution)/shard_map/reduce_scatter | solution.py:251
  236.8 1.7 fusion.45
  240.5 1.6 fusion.44
  244.7 63.1 %all-gather.11.cloned.1.call-done = bf16[2048,768]{1,0:T(8,128)(2,1)} async-done(((bf16[512,768]{1,0:T(8,128)(2,1)}), bf16[2048,768]{1,0:T(8,128)(2,1)}) %all-gather.11.cloned.1.call-update) | async-done | bytes 3145744 | tf_op jit(solution)/shard_map/all_gather | solution.py:263
  307.8 7.0 %convert_reduce_fusion = (f32[768]{0:T(1024)S(1)}, bf16[2048,768]{1,0:T(8,128)(2,1)S(1)}) fusion(f32[2048,768]{1,0:T(8,128)} %get-tuple-element.129, f32[768]{0:T(1024)S(1)} %convert_element_type.152, bf16[2048,768]{1,0:T(8,128)(2,1)} %all-gather.11.cloned.1.call-done, bf16[768,768]{1,0:T(8,128)(2,1)} %param.26), kind=kOutput, calls=%fused_computation.7 | convolution fusion | flops 2436365568 | bytes 13768704 | tf_op jit(solution)/shard_map/dot_general | solution.py:31
  314.8 1.7 copy-done.35
  316.4 4.0 convolution_convert_fusion
  320.5 5.7 %fusion.50 = f32[768,768]{1,0:T(8,128)S(1)} fusion(bf16[2048,768]{1,0:T(8,128)(2,1)} %copy-done.34, bf16[2048,768]{1,0:T(8,128)(2,1)} %all-gather.11.cloned.1.call-done), kind=kOutput, calls=%fused_computation.158 | convolution fusion | flops 2415919104 | bytes 8650752 | tf_op jit(solution)/shard_map/dot_general | solution.py:31
  326.3 2.7 fusion.49
  329.1 1.3 constant_dynamic-slice_fusion.2
  331.4 2.5 collective-permute-done.1
  333.8 1.8 dynamic-slice_add_fusion.1
  335.7 1.6 collective-permute-start.2
  337.2 1.4 dynamic-slice_add_fusion
  341.1 11.0 %collective-permute-done.2 = f32[192,768]{1,0:T(8,128)} collective-permute-done((f32[192,768]{1,0:T(8,128)S(1)}, f32[192,768]{1,0:T(8,128)}, u32[]{:S(2)}, u32[]{:S(2)}) %collective-permute-start.2) | collective-permute-done | bytes 589856 | tf_op jit(solution)/shard_map/ppermute | solution.py:155
  353.9 1.5 collective-permute-start.3
  355.4 8.5 %collective-permute-done.5 = f32[192,768]{1,0:T(8,128)} collective-permute-done((f32[192,768]{1,0:T(8,128)}, f32[192,768]{1,0:T(8,128)}, u32[]{:S(2)}, u32[]{:S(2)}) %collective-permute-start.5) | collective-permute-done | bytes 589856 | tf_op jit(solution)/shard_map/ppermute | solution.py:155
  365.7 1.5 collective-permute-start.6
  367.2 2.4 slice.151
  370.2 3.9 collective-permute-done.6
  374.8 4.9 reduce-scatter.7.cloned.1.call-done
  379.7 1.9 convert_add_fusion
  383.1 1.6 copy-done.15
  386.8 22.9 %shard_map.255 = (bf16[3,512,768]{2,1,0:T(8,128)(2,1)}, bf16[3,768,768]{2,1,0:T(8,128)(2,1)}) custom-call(s32[1]{0:T(128)} %dynamic_slice.57.len_ref, bf16[512,768]{1,0:T(8,128)(2,1)} %copy.71.q_ref, bf16[512,768]{1,0:T(8,128)(2,1)} %copy.72.k_ref, bf16[512,768]{1,0:T(8,128)(2,1)} %copy.73.v_ref, bf16[512,768]{1,0:T(8,128)(2,1)} %copy.78.grad_ref, ...), custom_call_target="tpu_custom_call" | custom-call | flops 3221225472 | bytes 7864320 | tf_op jit(solution)/shard_map/pallas_call | solution.py:123
  411.0 1.9 fusion.13
  413.3 1.8 collective-permute-done.7
  416.4 1.6 collective-permute-start.8
  418.3 7.3 %collective-permute-done.8 = bf16[192,768]{1,0:T(8,128)(2,1)S(1)} collective-permute-done((bf16[192,768]{1,0:T(8,128)(2,1)S(1)}, bf16[192,768]{1,0:T(8,128)(2,1)S(1)}, u32[]{:S(2)}, u32[]{:S(2)}) %collective-permute-start.8) | collective-permute-done | bytes 294944 | tf_op jit(solution)/shard_map/ppermute | solution.py:155
  425.6 1.6 collective-permute-start.9
  427.9 1.5 collective-permute-start.13
  429.4 2.9 collective-permute-done.9
  432.4 28.7 %reduce-scatter.9.cloned.1.call-done = bf16[288,768]{1,0:T(8,128)(2,1)} async-done(((bf16[2304,768]{1,0:T(8,128)(2,1)}), bf16[288,768]{1,0:T(8,128)(2,1)}) %reduce-scatter.9.cloned.1.call-update) | async-done | bytes 442384 | tf_op jit(solution)/shard_map/reduce_scatter | solution.py:346
  462.3 1.7 copy.82
  464.1 1.6 collective-permute-start.11
  466.3 7.7 %collective-permute-done.11 = bf16[192,768]{1,0:T(8,128)(2,1)S(1)} collective-permute-done((bf16[192,768]{1,0:T(8,128)(2,1)S(1)}, bf16[192,768]{1,0:T(8,128)(2,1)S(1)}, u32[]{:S(2)}, u32[]{:S(2)}) %collective-permute-start.11) | collective-permute-done | bytes 294944 | tf_op jit(solution)/shard_map/ppermute | solution.py:170
  474.3 4.8 collective-permute-done.14
  479.5 1.6 maximum_convert_fusion
  481.5 1.6 maximum_convert_fusion.1
  483.1 16.5 %reduce-scatter.11.cloned.1.call-done = f32[1,416,192]{1,2,0:T(8,128)} async-done(((f32[4,416,192]{1,2,0:T(8,128)}), f32[1,416,192]{1,2,0:T(8,128)}) %reduce-scatter.11.cloned.1.call-update) | async-done | bytes 319504 | tf_op jit(solution)/shard_map/reduce_scatter | solution.py:353
  499.6 1.3 fusion.46
  500.9 1.5 copy.80
  503.0 2.1 fusion.22
  505.1 2.2 fusion.25
  507.3 3.3 fusion.11
  510.6 21.9 %all-gather.15.cloned.1.call-done = f32[8,416,192]{1,2,0:T(8,128)} async-done(((f32[1,416,192]{1,2,0:T(8,128)}), f32[8,416,192]{1,2,0:T(8,128)}) %all-gather.15.cloned.1.call-update) | async-done | bytes 2555920 | tf_op jit(solution)/shard_map/all_gather | solution.py:367
  532.5 3.3 slice.152
  535.8 2.2 copy.83
  538.0 1.8 copy.91
  539.8 1.2 slice_reduce_fusion
  547.2 1.5 slice_bitcast_fusion.3
  (195 shorter events, 38.6 us)
Async XLA Ops:
  7.2 158.0 %copy-start = (bf16[768,768]{1,0:T(8,128)(2,1)S(1)}, bf16[768,768]{1,0:T(8,128)(2,1)}, u32[]{:S(2)}) copy-start(bf16[768,768]{1,0:T(8,128)(2,1)} %param.24) | copy-start | bytes 3538948
  7.2 1.4 copy-start.28
  7.2 1.6 copy-start.18
  7.2 59.4 %all-gather.13.cloned.1.call-start = ((), (), s32[]{:S(2)}) async-start(), calls=%async_computation.10 | async-start | bytes 3194880 | tf_op jit(solution)/shard_map/all_gather | solution.py:213
  8.6 58.0 %copy-start.33 = (s32[4]{0:T(128)S(1)}, s32[4]{0:T(128)}, u32[]{:S(2)}) copy-start(s32[4]{0:T(128)} %param.17) | copy-start | bytes 52
  9.8 155.4 %all-gather.9.cloned.1.call-start = ((), (), s32[]{:S(2)}) async-start(), calls=%async_computation.4 | async-start | bytes 3932160 | tf_op jit(solution)/shard_map/all_gather | solution.py:247
  66.6 5.2 collective-permute-start
  67.2 9.3 %copy-start.31 = (bf16[512,768]{1,0:T(8,128)(2,1)S(1)}, bf16[512,768]{1,0:T(8,128)(2,1)}, u32[]{:S(2)}) copy-start(bf16[512,768]{1,0:T(8,128)(2,1)} %rest_0_.1) | copy-start | bytes 2359300
  76.2 1.4 copy-start.9
  97.0 1.4 copy-start.32
  100.9 0.7 copy-start.19
  100.9 0.7 copy-start.20
  101.6 1.3 copy-start.27
  102.8 134.0 %reduce-scatter.5.cloned.1.call-start = ((), (), s32[]{:S(2)}) async-start(), calls=%async_computation.5 | async-start | bytes 3932160 | tf_op jit(solution)/shard_map/reduce_scatter | solution.py:251
  165.2 8.4 %copy-start.30 = (bf16[768,768]{1,0:T(8,128)(2,1)S(1)}, bf16[768,768]{1,0:T(8,128)(2,1)}, u32[]{:S(2)}) copy-start(bf16[768,768]{1,0:T(8,128)(2,1)} %param.26) | copy-start | bytes 3538948
  171.9 1.7 copy-start.34
  177.6 59.2 %copy-start.25 = (f32[768]{0:T(1024)S(1)}, f32[768]{0:T(1024)}, u32[]{:S(2)}) copy-start(f32[768]{0:T(1024)} %param.27) | copy-start | bytes 9220
  177.6 130.2 %all-gather.11.cloned.1.call-start = ((), (), s32[]{:S(2)}) async-start(), calls=%async_computation.6 | async-start | bytes 3932160 | tf_op jit(solution)/shard_map/all_gather | solution.py:263
  238.6 1.1 copy-start.11
  238.6 1.1 copy-start.21
  238.9 1.5 copy-start.26
  242.1 1.1 copy-start.2
  244.3 135.4 %reduce-scatter.7.cloned.1.call-start = ((), (), s32[]{:S(2)}) async-start(), calls=%async_computation.7 | async-start | bytes 3932160 | tf_op jit(solution)/shard_map/reduce_scatter | solution.py:275
  314.8 1.7 copy-start.35
  320.5 140.7 %reduce-scatter.9.cloned.1.call-start = ((), (), s32[]{:S(2)}) async-start(), calls=%async_computation.8 | async-start | bytes 3981312 | tf_op jit(solution)/shard_map/reduce_scatter | solution.py:346
  320.5 5.7 %copy-start.29 = (bf16[2048,768]{1,0:T(8,128)(2,1)S(1)}, bf16[2048,768]{1,0:T(8,128)(2,1)}, u32[]{:S(2)}) copy-start(bf16[2048,768]{1,0:T(8,128)(2,1)} %all-gather.9.cloned.1.call-done) | copy-start | bytes 9437188
  320.5 5.7 %copy-start.36 = (bf16[2048,768]{1,0:T(8,128)(2,1)S(1)}, bf16[2048,768]{1,0:T(8,128)(2,1)}, u32[]{:S(2)}) copy-start(bf16[2048,768]{1,0:T(8,128)(2,1)} %copy-done.35) | copy-start | bytes 9437188
  326.3 2.8 copy-start.12
  329.1 1.8 copy-start.14
  330.8 3.0 collective-permute-start.1
  330.9 6.4 %collective-permute-start.4 = (f32[384,768]{1,0:T(8,128)}, f32[384,768]{1,0:T(8,128)}, u32[]{:S(2)}, u32[]{:S(2)}) collective-permute-start(f32[384,768]{1,0:T(8,128)} %get-tuple-element.132), channel_id=1, source_target_pairs={{0,4},{4,0},{8,12},{12,8},{16,20},{20,16},{24,28},{28,24},{1,5},{5... | collective-permute-start | bytes 3538952 | tf_op jit(solution)/shard_map/ppermute | solution.py:155
  331.4 5.9 %copy-start.13 = (f32[768,768]{1,0:T(8,128)S(1)}, f32[768,768]{1,0:T(8,128)}, u32[]{:S(2)}) copy-start(f32[768,768]{1,0:T(8,128)} %copy-done.12) | copy-start | bytes 7077892
  335.7 16.4 %collective-permute-start.2 = (f32[192,768]{1,0:T(8,128)S(1)}, f32[192,768]{1,0:T(8,128)}, u32[]{:S(2)}, u32[]{:S(2)}) collective-permute-start(f32[192,768]{1,0:T(8,128)S(1)} %constant_dynamic-slice_fusion.4), channel_id=1, source_target_pairs={{0,8},{4,12},{8,0},{12,4},{16,24},{20,28},{24,16},{28,20},{1,9},{5... | collective-permute-start | bytes 1769480 | tf_op jit(solution)/shard_map/ppermute | solution.py:155
  338.7 1.0 copy-start.7
  340.5 23.3 %collective-permute-start.5 = (f32[192,768]{1,0:T(8,128)}, f32[192,768]{1,0:T(8,128)}, u32[]{:S(2)}, u32[]{:S(2)}) collective-permute-start(f32[192,768]{1,0:T(8,128)} %constant_dynamic-slice_fusion.1), channel_id=1, source_target_pairs={{0,8},{4,12},{8,0},{12,4},{16,24},{20,28},{24,16},{28,20},{1,9},{5... | collective-permute-start | bytes 1769480 | tf_op jit(solution)/shard_map/ppermute | solution.py:155
  341.1 22.8 %copy-start.8 = (f32[384,768]{1,0:T(8,128)S(1)}, f32[384,768]{1,0:T(8,128)}, u32[]{:S(2)}) copy-start(f32[384,768]{1,0:T(8,128)} %copy-done.7) | copy-start | bytes 3538948
  353.9 15.7 %collective-permute-start.3 = (f32[96,768]{1,0:T(8,128)}, f32[96,768]{1,0:T(8,128)S(1)}, u32[]{:S(2)}, u32[]{:S(2)}) collective-permute-start(f32[96,768]{1,0:T(8,128)} %constant_dynamic-slice_fusion.3), channel_id=1, source_target_pairs={{0,16},{4,20},{8,24},{12,28},{16,0},{20,4},{24,8},{28,12},{1,17},{... | collective-permute-start | bytes 884744 | tf_op jit(solution)/shard_map/ppermute | solution.py:155
  365.7 8.4 %collective-permute-start.6 = (f32[96,768]{1,0:T(8,128)}, f32[96,768]{1,0:T(8,128)S(1)}, u32[]{:S(2)}, u32[]{:S(2)}) collective-permute-start(f32[96,768]{1,0:T(8,128)} %constant_dynamic-slice_fusion), channel_id=1, source_target_pairs={{0,16},{4,20},{8,24},{12,28},{16,0},{20,4},{24,8},{28,12},{1,17},{... | collective-permute-start | bytes 884744 | tf_op jit(solution)/shard_map/ppermute | solution.py:155
  382.9 2.7 copy-start.5
  382.9 1.8 copy-start.15
  382.9 2.6 copy-start.23
  409.7 89.9 %reduce-scatter.11.cloned.1.call-start = ((), (), s32[]{:S(2)}) async-start(), calls=%async_computation.9 | async-start | bytes 1966080 | tf_op jit(solution)/shard_map/reduce_scatter | solution.py:353
  413.0 2.2 collective-permute-start.7
  413.3 4.6 copy-start.22
  413.3 4.7 copy-start.3
  416.4 9.1 %collective-permute-start.8 = (bf16[192,768]{1,0:T(8,128)(2,1)S(1)}, bf16[192,768]{1,0:T(8,128)(2,1)S(1)}, u32[]{:S(2)}, u32[]{:S(2)}) collective-permute-start(bf16[192,768]{1,0:T(8,128)(2,1)S(1)} %dynamic-slice_convert_fusion.1), channel_id=1, source_target_pairs={{0,8},{4,12},{8,0},{12,4},{16,24},{20,28},{24,16},{28,20},{1,9},{5... | collective-permute-start | bytes 884744 | tf_op jit(solution)/shard_map/ppermute | solution.py:155
  418.0 9.3 %copy-start.17 = (bf16[96,768]{1,0:T(8,128)(2,1)S(1)}, bf16[96,768]{1,0:T(8,128)(2,1)}, u32[]{:S(2)}) copy-start(bf16[96,768]{1,0:T(8,128)(2,1)} %dynamic-slice_add_fusion.5) | copy-start | bytes 442372
  418.0 9.9 %copy-start.16 = (bf16[96,768]{1,0:T(8,128)(2,1)S(1)}, bf16[96,768]{1,0:T(8,128)(2,1)}, u32[]{:S(2)}) copy-start(bf16[96,768]{1,0:T(8,128)(2,1)} %dynamic-slice_add_fusion.4) | copy-start | bytes 442372
  425.6 6.8 %collective-permute-start.9 = (bf16[96,768]{1,0:T(8,128)(2,1)S(1)}, bf16[96,768]{1,0:T(8,128)(2,1)S(1)}, u32[]{:S(2)}, u32[]{:S(2)}) collective-permute-start(bf16[96,768]{1,0:T(8,128)(2,1)S(1)} %dynamic-slice_convert_fusion.2), channel_id=1, source_target_pairs={{0,16},{4,20},{8,24},{12,28},{16,0},{20,4},{24,8},{28,12},{1,17},{... | collective-permute-start | bytes 442376 | tf_op jit(solution)/shard_map/ppermute | solution.py:155
  427.3 36.7 %collective-permute-start.10 = (bf16[96,768]{1,0:T(8,128)(2,1)S(1)}, bf16[96,768]{1,0:T(8,128)(2,1)S(1)}, u32[]{:S(2)}, u32[]{:S(2)}) collective-permute-start(bf16[96,768]{1,0:T(8,128)(2,1)S(1)} %copy-done.17), channel_id=1, source_target_pairs={{0,16},{4,20},{8,24},{12,28},{16,0},{20,4},{24,8},{28,12},{1,17},{... | collective-permute-start | bytes 442376 | tf_op jit(solution)/shard_map/ppermute | solution.py:170
  427.9 37.7 %collective-permute-start.13 = (bf16[96,768]{1,0:T(8,128)(2,1)S(1)}, bf16[96,768]{1,0:T(8,128)(2,1)S(1)}, u32[]{:S(2)}, u32[]{:S(2)}) collective-permute-start(bf16[96,768]{1,0:T(8,128)(2,1)S(1)} %copy-done.16), channel_id=1, source_target_pairs={{0,16},{4,20},{8,24},{12,28},{16,0},{20,4},{24,8},{28,12},{1,17},{... | collective-permute-start | bytes 442376 | tf_op jit(solution)/shard_map/ppermute | solution.py:170
  464.0 68.5 %all-gather.15.cloned.1.call-start = ((), (), s32[]{:S(2)}) async-start(), calls=%async_computation.11 | async-start | bytes 3538944 | tf_op jit(solution)/shard_map/all_gather | solution.py:367
  464.1 9.9 %collective-permute-start.11 = (bf16[192,768]{1,0:T(8,128)(2,1)S(1)}, bf16[192,768]{1,0:T(8,128)(2,1)S(1)}, u32[]{:S(2)}, u32[]{:S(2)}) collective-permute-start(bf16[192,768]{1,0:T(8,128)(2,1)S(1)} %pad_maximum_fusion.3), channel_id=1, source_target_pairs={{0,8},{4,12},{8,0},{12,4},{16,24},{20,28},{24,16},{28,20},{1,9},{5... | collective-permute-start | bytes 884744 | tf_op jit(solution)/shard_map/ppermute | solution.py:170
  465.7 13.4 %collective-permute-start.14 = (bf16[192,768]{1,0:T(8,128)(2,1)S(1)}, bf16[192,768]{1,0:T(8,128)(2,1)S(1)}, u32[]{:S(2)}, u32[]{:S(2)}) collective-permute-start(bf16[192,768]{1,0:T(8,128)(2,1)S(1)} %pad_maximum_fusion.4), channel_id=1, source_target_pairs={{0,8},{4,12},{8,0},{12,4},{16,24},{20,28},{24,16},{28,20},{1,9},{5... | collective-permute-start | bytes 884744 | tf_op jit(solution)/shard_map/ppermute | solution.py:170
  474.2 5.1 collective-permute-start.12
  479.2 2.1 collective-permute-start.15
  481.5 18.1 %copy-start.4 = (bf16[3,512,768]{2,1,0:T(8,128)(2,1)S(1)}, bf16[3,512,768]{2,1,0:T(8,128)(2,1)}, u32[]{:S(2)}) copy-start(bf16[3,512,768]{2,1,0:T(8,128)(2,1)} %get-tuple-element.23) | copy-start | bytes 7077892
  500.9 1.5 copy-start.10
  505.1 2.2 copy-start.6
  505.1 2.2 copy-start.24
  545.7 4.0 copy-start.1
Sparse Core Ops, SparseCore 0:
  10.2 56.3 all-gather.12
  102.9 62.2 all-gather.8
  177.8 59.0 reduce-scatter.4
  244.4 63.3 all-gather.10
  320.6 59.0 reduce-scatter.6
  409.8 51.2 reduce-scatter.8
  464.1 35.4 reduce-scatter.10
  501.5 31.0 all-gather.14

commit v13 on v12

--- a/solution.py
+++ b/solution.py
@@ -137,6 +137,32 @@
     )(*operands)
 
 
+def _tn_kernel(left_ref, right_ref, out_ref):
+    out_ref[...] = lax.dot_general(
+        left_ref[...], right_ref[...], (((0,), (0,)), ((), ())), preferred_element_type=jnp.float32
+    )
+
+
+def tn_matmul(left, right, tile=256):
+    depth, rows = left.shape
+    cols = right.shape[1]
+    return pl.pallas_call(
+        _tn_kernel,
+        out_shape=jax.ShapeDtypeStruct((rows, cols), jnp.float32),
+        grid=(rows // tile, cols // tile),
+        in_specs=[
+            pl.BlockSpec((depth, tile), lambda i, j: (0, i)),
+            pl.BlockSpec((depth, tile), lambda i, j: (0, j)),
+        ],
+        out_specs=pl.BlockSpec((tile, tile), lambda i, j: (i, j)),
+        cost_estimate=pl.CostEstimate(
+            flops=2 * depth * rows * cols,
+            transcendentals=0,
+            bytes_accessed=2 * depth * (rows + cols) + 4 * rows * cols,
+        ),
+    )(left, right)
+
+
 def dp_pow2(values, dp_size):
     steps = dp_size.bit_length() - 1
     return dp_size == 1 << steps and values.shape[0] % dp_size == 0
@@ -262,10 +288,10 @@
         grad_down_bias = jnp.sum(branch_grad, axis=0, dtype=jnp.float32)
         branch_rows = lax.all_gather(branch_grad, "tensor", axis=0, tiled=True)
         hidden_grad = contract(branch_rows, down_weight, 1, 1)
-        grad_down_weight = contract(hidden, branch_rows, 0, 0)
+        grad_down_weight = tn_matmul(hidden, branch_rows)
         pre_grad = (hidden_grad * gelu_slope).astype(jnp.bfloat16)
         grad_up_bias = jnp.sum(pre_grad, axis=0, dtype=jnp.float32)
-        grad_up_weight = contract(ffn_rows, pre_grad, 0, 0)
+        grad_up_weight = tn_matmul(ffn_rows, pre_grad)
         ffn_grads = (grad_up_weight, grad_down_weight)
         halved = all(dp_pow2(g, dp_size) for g in ffn_grads)
         if halved:

time: 566 us -> 566 us (level); the launches traced: 557 us -> 565 us
  Pallas kernels: 35.9 us -> 57.4 us
  matrix products: 46.5 us -> 38.1 us
    pallas_call x0 -> x2, Pallas kernels: none -> 21.5 us  [tn_matmul(): pl.pallas_call(_tn_kernel, out_shape=jax.ShapeDtypeStruct((rows, cols), j...]
    dot_general x5 -> x3, matrix products: 21.3 us -> 12.9 us  [contract(): lax.dot_general(left, right, (((left_dim,), (right_dim,)), ((), ())), pre...]
    unnamed x82 -> x74, local copies, waits for them, and re-layouts: 11.8 us -> 11.3 us
  transfers between devices with their start and end apart: 24 -> 24, of which waited for: 19 -> 18; matrix products, arithmetic and copies ran while one was open for 8% -> 7% of each run, Pallas kernels for 0% -> 4%
where the time goes in v13:
time: 566 us; the launch traced here: 565 us
  waiting for transfers between devices  363 us (64%)
  Pallas kernels  57.4 us (10%)
  local copies, waits for them, and re-layouts  46.8 us (8%)
  matrix products  38.1 us (7%)
  other arithmetic  31 us (5%)
  between operations  14.9 us (3%)
  starting transfers between devices  13.5 us (2%)
    all_gather x1, waiting for transfers between devices, per_device(): branch_rows = lax.all_gather(branch_grad, 'tensor', axis=0, tiled=True)  63.3 us
    all_gather x1, waiting for transfers between devices, per_device(): ffn_rows = lax.all_gather(middle_low, 'tensor', axis=0, tiled=True)  62.3 us
    reduce_scatter x1, waiting for transfers between devices, per_device(): lax.psum_scatter(jnp.dot(hidden, down_weight, preferred_element_type=jnp....  59.2 us
    all_gather x1, waiting for transfers between devices, per_device(): mine = lax.all_gather(mine, 'tensor', axis=0, tiled=False)  56.8 us
    ppermute x9, waiting for transfers between devices, dp_halve(): got = lax.ppermute(give, 'dp', [(i, i ^ 1 << step) for i in range(dp_size)])  39.3 us
    reduce_scatter x1, waiting for transfers between devices, per_device(): lax.psum_scatter(grad_qkv_low.reshape(3 * width, width), 'dp', scatter_di...  26.4 us
    pallas_call x1, Pallas kernels, attention_backward(): pl.pallas_call(functools.partial(_bwd_kernel, heads=pair, factor=factor),...  22.8 us
    all_gather x1, waiting for transfers between devices, per_device(): joined = lax.all_gather(joined, 'dp', axis=0, tiled=False)  21.9 us
  transfers between devices with their start and end apart: 24, of which 18 were waited for; matrix products, arithmetic and copies ran while one was open for 7% of the time, Pallas kernels for 4%

profile of v13, /device:TPU:0, one launch (start us, length us, event | category | flops | bytes accessed | tf_op | source)
XLA Modules:
  0.0 564.7 jit_solution(2974494327355119704)
XLA Ops:
  7.3 1.3 slice_bitcast_fusion.2
  9.8 56.8 %all-gather.13.cloned.1.call-done = bf16[4,1544,192]{1,2,0:T(8,128)(2,1)} async-done(((bf16[1,1544,192]{1,2,0:T(8,128)(2,1)}), bf16[4,1544,192]{1,2,0:T(8,128)(2,1)}) %all-gather.13.cloned.1.call-update) | async-done | bytes 2371600 | tf_op jit(solution)/shard_map/all_gather | solution.py:239
  67.2 4.6 collective-permute-done
  71.8 4.4 broadcast_select_fusion
  79.6 1.2 copy.72.k_ref
  80.8 2.1 add_convert_fusion.1
  84.0 13.1 %shard_map.254 = bf16[512,768]{1,0:T(8,128)(2,1)} custom-call(s32[1]{0:T(128)} %dynamic_slice.57.len_ref, bf16[512,768]{1,0:T(8,128)(2,1)} %copy.71.q_ref, bf16[512,768]{1,0:T(8,128)(2,1)} %copy.72.k_ref, bf16[512,768]{1,0:T(8,128)(2,1)} %copy.73.v_ref), custom_call_target="tpu_custom_call" | custom-call | flops 805306368 | bytes 3145728 | tf_op jit(solution)/shard_map/pallas_call | solution.py:92
  97.1 1.4 copy.74
  98.6 2.4 fusion.48
  101.7 1.2 fusion.14
  103.0 62.3 %all-gather.9.cloned.1.call-done.left_ref = bf16[2048,768]{1,0:T(8,128)(2,1)} async-done(((bf16[512,768]{1,0:T(8,128)(2,1)}), bf16[2048,768]{1,0:T(8,128)(2,1)}) %all-gather.9.cloned.1.call-update) | async-done | bytes 3145744 | tf_op jit(solution)/shard_map/all_gather | solution.py:273
  165.3 6.8 %multiply_convert_fusion = (bf16[2048,768]{1,0:T(8,128)(2,1)S(1)}, f32[2048,768]{1,0:T(8,128)}) fusion(f32[768]{0:T(1024)S(1)} %convert_element_type.152, bf16[2048,768]{1,0:T(8,128)(2,1)} %all-gather.9.cloned.1.call-done.left_ref, bf16[768,768]{1,0:T(8,128)(2,1)S(1)} %copy-done), kind=kOutput, calls=%fused_computation.8 | convolution fusion | flops 2425356288 | bytes 13765632 | tf_op jit(solution)/shard_map/dot_general | solution.py:274
  172.1 1.7 copy-done.31
  173.8 4.0 convolution_convert_fusion.1
  177.8 59.2 %reduce-scatter.5.cloned.1.call-done = bf16[512,768]{1,0:T(8,128)(2,1)} async-done(((bf16[2048,768]{1,0:T(8,128)(2,1)}), bf16[512,768]{1,0:T(8,128)(2,1)}) %reduce-scatter.5.cloned.1.call-update) | async-done | bytes 786448 | tf_op jit(solution)/shard_map/reduce_scatter | solution.py:277
  237.0 1.7 fusion.45
  240.6 1.6 fusion.44
  244.6 63.3 %all-gather.11.cloned.1.call-done.right_ref = bf16[2048,768]{1,0:T(8,128)(2,1)} async-done(((bf16[512,768]{1,0:T(8,128)(2,1)}), bf16[2048,768]{1,0:T(8,128)(2,1)}) %all-gather.11.cloned.1.call-update) | async-done | bytes 3145744 | tf_op jit(solution)/shard_map/all_gather | solution.py:289
  307.9 7.0 %convert_reduce_fusion = (f32[768]{0:T(1024)S(1)}, bf16[2048,768]{1,0:T(8,128)(2,1)S(1)}) fusion(f32[2048,768]{1,0:T(8,128)} %get-tuple-element.129, f32[768]{0:T(1024)S(1)} %convert_element_type.152, bf16[2048,768]{1,0:T(8,128)(2,1)} %all-gather.11.cloned.1.call-done.right_ref, bf16[768,768]{1,0:T(8,128)(2,1)} %param.26), kind=kOutput, calls=%fused_computation.7 | convolution fusion | flops 2436365568 | bytes 13768704 | tf_op jit(solution)/shard_map/dot_general | solution.py:31
  314.9 1.7 copy-done.32
  316.6 4.0 convolution_convert_fusion
  320.6 10.9 %shard_map.256 = f32[768,768]{1,0:T(8,128)} custom-call(bf16[2048,768]{1,0:T(8,128)(2,1)} %copy-done.31, bf16[2048,768]{1,0:T(8,128)(2,1)} %all-gather.11.cloned.1.call-done.right_ref), custom_call_target="tpu_custom_call" | custom-call | flops 2415919104 | bytes 8650752 | tf_op jit(solution)/shard_map/pallas_call | solution.py:149
  331.6 10.6 %shard_map.255 = f32[768,768]{1,0:T(8,128)} custom-call(bf16[2048,768]{1,0:T(8,128)(2,1)} %all-gather.9.cloned.1.call-done.left_ref, bf16[2048,768]{1,0:T(8,128)(2,1)} %copy-done.32), custom_call_target="tpu_custom_call" | custom-call | flops 2415919104 | bytes 8650752 | tf_op jit(solution)/shard_map/pallas_call | solution.py:149
  342.2 2.8 constant_dynamic-slice_fusion.2
  345.5 2.5 collective-permute-done.1
  347.9 1.8 dynamic-slice_add_fusion.1
  349.8 1.4 collective-permute-start.2
  351.2 1.5 dynamic-slice_add_fusion
  355.2 11.0 %collective-permute-done.2 = f32[192,768]{1,0:T(8,128)} collective-permute-done((f32[192,768]{1,0:T(8,128)S(1)}, f32[192,768]{1,0:T(8,128)}, u32[]{:S(2)}, u32[]{:S(2)}) %collective-permute-start.2) | collective-permute-done | bytes 589856 | tf_op jit(solution)/shard_map/ppermute | solution.py:181
  368.0 1.4 collective-permute-start.3
  369.4 8.6 %collective-permute-done.5 = f32[192,768]{1,0:T(8,128)} collective-permute-done((f32[192,768]{1,0:T(8,128)}, f32[192,768]{1,0:T(8,128)}, u32[]{:S(2)}, u32[]{:S(2)}) %collective-permute-start.5) | collective-permute-done | bytes 589856 | tf_op jit(solution)/shard_map/ppermute | solution.py:181
  379.8 1.3 collective-permute-start.6
  381.2 2.4 slice.151
  384.2 4.0 collective-permute-done.6
  388.9 1.9 convert_add_fusion
  392.4 1.6 copy-done.13
  396.1 22.8 %shard_map.257 = (bf16[3,512,768]{2,1,0:T(8,128)(2,1)}, bf16[3,768,768]{2,1,0:T(8,128)(2,1)}) custom-call(s32[1]{0:T(128)} %dynamic_slice.57.len_ref, bf16[512,768]{1,0:T(8,128)(2,1)} %copy.71.q_ref, bf16[512,768]{1,0:T(8,128)(2,1)} %copy.72.k_ref, bf16[512,768]{1,0:T(8,128)(2,1)} %copy.73.v_ref, bf16[512,768]{1,0:T(8,128)(2,1)} %copy.78.grad_ref, ...), custom_call_target="tpu_custom_call" | custom-call | flops 3221225472 | bytes 7864320 | tf_op jit(solution)/shard_map/pallas_call | solution.py:123
  420.2 1.9 fusion.13
  422.6 2.3 collective-permute-done.7
  425.0 1.2 convert_add_fusion.1
  426.2 1.5 collective-permute-start.8
  428.0 7.3 %collective-permute-done.8 = bf16[192,768]{1,0:T(8,128)(2,1)S(1)} collective-permute-done((bf16[192,768]{1,0:T(8,128)(2,1)S(1)}, bf16[192,768]{1,0:T(8,128)(2,1)S(1)}, u32[]{:S(2)}, u32[]{:S(2)}) %collective-permute-start.8) | collective-permute-done | bytes 294944 | tf_op jit(solution)/shard_map/ppermute | solution.py:181
  435.4 1.5 collective-permute-start.9
  437.7 1.5 collective-permute-start.13
  439.2 3.7 collective-permute-done.9
  442.9 26.4 %reduce-scatter.9.cloned.1.call-done = bf16[288,768]{1,0:T(8,128)(2,1)} async-done(((bf16[2304,768]{1,0:T(8,128)(2,1)}), bf16[288,768]{1,0:T(8,128)(2,1)}) %reduce-scatter.9.cloned.1.call-update) | async-done | bytes 442384 | tf_op jit(solution)/shard_map/reduce_scatter | solution.py:372
  470.4 1.6 copy.82
  472.2 1.5 collective-permute-start.11
  474.5 7.7 %collective-permute-done.11 = bf16[192,768]{1,0:T(8,128)(2,1)S(1)} collective-permute-done((bf16[192,768]{1,0:T(8,128)(2,1)S(1)}, bf16[192,768]{1,0:T(8,128)(2,1)S(1)}, u32[]{:S(2)}, u32[]{:S(2)}) %collective-permute-start.11) | collective-permute-done | bytes 294944 | tf_op jit(solution)/shard_map/ppermute | solution.py:196
  482.4 4.8 collective-permute-done.14
  487.7 1.6 maximum_convert_fusion
  489.6 1.6 maximum_convert_fusion.1
  491.2 16.5 %reduce-scatter.11.cloned.1.call-done = f32[1,416,192]{1,2,0:T(8,128)} async-done(((f32[4,416,192]{1,2,0:T(8,128)}), f32[1,416,192]{1,2,0:T(8,128)}) %reduce-scatter.11.cloned.1.call-update) | async-done | bytes 319504 | tf_op jit(solution)/shard_map/reduce_scatter | solution.py:379
  507.7 1.3 fusion.46
  509.0 1.5 copy.80
  511.1 2.1 fusion.22
  513.2 2.2 fusion.25
  515.4 3.3 fusion.11
  518.7 21.9 %all-gather.15.cloned.1.call-done = f32[8,416,192]{1,2,0:T(8,128)} async-done(((f32[1,416,192]{1,2,0:T(8,128)}), f32[8,416,192]{1,2,0:T(8,128)}) %all-gather.15.cloned.1.call-update) | async-done | bytes 2555920 | tf_op jit(solution)/shard_map/all_gather | solution.py:393
  540.6 3.2 slice.152
  543.9 2.2 copy.83
  546.1 1.8 copy.91
  547.9 1.2 slice_reduce_fusion
  555.3 1.5 slice_bitcast_fusion.3
  (187 shorter events, 37.1 us)
Async XLA Ops:
  7.2 158.1 %copy-start = (bf16[768,768]{1,0:T(8,128)(2,1)S(1)}, bf16[768,768]{1,0:T(8,128)(2,1)}, u32[]{:S(2)}) copy-start(bf16[768,768]{1,0:T(8,128)(2,1)} %param.24) | copy-start | bytes 3538948
  7.2 1.4 copy-start.26
  7.2 1.6 copy-start.16
  7.2 59.4 %all-gather.13.cloned.1.call-start = ((), (), s32[]{:S(2)}) async-start(), calls=%async_computation.10 | async-start | bytes 3194880 | tf_op jit(solution)/shard_map/all_gather | solution.py:239
  8.6 58.0 %copy-start.30 = (s32[4]{0:T(128)S(1)}, s32[4]{0:T(128)}, u32[]{:S(2)}) copy-start(s32[4]{0:T(128)} %param.17) | copy-start | bytes 52
  9.8 155.5 %all-gather.9.cloned.1.call-start = ((), (), s32[]{:S(2)}) async-start(), calls=%async_computation.4 | async-start | bytes 3932160 | tf_op jit(solution)/shard_map/all_gather | solution.py:273
  66.6 5.2 collective-permute-start
  67.2 9.3 %copy-start.28 = (bf16[512,768]{1,0:T(8,128)(2,1)S(1)}, bf16[512,768]{1,0:T(8,128)(2,1)}, u32[]{:S(2)}) copy-start(bf16[512,768]{1,0:T(8,128)(2,1)} %rest_0_.1) | copy-start | bytes 2359300
  76.2 1.4 copy-start.9
  97.1 1.4 copy-start.29
  101.0 0.7 copy-start.17
  101.0 0.7 copy-start.18
  101.7 1.3 copy-start.25
  102.9 134.1 %reduce-scatter.5.cloned.1.call-start = ((), (), s32[]{:S(2)}) async-start(), calls=%async_computation.5 | async-start | bytes 3932160 | tf_op jit(solution)/shard_map/reduce_scatter | solution.py:277
  165.3 8.5 %copy-start.27 = (bf16[768,768]{1,0:T(8,128)(2,1)S(1)}, bf16[768,768]{1,0:T(8,128)(2,1)}, u32[]{:S(2)}) copy-start(bf16[768,768]{1,0:T(8,128)(2,1)} %param.26) | copy-start | bytes 3538948
  172.1 1.7 copy-start.31
  177.7 59.2 %copy-start.23 = (f32[768]{0:T(1024)S(1)}, f32[768]{0:T(1024)}, u32[]{:S(2)}) copy-start(f32[768]{0:T(1024)} %param.27) | copy-start | bytes 9220
  177.8 130.2 %all-gather.11.cloned.1.call-start = ((), (), s32[]{:S(2)}) async-start(), calls=%async_computation.6 | async-start | bytes 3932160 | tf_op jit(solution)/shard_map/all_gather | solution.py:289
  238.7 1.1 copy-start.11
  238.7 1.1 copy-start.19
  239.0 1.5 copy-start.24
  242.2 1.1 copy-start.2
  244.4 144.5 %reduce-scatter.7.cloned.1.call-start = ((), (), s32[]{:S(2)}) async-start(), calls=%async_computation.7 | async-start | bytes 3932160 | tf_op jit(solution)/shard_map/reduce_scatter | solution.py:301
  314.9 1.7 copy-start.32
  320.6 148.7 %reduce-scatter.9.cloned.1.call-start = ((), (), s32[]{:S(2)}) async-start(), calls=%async_computation.8 | async-start | bytes 3981312 | tf_op jit(solution)/shard_map/reduce_scatter | solution.py:372
  345.0 3.0 collective-permute-start.1
  345.0 6.2 %collective-permute-start.4 = (f32[384,768]{1,0:T(8,128)}, f32[384,768]{1,0:T(8,128)}, u32[]{:S(2)}, u32[]{:S(2)}) collective-permute-start(f32[384,768]{1,0:T(8,128)} %get-tuple-element.132), channel_id=1, source_target_pairs={{0,4},{4,0},{8,12},{12,8},{16,20},{20,16},{24,28},{28,24},{1,5},{5... | collective-permute-start | bytes 3538952 | tf_op jit(solution)/shard_map/ppermute | solution.py:181
  345.5 5.7 %copy-start.12 = (f32[768,768]{1,0:T(8,128)S(1)}, f32[768,768]{1,0:T(8,128)}, u32[]{:S(2)}) copy-start(f32[768,768]{1,0:T(8,128)} %shard_map.256) | copy-start | bytes 7077892
  349.8 16.4 %collective-permute-start.2 = (f32[192,768]{1,0:T(8,128)S(1)}, f32[192,768]{1,0:T(8,128)}, u32[]{:S(2)}, u32[]{:S(2)}) collective-permute-start(f32[192,768]{1,0:T(8,128)S(1)} %constant_dynamic-slice_fusion.4), channel_id=1, source_target_pairs={{0,8},{4,12},{8,0},{12,4},{16,24},{20,28},{24,16},{28,20},{1,9},{5... | collective-permute-start | bytes 1769480 | tf_op jit(solution)/shard_map/ppermute | solution.py:181
  352.7 1.0 copy-start.7
  354.5 23.4 %collective-permute-start.5 = (f32[192,768]{1,0:T(8,128)}, f32[192,768]{1,0:T(8,128)}, u32[]{:S(2)}, u32[]{:S(2)}) collective-permute-start(f32[192,768]{1,0:T(8,128)} %constant_dynamic-slice_fusion.1), channel_id=1, source_target_pairs={{0,8},{4,12},{8,0},{12,4},{16,24},{20,28},{24,16},{28,20},{1,9},{5... | collective-permute-start | bytes 1769480 | tf_op jit(solution)/shard_map/ppermute | solution.py:181
  355.2 22.8 %copy-start.8 = (f32[384,768]{1,0:T(8,128)S(1)}, f32[384,768]{1,0:T(8,128)}, u32[]{:S(2)}) copy-start(f32[384,768]{1,0:T(8,128)} %copy-done.7) | copy-start | bytes 3538948
  368.0 15.5 %collective-permute-start.3 = (f32[96,768]{1,0:T(8,128)}, f32[96,768]{1,0:T(8,128)S(1)}, u32[]{:S(2)}, u32[]{:S(2)}) collective-permute-start(f32[96,768]{1,0:T(8,128)} %constant_dynamic-slice_fusion.3), channel_id=1, source_target_pairs={{0,16},{4,20},{8,24},{12,28},{16,0},{20,4},{24,8},{28,12},{1,17},{... | collective-permute-start | bytes 884744 | tf_op jit(solution)/shard_map/ppermute | solution.py:181
  379.8 8.4 %collective-permute-start.6 = (f32[96,768]{1,0:T(8,128)}, f32[96,768]{1,0:T(8,128)S(1)}, u32[]{:S(2)}, u32[]{:S(2)}) collective-permute-start(f32[96,768]{1,0:T(8,128)} %constant_dynamic-slice_fusion), channel_id=1, source_target_pairs={{0,16},{4,20},{8,24},{12,28},{16,0},{20,4},{24,8},{28,12},{1,17},{... | collective-permute-start | bytes 884744 | tf_op jit(solution)/shard_map/ppermute | solution.py:181
  392.1 2.7 copy-start.5
  392.1 1.8 copy-start.13
  392.2 2.6 copy-start.21
  418.9 88.7 %reduce-scatter.11.cloned.1.call-start = ((), (), s32[]{:S(2)}) async-start(), calls=%async_computation.9 | async-start | bytes 1966080 | tf_op jit(solution)/shard_map/reduce_scatter | solution.py:379
  422.2 2.7 collective-permute-start.7
  422.6 5.1 copy-start.20
  422.6 5.1 copy-start.3
  426.2 9.1 %collective-permute-start.8 = (bf16[192,768]{1,0:T(8,128)(2,1)S(1)}, bf16[192,768]{1,0:T(8,128)(2,1)S(1)}, u32[]{:S(2)}, u32[]{:S(2)}) collective-permute-start(bf16[192,768]{1,0:T(8,128)(2,1)S(1)} %dynamic-slice_convert_fusion.1), channel_id=1, source_target_pairs={{0,8},{4,12},{8,0},{12,4},{16,24},{20,28},{24,16},{28,20},{1,9},{5... | collective-permute-start | bytes 884744 | tf_op jit(solution)/shard_map/ppermute | solution.py:181
  427.8 9.3 %copy-start.15 = (bf16[96,768]{1,0:T(8,128)(2,1)S(1)}, bf16[96,768]{1,0:T(8,128)(2,1)}, u32[]{:S(2)}) copy-start(bf16[96,768]{1,0:T(8,128)(2,1)} %dynamic-slice_add_fusion.5) | copy-start | bytes 442372
  427.8 10.0 %copy-start.14 = (bf16[96,768]{1,0:T(8,128)(2,1)S(1)}, bf16[96,768]{1,0:T(8,128)(2,1)}, u32[]{:S(2)}) copy-start(bf16[96,768]{1,0:T(8,128)(2,1)} %dynamic-slice_add_fusion.4) | copy-start | bytes 442372
  435.4 7.4 %collective-permute-start.9 = (bf16[96,768]{1,0:T(8,128)(2,1)S(1)}, bf16[96,768]{1,0:T(8,128)(2,1)S(1)}, u32[]{:S(2)}, u32[]{:S(2)}) collective-permute-start(bf16[96,768]{1,0:T(8,128)(2,1)S(1)} %dynamic-slice_convert_fusion.2), channel_id=1, source_target_pairs={{0,16},{4,20},{8,24},{12,28},{16,0},{20,4},{24,8},{28,12},{1,17},{... | collective-permute-start | bytes 442376 | tf_op jit(solution)/shard_map/ppermute | solution.py:181
  437.1 35.1 %collective-permute-start.10 = (bf16[96,768]{1,0:T(8,128)(2,1)S(1)}, bf16[96,768]{1,0:T(8,128)(2,1)S(1)}, u32[]{:S(2)}, u32[]{:S(2)}) collective-permute-start(bf16[96,768]{1,0:T(8,128)(2,1)S(1)} %copy-done.15), channel_id=1, source_target_pairs={{0,16},{4,20},{8,24},{12,28},{16,0},{20,4},{24,8},{28,12},{1,17},{... | collective-permute-start | bytes 442376 | tf_op jit(solution)/shard_map/ppermute | solution.py:196
  437.7 36.1 %collective-permute-start.13 = (bf16[96,768]{1,0:T(8,128)(2,1)S(1)}, bf16[96,768]{1,0:T(8,128)(2,1)S(1)}, u32[]{:S(2)}, u32[]{:S(2)}) collective-permute-start(bf16[96,768]{1,0:T(8,128)(2,1)S(1)} %copy-done.14), channel_id=1, source_target_pairs={{0,16},{4,20},{8,24},{12,28},{16,0},{20,4},{24,8},{28,12},{1,17},{... | collective-permute-start | bytes 442376 | tf_op jit(solution)/shard_map/ppermute | solution.py:196
  472.1 68.5 %all-gather.15.cloned.1.call-start = ((), (), s32[]{:S(2)}) async-start(), calls=%async_computation.11 | async-start | bytes 3538944 | tf_op jit(solution)/shard_map/all_gather | solution.py:393
  472.2 9.9 %collective-permute-start.11 = (bf16[192,768]{1,0:T(8,128)(2,1)S(1)}, bf16[192,768]{1,0:T(8,128)(2,1)S(1)}, u32[]{:S(2)}, u32[]{:S(2)}) collective-permute-start(bf16[192,768]{1,0:T(8,128)(2,1)S(1)} %pad_maximum_fusion.3), channel_id=1, source_target_pairs={{0,8},{4,12},{8,0},{12,4},{16,24},{20,28},{24,16},{28,20},{1,9},{5... | collective-permute-start | bytes 884744 | tf_op jit(solution)/shard_map/ppermute | solution.py:196
  473.8 13.4 %collective-permute-start.14 = (bf16[192,768]{1,0:T(8,128)(2,1)S(1)}, bf16[192,768]{1,0:T(8,128)(2,1)S(1)}, u32[]{:S(2)}, u32[]{:S(2)}) collective-permute-start(bf16[192,768]{1,0:T(8,128)(2,1)S(1)} %pad_maximum_fusion.4), channel_id=1, source_target_pairs={{0,8},{4,12},{8,0},{12,4},{16,24},{20,28},{24,16},{28,20},{1,9},{5... | collective-permute-start | bytes 884744 | tf_op jit(solution)/shard_map/ppermute | solution.py:196
  482.3 5.1 collective-permute-start.12
  487.3 2.1 collective-permute-start.15
  489.6 18.1 %copy-start.4 = (bf16[3,512,768]{2,1,0:T(8,128)(2,1)S(1)}, bf16[3,512,768]{2,1,0:T(8,128)(2,1)}, u32[]{:S(2)}) copy-start(bf16[3,512,768]{2,1,0:T(8,128)(2,1)} %get-tuple-element.23) | copy-start | bytes 7077892
  509.0 1.5 copy-start.10
  513.2 2.2 copy-start.6
  513.2 2.2 copy-start.22
  553.8 4.0 copy-start.1
Sparse Core Ops, SparseCore 0:
  10.2 56.3 all-gather.12
  103.0 62.2 all-gather.8
  177.9 59.0 reduce-scatter.4
  244.5 63.3 all-gather.10
  320.7 59.0 reduce-scatter.6
  419.0 50.1 reduce-scatter.8
  472.2 35.3 reduce-scatter.10
  509.6 31.0 all-gather.14

commit v14 on v13

--- a/solution.py
+++ b/solution.py
@@ -149,12 +149,12 @@
     return pl.pallas_call(
         _tn_kernel,
         out_shape=jax.ShapeDtypeStruct((rows, cols), jnp.float32),
-        grid=(rows // tile, cols // tile),
+        grid=(rows // tile,),
         in_specs=[
-            pl.BlockSpec((depth, tile), lambda i, j: (0, i)),
-            pl.BlockSpec((depth, tile), lambda i, j: (0, j)),
+            pl.BlockSpec((depth, tile), lambda i: (0, i)),
+            pl.BlockSpec((depth, cols), lambda i: (0, 0)),
         ],
-        out_specs=pl.BlockSpec((tile, tile), lambda i, j: (i, j)),
+        out_specs=pl.BlockSpec((tile, cols), lambda i: (i, 0)),
         cost_estimate=pl.CostEstimate(
             flops=2 * depth * rows * cols,
             transcendentals=0,
@@ -304,8 +304,7 @@
             scatter_dimension=0,
             tiled=True,
         ).astype(jnp.float32)
-        norm1_in, ffn_grads = lax.optimization_barrier((second_grad + middle_part, ffn_grads))
-        first_grad, grad_norm1_gain, grad_norm1_shift = norm1_back(norm1_in)
+        first_grad, grad_norm1_gain, grad_norm1_shift = norm1_back(second_grad + middle_part)
         attn_grad = first_grad.astype(jnp.bfloat16)
         grad_out_bias = jnp.sum(attn_grad, axis=0, dtype=jnp.float32)
         context_grad = (
@@ -323,6 +322,7 @@
             proj_grad, grad_qkv_low = attention_backward(
                 query_low, key_low, value_low, context_grad, own_lengths, factor, tokens
             )
+            grad_qkv_low, ffn_grads = lax.optimization_barrier((grad_qkv_low, ffn_grads))
         else:
             proj_grad = attention_backward(
                 query_low, key_low, value_low, context_grad, own_lengths, factor

time: 566 us -> 553 us (0.977)
  Pallas kernels: 57.4 us -> 49.4 us
    pallas_call x2, Pallas kernels: 21.5 us -> 13.5 us  [tn_matmul(): pl.pallas_call(_tn_kernel, out_shape=jax.ShapeDtypeStruct((rows, cols), j...]
  transfers between devices with their start and end apart: 24 -> 24, of which waited for: 18 -> 18; matrix products, arithmetic and copies ran while one was open for 7% -> 7% of each run, Pallas kernels for 4% -> 2%
where the time goes in v14:
time: 553 us; the launch traced here: 552 us
  waiting for transfers between devices  358 us (65%)
  Pallas kernels  49.4 us (9%)
  local copies, waits for them, and re-layouts  46.8 us (8%)
  matrix products  38.1 us (7%)
  other arithmetic  32 us (6%)
  between operations  14.9 us (3%)
  starting transfers between devices  13.4 us (2%)
    all_gather x1, waiting for transfers between devices, per_device(): branch_rows = lax.all_gather(branch_grad, 'tensor', axis=0, tiled=True)  63.3 us
    all_gather x1, waiting for transfers between devices, per_device(): ffn_rows = lax.all_gather(middle_low, 'tensor', axis=0, tiled=True)  62.3 us
    reduce_scatter x1, waiting for transfers between devices, per_device(): lax.psum_scatter(jnp.dot(hidden, down_weight, preferred_element_type=jnp....  59.2 us
    all_gather x1, waiting for transfers between devices, per_device(): mine = lax.all_gather(mine, 'tensor', axis=0, tiled=False)  56.8 us
    ppermute x9, waiting for transfers between devices, dp_halve(): got = lax.ppermute(give, 'dp', [(i, i ^ 1 << step) for i in range(dp_size)])  37.5 us
    reduce_scatter x1, waiting for transfers between devices, per_device(): lax.psum_scatter(grad_qkv_low.reshape(3 * width, width), 'dp', scatter_di...  24.7 us
    pallas_call x1, Pallas kernels, attention_backward(): pl.pallas_call(functools.partial(_bwd_kernel, heads=pair, factor=factor),...  22.9 us
    all_gather x1, waiting for transfers between devices, per_device(): joined = lax.all_gather(joined, 'dp', axis=0, tiled=False)  22 us
  transfers between devices with their start and end apart: 24, of which 18 were waited for; matrix products, arithmetic and copies ran while one was open for 7% of the time, Pallas kernels for 2%

profile of v14, /device:TPU:0, one launch (start us, length us, event | category | flops | bytes accessed | tf_op | source)
XLA Modules:
  0.0 552.1 jit_solution(11947294950015508418)
XLA Ops:
  7.3 1.3 slice_bitcast_fusion.2
  9.8 56.8 %all-gather.13.cloned.1.call-done = bf16[4,1544,192]{1,2,0:T(8,128)(2,1)} async-done(((bf16[1,1544,192]{1,2,0:T(8,128)(2,1)}), bf16[4,1544,192]{1,2,0:T(8,128)(2,1)}) %all-gather.13.cloned.1.call-update) | async-done | bytes 2371600 | tf_op jit(solution)/shard_map/all_gather | solution.py:239
  67.2 4.6 collective-permute-done
  71.8 3.0 broadcast_select_fusion
  77.0 1.2 copy.73.v_ref
  78.2 2.1 add_convert_fusion.2
  81.4 1.2 copy.72.k_ref
  82.6 13.0 %shard_map.254 = bf16[512,768]{1,0:T(8,128)(2,1)} custom-call(s32[1]{0:T(128)} %dynamic_slice.57.len_ref, bf16[512,768]{1,0:T(8,128)(2,1)} %copy.71.q_ref, bf16[512,768]{1,0:T(8,128)(2,1)} %copy.72.k_ref, bf16[512,768]{1,0:T(8,128)(2,1)} %copy.73.v_ref), custom_call_target="tpu_custom_call" | custom-call | flops 805306368 | bytes 3145728 | tf_op jit(solution)/shard_map/pallas_call | solution.py:92
  95.6 1.4 copy.74
  97.0 2.4 fusion.49
  100.2 1.2 fusion.14
  101.5 62.3 %all-gather.9.cloned.1.call-done.left_ref = bf16[2048,768]{1,0:T(8,128)(2,1)} async-done(((bf16[512,768]{1,0:T(8,128)(2,1)}), bf16[2048,768]{1,0:T(8,128)(2,1)}) %all-gather.9.cloned.1.call-update) | async-done | bytes 3145744 | tf_op jit(solution)/shard_map/all_gather | solution.py:273
  163.8 6.7 %multiply_convert_fusion = (bf16[2048,768]{1,0:T(8,128)(2,1)S(1)}, f32[2048,768]{1,0:T(8,128)}) fusion(f32[768]{0:T(1024)S(1)} %convert_element_type.152, bf16[2048,768]{1,0:T(8,128)(2,1)} %all-gather.9.cloned.1.call-done.left_ref, bf16[768,768]{1,0:T(8,128)(2,1)S(1)} %copy-done), kind=kOutput, calls=%fused_computation.8 | convolution fusion | flops 2425356288 | bytes 13765632 | tf_op jit(solution)/shard_map/dot_general | solution.py:274
  170.5 1.7 copy-done.32
  172.2 4.0 convolution_convert_fusion.1
  176.2 59.2 %reduce-scatter.5.cloned.1.call-done = bf16[512,768]{1,0:T(8,128)(2,1)} async-done(((bf16[2048,768]{1,0:T(8,128)(2,1)}), bf16[512,768]{1,0:T(8,128)(2,1)}) %reduce-scatter.5.cloned.1.call-update) | async-done | bytes 786448 | tf_op jit(solution)/shard_map/reduce_scatter | solution.py:277
  235.4 1.7 fusion.46
  239.0 1.6 fusion.45
  243.0 63.3 %all-gather.11.cloned.1.call-done.right_ref = bf16[2048,768]{1,0:T(8,128)(2,1)} async-done(((bf16[512,768]{1,0:T(8,128)(2,1)}), bf16[2048,768]{1,0:T(8,128)(2,1)}) %all-gather.11.cloned.1.call-update) | async-done | bytes 3145744 | tf_op jit(solution)/shard_map/all_gather | solution.py:289
  306.3 7.0 %convert_reduce_fusion = (f32[768]{0:T(1024)S(1)}, bf16[2048,768]{1,0:T(8,128)(2,1)S(1)}) fusion(f32[2048,768]{1,0:T(8,128)} %get-tuple-element.129, f32[768]{0:T(1024)S(1)} %convert_element_type.152, bf16[2048,768]{1,0:T(8,128)(2,1)} %all-gather.11.cloned.1.call-done.right_ref, bf16[768,768]{1,0:T(8,128)(2,1)} %param.26), kind=kOutput, calls=%fused_computation.7 | convolution fusion | flops 2436365568 | bytes 13768704 | tf_op jit(solution)/shard_map/dot_general | solution.py:31
  313.3 1.7 copy-done.33
  315.0 4.0 convolution_convert_fusion
  319.0 6.8 %shard_map.257 = f32[768,768]{1,0:T(8,128)} custom-call(bf16[2048,768]{1,0:T(8,128)(2,1)} %copy-done.32, bf16[2048,768]{1,0:T(8,128)(2,1)} %all-gather.11.cloned.1.call-done.right_ref), custom_call_target="tpu_custom_call" | custom-call | flops 2415919104 | bytes 8650752 | tf_op jit(solution)/shard_map/pallas_call | solution.py:149
  325.8 6.7 %shard_map.256 = f32[768,768]{1,0:T(8,128)} custom-call(bf16[2048,768]{1,0:T(8,128)(2,1)} %all-gather.9.cloned.1.call-done.left_ref, bf16[2048,768]{1,0:T(8,128)(2,1)} %copy-done.33), custom_call_target="tpu_custom_call" | custom-call | flops 2415919104 | bytes 8650752 | tf_op jit(solution)/shard_map/pallas_call | solution.py:149
  332.5 2.8 constant_dynamic-slice_fusion.2
  335.8 2.5 collective-permute-done.4
  338.3 1.8 dynamic-slice_add_fusion
  340.1 1.4 collective-permute-start.5
  341.6 1.4 dynamic-slice_add_fusion.1
  345.5 11.0 %collective-permute-done.5 = f32[192,768]{1,0:T(8,128)} collective-permute-done((f32[192,768]{1,0:T(8,128)S(1)}, f32[192,768]{1,0:T(8,128)}, u32[]{:S(2)}, u32[]{:S(2)}) %collective-permute-start.5) | collective-permute-done | bytes 589856 | tf_op jit(solution)/shard_map/ppermute | solution.py:181
  358.4 1.4 collective-permute-start.6
  359.7 8.6 %collective-permute-done.2 = f32[192,768]{1,0:T(8,128)} collective-permute-done((f32[192,768]{1,0:T(8,128)}, f32[192,768]{1,0:T(8,128)}, u32[]{:S(2)}, u32[]{:S(2)}) %collective-permute-start.2) | collective-permute-done | bytes 589856 | tf_op jit(solution)/shard_map/ppermute | solution.py:181
  370.2 1.3 collective-permute-start.3
  371.6 2.4 slice.151
  374.6 4.1 collective-permute-done.3
  379.4 2.6 multiply_reduce_fusion
  383.2 1.6 copy-done.16
  386.8 22.9 %shard_map.255 = (bf16[3,512,768]{2,1,0:T(8,128)(2,1)}, bf16[3,768,768]{2,1,0:T(8,128)(2,1)}) custom-call(s32[1]{0:T(128)} %dynamic_slice.57.len_ref, bf16[512,768]{1,0:T(8,128)(2,1)} %copy.71.q_ref, bf16[512,768]{1,0:T(8,128)(2,1)} %copy.72.k_ref, bf16[512,768]{1,0:T(8,128)(2,1)} %copy.73.v_ref, bf16[512,768]{1,0:T(8,128)(2,1)} %copy.78.grad_ref, ...), custom_call_target="tpu_custom_call" | custom-call | flops 3221225472 | bytes 7864320 | tf_op jit(solution)/shard_map/pallas_call | solution.py:123
  411.0 1.9 fusion.13
  413.2 1.4 collective-permute-start.13
  415.8 1.5 convert_add_fusion.1
  417.4 1.5 collective-permute-start.8
  419.2 7.4 %collective-permute-done.8 = bf16[192,768]{1,0:T(8,128)(2,1)S(1)} collective-permute-done((bf16[192,768]{1,0:T(8,128)(2,1)S(1)}, bf16[192,768]{1,0:T(8,128)(2,1)S(1)}, u32[]{:S(2)}, u32[]{:S(2)}) %collective-permute-start.8) | collective-permute-done | bytes 294944 | tf_op jit(solution)/shard_map/ppermute | solution.py:181
  426.7 1.3 collective-permute-start.9
  428.2 3.7 collective-permute-done.9
  431.9 24.7 %reduce-scatter.9.cloned.1.call-done = bf16[288,768]{1,0:T(8,128)(2,1)} async-done(((bf16[2304,768]{1,0:T(8,128)(2,1)}), bf16[288,768]{1,0:T(8,128)(2,1)}) %reduce-scatter.9.cloned.1.call-update) | async-done | bytes 442384 | tf_op jit(solution)/shard_map/reduce_scatter | solution.py:372
  457.8 1.7 copy.82
  460.6 1.5 collective-permute-start.14
  463.8 6.7 %collective-permute-done.14 = bf16[192,768]{1,0:T(8,128)(2,1)S(1)} collective-permute-done((bf16[192,768]{1,0:T(8,128)(2,1)S(1)}, bf16[192,768]{1,0:T(8,128)(2,1)S(1)}, u32[]{:S(2)}, u32[]{:S(2)}) %collective-permute-start.14) | collective-permute-done | bytes 294944 | tf_op jit(solution)/shard_map/ppermute | solution.py:196
  470.8 4.8 collective-permute-done.11
  476.0 1.6 maximum_convert_fusion.1
  478.0 1.6 maximum_convert_fusion
  479.6 15.5 %reduce-scatter.11.cloned.1.call-done = f32[1,416,192]{1,2,0:T(8,128)} async-done(((f32[4,416,192]{1,2,0:T(8,128)}), f32[1,416,192]{1,2,0:T(8,128)}) %reduce-scatter.11.cloned.1.call-update) | async-done | bytes 319504 | tf_op jit(solution)/shard_map/reduce_scatter | solution.py:379
  495.1 1.3 fusion.47
  496.4 1.5 copy.79
  498.5 2.1 fusion.25
  500.6 2.2 fusion.22
  502.8 3.3 fusion.11
  506.1 22.0 %all-gather.15.cloned.1.call-done = f32[8,416,192]{1,2,0:T(8,128)} async-done(((f32[1,416,192]{1,2,0:T(8,128)}), f32[8,416,192]{1,2,0:T(8,128)}) %all-gather.15.cloned.1.call-update) | async-done | bytes 2555920 | tf_op jit(solution)/shard_map/all_gather | solution.py:393
  528.1 3.2 slice.152
  531.3 2.2 copy.83
  533.5 1.8 copy.91
  535.3 1.2 slice_reduce_fusion
  542.7 1.5 slice_bitcast_fusion.3
  (188 shorter events, 37.7 us)
Async XLA Ops:
  7.2 156.6 %copy-start = (bf16[768,768]{1,0:T(8,128)(2,1)S(1)}, bf16[768,768]{1,0:T(8,128)(2,1)}, u32[]{:S(2)}) copy-start(bf16[768,768]{1,0:T(8,128)(2,1)} %param.24) | copy-start | bytes 3538948
  7.2 1.4 copy-start.27
  7.2 1.5 copy-start.17
  7.2 59.4 %all-gather.13.cloned.1.call-start = ((), (), s32[]{:S(2)}) async-start(), calls=%async_computation.10 | async-start | bytes 3194880 | tf_op jit(solution)/shard_map/all_gather | solution.py:239
  8.6 58.0 %copy-start.31 = (s32[4]{0:T(128)S(1)}, s32[4]{0:T(128)}, u32[]{:S(2)}) copy-start(s32[4]{0:T(128)} %param.17) | copy-start | bytes 52
  9.8 154.0 %all-gather.9.cloned.1.call-start = ((), (), s32[]{:S(2)}) async-start(), calls=%async_computation.4 | async-start | bytes 3932160 | tf_op jit(solution)/shard_map/all_gather | solution.py:273
  66.6 5.2 collective-permute-start
  67.2 7.9 %copy-start.29 = (bf16[512,768]{1,0:T(8,128)(2,1)S(1)}, bf16[512,768]{1,0:T(8,128)(2,1)}, u32[]{:S(2)}) copy-start(bf16[512,768]{1,0:T(8,128)(2,1)} %rest_0_.1) | copy-start | bytes 2359300
  74.7 1.5 copy-start.8
  74.7 2.3 copy-start.11
  95.6 1.4 copy-start.30
  99.5 0.7 copy-start.18
  99.5 0.7 copy-start.19
  100.2 1.3 copy-start.26
  101.4 134.0 %reduce-scatter.5.cloned.1.call-start = ((), (), s32[]{:S(2)}) async-start(), calls=%async_computation.5 | async-start | bytes 3932160 | tf_op jit(solution)/shard_map/reduce_scatter | solution.py:277
  163.8 8.4 %copy-start.28 = (bf16[768,768]{1,0:T(8,128)(2,1)S(1)}, bf16[768,768]{1,0:T(8,128)(2,1)}, u32[]{:S(2)}) copy-start(bf16[768,768]{1,0:T(8,128)(2,1)} %param.26) | copy-start | bytes 3538948
  170.5 1.7 copy-start.32
  176.1 59.2 %copy-start.24 = (f32[768]{0:T(1024)S(1)}, f32[768]{0:T(1024)}, u32[]{:S(2)}) copy-start(f32[768]{0:T(1024)} %param.27) | copy-start | bytes 9220
  176.2 130.2 %all-gather.11.cloned.1.call-start = ((), (), s32[]{:S(2)}) async-start(), calls=%async_computation.6 | async-start | bytes 3932160 | tf_op jit(solution)/shard_map/all_gather | solution.py:289
  237.1 1.1 copy-start.13
  237.1 1.1 copy-start.20
  237.4 1.5 copy-start.25
  240.6 1.1 copy-start.2
  242.8 136.6 %reduce-scatter.7.cloned.1.call-start = ((), (), s32[]{:S(2)}) async-start(), calls=%async_computation.7 | async-start | bytes 3932160 | tf_op jit(solution)/shard_map/reduce_scatter | solution.py:301
  313.3 1.7 copy-start.33
  319.0 137.7 %reduce-scatter.9.cloned.1.call-start = ((), (), s32[]{:S(2)}) async-start(), calls=%async_computation.8 | async-start | bytes 3981312 | tf_op jit(solution)/shard_map/reduce_scatter | solution.py:372
  335.3 3.0 collective-permute-start.4
  335.3 6.2 %collective-permute-start.1 = (f32[384,768]{1,0:T(8,128)}, f32[384,768]{1,0:T(8,128)}, u32[]{:S(2)}, u32[]{:S(2)}) collective-permute-start(f32[384,768]{1,0:T(8,128)} %get-tuple-element.133), channel_id=1, source_target_pairs={{0,4},{4,0},{8,12},{12,8},{16,20},{20,16},{24,28},{28,24},{1,5},{5... | collective-permute-start | bytes 3538952 | tf_op jit(solution)/shard_map/ppermute | solution.py:181
  335.8 5.7 %copy-start.15 = (f32[768,768]{1,0:T(8,128)S(1)}, f32[768,768]{1,0:T(8,128)}, u32[]{:S(2)}) copy-start(f32[768,768]{1,0:T(8,128)} %shard_map.256) | copy-start | bytes 7077892
  340.1 16.4 %collective-permute-start.5 = (f32[192,768]{1,0:T(8,128)S(1)}, f32[192,768]{1,0:T(8,128)}, u32[]{:S(2)}, u32[]{:S(2)}) collective-permute-start(f32[192,768]{1,0:T(8,128)S(1)} %constant_dynamic-slice_fusion.1), channel_id=1, source_target_pairs={{0,8},{4,12},{8,0},{12,4},{16,24},{20,28},{24,16},{28,20},{1,9},{5... | collective-permute-start | bytes 1769480 | tf_op jit(solution)/shard_map/ppermute | solution.py:181
  343.0 1.0 copy-start.9
  344.9 23.5 %collective-permute-start.2 = (f32[192,768]{1,0:T(8,128)}, f32[192,768]{1,0:T(8,128)}, u32[]{:S(2)}, u32[]{:S(2)}) collective-permute-start(f32[192,768]{1,0:T(8,128)} %constant_dynamic-slice_fusion.4), channel_id=1, source_target_pairs={{0,8},{4,12},{8,0},{12,4},{16,24},{20,28},{24,16},{28,20},{1,9},{5... | collective-permute-start | bytes 1769480 | tf_op jit(solution)/shard_map/ppermute | solution.py:181
  345.5 22.8 %copy-start.10 = (f32[384,768]{1,0:T(8,128)S(1)}, f32[384,768]{1,0:T(8,128)}, u32[]{:S(2)}) copy-start(f32[384,768]{1,0:T(8,128)} %copy-done.9) | copy-start | bytes 3538948
  358.4 15.6 %collective-permute-start.6 = (f32[96,768]{1,0:T(8,128)}, f32[96,768]{1,0:T(8,128)S(1)}, u32[]{:S(2)}, u32[]{:S(2)}) collective-permute-start(f32[96,768]{1,0:T(8,128)} %constant_dynamic-slice_fusion), channel_id=1, source_target_pairs={{0,16},{4,20},{8,24},{12,28},{16,0},{20,4},{24,8},{28,12},{1,17},{... | collective-permute-start | bytes 884744 | tf_op jit(solution)/shard_map/ppermute | solution.py:181
  370.2 8.5 %collective-permute-start.3 = (f32[96,768]{1,0:T(8,128)}, f32[96,768]{1,0:T(8,128)S(1)}, u32[]{:S(2)}, u32[]{:S(2)}) collective-permute-start(f32[96,768]{1,0:T(8,128)} %constant_dynamic-slice_fusion.3), channel_id=1, source_target_pairs={{0,16},{4,20},{8,24},{12,28},{16,0},{20,4},{24,8},{28,12},{1,17},{... | collective-permute-start | bytes 884744 | tf_op jit(solution)/shard_map/ppermute | solution.py:181
  379.4 2.6 copy-start.3
  379.4 2.6 copy-start.14
  382.9 2.7 copy-start.6
  382.9 1.8 copy-start.16
  382.9 2.6 copy-start.22
  409.7 85.3 %reduce-scatter.11.cloned.1.call-start = ((), (), s32[]{:S(2)}) async-start(), calls=%async_computation.9 | async-start | bytes 1966080 | tf_op jit(solution)/shard_map/reduce_scatter | solution.py:379
  413.1 2.8 collective-permute-start.7
  413.2 46.4 %collective-permute-start.13 = (bf16[96,768]{1,0:T(8,128)(2,1)}, bf16[96,768]{1,0:T(8,128)(2,1)}, u32[]{:S(2)}, u32[]{:S(2)}) collective-permute-start(bf16[96,768]{1,0:T(8,128)(2,1)} %dynamic-slice_add_fusion.4), channel_id=1, source_target_pairs={{0,16},{4,20},{8,24},{12,28},{16,0},{20,4},{24,8},{28,12},{1,17},{... | collective-permute-start | bytes 442376 | tf_op jit(solution)/shard_map/ppermute | solution.py:196
  414.6 47.6 %collective-permute-start.10 = (bf16[96,768]{1,0:T(8,128)(2,1)}, bf16[96,768]{1,0:T(8,128)(2,1)}, u32[]{:S(2)}, u32[]{:S(2)}) collective-permute-start(bf16[96,768]{1,0:T(8,128)(2,1)} %dynamic-slice_add_fusion.5), channel_id=1, source_target_pairs={{0,16},{4,20},{8,24},{12,28},{16,0},{20,4},{24,8},{28,12},{1,17},{... | collective-permute-start | bytes 442376 | tf_op jit(solution)/shard_map/ppermute | solution.py:196
  415.5 3.4 copy-start.21
  415.5 3.4 copy-start.4
  417.4 9.2 %collective-permute-start.8 = (bf16[192,768]{1,0:T(8,128)(2,1)S(1)}, bf16[192,768]{1,0:T(8,128)(2,1)S(1)}, u32[]{:S(2)}, u32[]{:S(2)}) collective-permute-start(bf16[192,768]{1,0:T(8,128)(2,1)S(1)} %dynamic-slice_convert_fusion.1), channel_id=1, source_target_pairs={{0,8},{4,12},{8,0},{12,4},{16,24},{20,28},{24,16},{28,20},{1,9},{5... | collective-permute-start | bytes 884744 | tf_op jit(solution)/shard_map/ppermute | solution.py:181
  426.7 5.2 collective-permute-start.9
  459.5 68.6 %all-gather.15.cloned.1.call-start = ((), (), s32[]{:S(2)}) async-start(), calls=%async_computation.11 | async-start | bytes 3538944 | tf_op jit(solution)/shard_map/all_gather | solution.py:393
  460.6 9.9 %collective-permute-start.14 = (bf16[192,768]{1,0:T(8,128)(2,1)S(1)}, bf16[192,768]{1,0:T(8,128)(2,1)S(1)}, u32[]{:S(2)}, u32[]{:S(2)}) collective-permute-start(bf16[192,768]{1,0:T(8,128)(2,1)S(1)} %pad_maximum_fusion.4), channel_id=1, source_target_pairs={{0,8},{4,12},{8,0},{12,4},{16,24},{20,28},{24,16},{28,20},{1,9},{5... | collective-permute-start | bytes 884744 | tf_op jit(solution)/shard_map/ppermute | solution.py:196
  463.2 12.4 %collective-permute-start.11 = (bf16[192,768]{1,0:T(8,128)(2,1)S(1)}, bf16[192,768]{1,0:T(8,128)(2,1)S(1)}, u32[]{:S(2)}, u32[]{:S(2)}) collective-permute-start(bf16[192,768]{1,0:T(8,128)(2,1)S(1)} %pad_maximum_fusion.3), channel_id=1, source_target_pairs={{0,8},{4,12},{8,0},{12,4},{16,24},{20,28},{24,16},{28,20},{1,9},{5... | collective-permute-start | bytes 884744 | tf_op jit(solution)/shard_map/ppermute | solution.py:196
  470.7 5.1 collective-permute-start.15
  475.7 2.1 collective-permute-start.12
  478.0 17.1 %copy-start.5 = (bf16[3,512,768]{2,1,0:T(8,128)(2,1)S(1)}, bf16[3,512,768]{2,1,0:T(8,128)(2,1)}, u32[]{:S(2)}) copy-start(bf16[3,512,768]{2,1,0:T(8,128)(2,1)} %get-tuple-element.22) | copy-start | bytes 7077892
  496.4 1.5 copy-start.12
  500.6 2.2 copy-start.7
  500.6 2.2 copy-start.23
  541.3 3.9 copy-start.1
Sparse Core Ops, SparseCore 0:
  10.2 56.3 all-gather.12
  101.5 62.1 all-gather.8
  176.3 59.0 reduce-scatter.4
  242.9 63.3 all-gather.10
  319.1 59.0 reduce-scatter.6
  409.9 46.7 reduce-scatter.8
  459.6 35.4 reduce-scatter.10
  497.0 31.0 all-gather.14

commit v15 on v14

--- a/solution.py
+++ b/solution.py
@@ -168,12 +168,12 @@
     return dp_size == 1 << steps and values.shape[0] % dp_size == 0
 
 
-def dp_halve(values, dp_size, sum_dtype=None):
+def dp_halve(values, dp_size, sum_dtype=None, high_first=False):
     steps = dp_size.bit_length() - 1
     index = lax.axis_index("dp")
     link = values.dtype
     kept = values if sum_dtype is None else values.astype(sum_dtype)
-    for step in range(steps):
+    for step in reversed(range(steps)) if high_first else range(steps):
         bit = (index >> step) & 1
         half = kept.shape[0] // 2
         keep = lax.dynamic_slice_in_dim(kept, bit * half, half)
@@ -181,11 +181,6 @@
         got = lax.ppermute(give, "dp", [(i, i ^ (1 << step)) for i in range(dp_size)])
         kept = keep + got.astype(kept.dtype)
     return kept
-
-
-def bit_reversed(count):
-    steps = count.bit_length() - 1
-    return [int(format(i, f"0{steps}b")[::-1], 2) if steps else 0 for i in range(count)]
 
 
 def dp_double(kept, dp_size):
@@ -315,7 +310,7 @@
         early = contract(attn_grad, context_low, 0, 0)
         early_halved = dp_pow2(early, dp_size)
         if early_halved:
-            early = dp_halve(early.astype(jnp.bfloat16), dp_size, jnp.float32)
+            early = dp_halve(early.astype(jnp.bfloat16), dp_size, jnp.float32, high_first=True)
         else:
             early = lax.psum_scatter(early, "dp", scatter_dimension=0, tiled=True)
         if passages == 1:
@@ -392,10 +387,6 @@
         early_rows = early.shape[0]
         joined = lax.all_gather(joined, "dp", axis=0, tiled=False)
         early = joined[:, late_rows : late_rows + early_rows]
-        if early_halved:
-            order = bit_reversed(dp_size)
-            place = [order.index(b) for b in range(dp_size)]
-            early = jnp.concatenate([early[p] for p in place], axis=0)
         pieces = [
             joined[:, :late_rows].reshape(-1, shard),
             early.reshape(-1, shard),

time: 553 us -> 557 us (level)
    reduce_scatter x1 -> x0, waiting for transfers between devices: 24.7 us -> none  [per_device(): lax.psum_scatter(grad_qkv_low.reshape(3 * width, width), 'dp', scatter_di...]
    unnamed x8 -> x9, waiting for transfers between devices: 0.13 us -> 14.6 us
    ppermute x9, waiting for transfers between devices: 37.5 us -> 51.5 us  [dp_halve(): got = lax.ppermute(give, 'dp', [(i, i ^ 1 << step) for i in range(dp_size)])]
    unnamed x76 -> x78, local copies, waits for them, and re-layouts: 11.3 us -> 12.8 us
where the time goes in v15:
time: 557 us; the launch traced here: 556 us
  waiting for transfers between devices  361 us (65%)
  Pallas kernels  49.4 us (9%)
  local copies, waits for them, and re-layouts  47.2 us (8%)
  matrix products  38.2 us (7%)
  other arithmetic  32.1 us (6%)
  between operations  14.9 us (3%)
  starting transfers between devices  13.1 us (2%)
    all_gather x1, waiting for transfers between devices, per_device(): branch_rows = lax.all_gather(branch_grad, 'tensor', axis=0, tiled=True)  63.3 us
    all_gather x1, waiting for transfers between devices, per_device(): ffn_rows = lax.all_gather(middle_low, 'tensor', axis=0, tiled=True)  62.3 us
    reduce_scatter x1, waiting for transfers between devices, per_device(): lax.psum_scatter(jnp.dot(hidden, down_weight, preferred_element_type=jnp....  59.2 us
    all_gather x1, waiting for transfers between devices, per_device(): mine = lax.all_gather(mine, 'tensor', axis=0, tiled=False)  56.8 us
    ppermute x9, waiting for transfers between devices, dp_halve(): got = lax.ppermute(give, 'dp', [(i, i ^ 1 << step) for i in range(dp_size)])  51.5 us
    pallas_call x1, Pallas kernels, attention_backward(): pl.pallas_call(functools.partial(_bwd_kernel, heads=pair, factor=factor),...  22.8 us
    all_gather x1, waiting for transfers between devices, per_device(): joined = lax.all_gather(joined, 'dp', axis=0, tiled=False)  21.9 us
    reduce_scatter x1, waiting for transfers between devices, per_device(): lax.psum_scatter(joined.reshape(joined.shape[0], groups, shard).transpose...  15.5 us
  transfers between devices with their start and end apart: 24, of which 18 were waited for; matrix products, arithmetic and copies ran while one was open for 7% of the time, Pallas kernels for 2%

profile of v15, /device:TPU:0, one launch (start us, length us, event | category | flops | bytes accessed | tf_op | source)
XLA Modules:
  0.0 556.3 jit_solution(10839022499433126676)
XLA Ops:
  7.3 1.3 slice_bitcast_fusion.2
  9.8 56.8 %all-gather.13.cloned.1.call-done = bf16[4,1544,192]{1,2,0:T(8,128)(2,1)} async-done(((bf16[1,1544,192]{1,2,0:T(8,128)(2,1)}), bf16[4,1544,192]{1,2,0:T(8,128)(2,1)}) %all-gather.13.cloned.1.call-update) | async-done | bytes 2371600 | tf_op jit(solution)/shard_map/all_gather | solution.py:234
  67.2 4.6 collective-permute-done
  71.8 3.0 broadcast_select_fusion
  78.2 2.1 add_convert_fusion.2
  81.4 1.2 copy.94.k_ref
  82.6 13.1 %shard_map.254 = bf16[512,768]{1,0:T(8,128)(2,1)} custom-call(s32[1]{0:T(128)} %dynamic_slice.57.len_ref, bf16[512,768]{1,0:T(8,128)(2,1)} %copy.93.q_ref, bf16[512,768]{1,0:T(8,128)(2,1)} %copy.94.k_ref, bf16[512,768]{1,0:T(8,128)(2,1)} %copy.95.v_ref), custom_call_target="tpu_custom_call" | custom-call | flops 805306368 | bytes 3145728 | tf_op jit(solution)/shard_map/pallas_call | solution.py:92
  95.7 1.4 copy.96
  97.1 2.4 fusion.49
  100.2 1.2 fusion.14
  101.5 62.3 %all-gather.9.cloned.1.call-done.left_ref = bf16[2048,768]{1,0:T(8,128)(2,1)} async-done(((bf16[512,768]{1,0:T(8,128)(2,1)}), bf16[2048,768]{1,0:T(8,128)(2,1)}) %all-gather.9.cloned.1.call-update) | async-done | bytes 3145744 | tf_op jit(solution)/shard_map/all_gather | solution.py:268
  163.8 6.8 %multiply_convert_fusion = (bf16[2048,768]{1,0:T(8,128)(2,1)S(1)}, f32[2048,768]{1,0:T(8,128)}) fusion(f32[768]{0:T(1024)S(1)} %convert_element_type.152, bf16[2048,768]{1,0:T(8,128)(2,1)} %all-gather.9.cloned.1.call-done.left_ref, bf16[768,768]{1,0:T(8,128)(2,1)S(1)} %copy-done), kind=kOutput, calls=%fused_computation.8 | convolution fusion | flops 2425356288 | bytes 13765632 | tf_op jit(solution)/shard_map/dot_general | solution.py:269
  170.6 1.7 copy-done.32
  172.3 4.0 convolution_convert_fusion.1
  176.4 59.2 %reduce-scatter.7.cloned.1.call-done = bf16[512,768]{1,0:T(8,128)(2,1)} async-done(((bf16[2048,768]{1,0:T(8,128)(2,1)}), bf16[512,768]{1,0:T(8,128)(2,1)}) %reduce-scatter.7.cloned.1.call-update) | async-done | bytes 786448 | tf_op jit(solution)/shard_map/reduce_scatter | solution.py:272
  235.5 1.7 fusion.46
  239.1 1.6 fusion.45
  243.2 63.3 %all-gather.11.cloned.1.call-done.right_ref = bf16[2048,768]{1,0:T(8,128)(2,1)} async-done(((bf16[512,768]{1,0:T(8,128)(2,1)}), bf16[2048,768]{1,0:T(8,128)(2,1)}) %all-gather.11.cloned.1.call-update) | async-done | bytes 3145744 | tf_op jit(solution)/shard_map/all_gather | solution.py:284
  306.5 7.0 %convert_reduce_fusion = (f32[768]{0:T(1024)S(1)}, bf16[2048,768]{1,0:T(8,128)(2,1)S(1)}) fusion(f32[2048,768]{1,0:T(8,128)} %get-tuple-element.135, f32[768]{0:T(1024)S(1)} %convert_element_type.152, bf16[2048,768]{1,0:T(8,128)(2,1)} %all-gather.11.cloned.1.call-done.right_ref, bf16[768,768]{1,0:T(8,128)(2,1)} %param.26), kind=kOutput, calls=%fused_computation.7 | convolution fusion | flops 2436365568 | bytes 13768704 | tf_op jit(solution)/shard_map/dot_general | solution.py:31
  313.5 1.7 copy-done.33
  315.1 4.0 convolution_convert_fusion
  319.2 6.8 %shard_map.257 = f32[768,768]{1,0:T(8,128)} custom-call(bf16[2048,768]{1,0:T(8,128)(2,1)} %copy-done.32, bf16[2048,768]{1,0:T(8,128)(2,1)} %all-gather.11.cloned.1.call-done.right_ref), custom_call_target="tpu_custom_call" | custom-call | flops 2415919104 | bytes 8650752 | tf_op jit(solution)/shard_map/pallas_call | solution.py:149
  326.0 6.7 %shard_map.256 = f32[768,768]{1,0:T(8,128)} custom-call(bf16[2048,768]{1,0:T(8,128)(2,1)} %all-gather.9.cloned.1.call-done.left_ref, bf16[2048,768]{1,0:T(8,128)(2,1)} %copy-done.33), custom_call_target="tpu_custom_call" | custom-call | flops 2415919104 | bytes 8650752 | tf_op jit(solution)/shard_map/pallas_call | solution.py:149
  332.7 2.8 constant_dynamic-slice_fusion.2
  336.0 2.5 collective-permute-done.4
  338.5 1.8 dynamic-slice_add_fusion
  340.3 1.4 collective-permute-start.5
  341.7 1.4 dynamic-slice_add_fusion.1
  345.7 11.0 %collective-permute-done.5 = f32[192,768]{1,0:T(8,128)} collective-permute-done((f32[192,768]{1,0:T(8,128)S(1)}, f32[192,768]{1,0:T(8,128)}, u32[]{:S(2)}, u32[]{:S(2)}) %collective-permute-start.5) | collective-permute-done | bytes 589856 | tf_op jit(solution)/shard_map/ppermute | solution.py:181
  358.6 1.4 collective-permute-start.6
  359.9 8.6 %collective-permute-done.2 = f32[192,768]{1,0:T(8,128)} collective-permute-done((f32[192,768]{1,0:T(8,128)}, f32[192,768]{1,0:T(8,128)}, u32[]{:S(2)}, u32[]{:S(2)}) %collective-permute-start.2) | collective-permute-done | bytes 589856 | tf_op jit(solution)/shard_map/ppermute | solution.py:181
  370.4 1.3 collective-permute-start.3
  371.8 2.4 slice.114
  374.8 4.1 collective-permute-done.3
  379.6 2.6 multiply_reduce_fusion
  383.4 1.6 copy-done.16
  387.0 22.8 %shard_map.255 = (bf16[3,512,768]{2,1,0:T(8,128)(2,1)}, bf16[3,768,768]{2,1,0:T(8,128)(2,1)}) custom-call(s32[1]{0:T(128)} %dynamic_slice.57.len_ref, bf16[512,768]{1,0:T(8,128)(2,1)} %copy.93.q_ref, bf16[512,768]{1,0:T(8,128)(2,1)} %copy.94.k_ref, bf16[512,768]{1,0:T(8,128)(2,1)} %copy.95.v_ref, bf16[512,768]{1,0:T(8,128)(2,1)} %copy.100.grad_ref, ...), custom_call_target="tpu_custom_call" | custom-call | flops 3221225472 | bytes 7864320 | tf_op jit(solution)/shard_map/pallas_call | solution.py:123
  411.2 1.9 fusion.13
  413.2 1.4 collective-permute-start.7
  415.3 1.3 collective-permute-start.10
  416.9 12.7 %collective-permute-done.7 = bf16[384,768]{1,0:T(8,128)(2,1)} collective-permute-done((bf16[384,768]{1,0:T(8,128)(2,1)S(1)}, bf16[384,768]{1,0:T(8,128)(2,1)}, u32[]{:S(2)}, u32[]{:S(2)}) %collective-permute-start.7) | collective-permute-done | bytes 589856 | tf_op jit(solution)/shard_map/ppermute | solution.py:181
  429.6 1.3 convert_add_fusion.1
  430.9 1.3 collective-permute-start.8
  432.5 11.7 %collective-permute-done.8 = bf16[192,768]{1,0:T(8,128)(2,1)S(1)} collective-permute-done((bf16[192,768]{1,0:T(8,128)(2,1)S(1)}, bf16[192,768]{1,0:T(8,128)(2,1)S(1)}, u32[]{:S(2)}, u32[]{:S(2)}) %collective-permute-start.8) | collective-permute-done | bytes 294944 | tf_op jit(solution)/shard_map/ppermute | solution.py:181
  445.9 14.5 %reduce-scatter.13.cloned.1.call-done = bf16[288,768]{1,0:T(8,128)(2,1)} async-done(((bf16[2304,768]{1,0:T(8,128)(2,1)}), bf16[288,768]{1,0:T(8,128)(2,1)}) %reduce-scatter.13.cloned.1.call-update) | async-done | bytes 442384
  460.3 1.3 copy.119
  461.7 1.5 select_maximum_fusion
  464.4 1.6 collective-permute-start.14
  467.6 6.8 %collective-permute-done.14 = bf16[192,768]{1,0:T(8,128)(2,1)S(1)} collective-permute-done((bf16[192,768]{1,0:T(8,128)(2,1)S(1)}, bf16[192,768]{1,0:T(8,128)(2,1)S(1)}, u32[]{:S(2)}, u32[]{:S(2)}) %collective-permute-start.14) | collective-permute-done | bytes 294944 | tf_op jit(solution)/shard_map/ppermute | solution.py:191
  474.5 4.8 collective-permute-done.11
  479.8 1.6 maximum_convert_fusion.1
  481.8 1.6 maximum_convert_fusion
  483.4 15.5 %reduce-scatter.11.cloned.1.call-done = f32[1,416,192]{1,2,0:T(8,128)} async-done(((f32[4,416,192]{1,2,0:T(8,128)}), f32[1,416,192]{1,2,0:T(8,128)}) %reduce-scatter.11.cloned.1.call-update) | async-done | bytes 319504 | tf_op jit(solution)/shard_map/reduce_scatter | solution.py:374
  498.9 1.3 fusion.47
  500.2 1.5 copy.101
  502.3 2.1 fusion.25
  504.4 2.2 fusion.22
  506.6 3.3 fusion.11
  509.9 21.9 %all-gather.15.cloned.1.call-done = f32[8,416,192]{1,2,0:T(8,128)} async-done(((f32[1,416,192]{1,2,0:T(8,128)}), f32[8,416,192]{1,2,0:T(8,128)}) %all-gather.15.cloned.1.call-update) | async-done | bytes 2555920 | tf_op jit(solution)/shard_map/all_gather | solution.py:388
  531.8 3.2 slice.115
  535.1 2.2 copy.107
  537.3 1.8 copy.116
  539.1 1.4 slice.118
  542.0 1.2 slice_reduce_fusion
  (191 shorter events, 39.5 us)
Async XLA Ops:
  7.2 156.7 %copy-start = (bf16[768,768]{1,0:T(8,128)(2,1)S(1)}, bf16[768,768]{1,0:T(8,128)(2,1)}, u32[]{:S(2)}) copy-start(bf16[768,768]{1,0:T(8,128)(2,1)} %param.24) | copy-start | bytes 3538948
  7.2 1.4 copy-start.27
  7.2 1.5 copy-start.17
  7.2 59.4 %all-gather.13.cloned.1.call-start = ((), (), s32[]{:S(2)}) async-start(), calls=%async_computation.9 | async-start | bytes 3194880 | tf_op jit(solution)/shard_map/all_gather | solution.py:234
  8.6 58.0 %copy-start.31 = (s32[4]{0:T(128)S(1)}, s32[4]{0:T(128)}, u32[]{:S(2)}) copy-start(s32[4]{0:T(128)} %param.17) | copy-start | bytes 52
  9.8 154.1 %all-gather.9.cloned.1.call-start = ((), (), s32[]{:S(2)}) async-start(), calls=%async_computation.4 | async-start | bytes 3932160 | tf_op jit(solution)/shard_map/all_gather | solution.py:268
  66.6 5.2 collective-permute-start
  67.2 7.9 %copy-start.29 = (bf16[512,768]{1,0:T(8,128)(2,1)S(1)}, bf16[512,768]{1,0:T(8,128)(2,1)}, u32[]{:S(2)}) copy-start(bf16[512,768]{1,0:T(8,128)(2,1)} %rest_0_.1) | copy-start | bytes 2359300
  74.7 1.5 copy-start.8
  74.7 2.3 copy-start.11
  95.7 1.4 copy-start.30
  99.5 0.7 copy-start.18
  99.5 0.7 copy-start.19
  100.2 1.3 copy-start.26
  101.5 134.1 %reduce-scatter.7.cloned.1.call-start = ((), (), s32[]{:S(2)}) async-start(), calls=%async_computation.5 | async-start | bytes 3932160 | tf_op jit(solution)/shard_map/reduce_scatter | solution.py:272
  163.8 8.5 %copy-start.28 = (bf16[768,768]{1,0:T(8,128)(2,1)S(1)}, bf16[768,768]{1,0:T(8,128)(2,1)}, u32[]{:S(2)}) copy-start(bf16[768,768]{1,0:T(8,128)(2,1)} %param.26) | copy-start | bytes 3538948
  170.6 1.7 copy-start.32
  176.3 59.2 %copy-start.24 = (f32[768]{0:T(1024)S(1)}, f32[768]{0:T(1024)}, u32[]{:S(2)}) copy-start(f32[768]{0:T(1024)} %param.27) | copy-start | bytes 9220
  176.3 130.2 %all-gather.11.cloned.1.call-start = ((), (), s32[]{:S(2)}) async-start(), calls=%async_computation.6 | async-start | bytes 3932160 | tf_op jit(solution)/shard_map/all_gather | solution.py:284
  237.3 1.1 copy-start.13
  237.3 1.1 copy-start.20
  237.6 1.5 copy-start.25
  240.7 1.1 copy-start.2
  243.0 136.6 %reduce-scatter.9.cloned.1.call-start = ((), (), s32[]{:S(2)}) async-start(), calls=%async_computation.7 | async-start | bytes 3932160 | tf_op jit(solution)/shard_map/reduce_scatter | solution.py:296
  313.5 1.7 copy-start.33
  319.2 141.2 %reduce-scatter.13.cloned.1.call-start = ((), (), s32[]{:S(2)}) async-start(), calls=%async_computation.11 | async-start | bytes 3981312
  335.5 3.0 collective-permute-start.4
  335.5 6.2 %collective-permute-start.1 = (f32[384,768]{1,0:T(8,128)}, f32[384,768]{1,0:T(8,128)}, u32[]{:S(2)}, u32[]{:S(2)}) collective-permute-start(f32[384,768]{1,0:T(8,128)} %get-tuple-element.139), channel_id=1, source_target_pairs={{0,4},{4,0},{8,12},{12,8},{16,20},{20,16},{24,28},{28,24},{1,5},{5... | collective-permute-start | bytes 3538952 | tf_op jit(solution)/shard_map/ppermute | solution.py:181
  336.0 5.7 %copy-start.15 = (f32[768,768]{1,0:T(8,128)S(1)}, f32[768,768]{1,0:T(8,128)}, u32[]{:S(2)}) copy-start(f32[768,768]{1,0:T(8,128)} %shard_map.256) | copy-start | bytes 7077892
  340.3 16.4 %collective-permute-start.5 = (f32[192,768]{1,0:T(8,128)S(1)}, f32[192,768]{1,0:T(8,128)}, u32[]{:S(2)}, u32[]{:S(2)}) collective-permute-start(f32[192,768]{1,0:T(8,128)S(1)} %constant_dynamic-slice_fusion.1), channel_id=1, source_target_pairs={{0,8},{4,12},{8,0},{12,4},{16,24},{20,28},{24,16},{28,20},{1,9},{5... | collective-permute-start | bytes 1769480 | tf_op jit(solution)/shard_map/ppermute | solution.py:181
  343.2 1.0 copy-start.9
  345.0 23.5 %collective-permute-start.2 = (f32[192,768]{1,0:T(8,128)}, f32[192,768]{1,0:T(8,128)}, u32[]{:S(2)}, u32[]{:S(2)}) collective-permute-start(f32[192,768]{1,0:T(8,128)} %constant_dynamic-slice_fusion.4), channel_id=1, source_target_pairs={{0,8},{4,12},{8,0},{12,4},{16,24},{20,28},{24,16},{28,20},{1,9},{5... | collective-permute-start | bytes 1769480 | tf_op jit(solution)/shard_map/ppermute | solution.py:181
  345.7 22.8 %copy-start.10 = (f32[384,768]{1,0:T(8,128)S(1)}, f32[384,768]{1,0:T(8,128)}, u32[]{:S(2)}) copy-start(f32[384,768]{1,0:T(8,128)} %copy-done.9) | copy-start | bytes 3538948
  358.6 15.6 %collective-permute-start.6 = (f32[96,768]{1,0:T(8,128)}, f32[96,768]{1,0:T(8,128)S(1)}, u32[]{:S(2)}, u32[]{:S(2)}) collective-permute-start(f32[96,768]{1,0:T(8,128)} %constant_dynamic-slice_fusion), channel_id=1, source_target_pairs={{0,16},{4,20},{8,24},{12,28},{16,0},{20,4},{24,8},{28,12},{1,17},{... | collective-permute-start | bytes 884744 | tf_op jit(solution)/shard_map/ppermute | solution.py:181
  370.4 8.5 %collective-permute-start.3 = (f32[96,768]{1,0:T(8,128)}, f32[96,768]{1,0:T(8,128)S(1)}, u32[]{:S(2)}, u32[]{:S(2)}) collective-permute-start(f32[96,768]{1,0:T(8,128)} %constant_dynamic-slice_fusion.3), channel_id=1, source_target_pairs={{0,16},{4,20},{8,24},{12,28},{16,0},{20,4},{24,8},{28,12},{1,17},{... | collective-permute-start | bytes 884744 | tf_op jit(solution)/shard_map/ppermute | solution.py:181
  379.6 2.6 copy-start.3
  379.6 2.6 copy-start.14
  383.1 2.7 copy-start.6
  383.1 1.8 copy-start.16
  383.1 2.6 copy-start.22
  409.9 89.0 %reduce-scatter.11.cloned.1.call-start = ((), (), s32[]{:S(2)}) async-start(), calls=%async_computation.8 | async-start | bytes 1966080 | tf_op jit(solution)/shard_map/reduce_scatter | solution.py:374
  413.2 16.4 %collective-permute-start.7 = (bf16[384,768]{1,0:T(8,128)(2,1)S(1)}, bf16[384,768]{1,0:T(8,128)(2,1)}, u32[]{:S(2)}, u32[]{:S(2)}) collective-permute-start(bf16[384,768]{1,0:T(8,128)(2,1)S(1)} %dynamic-slice_convert_fusion), channel_id=1, source_target_pairs={{0,16},{4,20},{8,24},{12,28},{16,0},{20,4},{24,8},{28,12},{1,17},{... | collective-permute-start | bytes 1769480 | tf_op jit(solution)/shard_map/ppermute | solution.py:181
  414.6 48.7 %collective-permute-start.13 = (bf16[96,768]{1,0:T(8,128)(2,1)}, bf16[96,768]{1,0:T(8,128)(2,1)}, u32[]{:S(2)}, u32[]{:S(2)}) collective-permute-start(bf16[96,768]{1,0:T(8,128)(2,1)} %dynamic-slice_add_fusion.4), channel_id=1, source_target_pairs={{0,16},{4,20},{8,24},{12,28},{16,0},{20,4},{24,8},{28,12},{1,17},{... | collective-permute-start | bytes 442376 | tf_op jit(solution)/shard_map/ppermute | solution.py:191
  415.3 50.6 %collective-permute-start.10 = (bf16[96,768]{1,0:T(8,128)(2,1)}, bf16[96,768]{1,0:T(8,128)(2,1)}, u32[]{:S(2)}, u32[]{:S(2)}) collective-permute-start(bf16[96,768]{1,0:T(8,128)(2,1)} %dynamic-slice_add_fusion.5), channel_id=1, source_target_pairs={{0,16},{4,20},{8,24},{12,28},{16,0},{20,4},{24,8},{28,12},{1,17},{... | collective-permute-start | bytes 442376 | tf_op jit(solution)/shard_map/ppermute | solution.py:191
  416.9 15.3 %copy-start.21 = (f32[1,1,1,4,1,192]{5,3,4,2,1,0:T(4,128)S(1)}, f32[1,1,1,4,1,192]{5,3,4,2,1,0:T(4,128)}, u32[]{:S(2)}) copy-start(f32[1,1,1,4,1,192]{5,3,4,2,1,0:T(4,128)} %stack.25) | copy-start | bytes 9220
  416.9 15.3 %copy-start.4 = (bf16[3,512,768]{2,1,0:T(8,128)(2,1)S(1)}, bf16[3,512,768]{2,1,0:T(8,128)(2,1)}, u32[]{:S(2)}) copy-start(bf16[3,512,768]{2,1,0:T(8,128)(2,1)} %get-tuple-element.22) | copy-start | bytes 7077892
  430.9 13.2 %collective-permute-start.8 = (bf16[192,768]{1,0:T(8,128)(2,1)S(1)}, bf16[192,768]{1,0:T(8,128)(2,1)S(1)}, u32[]{:S(2)}, u32[]{:S(2)}) collective-permute-start(bf16[192,768]{1,0:T(8,128)(2,1)S(1)} %dynamic-slice_convert_fusion.1), channel_id=1, source_target_pairs={{0,8},{4,12},{8,0},{12,4},{16,24},{20,28},{24,16},{28,20},{1,9},{5... | collective-permute-start | bytes 884744 | tf_op jit(solution)/shard_map/ppermute | solution.py:181
  444.2 1.4 collective-permute-start.9
  463.3 68.6 %all-gather.15.cloned.1.call-start = ((), (), s32[]{:S(2)}) async-start(), calls=%async_computation.10 | async-start | bytes 3538944 | tf_op jit(solution)/shard_map/all_gather | solution.py:388
  464.4 9.9 %collective-permute-start.14 = (bf16[192,768]{1,0:T(8,128)(2,1)S(1)}, bf16[192,768]{1,0:T(8,128)(2,1)S(1)}, u32[]{:S(2)}, u32[]{:S(2)}) collective-permute-start(bf16[192,768]{1,0:T(8,128)(2,1)S(1)} %pad_maximum_fusion.3), channel_id=1, source_target_pairs={{0,8},{4,12},{8,0},{12,4},{16,24},{20,28},{24,16},{28,20},{1,9},{5... | collective-permute-start | bytes 884744 | tf_op jit(solution)/shard_map/ppermute | solution.py:191
  466.9 12.4 %collective-permute-start.11 = (bf16[192,768]{1,0:T(8,128)(2,1)S(1)}, bf16[192,768]{1,0:T(8,128)(2,1)S(1)}, u32[]{:S(2)}, u32[]{:S(2)}) collective-permute-start(bf16[192,768]{1,0:T(8,128)(2,1)S(1)} %pad_maximum_fusion.2), channel_id=1, source_target_pairs={{0,8},{4,12},{8,0},{12,4},{16,24},{20,28},{24,16},{28,20},{1,9},{5... | collective-permute-start | bytes 884744 | tf_op jit(solution)/shard_map/ppermute | solution.py:191
  474.5 5.1 collective-permute-start.15
  479.5 2.1 collective-permute-start.12
  481.8 17.1 %copy-start.5 = (bf16[3,512,768]{2,1,0:T(8,128)(2,1)S(1)}, bf16[3,512,768]{2,1,0:T(8,128)(2,1)}, u32[]{:S(2)}) copy-start(bf16[3,512,768]{2,1,0:T(8,128)(2,1)} %get-tuple-element.22) | copy-start | bytes 7077892
  500.2 1.5 copy-start.12
  504.4 2.2 copy-start.7
  504.4 2.2 copy-start.23
  540.9 8.5 %copy-start.1 = (bf16[768,768]{1,0:T(8,128)(2,1)S(1)}, bf16[768,768]{1,0:T(8,128)(2,1)}, u32[]{:S(2)}) copy-start(bf16[768,768]{1,0:T(8,128)(2,1)} %param.24) | copy-start | bytes 3538948
Sparse Core Ops, SparseCore 0:
  10.2 56.3 all-gather.12
  101.6 62.2 all-gather.8
  176.4 59.0 reduce-scatter.6
  243.1 63.3 all-gather.10
  319.3 59.0 reduce-scatter.8
  410.0 50.2 reduce-scatter.12
  463.4 35.4 reduce-scatter.10
  500.8 31.0 all-gather.14

commit v16 on v14

--- a/solution.py
+++ b/solution.py
@@ -377,7 +377,7 @@
         ).astype(jnp.float32)
         joined = jnp.concatenate([late, early, tail], axis=0)
         joined = lax.psum_scatter(
-            joined.reshape(joined.shape[0], groups, shard).transpose(1, 0, 2),
+            joined.reshape(joined.shape[0], groups, shard).transpose(1, 0, 2).astype(jnp.bfloat16),
             "tensor",
             scatter_dimension=0,
             tiled=True,
@@ -390,7 +390,7 @@
         grad_up_weight, grad_down_weight = ffn_grads
         late_rows = late.shape[0]
         early_rows = early.shape[0]
-        joined = lax.all_gather(joined, "dp", axis=0, tiled=False)
+        joined = lax.all_gather(joined, "dp", axis=0, tiled=False).astype(jnp.float32)
         early = joined[:, late_rows : late_rows + early_rows]
         if early_halved:
             order = bit_reversed(dp_size)

time: 553 us -> 542 us (0.980)
  waiting for transfers between devices: 358 us -> 344 us
  other arithmetic: 32 us -> 37.9 us
    ppermute x6, waiting for transfers between devices: 11.7 us -> 0.43 us  [dp_double(): got = lax.ppermute(kept, 'dp', [(i, i ^ 1 << step) for i in range(dp_size)])]
    ppermute x9, waiting for transfers between devices: 37.5 us -> 45.4 us  [dp_halve(): got = lax.ppermute(give, 'dp', [(i, i ^ 1 << step) for i in range(dp_size)])]
    reduce_scatter x1, waiting for transfers between devices: 24.7 us -> 18.2 us  [per_device(): lax.psum_scatter(grad_qkv_low.reshape(3 * width, width), 'dp', scatter_di...]
    all_gather x1, waiting for transfers between devices: 22 us -> 16 us  [per_device(): lax.all_gather(joined, 'dp', axis=0, tiled=False).astype(jnp.float32)]
    unnamed x76 -> x90, local copies, waits for them, and re-layouts: 11.3 us -> 12.6 us
  transfers between devices with their start and end apart: 24 -> 24, of which waited for: 18 -> 15; matrix products, arithmetic and copies ran while one was open for 7% -> 8% of each run, Pallas kernels for 2% -> 2%
where the time goes in v16:
time: 542 us; the launch traced here: 541 us
  waiting for transfers between devices  344 us (63%)
  Pallas kernels  49.3 us (9%)
  local copies, waits for them, and re-layouts  42.9 us (8%)
  matrix products  38.6 us (7%)
  other arithmetic  37.9 us (7%)
  between operations  14.9 us (3%)
  starting transfers between devices  13 us (2%)
    all_gather x1, waiting for transfers between devices, per_device(): branch_rows = lax.all_gather(branch_grad, 'tensor', axis=0, tiled=True)  63.3 us
    all_gather x1, waiting for transfers between devices, per_device(): ffn_rows = lax.all_gather(middle_low, 'tensor', axis=0, tiled=True)  62.3 us
    reduce_scatter x1, waiting for transfers between devices, per_device(): lax.psum_scatter(jnp.dot(hidden, down_weight, preferred_element_type=jnp....  59.2 us
    all_gather x1, waiting for transfers between devices, per_device(): mine = lax.all_gather(mine, 'tensor', axis=0, tiled=False)  56.8 us
    ppermute x9, waiting for transfers between devices, dp_halve(): got = lax.ppermute(give, 'dp', [(i, i ^ 1 << step) for i in range(dp_size)])  45.4 us
    pallas_call x1, Pallas kernels, attention_backward(): pl.pallas_call(functools.partial(_bwd_kernel, heads=pair, factor=factor),...  22.8 us
    reduce_scatter x1, waiting for transfers between devices, per_device(): lax.psum_scatter(grad_qkv_low.reshape(3 * width, width), 'dp', scatter_di...  18.2 us
    reduce_scatter x1, waiting for transfers between devices, per_device(): lax.psum_scatter(joined.reshape(joined.shape[0], groups, shard).transpose...  17.8 us
  transfers between devices with their start and end apart: 24, of which 15 were waited for; matrix products, arithmetic and copies ran while one was open for 8% of the time, Pallas kernels for 2%

profile of v16, /device:TPU:0, one launch (start us, length us, event | category | flops | bytes accessed | tf_op | source)
XLA Modules:
  0.0 540.8 jit_solution(8485908286097848488)
XLA Ops:
  7.3 1.3 slice_bitcast_fusion.2
  9.8 56.8 %all-gather.13.cloned.1.call-done = bf16[4,1544,192]{1,2,0:T(8,128)(2,1)} async-done(((bf16[1,1544,192]{1,2,0:T(8,128)(2,1)}), bf16[4,1544,192]{1,2,0:T(8,128)(2,1)}) %all-gather.13.cloned.1.call-update) | async-done | bytes 2371600 | tf_op jit(solution)/shard_map/all_gather | solution.py:239
  67.2 4.6 collective-permute-done
  71.8 3.0 broadcast_select_fusion
  77.0 1.2 copy.73.v_ref
  78.2 2.1 add_convert_fusion.2
  80.3 1.2 copy.71.q_ref
  81.4 1.2 copy.72.k_ref
  82.6 13.0 %shard_map.254 = bf16[512,768]{1,0:T(8,128)(2,1)} custom-call(s32[1]{0:T(128)} %dynamic_slice.57.len_ref, bf16[512,768]{1,0:T(8,128)(2,1)} %copy.71.q_ref, bf16[512,768]{1,0:T(8,128)(2,1)} %copy.72.k_ref, bf16[512,768]{1,0:T(8,128)(2,1)} %copy.73.v_ref), custom_call_target="tpu_custom_call" | custom-call | flops 805306368 | bytes 3145728 | tf_op jit(solution)/shard_map/pallas_call | solution.py:92
  95.6 1.4 copy.74
  97.1 2.4 fusion.54
  100.2 1.2 fusion.14
  101.5 62.3 %all-gather.9.cloned.1.call-done.left_ref = bf16[2048,768]{1,0:T(8,128)(2,1)} async-done(((bf16[512,768]{1,0:T(8,128)(2,1)}), bf16[2048,768]{1,0:T(8,128)(2,1)}) %all-gather.9.cloned.1.call-update) | async-done | bytes 3145744 | tf_op jit(solution)/shard_map/all_gather | solution.py:273
  163.8 6.8 %multiply_convert_fusion = (bf16[2048,768]{1,0:T(8,128)(2,1)S(1)}, f32[2048,768]{1,0:T(8,128)}) fusion(f32[768]{0:T(1024)S(1)} %convert_element_type.160, bf16[2048,768]{1,0:T(8,128)(2,1)} %all-gather.9.cloned.1.call-done.left_ref, bf16[768,768]{1,0:T(8,128)(2,1)S(1)} %copy-done), kind=kOutput, calls=%fused_computation.8 | convolution fusion | flops 2425356288 | bytes 13765632 | tf_op jit(solution)/shard_map/dot_general | solution.py:274
  170.6 1.7 copy-done.39
  172.3 4.0 convolution_convert_fusion.1
  176.4 59.2 %reduce-scatter.5.cloned.1.call-done = bf16[512,768]{1,0:T(8,128)(2,1)} async-done(((bf16[2048,768]{1,0:T(8,128)(2,1)}), bf16[512,768]{1,0:T(8,128)(2,1)}) %reduce-scatter.5.cloned.1.call-update) | async-done | bytes 786448 | tf_op jit(solution)/shard_map/reduce_scatter | solution.py:277
  235.5 1.7 fusion.51
  239.2 1.6 fusion.50
  243.2 63.3 %all-gather.11.cloned.1.call-done.right_ref = bf16[2048,768]{1,0:T(8,128)(2,1)} async-done(((bf16[512,768]{1,0:T(8,128)(2,1)}), bf16[2048,768]{1,0:T(8,128)(2,1)}) %all-gather.11.cloned.1.call-update) | async-done | bytes 3145744 | tf_op jit(solution)/shard_map/all_gather | solution.py:289
  306.5 7.4 %convert_reduce_fusion = (bf16[768]{0:T(1024)(128)(2,1)S(1)}, bf16[2048,768]{1,0:T(8,128)(2,1)S(1)}) fusion(f32[2048,768]{1,0:T(8,128)} %get-tuple-element.129, f32[768]{0:T(1024)S(1)} %convert_element_type.160, bf16[2048,768]{1,0:T(8,128)(2,1)} %all-gather.11.cloned.1.call-done.right_ref, bf16[768,768]{1,0:T(8,128)(2,1)} %param.26), kind=kOutput, calls=%fused_computation.7 | convolution fusion | flops 2436365568 | bytes 13767168 | tf_op jit(solution)/shard_map/dot_general | solution.py:31
  313.9 1.7 copy-done.40
  315.6 4.0 convolution_convert_fusion
  319.7 6.8 %shard_map.257 = f32[768,768]{1,0:T(8,128)} custom-call(bf16[2048,768]{1,0:T(8,128)(2,1)} %copy-done.39, bf16[2048,768]{1,0:T(8,128)(2,1)} %all-gather.11.cloned.1.call-done.right_ref), custom_call_target="tpu_custom_call" | custom-call | flops 2415919104 | bytes 8650752 | tf_op jit(solution)/shard_map/pallas_call | solution.py:149
  326.5 6.7 %shard_map.256 = f32[768,768]{1,0:T(8,128)} custom-call(bf16[2048,768]{1,0:T(8,128)(2,1)} %all-gather.9.cloned.1.call-done.left_ref, bf16[2048,768]{1,0:T(8,128)(2,1)} %copy-done.40), custom_call_target="tpu_custom_call" | custom-call | flops 2415919104 | bytes 8650752 | tf_op jit(solution)/shard_map/pallas_call | solution.py:149
  333.2 2.8 constant_dynamic-slice_fusion.2
  336.5 2.5 collective-permute-done.4
  339.0 1.8 dynamic-slice_add_fusion
  340.8 1.4 collective-permute-start.5
  342.2 1.4 dynamic-slice_add_fusion.1
  346.2 11.0 %collective-permute-done.5 = f32[192,768]{1,0:T(8,128)} collective-permute-done((f32[192,768]{1,0:T(8,128)S(1)}, f32[192,768]{1,0:T(8,128)}, u32[]{:S(2)}, u32[]{:S(2)}) %collective-permute-start.5) | collective-permute-done | bytes 589856 | tf_op jit(solution)/shard_map/ppermute | solution.py:181
  358.3 1.4 collective-permute-start.6
  359.8 9.3 %collective-permute-done.2 = f32[192,768]{1,0:T(8,128)} collective-permute-done((f32[192,768]{1,0:T(8,128)}, f32[192,768]{1,0:T(8,128)}, u32[]{:S(2)}, u32[]{:S(2)}) %collective-permute-start.2) | collective-permute-done | bytes 589856 | tf_op jit(solution)/shard_map/ppermute | solution.py:181
  370.9 1.4 collective-permute-start.3
  372.3 2.4 slice.151
  375.6 3.8 collective-permute-done.3
  379.5 1.7 dynamic-slice_add_fusion.5
  381.1 2.6 multiply_reduce_fusion
  384.9 1.6 copy-done.17
  387.4 1.2 copy.78.grad_ref
  388.5 22.8 %shard_map.255 = (bf16[3,512,768]{2,1,0:T(8,128)(2,1)}, bf16[3,768,768]{2,1,0:T(8,128)(2,1)}) custom-call(s32[1]{0:T(128)} %dynamic_slice.57.len_ref, bf16[512,768]{1,0:T(8,128)(2,1)} %copy.71.q_ref, bf16[512,768]{1,0:T(8,128)(2,1)} %copy.72.k_ref, bf16[512,768]{1,0:T(8,128)(2,1)} %copy.73.v_ref, bf16[512,768]{1,0:T(8,128)(2,1)} %copy.78.grad_ref, ...), custom_call_target="tpu_custom_call" | custom-call | flops 3221225472 | bytes 7864320 | tf_op jit(solution)/shard_map/pallas_call | solution.py:123
  412.2 1.4 collective-permute-start.13
  414.3 1.9 fusion.13
  416.7 1.8 slice_reduce_fusion
  419.3 1.3 collective-permute-start.14
  420.7 1.2 convert_add_fusion.1
  424.5 1.3 collective-permute-start.11
  425.8 11.1 %collective-permute-done.8 = bf16[192,768]{1,0:T(8,128)(2,1)S(1)} collective-permute-done((bf16[192,768]{1,0:T(8,128)(2,1)S(1)}, bf16[192,768]{1,0:T(8,128)(2,1)S(1)}, u32[]{:S(2)}, u32[]{:S(2)}) %collective-permute-start.8) | collective-permute-done | bytes 294944 | tf_op jit(solution)/shard_map/ppermute | solution.py:181
  437.0 1.2 collective-permute-start.9
  438.4 7.7 %collective-permute-done.9 = bf16[96,768]{1,0:T(8,128)(2,1)S(1)} collective-permute-done((bf16[96,768]{1,0:T(8,128)(2,1)S(1)}, bf16[96,768]{1,0:T(8,128)(2,1)S(1)}, u32[]{:S(2)}, u32[]{:S(2)}) %collective-permute-start.9) | collective-permute-done | bytes 147488 | tf_op jit(solution)/shard_map/ppermute | solution.py:181
  446.2 18.2 %reduce-scatter.9.cloned.1.call-done = bf16[288,768]{1,0:T(8,128)(2,1)} async-done(((bf16[2304,768]{1,0:T(8,128)(2,1)}), bf16[288,768]{1,0:T(8,128)(2,1)}) %reduce-scatter.9.cloned.1.call-update) | async-done | bytes 442384 | tf_op jit(solution)/shard_map/reduce_scatter | solution.py:372
  465.5 1.2 copy.82
  468.9 1.6 maximum_convert_fusion.1
  471.1 1.6 maximum_convert_fusion
  472.7 17.8 %reduce-scatter.11.cloned.1.call-done = bf16[1,416,192]{1,2,0:T(8,128)(2,1)} async-done(((bf16[4,416,192]{1,2,0:T(8,128)(2,1)}), bf16[1,416,192]{1,2,0:T(8,128)(2,1)}) %reduce-scatter.11.cloned.1.call-update) | async-done | bytes 159760 | tf_op jit(solution)/shard_map/reduce_scatter | solution.py:379
  490.6 1.3 fusion.52
  491.9 1.5 copy.79
  493.9 2.1 fusion.25
  496.0 2.2 fusion.22
  498.2 3.3 fusion.11
  501.5 16.0 %all-gather.15.cloned.1.call-done = bf16[8,416,192]{1,2,0:T(8,128)(2,1)} async-done(((bf16[1,416,192]{1,2,0:T(8,128)(2,1)}), bf16[8,416,192]{1,2,0:T(8,128)(2,1)}) %all-gather.15.cloned.1.call-update) | async-done | bytes 1277968 | tf_op jit(solution)/shard_map/all_gather | solution.py:393
  517.5 1.8 convert_element_type.195
  521.4 2.1 copy.83
  523.5 3.0 copy.91
  (202 shorter events, 37.8 us)
Async XLA Ops:
  7.2 156.6 %copy-start = (bf16[768,768]{1,0:T(8,128)(2,1)S(1)}, bf16[768,768]{1,0:T(8,128)(2,1)}, u32[]{:S(2)}) copy-start(bf16[768,768]{1,0:T(8,128)(2,1)} %param.24) | copy-start | bytes 3538948
  7.2 1.4 copy-start.34
  7.2 1.5 copy-start.26
  7.2 59.4 %all-gather.13.cloned.1.call-start = ((), (), s32[]{:S(2)}) async-start(), calls=%async_computation.10 | async-start | bytes 3194880 | tf_op jit(solution)/shard_map/all_gather | solution.py:239
  8.6 58.0 %copy-start.38 = (s32[4]{0:T(128)S(1)}, s32[4]{0:T(128)}, u32[]{:S(2)}) copy-start(s32[4]{0:T(128)} %param.17) | copy-start | bytes 52
  9.8 154.0 %all-gather.9.cloned.1.call-start = ((), (), s32[]{:S(2)}) async-start(), calls=%async_computation.4 | async-start | bytes 3932160 | tf_op jit(solution)/shard_map/all_gather | solution.py:273
  66.6 5.2 collective-permute-start
  67.2 7.9 %copy-start.36 = (bf16[512,768]{1,0:T(8,128)(2,1)S(1)}, bf16[512,768]{1,0:T(8,128)(2,1)}, u32[]{:S(2)}) copy-start(bf16[512,768]{1,0:T(8,128)(2,1)} %rest_0_.1) | copy-start | bytes 2359300
  74.7 1.5 copy-start.9
  74.7 2.3 copy-start.12
  95.6 1.4 copy-start.37
  99.5 0.7 copy-start.29
  100.2 1.3 copy-start.33
  101.4 134.1 %reduce-scatter.5.cloned.1.call-start = ((), (), s32[]{:S(2)}) async-start(), calls=%async_computation.5 | async-start | bytes 3932160 | tf_op jit(solution)/shard_map/reduce_scatter | solution.py:277
  163.8 8.5 %copy-start.35 = (bf16[768,768]{1,0:T(8,128)(2,1)S(1)}, bf16[768,768]{1,0:T(8,128)(2,1)}, u32[]{:S(2)}) copy-start(bf16[768,768]{1,0:T(8,128)(2,1)} %param.26) | copy-start | bytes 3538948
  170.6 1.7 copy-start.39
  176.3 59.2 %copy-start.31 = (f32[768]{0:T(1024)S(1)}, f32[768]{0:T(1024)}, u32[]{:S(2)}) copy-start(f32[768]{0:T(1024)} %param.27) | copy-start | bytes 9220
  176.3 130.2 %all-gather.11.cloned.1.call-start = ((), (), s32[]{:S(2)}) async-start(), calls=%async_computation.6 | async-start | bytes 3932160 | tf_op jit(solution)/shard_map/all_gather | solution.py:289
  237.3 1.1 copy-start.14
  237.3 1.1 copy-start.30
  237.6 1.5 copy-start.32
  240.8 1.1 copy-start.2
  243.0 138.1 %reduce-scatter.7.cloned.1.call-start = ((), (), s32[]{:S(2)}) async-start(), calls=%async_computation.7 | async-start | bytes 3932160 | tf_op jit(solution)/shard_map/reduce_scatter | solution.py:301
  313.9 1.7 copy-start.40
  319.6 144.8 %reduce-scatter.9.cloned.1.call-start = ((), (), s32[]{:S(2)}) async-start(), calls=%async_computation.8 | async-start | bytes 3981312 | tf_op jit(solution)/shard_map/reduce_scatter | solution.py:372
  336.0 3.0 collective-permute-start.4
  336.0 6.2 %collective-permute-start.1 = (f32[384,768]{1,0:T(8,128)}, f32[384,768]{1,0:T(8,128)}, u32[]{:S(2)}, u32[]{:S(2)}) collective-permute-start(f32[384,768]{1,0:T(8,128)} %get-tuple-element.133), channel_id=1, source_target_pairs={{0,4},{4,0},{8,12},{12,8},{16,20},{20,16},{24,28},{28,24},{1,5},{5... | collective-permute-start | bytes 3538952 | tf_op jit(solution)/shard_map/ppermute | solution.py:181
  336.5 5.7 %copy-start.16 = (f32[768,768]{1,0:T(8,128)S(1)}, f32[768,768]{1,0:T(8,128)}, u32[]{:S(2)}) copy-start(f32[768,768]{1,0:T(8,128)} %shard_map.256) | copy-start | bytes 7077892
  340.8 16.4 %collective-permute-start.5 = (f32[192,768]{1,0:T(8,128)S(1)}, f32[192,768]{1,0:T(8,128)}, u32[]{:S(2)}, u32[]{:S(2)}) collective-permute-start(f32[192,768]{1,0:T(8,128)S(1)} %constant_dynamic-slice_fusion.1), channel_id=1, source_target_pairs={{0,8},{4,12},{8,0},{12,4},{16,24},{20,28},{24,16},{28,20},{1,9},{5... | collective-permute-start | bytes 1769480 | tf_op jit(solution)/shard_map/ppermute | solution.py:181
  343.6 1.0 copy-start.10
  345.5 23.5 %collective-permute-start.2 = (f32[192,768]{1,0:T(8,128)}, f32[192,768]{1,0:T(8,128)}, u32[]{:S(2)}, u32[]{:S(2)}) collective-permute-start(f32[192,768]{1,0:T(8,128)} %constant_dynamic-slice_fusion.4), channel_id=1, source_target_pairs={{0,8},{4,12},{8,0},{12,4},{16,24},{20,28},{24,16},{28,20},{1,9},{5... | collective-permute-start | bytes 1769480 | tf_op jit(solution)/shard_map/ppermute | solution.py:181
  346.2 22.8 %copy-start.11 = (f32[384,768]{1,0:T(8,128)S(1)}, f32[384,768]{1,0:T(8,128)}, u32[]{:S(2)}) copy-start(f32[384,768]{1,0:T(8,128)} %copy-done.10) | copy-start | bytes 3538948
  358.3 16.3 %collective-permute-start.6 = (f32[96,768]{1,0:T(8,128)S(1)}, f32[96,768]{1,0:T(8,128)}, u32[]{:S(2)}, u32[]{:S(2)}) collective-permute-start(f32[96,768]{1,0:T(8,128)S(1)} %constant_dynamic-slice_fusion), channel_id=1, source_target_pairs={{0,16},{4,20},{8,24},{12,28},{16,0},{20,4},{24,8},{28,12},{1,17},{... | collective-permute-start | bytes 884744 | tf_op jit(solution)/shard_map/ppermute | solution.py:181
  370.9 8.6 %collective-permute-start.3 = (f32[96,768]{1,0:T(8,128)}, f32[96,768]{1,0:T(8,128)}, u32[]{:S(2)}, u32[]{:S(2)}) collective-permute-start(f32[96,768]{1,0:T(8,128)} %constant_dynamic-slice_fusion.3), channel_id=1, source_target_pairs={{0,16},{4,20},{8,24},{12,28},{16,0},{20,4},{24,8},{28,12},{1,17},{... | collective-permute-start | bytes 884744 | tf_op jit(solution)/shard_map/ppermute | solution.py:181
  381.1 2.6 copy-start.3
  381.1 2.6 copy-start.15
  384.6 2.7 copy-start.7
  384.6 1.8 copy-start.17
  411.4 79.1 %reduce-scatter.11.cloned.1.call-start = ((), (), s32[]{:S(2)}) async-start(), calls=%async_computation.9 | async-start | bytes 983040 | tf_op jit(solution)/shard_map/reduce_scatter | solution.py:379
  412.2 7.1 %collective-permute-start.13 = (bf16[96,768]{1,0:T(8,128)(2,1)S(1)}, bf16[96,768]{1,0:T(8,128)(2,1)S(1)}, u32[]{:S(2)}, u32[]{:S(2)}) collective-permute-start(bf16[96,768]{1,0:T(8,128)(2,1)S(1)} %dynamic-slice_add_fusion.4), channel_id=1, source_target_pairs={{0,16},{4,20},{8,24},{12,28},{16,0},{20,4},{24,8},{28,12},{1,17},{... | collective-permute-start | bytes 442376 | tf_op jit(solution)/shard_map/ppermute | solution.py:196
  413.6 9.2 %collective-permute-start.10 = (bf16[96,768]{1,0:T(8,128)(2,1)}, bf16[96,768]{1,0:T(8,128)(2,1)}, u32[]{:S(2)}, u32[]{:S(2)}) collective-permute-start(bf16[96,768]{1,0:T(8,128)(2,1)} %dynamic-slice_add_fusion.5), channel_id=1, source_target_pairs={{0,16},{4,20},{8,24},{12,28},{16,0},{20,4},{24,8},{28,12},{1,17},{... | collective-permute-start | bytes 442376 | tf_op jit(solution)/shard_map/ppermute | solution.py:196
  416.3 4.4 collective-permute-start.7
  419.3 18.9 %collective-permute-start.14 = (bf16[192,768]{1,0:T(8,128)(2,1)S(1)}, bf16[192,768]{1,0:T(8,128)(2,1)S(1)}, u32[]{:S(2)}, u32[]{:S(2)}) collective-permute-start(bf16[192,768]{1,0:T(8,128)(2,1)S(1)} %pad_maximum_fusion.4), channel_id=1, source_target_pairs={{0,8},{4,12},{8,0},{12,4},{16,24},{20,28},{24,16},{28,20},{1,9},{5... | collective-permute-start | bytes 884744 | tf_op jit(solution)/shard_map/ppermute | solution.py:196
  421.9 15.0 %collective-permute-start.8 = (bf16[192,768]{1,0:T(8,128)(2,1)S(1)}, bf16[192,768]{1,0:T(8,128)(2,1)S(1)}, u32[]{:S(2)}, u32[]{:S(2)}) collective-permute-start(bf16[192,768]{1,0:T(8,128)(2,1)S(1)} %dynamic-slice_convert_fusion.1), channel_id=1, source_target_pairs={{0,8},{4,12},{8,0},{12,4},{16,24},{20,28},{24,16},{28,20},{1,9},{5... | collective-permute-start | bytes 884744 | tf_op jit(solution)/shard_map/ppermute | solution.py:181
  424.5 42.2 %collective-permute-start.11 = (bf16[192,768]{1,0:T(8,128)(2,1)}, bf16[192,768]{1,0:T(8,128)(2,1)}, u32[]{:S(2)}, u32[]{:S(2)}) collective-permute-start(bf16[192,768]{1,0:T(8,128)(2,1)} %pad_maximum_fusion.3), channel_id=1, source_target_pairs={{0,8},{4,12},{8,0},{12,4},{16,24},{20,28},{24,16},{28,20},{1,9},{5... | collective-permute-start | bytes 884744 | tf_op jit(solution)/shard_map/ppermute | solution.py:196
  437.0 27.5 %copy-start.27 = (bf16[32,768]{1,0:T(8,128)(2,1)S(1)}, bf16[32,768]{1,0:T(8,128)(2,1)}, u32[]{:S(2)}) copy-start(bf16[32,768]{1,0:T(8,128)(2,1)} %fusion.40) | copy-start | bytes 147460
  437.0 9.1 %collective-permute-start.9 = (bf16[96,768]{1,0:T(8,128)(2,1)S(1)}, bf16[96,768]{1,0:T(8,128)(2,1)S(1)}, u32[]{:S(2)}, u32[]{:S(2)}) collective-permute-start(bf16[96,768]{1,0:T(8,128)(2,1)S(1)} %dynamic-slice_convert_fusion.2), channel_id=1, source_target_pairs={{0,16},{4,20},{8,24},{12,28},{16,0},{20,4},{24,8},{28,12},{1,17},{... | collective-permute-start | bytes 442376 | tf_op jit(solution)/shard_map/ppermute | solution.py:181
  438.4 30.3 %collective-permute-start.15 = (bf16[384,768]{1,0:T(8,128)(2,1)S(1)}, bf16[384,768]{1,0:T(8,128)(2,1)S(1)}, u32[]{:S(2)}, u32[]{:S(2)}) collective-permute-start(bf16[384,768]{1,0:T(8,128)(2,1)S(1)} %pad_maximum_fusion.2), channel_id=1, source_target_pairs={{0,4},{4,0},{8,12},{12,8},{16,20},{20,16},{24,28},{28,24},{1,5},{5... | collective-permute-start | bytes 1769480 | tf_op jit(solution)/shard_map/ppermute | solution.py:196
  466.7 50.8 %all-gather.15.cloned.1.call-start = ((), (), s32[]{:S(2)}) async-start(), calls=%async_computation.11 | async-start | bytes 1769472 | tf_op jit(solution)/shard_map/all_gather | solution.py:393
  468.7 2.2 collective-permute-start.12
  471.1 19.4 %copy-start.6 = (bf16[3,512,768]{2,1,0:T(8,128)(2,1)S(1)}, bf16[3,512,768]{2,1,0:T(8,128)(2,1)}, u32[]{:S(2)}) copy-start(bf16[3,512,768]{2,1,0:T(8,128)(2,1)} %get-tuple-element.22) | copy-start | bytes 7077892
  491.9 1.5 copy-start.13
  496.0 2.2 copy-start.8
  519.4 1.9 copy-start.4
  523.5 3.0 copy-start.5
  523.5 10.4 %copy-start.1 = (bf16[768,768]{1,0:T(8,128)(2,1)S(1)}, bf16[768,768]{1,0:T(8,128)(2,1)}, u32[]{:S(2)}) copy-start(bf16[768,768]{1,0:T(8,128)(2,1)} %param.24) | copy-start | bytes 3538948
  526.5 6.3 %copy-start.18 = (f32[96,192]{0,1:T(8,128)S(1)}, f32[96,192]{0,1:T(8,128)}, u32[]{:S(2)}) copy-start(f32[96,192]{0,1:T(8,128)} %get-tuple-element.92) | copy-start | bytes 221188
  526.5 6.3 %copy-start.19 = (f32[96,192]{0,1:T(8,128)S(1)}, f32[96,192]{0,1:T(8,128)}, u32[]{:S(2)}) copy-start(f32[96,192]{0,1:T(8,128)} %get-tuple-element.93) | copy-start | bytes 221188
  526.6 6.3 %copy-start.20 = (f32[96,192]{0,1:T(8,128)S(1)}, f32[96,192]{0,1:T(8,128)}, u32[]{:S(2)}) copy-start(f32[96,192]{0,1:T(8,128)} %get-tuple-element.94) | copy-start | bytes 221188
  526.6 6.3 %copy-start.21 = (f32[96,192]{0,1:T(8,128)S(1)}, f32[96,192]{0,1:T(8,128)}, u32[]{:S(2)}) copy-start(f32[96,192]{0,1:T(8,128)} %get-tuple-element.95) | copy-start | bytes 221188
  526.6 6.3 %copy-start.22 = (f32[96,192]{0,1:T(8,128)S(1)}, f32[96,192]{0,1:T(8,128)}, u32[]{:S(2)}) copy-start(f32[96,192]{0,1:T(8,128)} %get-tuple-element.96) | copy-start | bytes 221188
  526.6 6.3 %copy-start.23 = (f32[96,192]{0,1:T(8,128)S(1)}, f32[96,192]{0,1:T(8,128)}, u32[]{:S(2)}) copy-start(f32[96,192]{0,1:T(8,128)} %get-tuple-element.97) | copy-start | bytes 221188
  526.6 6.3 %copy-start.24 = (f32[96,192]{0,1:T(8,128)S(1)}, f32[96,192]{0,1:T(8,128)}, u32[]{:S(2)}) copy-start(f32[96,192]{0,1:T(8,128)} %get-tuple-element.98) | copy-start | bytes 221188
  526.6 6.3 %copy-start.25 = (f32[96,192]{0,1:T(8,128)S(1)}, f32[96,192]{0,1:T(8,128)}, u32[]{:S(2)}) copy-start(f32[96,192]{0,1:T(8,128)} %get-tuple-element.99) | copy-start | bytes 221188
  (1 other events, 0.7 us)
Sparse Core Ops, SparseCore 0:
  10.2 56.3 all-gather.12
  101.5 62.2 all-gather.8
  176.5 59.0 reduce-scatter.4
  243.1 63.3 all-gather.10
  319.7 59.0 reduce-scatter.6
  411.5 52.8 reduce-scatter.8
  467.3 23.1 reduce-scatter.10
  492.4 25.0 all-gather.14

commit v17 on v16

--- a/solution.py
+++ b/solution.py
@@ -295,7 +295,9 @@
         ffn_grads = (grad_up_weight, grad_down_weight)
         halved = all(dp_pow2(g, dp_size) for g in ffn_grads)
         if halved:
-            ffn_grads = tuple(dp_halve(g, dp_size) for g in ffn_grads)
+            ffn_grads = tuple(
+                dp_halve(g.astype(jnp.bfloat16), dp_size, jnp.float32) for g in ffn_grads
+            )
         else:
             ffn_grads = lax.psum(ffn_grads, "dp")
         middle_part = lax.psum_scatter(

time: 542 us -> 540 us (level)
    ppermute x9, waiting for transfers between devices: 45.4 us -> 24.1 us  [dp_halve(): got = lax.ppermute(give, 'dp', [(i, i ^ 1 << step) for i in range(dp_size)])]
    reduce_scatter x1, waiting for transfers between devices: 0.01 us -> 13.8 us  [per_device(): lax.psum_scatter(contract(pre_grad, up_weight, 1, 1).astype(jnp.bfloat16)...]
    ppermute x6, waiting for transfers between devices: 0.43 us -> 11 us  [dp_double(): got = lax.ppermute(kept, 'dp', [(i, i ^ 1 << step) for i in range(dp_size)])]
    unnamed x90 -> x92, local copies, waits for them, and re-layouts: 12.6 us -> 14.4 us
  transfers between devices with their start and end apart: 24 -> 24, of which waited for: 15 -> 15; matrix products, arithmetic and copies ran while one was open for 8% -> 7% of each run, Pallas kernels for 2% -> 3%
where the time goes in v17:
time: 540 us; the launch traced here: 539 us
  waiting for transfers between devices  347 us (64%)
  Pallas kernels  49.4 us (9%)
  local copies, waits for them, and re-layouts  40.6 us (8%)
  matrix products  38.5 us (7%)
  other arithmetic  35.1 us (6%)
  between operations  14.9 us (3%)
  starting transfers between devices  13.9 us (3%)
    all_gather x1, waiting for transfers between devices, per_device(): branch_rows = lax.all_gather(branch_grad, 'tensor', axis=0, tiled=True)  63.3 us
    all_gather x1, waiting for transfers between devices, per_device(): ffn_rows = lax.all_gather(middle_low, 'tensor', axis=0, tiled=True)  62.3 us
    reduce_scatter x1, waiting for transfers between devices, per_device(): lax.psum_scatter(jnp.dot(hidden, down_weight, preferred_element_type=jnp....  59.2 us
    all_gather x1, waiting for transfers between devices, per_device(): mine = lax.all_gather(mine, 'tensor', axis=0, tiled=False)  56.8 us
    ppermute x9, waiting for transfers between devices, dp_halve(): got = lax.ppermute(give, 'dp', [(i, i ^ 1 << step) for i in range(dp_size)])  24.1 us
    pallas_call x1, Pallas kernels, attention_backward(): pl.pallas_call(functools.partial(_bwd_kernel, heads=pair, factor=factor),...  22.9 us
    reduce_scatter x1, waiting for transfers between devices, per_device(): lax.psum_scatter(joined.reshape(joined.shape[0], groups, shard).transpose...  18.7 us
    reduce_scatter x1, waiting for transfers between devices, per_device(): lax.psum_scatter(grad_qkv_low.reshape(3 * width, width), 'dp', scatter_di...  17.1 us
  transfers between devices with their start and end apart: 24, of which 15 were waited for; matrix products, arithmetic and copies ran while one was open for 7% of the time, Pallas kernels for 3%

profile of v17, /device:TPU:0, one launch (start us, length us, event | category | flops | bytes accessed | tf_op | source)
XLA Modules:
  0.0 539.1 jit_solution(16135501716912936914)
XLA Ops:
  7.3 1.3 slice_bitcast_fusion.2
  9.8 56.8 %all-gather.13.cloned.1.call-done = bf16[4,1544,192]{1,2,0:T(8,128)(2,1)} async-done(((bf16[1,1544,192]{1,2,0:T(8,128)(2,1)}), bf16[4,1544,192]{1,2,0:T(8,128)(2,1)}) %all-gather.13.cloned.1.call-update) | async-done | bytes 2371600 | tf_op jit(solution)/shard_map/all_gather | solution.py:239
  67.2 4.6 collective-permute-done
  71.8 3.0 broadcast_select_fusion
  77.0 1.2 copy.73.v_ref
  78.2 2.1 add_convert_fusion.2
  80.3 1.2 copy.71.q_ref
  81.4 1.2 copy.72.k_ref
  82.6 13.0 %shard_map.254 = bf16[512,768]{1,0:T(8,128)(2,1)} custom-call(s32[1]{0:T(128)} %dynamic_slice.57.len_ref, bf16[512,768]{1,0:T(8,128)(2,1)} %copy.71.q_ref, bf16[512,768]{1,0:T(8,128)(2,1)} %copy.72.k_ref, bf16[512,768]{1,0:T(8,128)(2,1)} %copy.73.v_ref), custom_call_target="tpu_custom_call" | custom-call | flops 805306368 | bytes 3145728 | tf_op jit(solution)/shard_map/pallas_call | solution.py:92
  95.6 1.4 copy.74
  97.0 2.4 fusion.54
  100.2 1.2 fusion.14
  101.5 62.3 %all-gather.9.cloned.1.call-done.left_ref = bf16[2048,768]{1,0:T(8,128)(2,1)} async-done(((bf16[512,768]{1,0:T(8,128)(2,1)}), bf16[2048,768]{1,0:T(8,128)(2,1)}) %all-gather.9.cloned.1.call-update) | async-done | bytes 3145744 | tf_op jit(solution)/shard_map/all_gather | solution.py:273
  163.8 6.7 %multiply_convert_fusion = (bf16[2048,768]{1,0:T(8,128)(2,1)S(1)}, f32[2048,768]{1,0:T(8,128)}) fusion(f32[768]{0:T(1024)S(1)} %convert_element_type.208, bf16[2048,768]{1,0:T(8,128)(2,1)} %all-gather.9.cloned.1.call-done.left_ref, bf16[768,768]{1,0:T(8,128)(2,1)S(1)} %copy-done), kind=kOutput, calls=%fused_computation.8 | convolution fusion | flops 2425356288 | bytes 13765632 | tf_op jit(solution)/shard_map/dot_general | solution.py:274
  170.5 1.7 copy-done.40
  172.2 4.0 convolution_convert_fusion.1
  176.3 59.2 %reduce-scatter.5.cloned.1.call-done = bf16[512,768]{1,0:T(8,128)(2,1)} async-done(((bf16[2048,768]{1,0:T(8,128)(2,1)}), bf16[512,768]{1,0:T(8,128)(2,1)}) %reduce-scatter.5.cloned.1.call-update) | async-done | bytes 786448 | tf_op jit(solution)/shard_map/reduce_scatter | solution.py:277
  235.4 1.7 fusion.51
  239.0 1.6 fusion.50
  243.1 63.3 %all-gather.11.cloned.1.call-done.right_ref = bf16[2048,768]{1,0:T(8,128)(2,1)} async-done(((bf16[512,768]{1,0:T(8,128)(2,1)}), bf16[2048,768]{1,0:T(8,128)(2,1)}) %all-gather.11.cloned.1.call-update) | async-done | bytes 3145744 | tf_op jit(solution)/shard_map/all_gather | solution.py:289
  306.4 7.4 %convert_reduce_fusion = (bf16[768]{0:T(1024)(128)(2,1)S(1)}, bf16[2048,768]{1,0:T(8,128)(2,1)S(1)}) fusion(f32[2048,768]{1,0:T(8,128)} %get-tuple-element.129, f32[768]{0:T(1024)S(1)} %convert_element_type.208, bf16[2048,768]{1,0:T(8,128)(2,1)} %all-gather.11.cloned.1.call-done.right_ref, bf16[768,768]{1,0:T(8,128)(2,1)} %param.26), kind=kOutput, calls=%fused_computation.7 | convolution fusion | flops 2436365568 | bytes 13767168 | tf_op jit(solution)/shard_map/dot_general | solution.py:31
  313.8 1.7 copy-done.41
  315.5 4.0 convolution_convert_fusion
  319.6 6.8 %shard_map.257 = f32[768,768]{1,0:T(8,128)} custom-call(bf16[2048,768]{1,0:T(8,128)(2,1)} %copy-done.40, bf16[2048,768]{1,0:T(8,128)(2,1)} %all-gather.11.cloned.1.call-done.right_ref), custom_call_target="tpu_custom_call" | custom-call | flops 2415919104 | bytes 8650752 | tf_op jit(solution)/shard_map/pallas_call | solution.py:149
  326.4 1.8 convert_convert_fusion
  328.2 1.4 copy-done.8
  329.7 6.7 %shard_map.256 = f32[768,768]{1,0:T(8,128)} custom-call(bf16[2048,768]{1,0:T(8,128)(2,1)} %all-gather.9.cloned.1.call-done.left_ref, bf16[2048,768]{1,0:T(8,128)(2,1)} %copy-done.41), custom_call_target="tpu_custom_call" | custom-call | flops 2415919104 | bytes 8650752 | tf_op jit(solution)/shard_map/pallas_call | solution.py:149
  336.4 1.8 convert_convert_fusion.1
  338.3 1.4 copy-done.6
  340.3 2.5 slice.151
  342.9 1.3 convert_add_fusion.2
  344.3 1.4 collective-permute-start.5
  345.7 1.2 convert_add_fusion.3
  347.6 6.6 %collective-permute-done.5 = bf16[192,768]{1,0:T(8,128)(2,1)S(1)} collective-permute-done((bf16[192,768]{1,0:T(8,128)(2,1)S(1)}, bf16[192,768]{1,0:T(8,128)(2,1)S(1)}, u32[]{:S(2)}, u32[]{:S(2)}) %collective-permute-start.5) | collective-permute-done | bytes 294944 | tf_op jit(solution)/shard_map/ppermute | solution.py:181
  354.3 1.4 collective-permute-start.6
  355.7 3.9 collective-permute-done.2
  359.7 1.4 collective-permute-start.3
  361.8 3.1 collective-permute-done.3
  364.9 13.8 %reduce-scatter.7.cloned.1.call-done = bf16[512,768]{1,0:T(8,128)(2,1)} async-done(((bf16[2048,768]{1,0:T(8,128)(2,1)}), bf16[512,768]{1,0:T(8,128)(2,1)}) %reduce-scatter.7.cloned.1.call-update) | async-done | bytes 786448 | tf_op jit(solution)/shard_map/reduce_scatter | solution.py:303
  378.7 2.6 multiply_reduce_fusion
  382.4 1.6 copy-done.18
  386.1 22.9 %shard_map.255 = (bf16[3,512,768]{2,1,0:T(8,128)(2,1)}, bf16[3,768,768]{2,1,0:T(8,128)(2,1)}) custom-call(s32[1]{0:T(128)} %dynamic_slice.57.len_ref, bf16[512,768]{1,0:T(8,128)(2,1)} %copy.71.q_ref, bf16[512,768]{1,0:T(8,128)(2,1)} %copy.72.k_ref, bf16[512,768]{1,0:T(8,128)(2,1)} %copy.73.v_ref, bf16[512,768]{1,0:T(8,128)(2,1)} %copy.78.grad_ref, ...), custom_call_target="tpu_custom_call" | custom-call | flops 3221225472 | bytes 7864320 | tf_op jit(solution)/shard_map/pallas_call | solution.py:123
  409.6 1.5 collective-permute-start.10
  411.6 1.9 fusion.13
  414.0 1.7 slice_reduce_fusion
  416.6 1.7 collective-permute-start.11
  418.3 1.2 convert_add_fusion.1
  421.1 1.7 collective-permute-start.14
  422.8 10.5 %collective-permute-done.8 = bf16[192,768]{1,0:T(8,128)(2,1)S(1)} collective-permute-done((bf16[192,768]{1,0:T(8,128)(2,1)S(1)}, bf16[192,768]{1,0:T(8,128)(2,1)S(1)}, u32[]{:S(2)}, u32[]{:S(2)}) %collective-permute-start.8) | collective-permute-done | bytes 294944 | tf_op jit(solution)/shard_map/ppermute | solution.py:181
  433.5 1.3 collective-permute-start.9
  434.8 10.6 %collective-permute-done.14 = bf16[192,768]{1,0:T(8,128)(2,1)S(1)} collective-permute-done((bf16[192,768]{1,0:T(8,128)(2,1)S(1)}, bf16[192,768]{1,0:T(8,128)(2,1)S(1)}, u32[]{:S(2)}, u32[]{:S(2)}) %collective-permute-start.14) | collective-permute-done | bytes 294944 | tf_op jit(solution)/shard_map/ppermute | solution.py:196
  445.7 17.1 %reduce-scatter.9.cloned.1.call-done = bf16[288,768]{1,0:T(8,128)(2,1)} async-done(((bf16[2304,768]{1,0:T(8,128)(2,1)}), bf16[288,768]{1,0:T(8,128)(2,1)}) %reduce-scatter.9.cloned.1.call-update) | async-done | bytes 442384 | tf_op jit(solution)/shard_map/reduce_scatter | solution.py:374
  466.4 1.6 maximum_convert_fusion.1
  468.6 1.6 maximum_convert_fusion
  470.2 18.7 %reduce-scatter.11.cloned.1.call-done = bf16[1,416,192]{1,2,0:T(8,128)(2,1)} async-done(((bf16[4,416,192]{1,2,0:T(8,128)(2,1)}), bf16[1,416,192]{1,2,0:T(8,128)(2,1)}) %reduce-scatter.11.cloned.1.call-update) | async-done | bytes 159760 | tf_op jit(solution)/shard_map/reduce_scatter | solution.py:381
  488.9 1.3 fusion.52
  490.2 1.5 copy.79
  492.3 2.1 fusion.25
  494.4 2.2 fusion.22
  496.6 3.3 fusion.11
  499.9 16.0 %all-gather.15.cloned.1.call-done = bf16[8,416,192]{1,2,0:T(8,128)(2,1)} async-done(((bf16[1,416,192]{1,2,0:T(8,128)(2,1)}), bf16[8,416,192]{1,2,0:T(8,128)(2,1)}) %all-gather.15.cloned.1.call-update) | async-done | bytes 1277968 | tf_op jit(solution)/shard_map/all_gather | solution.py:395
  515.9 1.8 convert_element_type.259
  519.8 2.1 copy.83
  521.9 3.0 copy.91
  (206 shorter events, 33.4 us)
Async XLA Ops:
  7.2 156.6 %copy-start = (bf16[768,768]{1,0:T(8,128)(2,1)S(1)}, bf16[768,768]{1,0:T(8,128)(2,1)}, u32[]{:S(2)}) copy-start(bf16[768,768]{1,0:T(8,128)(2,1)} %param.24) | copy-start | bytes 3538948
  7.2 1.4 copy-start.35
  7.2 1.5 copy-start.27
  7.2 59.4 %all-gather.13.cloned.1.call-start = ((), (), s32[]{:S(2)}) async-start(), calls=%async_computation.10 | async-start | bytes 3194880 | tf_op jit(solution)/shard_map/all_gather | solution.py:239
  8.6 58.0 %copy-start.39 = (s32[4]{0:T(128)S(1)}, s32[4]{0:T(128)}, u32[]{:S(2)}) copy-start(s32[4]{0:T(128)} %param.17) | copy-start | bytes 52
  9.8 154.0 %all-gather.9.cloned.1.call-start = ((), (), s32[]{:S(2)}) async-start(), calls=%async_computation.4 | async-start | bytes 3932160 | tf_op jit(solution)/shard_map/all_gather | solution.py:273
  66.6 5.2 collective-permute-start
  67.2 7.9 %copy-start.37 = (bf16[512,768]{1,0:T(8,128)(2,1)S(1)}, bf16[512,768]{1,0:T(8,128)(2,1)}, u32[]{:S(2)}) copy-start(bf16[512,768]{1,0:T(8,128)(2,1)} %rest_0_.1) | copy-start | bytes 2359300
  74.7 1.5 copy-start.13
  74.7 2.3 copy-start.14
  95.6 1.4 copy-start.38
  100.2 1.3 copy-start.34
  101.4 134.0 %reduce-scatter.5.cloned.1.call-start = ((), (), s32[]{:S(2)}) async-start(), calls=%async_computation.5 | async-start | bytes 3932160 | tf_op jit(solution)/shard_map/reduce_scatter | solution.py:277
  163.8 8.4 %copy-start.36 = (bf16[768,768]{1,0:T(8,128)(2,1)S(1)}, bf16[768,768]{1,0:T(8,128)(2,1)}, u32[]{:S(2)}) copy-start(bf16[768,768]{1,0:T(8,128)(2,1)} %param.26) | copy-start | bytes 3538948
  170.5 1.7 copy-start.40
  176.2 59.2 %copy-start.32 = (f32[768]{0:T(1024)S(1)}, f32[768]{0:T(1024)}, u32[]{:S(2)}) copy-start(f32[768]{0:T(1024)} %param.27) | copy-start | bytes 9220
  176.2 130.2 %all-gather.11.cloned.1.call-start = ((), (), s32[]{:S(2)}) async-start(), calls=%async_computation.6 | async-start | bytes 3932160 | tf_op jit(solution)/shard_map/all_gather | solution.py:289
  237.2 1.1 copy-start.16
  237.2 1.1 copy-start.31
  237.5 1.5 copy-start.33
  240.6 1.1 copy-start.2
  242.9 135.8 %reduce-scatter.7.cloned.1.call-start = ((), (), s32[]{:S(2)}) async-start(), calls=%async_computation.7 | async-start | bytes 3932160 | tf_op jit(solution)/shard_map/reduce_scatter | solution.py:303
  313.8 1.7 copy-start.41
  319.5 143.3 %reduce-scatter.9.cloned.1.call-start = ((), (), s32[]{:S(2)}) async-start(), calls=%async_computation.8 | async-start | bytes 3981312 | tf_op jit(solution)/shard_map/reduce_scatter | solution.py:374
  328.2 1.4 copy-start.8
  329.7 13.2 %collective-permute-start.4 = (bf16[384,768]{1,0:T(8,128)(2,1)S(1)}, bf16[384,768]{1,0:T(8,128)(2,1)}, u32[]{:S(2)}, u32[]{:S(2)}) collective-permute-start(bf16[384,768]{1,0:T(8,128)(2,1)S(1)} %dynamic-slice_convert_fusion.1), channel_id=1, source_target_pairs={{0,4},{4,0},{8,12},{12,8},{16,20},{20,16},{24,28},{28,24},{1,5},{5... | collective-permute-start | bytes 1769480 | tf_op jit(solution)/shard_map/ppermute | solution.py:181
  338.3 1.4 copy-start.6
  339.7 6.0 %collective-permute-start.1 = (bf16[384,768]{1,0:T(8,128)(2,1)S(1)}, bf16[384,768]{1,0:T(8,128)(2,1)}, u32[]{:S(2)}, u32[]{:S(2)}) collective-permute-start(bf16[384,768]{1,0:T(8,128)(2,1)S(1)} %dynamic-slice_convert_fusion.2), channel_id=1, source_target_pairs={{0,4},{4,0},{8,12},{12,8},{16,20},{20,16},{24,28},{28,24},{1,5},{5... | collective-permute-start | bytes 1769480 | tf_op jit(solution)/shard_map/ppermute | solution.py:181
  340.3 2.6 copy-start.9
  342.9 2.8 copy-start.7
  344.3 9.9 %collective-permute-start.5 = (bf16[192,768]{1,0:T(8,128)(2,1)S(1)}, bf16[192,768]{1,0:T(8,128)(2,1)S(1)}, u32[]{:S(2)}, u32[]{:S(2)}) collective-permute-start(bf16[192,768]{1,0:T(8,128)(2,1)S(1)} %dynamic-slice_convert_fusion.4), channel_id=1, source_target_pairs={{0,8},{4,12},{8,0},{12,4},{16,24},{20,28},{24,16},{28,20},{1,9},{5... | collective-permute-start | bytes 884744 | tf_op jit(solution)/shard_map/ppermute | solution.py:181
  346.9 12.7 %collective-permute-start.2 = (bf16[192,768]{1,0:T(8,128)(2,1)S(1)}, bf16[192,768]{1,0:T(8,128)(2,1)S(1)}, u32[]{:S(2)}, u32[]{:S(2)}) collective-permute-start(bf16[192,768]{1,0:T(8,128)(2,1)S(1)} %dynamic-slice_convert_fusion.5), channel_id=1, source_target_pairs={{0,8},{4,12},{8,0},{12,4},{16,24},{20,28},{24,16},{28,20},{1,9},{5... | collective-permute-start | bytes 884744 | tf_op jit(solution)/shard_map/ppermute | solution.py:181
  354.3 6.8 %collective-permute-start.6 = (bf16[96,768]{1,0:T(8,128)(2,1)S(1)}, bf16[96,768]{1,0:T(8,128)(2,1)S(1)}, u32[]{:S(2)}, u32[]{:S(2)}) collective-permute-start(bf16[96,768]{1,0:T(8,128)(2,1)S(1)} %dynamic-slice_convert_fusion.7), channel_id=1, source_target_pairs={{0,16},{4,20},{8,24},{12,28},{16,0},{20,4},{24,8},{28,12},{1,17},{... | collective-permute-start | bytes 442376 | tf_op jit(solution)/shard_map/ppermute | solution.py:181
  359.7 5.2 collective-permute-start.3
  378.7 2.6 copy-start.3
  378.7 2.6 copy-start.17
  382.2 2.7 copy-start.11
  382.2 1.8 copy-start.18
  409.0 79.9 %reduce-scatter.11.cloned.1.call-start = ((), (), s32[]{:S(2)}) async-start(), calls=%async_computation.9 | async-start | bytes 983040 | tf_op jit(solution)/shard_map/reduce_scatter | solution.py:381
  409.6 7.0 %collective-permute-start.10 = (bf16[96,768]{1,0:T(8,128)(2,1)S(1)}, bf16[96,768]{1,0:T(8,128)(2,1)S(1)}, u32[]{:S(2)}, u32[]{:S(2)}) collective-permute-start(bf16[96,768]{1,0:T(8,128)(2,1)S(1)} %convert_add_fusion.8), channel_id=1, source_target_pairs={{0,16},{4,20},{8,24},{12,28},{16,0},{20,4},{24,8},{28,12},{1,17},{... | collective-permute-start | bytes 442376 | tf_op jit(solution)/shard_map/ppermute | solution.py:196
  411.1 8.9 %collective-permute-start.13 = (bf16[96,768]{1,0:T(8,128)(2,1)}, bf16[96,768]{1,0:T(8,128)(2,1)}, u32[]{:S(2)}, u32[]{:S(2)}) collective-permute-start(bf16[96,768]{1,0:T(8,128)(2,1)} %convert_add_fusion.7), channel_id=1, source_target_pairs={{0,16},{4,20},{8,24},{12,28},{16,0},{20,4},{24,8},{28,12},{1,17},{... | collective-permute-start | bytes 442376 | tf_op jit(solution)/shard_map/ppermute | solution.py:196
  413.7 4.7 collective-permute-start.7
  416.6 18.2 %collective-permute-start.11 = (bf16[192,768]{1,0:T(8,128)(2,1)S(1)}, bf16[192,768]{1,0:T(8,128)(2,1)S(1)}, u32[]{:S(2)}, u32[]{:S(2)}) collective-permute-start(bf16[192,768]{1,0:T(8,128)(2,1)S(1)} %pad_maximum_fusion.3), channel_id=1, source_target_pairs={{0,8},{4,12},{8,0},{12,4},{16,24},{20,28},{24,16},{28,20},{1,9},{5... | collective-permute-start | bytes 884744 | tf_op jit(solution)/shard_map/ppermute | solution.py:196
  419.6 13.8 %collective-permute-start.8 = (bf16[192,768]{1,0:T(8,128)(2,1)S(1)}, bf16[192,768]{1,0:T(8,128)(2,1)S(1)}, u32[]{:S(2)}, u32[]{:S(2)}) collective-permute-start(bf16[192,768]{1,0:T(8,128)(2,1)S(1)} %dynamic-slice_convert_fusion.3), channel_id=1, source_target_pairs={{0,8},{4,12},{8,0},{12,4},{16,24},{20,28},{24,16},{28,20},{1,9},{5... | collective-permute-start | bytes 884744 | tf_op jit(solution)/shard_map/ppermute | solution.py:181
  421.1 24.3 %collective-permute-start.14 = (bf16[192,768]{1,0:T(8,128)(2,1)S(1)}, bf16[192,768]{1,0:T(8,128)(2,1)S(1)}, u32[]{:S(2)}, u32[]{:S(2)}) collective-permute-start(bf16[192,768]{1,0:T(8,128)(2,1)S(1)} %pad_maximum_fusion.4), channel_id=1, source_target_pairs={{0,8},{4,12},{8,0},{12,4},{16,24},{20,28},{24,16},{28,20},{1,9},{5... | collective-permute-start | bytes 884744 | tf_op jit(solution)/shard_map/ppermute | solution.py:196
  433.4 29.4 %copy-start.28 = (bf16[32,768]{1,0:T(8,128)(2,1)S(1)}, bf16[32,768]{1,0:T(8,128)(2,1)}, u32[]{:S(2)}) copy-start(bf16[32,768]{1,0:T(8,128)(2,1)} %fusion.40) | copy-start | bytes 147460
  433.5 12.2 %collective-permute-start.9 = (bf16[96,768]{1,0:T(8,128)(2,1)S(1)}, bf16[96,768]{1,0:T(8,128)(2,1)S(1)}, u32[]{:S(2)}, u32[]{:S(2)}) collective-permute-start(bf16[96,768]{1,0:T(8,128)(2,1)S(1)} %dynamic-slice_convert_fusion.6), channel_id=1, source_target_pairs={{0,16},{4,20},{8,24},{12,28},{16,0},{20,4},{24,8},{28,12},{1,17},{... | collective-permute-start | bytes 442376 | tf_op jit(solution)/shard_map/ppermute | solution.py:181
  445.6 20.6 %collective-permute-start.15 = (bf16[384,768]{1,0:T(8,128)(2,1)S(1)}, bf16[384,768]{1,0:T(8,128)(2,1)S(1)}, u32[]{:S(2)}, u32[]{:S(2)}) collective-permute-start(bf16[384,768]{1,0:T(8,128)(2,1)S(1)} %pad_maximum_fusion.2), channel_id=1, source_target_pairs={{0,4},{4,0},{8,12},{12,8},{16,20},{20,16},{24,28},{28,24},{1,5},{5... | collective-permute-start | bytes 1769480 | tf_op jit(solution)/shard_map/ppermute | solution.py:196
  465.1 50.8 %all-gather.15.cloned.1.call-start = ((), (), s32[]{:S(2)}) async-start(), calls=%async_computation.11 | async-start | bytes 1769472 | tf_op jit(solution)/shard_map/all_gather | solution.py:395
  466.2 2.2 collective-permute-start.12
  468.6 20.3 %copy-start.10 = (bf16[3,512,768]{2,1,0:T(8,128)(2,1)S(1)}, bf16[3,512,768]{2,1,0:T(8,128)(2,1)}, u32[]{:S(2)}) copy-start(bf16[3,512,768]{2,1,0:T(8,128)(2,1)} %get-tuple-element.22) | copy-start | bytes 7077892
  490.2 1.5 copy-start.15
  494.4 2.2 copy-start.12
  517.7 1.9 copy-start.4
  521.9 3.0 copy-start.5
  521.9 10.4 %copy-start.1 = (bf16[768,768]{1,0:T(8,128)(2,1)S(1)}, bf16[768,768]{1,0:T(8,128)(2,1)}, u32[]{:S(2)}) copy-start(bf16[768,768]{1,0:T(8,128)(2,1)} %param.24) | copy-start | bytes 3538948
  524.9 6.3 %copy-start.19 = (f32[96,192]{0,1:T(8,128)S(1)}, f32[96,192]{0,1:T(8,128)}, u32[]{:S(2)}) copy-start(f32[96,192]{0,1:T(8,128)} %get-tuple-element.92) | copy-start | bytes 221188
  524.9 6.3 %copy-start.20 = (f32[96,192]{0,1:T(8,128)S(1)}, f32[96,192]{0,1:T(8,128)}, u32[]{:S(2)}) copy-start(f32[96,192]{0,1:T(8,128)} %get-tuple-element.93) | copy-start | bytes 221188
  524.9 6.3 %copy-start.21 = (f32[96,192]{0,1:T(8,128)S(1)}, f32[96,192]{0,1:T(8,128)}, u32[]{:S(2)}) copy-start(f32[96,192]{0,1:T(8,128)} %get-tuple-element.94) | copy-start | bytes 221188
  524.9 6.3 %copy-start.22 = (f32[96,192]{0,1:T(8,128)S(1)}, f32[96,192]{0,1:T(8,128)}, u32[]{:S(2)}) copy-start(f32[96,192]{0,1:T(8,128)} %get-tuple-element.95) | copy-start | bytes 221188
  524.9 6.3 %copy-start.23 = (f32[96,192]{0,1:T(8,128)S(1)}, f32[96,192]{0,1:T(8,128)}, u32[]{:S(2)}) copy-start(f32[96,192]{0,1:T(8,128)} %get-tuple-element.96) | copy-start | bytes 221188
  524.9 6.3 %copy-start.24 = (f32[96,192]{0,1:T(8,128)S(1)}, f32[96,192]{0,1:T(8,128)}, u32[]{:S(2)}) copy-start(f32[96,192]{0,1:T(8,128)} %get-tuple-element.97) | copy-start | bytes 221188
  525.0 6.3 %copy-start.25 = (f32[96,192]{0,1:T(8,128)S(1)}, f32[96,192]{0,1:T(8,128)}, u32[]{:S(2)}) copy-start(f32[96,192]{0,1:T(8,128)} %get-tuple-element.98) | copy-start | bytes 221188
  525.0 6.3 %copy-start.26 = (f32[96,192]{0,1:T(8,128)S(1)}, f32[96,192]{0,1:T(8,128)}, u32[]{:S(2)}) copy-start(f32[96,192]{0,1:T(8,128)} %get-tuple-element.99) | copy-start | bytes 221188
  (2 other events, 1.4 us)
Sparse Core Ops, SparseCore 0:
  10.2 56.3 all-gather.12
  101.5 62.2 all-gather.8
  176.3 59.0 reduce-scatter.4
  243.0 63.3 all-gather.10
  319.6 59.0 reduce-scatter.6
  409.1 53.6 reduce-scatter.8
  465.7 23.1 reduce-scatter.10
  490.8 25.0 all-gather.14

commit v18 on v17

--- a/solution.py
+++ b/solution.py
@@ -39,7 +39,7 @@
     scores = jnp.where(col < length, scores, NEG)
     top = jnp.max(scores, axis=1, keepdims=True)
     raised = jnp.exp(scores - top)
-    return raised / jnp.sum(raised, axis=1, keepdims=True)
+    return raised * (1.0 / jnp.sum(raised, axis=1, keepdims=True))
 
 
 def _fwd_kernel(len_ref, q_ref, k_ref, v_ref, out_ref, *, heads, factor):

time: 540 us -> 540 us (level)
  no operation moved by 1% of the time
where the time goes in v18:
time: 540 us; the launch traced here: 539 us
  waiting for transfers between devices  347 us (64%)
  Pallas kernels  49.4 us (9%)
  local copies, waits for them, and re-layouts  40.6 us (8%)
  matrix products  38.5 us (7%)
  other arithmetic  35.1 us (6%)
  between operations  14.9 us (3%)
  starting transfers between devices  13.9 us (3%)
    all_gather x1, waiting for transfers between devices, per_device(): branch_rows = lax.all_gather(branch_grad, 'tensor', axis=0, tiled=True)  63.3 us
    all_gather x1, waiting for transfers between devices, per_device(): ffn_rows = lax.all_gather(middle_low, 'tensor', axis=0, tiled=True)  62.3 us
    reduce_scatter x1, waiting for transfers between devices, per_device(): lax.psum_scatter(jnp.dot(hidden, down_weight, preferred_element_type=jnp....  59.2 us
    all_gather x1, waiting for transfers between devices, per_device(): mine = lax.all_gather(mine, 'tensor', axis=0, tiled=False)  56.8 us
    ppermute x9, waiting for transfers between devices, dp_halve(): got = lax.ppermute(give, 'dp', [(i, i ^ 1 << step) for i in range(dp_size)])  24.1 us
    pallas_call x1, Pallas kernels, attention_backward(): pl.pallas_call(functools.partial(_bwd_kernel, heads=pair, factor=factor),...  22.9 us
    reduce_scatter x1, waiting for transfers between devices, per_device(): lax.psum_scatter(joined.reshape(joined.shape[0], groups, shard).transpose...  18.7 us
    reduce_scatter x1, waiting for transfers between devices, per_device(): lax.psum_scatter(grad_qkv_low.reshape(3 * width, width), 'dp', scatter_di...  17.1 us
  transfers between devices with their start and end apart: 24, of which 15 were waited for; matrix products, arithmetic and copies ran while one was open for 7% of the time, Pallas kernels for 3%

profile of v18, /device:TPU:0, one launch (start us, length us, event | category | flops | bytes accessed | tf_op | source)
XLA Modules:
  0.0 539.1 jit_solution(16135501716912936914)
XLA Ops:
  7.3 1.3 slice_bitcast_fusion.2
  9.8 56.8 %all-gather.13.cloned.1.call-done = bf16[4,1544,192]{1,2,0:T(8,128)(2,1)} async-done(((bf16[1,1544,192]{1,2,0:T(8,128)(2,1)}), bf16[4,1544,192]{1,2,0:T(8,128)(2,1)}) %all-gather.13.cloned.1.call-update) | async-done | bytes 2371600 | tf_op jit(solution)/shard_map/all_gather | solution.py:239
  67.2 4.6 collective-permute-done
  71.8 3.0 broadcast_select_fusion
  77.0 1.2 copy.73.v_ref
  78.2 2.1 add_convert_fusion.2
  80.3 1.2 copy.71.q_ref
  81.4 1.2 copy.72.k_ref
  82.6 13.0 %shard_map.254 = bf16[512,768]{1,0:T(8,128)(2,1)} custom-call(s32[1]{0:T(128)} %dynamic_slice.57.len_ref, bf16[512,768]{1,0:T(8,128)(2,1)} %copy.71.q_ref, bf16[512,768]{1,0:T(8,128)(2,1)} %copy.72.k_ref, bf16[512,768]{1,0:T(8,128)(2,1)} %copy.73.v_ref), custom_call_target="tpu_custom_call" | custom-call | flops 805306368 | bytes 3145728 | tf_op jit(solution)/shard_map/pallas_call | solution.py:92
  95.6 1.4 copy.74
  97.0 2.4 fusion.54
  100.2 1.2 fusion.14
  101.5 62.3 %all-gather.9.cloned.1.call-done.left_ref = bf16[2048,768]{1,0:T(8,128)(2,1)} async-done(((bf16[512,768]{1,0:T(8,128)(2,1)}), bf16[2048,768]{1,0:T(8,128)(2,1)}) %all-gather.9.cloned.1.call-update) | async-done | bytes 3145744 | tf_op jit(solution)/shard_map/all_gather | solution.py:273
  163.8 6.7 %multiply_convert_fusion = (bf16[2048,768]{1,0:T(8,128)(2,1)S(1)}, f32[2048,768]{1,0:T(8,128)}) fusion(f32[768]{0:T(1024)S(1)} %convert_element_type.208, bf16[2048,768]{1,0:T(8,128)(2,1)} %all-gather.9.cloned.1.call-done.left_ref, bf16[768,768]{1,0:T(8,128)(2,1)S(1)} %copy-done), kind=kOutput, calls=%fused_computation.8 | convolution fusion | flops 2425356288 | bytes 13765632 | tf_op jit(solution)/shard_map/dot_general | solution.py:274
  170.5 1.7 copy-done.40
  172.2 4.0 convolution_convert_fusion.1
  176.3 59.2 %reduce-scatter.5.cloned.1.call-done = bf16[512,768]{1,0:T(8,128)(2,1)} async-done(((bf16[2048,768]{1,0:T(8,128)(2,1)}), bf16[512,768]{1,0:T(8,128)(2,1)}) %reduce-scatter.5.cloned.1.call-update) | async-done | bytes 786448 | tf_op jit(solution)/shard_map/reduce_scatter | solution.py:277
  235.4 1.7 fusion.51
  239.0 1.6 fusion.50
  243.1 63.3 %all-gather.11.cloned.1.call-done.right_ref = bf16[2048,768]{1,0:T(8,128)(2,1)} async-done(((bf16[512,768]{1,0:T(8,128)(2,1)}), bf16[2048,768]{1,0:T(8,128)(2,1)}) %all-gather.11.cloned.1.call-update) | async-done | bytes 3145744 | tf_op jit(solution)/shard_map/all_gather | solution.py:289
  306.4 7.4 %convert_reduce_fusion = (bf16[768]{0:T(1024)(128)(2,1)S(1)}, bf16[2048,768]{1,0:T(8,128)(2,1)S(1)}) fusion(f32[2048,768]{1,0:T(8,128)} %get-tuple-element.129, f32[768]{0:T(1024)S(1)} %convert_element_type.208, bf16[2048,768]{1,0:T(8,128)(2,1)} %all-gather.11.cloned.1.call-done.right_ref, bf16[768,768]{1,0:T(8,128)(2,1)} %param.26), kind=kOutput, calls=%fused_computation.7 | convolution fusion | flops 2436365568 | bytes 13767168 | tf_op jit(solution)/shard_map/dot_general | solution.py:31
  313.8 1.7 copy-done.41
  315.5 4.0 convolution_convert_fusion
  319.6 6.8 %shard_map.257 = f32[768,768]{1,0:T(8,128)} custom-call(bf16[2048,768]{1,0:T(8,128)(2,1)} %copy-done.40, bf16[2048,768]{1,0:T(8,128)(2,1)} %all-gather.11.cloned.1.call-done.right_ref), custom_call_target="tpu_custom_call" | custom-call | flops 2415919104 | bytes 8650752 | tf_op jit(solution)/shard_map/pallas_call | solution.py:149
  326.4 1.8 convert_convert_fusion
  328.2 1.4 copy-done.8
  329.7 6.7 %shard_map.256 = f32[768,768]{1,0:T(8,128)} custom-call(bf16[2048,768]{1,0:T(8,128)(2,1)} %all-gather.9.cloned.1.call-done.left_ref, bf16[2048,768]{1,0:T(8,128)(2,1)} %copy-done.41), custom_call_target="tpu_custom_call" | custom-call | flops 2415919104 | bytes 8650752 | tf_op jit(solution)/shard_map/pallas_call | solution.py:149
  336.4 1.8 convert_convert_fusion.1
  338.3 1.4 copy-done.6
  340.3 2.5 slice.151
  342.9 1.3 convert_add_fusion.2
  344.3 1.4 collective-permute-start.5
  345.7 1.2 convert_add_fusion.3
  347.6 6.6 %collective-permute-done.5 = bf16[192,768]{1,0:T(8,128)(2,1)S(1)} collective-permute-done((bf16[192,768]{1,0:T(8,128)(2,1)S(1)}, bf16[192,768]{1,0:T(8,128)(2,1)S(1)}, u32[]{:S(2)}, u32[]{:S(2)}) %collective-permute-start.5) | collective-permute-done | bytes 294944 | tf_op jit(solution)/shard_map/ppermute | solution.py:181
  354.3 1.4 collective-permute-start.6
  355.7 3.9 collective-permute-done.2
  359.7 1.4 collective-permute-start.3
  361.8 3.1 collective-permute-done.3
  364.9 13.8 %reduce-scatter.7.cloned.1.call-done = bf16[512,768]{1,0:T(8,128)(2,1)} async-done(((bf16[2048,768]{1,0:T(8,128)(2,1)}), bf16[512,768]{1,0:T(8,128)(2,1)}) %reduce-scatter.7.cloned.1.call-update) | async-done | bytes 786448 | tf_op jit(solution)/shard_map/reduce_scatter | solution.py:303
  378.7 2.6 multiply_reduce_fusion
  382.4 1.6 copy-done.18
  386.1 22.9 %shard_map.255 = (bf16[3,512,768]{2,1,0:T(8,128)(2,1)}, bf16[3,768,768]{2,1,0:T(8,128)(2,1)}) custom-call(s32[1]{0:T(128)} %dynamic_slice.57.len_ref, bf16[512,768]{1,0:T(8,128)(2,1)} %copy.71.q_ref, bf16[512,768]{1,0:T(8,128)(2,1)} %copy.72.k_ref, bf16[512,768]{1,0:T(8,128)(2,1)} %copy.73.v_ref, bf16[512,768]{1,0:T(8,128)(2,1)} %copy.78.grad_ref, ...), custom_call_target="tpu_custom_call" | custom-call | flops 3221225472 | bytes 7864320 | tf_op jit(solution)/shard_map/pallas_call | solution.py:123
  409.6 1.5 collective-permute-start.10
  411.6 1.9 fusion.13
  414.0 1.7 slice_reduce_fusion
  416.6 1.7 collective-permute-start.11
  418.3 1.2 convert_add_fusion.1
  421.1 1.7 collective-permute-start.14
  422.8 10.5 %collective-permute-done.8 = bf16[192,768]{1,0:T(8,128)(2,1)S(1)} collective-permute-done((bf16[192,768]{1,0:T(8,128)(2,1)S(1)}, bf16[192,768]{1,0:T(8,128)(2,1)S(1)}, u32[]{:S(2)}, u32[]{:S(2)}) %collective-permute-start.8) | collective-permute-done | bytes 294944 | tf_op jit(solution)/shard_map/ppermute | solution.py:181
  433.5 1.3 collective-permute-start.9
  434.8 10.6 %collective-permute-done.14 = bf16[192,768]{1,0:T(8,128)(2,1)S(1)} collective-permute-done((bf16[192,768]{1,0:T(8,128)(2,1)S(1)}, bf16[192,768]{1,0:T(8,128)(2,1)S(1)}, u32[]{:S(2)}, u32[]{:S(2)}) %collective-permute-start.14) | collective-permute-done | bytes 294944 | tf_op jit(solution)/shard_map/ppermute | solution.py:196
  445.7 17.1 %reduce-scatter.9.cloned.1.call-done = bf16[288,768]{1,0:T(8,128)(2,1)} async-done(((bf16[2304,768]{1,0:T(8,128)(2,1)}), bf16[288,768]{1,0:T(8,128)(2,1)}) %reduce-scatter.9.cloned.1.call-update) | async-done | bytes 442384 | tf_op jit(solution)/shard_map/reduce_scatter | solution.py:374
  466.4 1.6 maximum_convert_fusion.1
  468.6 1.6 maximum_convert_fusion
  470.2 18.7 %reduce-scatter.11.cloned.1.call-done = bf16[1,416,192]{1,2,0:T(8,128)(2,1)} async-done(((bf16[4,416,192]{1,2,0:T(8,128)(2,1)}), bf16[1,416,192]{1,2,0:T(8,128)(2,1)}) %reduce-scatter.11.cloned.1.call-update) | async-done | bytes 159760 | tf_op jit(solution)/shard_map/reduce_scatter | solution.py:381
  488.9 1.3 fusion.52
  490.2 1.5 copy.79
  492.3 2.1 fusion.25
  494.4 2.2 fusion.22
  496.6 3.3 fusion.11
  499.9 16.0 %all-gather.15.cloned.1.call-done = bf16[8,416,192]{1,2,0:T(8,128)(2,1)} async-done(((bf16[1,416,192]{1,2,0:T(8,128)(2,1)}), bf16[8,416,192]{1,2,0:T(8,128)(2,1)}) %all-gather.15.cloned.1.call-update) | async-done | bytes 1277968 | tf_op jit(solution)/shard_map/all_gather | solution.py:395
  515.9 1.8 convert_element_type.259
  519.8 2.1 copy.83
  521.9 3.0 copy.91
  (206 shorter events, 33.4 us)
Async XLA Ops:
  7.2 156.6 %copy-start = (bf16[768,768]{1,0:T(8,128)(2,1)S(1)}, bf16[768,768]{1,0:T(8,128)(2,1)}, u32[]{:S(2)}) copy-start(bf16[768,768]{1,0:T(8,128)(2,1)} %param.24) | copy-start | bytes 3538948
  7.2 1.4 copy-start.35
  7.2 1.5 copy-start.27
  7.2 59.4 %all-gather.13.cloned.1.call-start = ((), (), s32[]{:S(2)}) async-start(), calls=%async_computation.10 | async-start | bytes 3194880 | tf_op jit(solution)/shard_map/all_gather | solution.py:239
  8.6 58.0 %copy-start.39 = (s32[4]{0:T(128)S(1)}, s32[4]{0:T(128)}, u32[]{:S(2)}) copy-start(s32[4]{0:T(128)} %param.17) | copy-start | bytes 52
  9.8 154.0 %all-gather.9.cloned.1.call-start = ((), (), s32[]{:S(2)}) async-start(), calls=%async_computation.4 | async-start | bytes 3932160 | tf_op jit(solution)/shard_map/all_gather | solution.py:273
  66.6 5.2 collective-permute-start
  67.2 7.9 %copy-start.37 = (bf16[512,768]{1,0:T(8,128)(2,1)S(1)}, bf16[512,768]{1,0:T(8,128)(2,1)}, u32[]{:S(2)}) copy-start(bf16[512,768]{1,0:T(8,128)(2,1)} %rest_0_.1) | copy-start | bytes 2359300
  74.7 1.5 copy-start.13
  74.7 2.3 copy-start.14
  95.6 1.4 copy-start.38
  100.2 1.3 copy-start.34
  101.4 134.0 %reduce-scatter.5.cloned.1.call-start = ((), (), s32[]{:S(2)}) async-start(), calls=%async_computation.5 | async-start | bytes 3932160 | tf_op jit(solution)/shard_map/reduce_scatter | solution.py:277
  163.8 8.4 %copy-start.36 = (bf16[768,768]{1,0:T(8,128)(2,1)S(1)}, bf16[768,768]{1,0:T(8,128)(2,1)}, u32[]{:S(2)}) copy-start(bf16[768,768]{1,0:T(8,128)(2,1)} %param.26) | copy-start | bytes 3538948
  170.5 1.7 copy-start.40
  176.2 59.2 %copy-start.32 = (f32[768]{0:T(1024)S(1)}, f32[768]{0:T(1024)}, u32[]{:S(2)}) copy-start(f32[768]{0:T(1024)} %param.27) | copy-start | bytes 9220
  176.2 130.2 %all-gather.11.cloned.1.call-start = ((), (), s32[]{:S(2)}) async-start(), calls=%async_computation.6 | async-start | bytes 3932160 | tf_op jit(solution)/shard_map/all_gather | solution.py:289
  237.2 1.1 copy-start.16
  237.2 1.1 copy-start.31
  237.5 1.5 copy-start.33
  240.6 1.1 copy-start.2
  242.9 135.8 %reduce-scatter.7.cloned.1.call-start = ((), (), s32[]{:S(2)}) async-start(), calls=%async_computation.7 | async-start | bytes 3932160 | tf_op jit(solution)/shard_map/reduce_scatter | solution.py:303
  313.8 1.7 copy-start.41
  319.5 143.3 %reduce-scatter.9.cloned.1.call-start = ((), (), s32[]{:S(2)}) async-start(), calls=%async_computation.8 | async-start | bytes 3981312 | tf_op jit(solution)/shard_map/reduce_scatter | solution.py:374
  328.2 1.4 copy-start.8
  329.7 13.2 %collective-permute-start.4 = (bf16[384,768]{1,0:T(8,128)(2,1)S(1)}, bf16[384,768]{1,0:T(8,128)(2,1)}, u32[]{:S(2)}, u32[]{:S(2)}) collective-permute-start(bf16[384,768]{1,0:T(8,128)(2,1)S(1)} %dynamic-slice_convert_fusion.1), channel_id=1, source_target_pairs={{0,4},{4,0},{8,12},{12,8},{16,20},{20,16},{24,28},{28,24},{1,5},{5... | collective-permute-start | bytes 1769480 | tf_op jit(solution)/shard_map/ppermute | solution.py:181
  338.3 1.4 copy-start.6
  339.7 6.0 %collective-permute-start.1 = (bf16[384,768]{1,0:T(8,128)(2,1)S(1)}, bf16[384,768]{1,0:T(8,128)(2,1)}, u32[]{:S(2)}, u32[]{:S(2)}) collective-permute-start(bf16[384,768]{1,0:T(8,128)(2,1)S(1)} %dynamic-slice_convert_fusion.2), channel_id=1, source_target_pairs={{0,4},{4,0},{8,12},{12,8},{16,20},{20,16},{24,28},{28,24},{1,5},{5... | collective-permute-start | bytes 1769480 | tf_op jit(solution)/shard_map/ppermute | solution.py:181
  340.3 2.6 copy-start.9
  342.9 2.8 copy-start.7
  344.3 9.9 %collective-permute-start.5 = (bf16[192,768]{1,0:T(8,128)(2,1)S(1)}, bf16[192,768]{1,0:T(8,128)(2,1)S(1)}, u32[]{:S(2)}, u32[]{:S(2)}) collective-permute-start(bf16[192,768]{1,0:T(8,128)(2,1)S(1)} %dynamic-slice_convert_fusion.4), channel_id=1, source_target_pairs={{0,8},{4,12},{8,0},{12,4},{16,24},{20,28},{24,16},{28,20},{1,9},{5... | collective-permute-start | bytes 884744 | tf_op jit(solution)/shard_map/ppermute | solution.py:181
  346.9 12.7 %collective-permute-start.2 = (bf16[192,768]{1,0:T(8,128)(2,1)S(1)}, bf16[192,768]{1,0:T(8,128)(2,1)S(1)}, u32[]{:S(2)}, u32[]{:S(2)}) collective-permute-start(bf16[192,768]{1,0:T(8,128)(2,1)S(1)} %dynamic-slice_convert_fusion.5), channel_id=1, source_target_pairs={{0,8},{4,12},{8,0},{12,4},{16,24},{20,28},{24,16},{28,20},{1,9},{5... | collective-permute-start | bytes 884744 | tf_op jit(solution)/shard_map/ppermute | solution.py:181
  354.3 6.8 %collective-permute-start.6 = (bf16[96,768]{1,0:T(8,128)(2,1)S(1)}, bf16[96,768]{1,0:T(8,128)(2,1)S(1)}, u32[]{:S(2)}, u32[]{:S(2)}) collective-permute-start(bf16[96,768]{1,0:T(8,128)(2,1)S(1)} %dynamic-slice_convert_fusion.7), channel_id=1, source_target_pairs={{0,16},{4,20},{8,24},{12,28},{16,0},{20,4},{24,8},{28,12},{1,17},{... | collective-permute-start | bytes 442376 | tf_op jit(solution)/shard_map/ppermute | solution.py:181
  359.7 5.2 collective-permute-start.3
  378.7 2.6 copy-start.3
  378.7 2.6 copy-start.17
  382.2 2.7 copy-start.11
  382.2 1.8 copy-start.18
  409.0 79.9 %reduce-scatter.11.cloned.1.call-start = ((), (), s32[]{:S(2)}) async-start(), calls=%async_computation.9 | async-start | bytes 983040 | tf_op jit(solution)/shard_map/reduce_scatter | solution.py:381
  409.6 7.0 %collective-permute-start.10 = (bf16[96,768]{1,0:T(8,128)(2,1)S(1)}, bf16[96,768]{1,0:T(8,128)(2,1)S(1)}, u32[]{:S(2)}, u32[]{:S(2)}) collective-permute-start(bf16[96,768]{1,0:T(8,128)(2,1)S(1)} %convert_add_fusion.8), channel_id=1, source_target_pairs={{0,16},{4,20},{8,24},{12,28},{16,0},{20,4},{24,8},{28,12},{1,17},{... | collective-permute-start | bytes 442376 | tf_op jit(solution)/shard_map/ppermute | solution.py:196
  411.1 8.9 %collective-permute-start.13 = (bf16[96,768]{1,0:T(8,128)(2,1)}, bf16[96,768]{1,0:T(8,128)(2,1)}, u32[]{:S(2)}, u32[]{:S(2)}) collective-permute-start(bf16[96,768]{1,0:T(8,128)(2,1)} %convert_add_fusion.7), channel_id=1, source_target_pairs={{0,16},{4,20},{8,24},{12,28},{16,0},{20,4},{24,8},{28,12},{1,17},{... | collective-permute-start | bytes 442376 | tf_op jit(solution)/shard_map/ppermute | solution.py:196
  413.7 4.7 collective-permute-start.7
  416.6 18.2 %collective-permute-start.11 = (bf16[192,768]{1,0:T(8,128)(2,1)S(1)}, bf16[192,768]{1,0:T(8,128)(2,1)S(1)}, u32[]{:S(2)}, u32[]{:S(2)}) collective-permute-start(bf16[192,768]{1,0:T(8,128)(2,1)S(1)} %pad_maximum_fusion.3), channel_id=1, source_target_pairs={{0,8},{4,12},{8,0},{12,4},{16,24},{20,28},{24,16},{28,20},{1,9},{5... | collective-permute-start | bytes 884744 | tf_op jit(solution)/shard_map/ppermute | solution.py:196
  419.6 13.8 %collective-permute-start.8 = (bf16[192,768]{1,0:T(8,128)(2,1)S(1)}, bf16[192,768]{1,0:T(8,128)(2,1)S(1)}, u32[]{:S(2)}, u32[]{:S(2)}) collective-permute-start(bf16[192,768]{1,0:T(8,128)(2,1)S(1)} %dynamic-slice_convert_fusion.3), channel_id=1, source_target_pairs={{0,8},{4,12},{8,0},{12,4},{16,24},{20,28},{24,16},{28,20},{1,9},{5... | collective-permute-start | bytes 884744 | tf_op jit(solution)/shard_map/ppermute | solution.py:181
  421.1 24.3 %collective-permute-start.14 = (bf16[192,768]{1,0:T(8,128)(2,1)S(1)}, bf16[192,768]{1,0:T(8,128)(2,1)S(1)}, u32[]{:S(2)}, u32[]{:S(2)}) collective-permute-start(bf16[192,768]{1,0:T(8,128)(2,1)S(1)} %pad_maximum_fusion.4), channel_id=1, source_target_pairs={{0,8},{4,12},{8,0},{12,4},{16,24},{20,28},{24,16},{28,20},{1,9},{5... | collective-permute-start | bytes 884744 | tf_op jit(solution)/shard_map/ppermute | solution.py:196
  433.4 29.4 %copy-start.28 = (bf16[32,768]{1,0:T(8,128)(2,1)S(1)}, bf16[32,768]{1,0:T(8,128)(2,1)}, u32[]{:S(2)}) copy-start(bf16[32,768]{1,0:T(8,128)(2,1)} %fusion.40) | copy-start | bytes 147460
  433.5 12.2 %collective-permute-start.9 = (bf16[96,768]{1,0:T(8,128)(2,1)S(1)}, bf16[96,768]{1,0:T(8,128)(2,1)S(1)}, u32[]{:S(2)}, u32[]{:S(2)}) collective-permute-start(bf16[96,768]{1,0:T(8,128)(2,1)S(1)} %dynamic-slice_convert_fusion.6), channel_id=1, source_target_pairs={{0,16},{4,20},{8,24},{12,28},{16,0},{20,4},{24,8},{28,12},{1,17},{... | collective-permute-start | bytes 442376 | tf_op jit(solution)/shard_map/ppermute | solution.py:181
  445.6 20.6 %collective-permute-start.15 = (bf16[384,768]{1,0:T(8,128)(2,1)S(1)}, bf16[384,768]{1,0:T(8,128)(2,1)S(1)}, u32[]{:S(2)}, u32[]{:S(2)}) collective-permute-start(bf16[384,768]{1,0:T(8,128)(2,1)S(1)} %pad_maximum_fusion.2), channel_id=1, source_target_pairs={{0,4},{4,0},{8,12},{12,8},{16,20},{20,16},{24,28},{28,24},{1,5},{5... | collective-permute-start | bytes 1769480 | tf_op jit(solution)/shard_map/ppermute | solution.py:196
  465.1 50.8 %all-gather.15.cloned.1.call-start = ((), (), s32[]{:S(2)}) async-start(), calls=%async_computation.11 | async-start | bytes 1769472 | tf_op jit(solution)/shard_map/all_gather | solution.py:395
  466.2 2.2 collective-permute-start.12
  468.6 20.3 %copy-start.10 = (bf16[3,512,768]{2,1,0:T(8,128)(2,1)S(1)}, bf16[3,512,768]{2,1,0:T(8,128)(2,1)}, u32[]{:S(2)}) copy-start(bf16[3,512,768]{2,1,0:T(8,128)(2,1)} %get-tuple-element.22) | copy-start | bytes 7077892
  490.2 1.5 copy-start.15
  494.4 2.2 copy-start.12
  517.7 1.9 copy-start.4
  521.9 3.0 copy-start.5
  521.9 10.4 %copy-start.1 = (bf16[768,768]{1,0:T(8,128)(2,1)S(1)}, bf16[768,768]{1,0:T(8,128)(2,1)}, u32[]{:S(2)}) copy-start(bf16[768,768]{1,0:T(8,128)(2,1)} %param.24) | copy-start | bytes 3538948
  524.9 6.3 %copy-start.19 = (f32[96,192]{0,1:T(8,128)S(1)}, f32[96,192]{0,1:T(8,128)}, u32[]{:S(2)}) copy-start(f32[96,192]{0,1:T(8,128)} %get-tuple-element.92) | copy-start | bytes 221188
  524.9 6.3 %copy-start.20 = (f32[96,192]{0,1:T(8,128)S(1)}, f32[96,192]{0,1:T(8,128)}, u32[]{:S(2)}) copy-start(f32[96,192]{0,1:T(8,128)} %get-tuple-element.93) | copy-start | bytes 221188
  524.9 6.3 %copy-start.21 = (f32[96,192]{0,1:T(8,128)S(1)}, f32[96,192]{0,1:T(8,128)}, u32[]{:S(2)}) copy-start(f32[96,192]{0,1:T(8,128)} %get-tuple-element.94) | copy-start | bytes 221188
  524.9 6.3 %copy-start.22 = (f32[96,192]{0,1:T(8,128)S(1)}, f32[96,192]{0,1:T(8,128)}, u32[]{:S(2)}) copy-start(f32[96,192]{0,1:T(8,128)} %get-tuple-element.95) | copy-start | bytes 221188
  524.9 6.3 %copy-start.23 = (f32[96,192]{0,1:T(8,128)S(1)}, f32[96,192]{0,1:T(8,128)}, u32[]{:S(2)}) copy-start(f32[96,192]{0,1:T(8,128)} %get-tuple-element.96) | copy-start | bytes 221188
  524.9 6.3 %copy-start.24 = (f32[96,192]{0,1:T(8,128)S(1)}, f32[96,192]{0,1:T(8,128)}, u32[]{:S(2)}) copy-start(f32[96,192]{0,1:T(8,128)} %get-tuple-element.97) | copy-start | bytes 221188
  525.0 6.3 %copy-start.25 = (f32[96,192]{0,1:T(8,128)S(1)}, f32[96,192]{0,1:T(8,128)}, u32[]{:S(2)}) copy-start(f32[96,192]{0,1:T(8,128)} %get-tuple-element.98) | copy-start | bytes 221188
  525.0 6.3 %copy-start.26 = (f32[96,192]{0,1:T(8,128)S(1)}, f32[96,192]{0,1:T(8,128)}, u32[]{:S(2)}) copy-start(f32[96,192]{0,1:T(8,128)} %get-tuple-element.99) | copy-start | bytes 221188
  (2 other events, 1.4 us)
Sparse Core Ops, SparseCore 0:
  10.2 56.3 all-gather.12
  101.5 62.2 all-gather.8
  176.3 59.0 reduce-scatter.4
  243.0 63.3 all-gather.10
  319.6 59.0 reduce-scatter.6
  409.1 53.6 reduce-scatter.8
  465.7 23.1 reduce-scatter.10
  490.8 25.0 all-gather.14
